TPU v7x, 256 devices: a whole 4x4x8 slice. The times are simulated.
256 devices in a mesh: vel: 16 (over y, z_lo), space: 16 (over x, z_hi, core).
Axes of the slice: x: 4, y: 4, z: 8 (z_hi: 2, z_lo: 4; z = z_hi * 4 + z_lo), core: 2. Of those that a mesh axis runs over, the one named last changes fastest.
Arguments:
- initial: float32 [13824, 64, 128], P('vel', 'space'), as said below
- site_kind: int32 [64, 128], P('space'), may hold values from 0 to 2, as said below
Outputs:
- distribution: float32 [13824, 64, 128], P('vel', 'space')
- kelvin_level: float32 [64, 128], P('space')
Inputs may be any that keep to these rules, and one draw needn't show every extreme that they name: `site_kind`: 0 marks a gas cell, 1 a wall cell, 2 an inflow cell. `initial`: every entry is positive.
All inputs are finite; a program needn't handle non-finite values.
Results may differ from a plain program's by a relative error of at most 0.0003.
Values sent between devices are 32-bit elements; how exact they have to be, the bound alone decides.
No kernel may reach another device: no remote copies, remote signals or barrier semaphores. Data moves between devices by JAX's collectives and lax.ppermute only.
A program may use at most 64 MiB of HBM per device.

v0:
```python
import math

import jax
import jax.numpy as jnp
from jax import lax
from jax.sharding import PartitionSpec as P

NVX = 24
STEPS = 2


speed_limit = 4.0
courant = 0.1
diffusivity_ratio = 2.0 / 3.0
power_law_index = 0.81
encounter_rate = 0.25
wall_kelvin = 1.0
inflow_concentration = 1.0
inflow_speed = 0.5
inflow_kelvin = 1.0


def with_halo(block, sides, width):
    for axis, dim in sides:
        count = lax.axis_size(axis)
        forward = [(i, i + 1) for i in range(count - 1)]
        backward = [(target, source) for source, target in forward]
        low = lax.ppermute(
            lax.slice_in_dim(block, block.shape[dim] - width, None, axis=dim), axis, forward
        )
        high = lax.ppermute(lax.slice_in_dim(block, 0, width, axis=dim), axis, backward)
        block = jnp.concatenate([low, block, high], axis=dim)
    return block


def speeds(offset, amount):
    index = offset + jnp.arange(amount, dtype=jnp.int32)
    spacing = 2.0 * speed_limit / (NVX - 1)
    along_x_part = -speed_limit + spacing * (index // (NVX * NVX)).astype(jnp.float32)
    along_y_part = -speed_limit + spacing * (index // NVX % NVX).astype(jnp.float32)
    along_z_part = -speed_limit + spacing * (index % NVX).astype(jnp.float32)
    return (along_x_part, along_y_part, along_z_part)


def quad_weight():
    return (2.0 * speed_limit / (NVX - 1)) ** 3 / (2.0 * math.pi) ** 1.5


def minmod(left, right):
    return 0.5 * (jnp.sign(left) + jnp.sign(right)) * jnp.minimum(jnp.abs(left), jnp.abs(right))


def sweep(distribution_table, number, along):
    length = distribution_table.shape[along]

    def piece(source, low, high):
        return lax.slice_in_dim(source, low, high, axis=along)

    jumps = piece(distribution_table, 1, length) - piece(distribution_table, 0, length - 1)
    slopes = minmod(piece(jumps, 0, length - 2), piece(jumps, 1, length - 1))
    left_face = piece(distribution_table, 1, length - 2) + 0.5 * (1.0 - number) * piece(
        slopes, 0, length - 3
    )
    right_face = piece(distribution_table, 2, length - 1) - 0.5 * (1.0 + number) * piece(
        slopes, 1, length - 2
    )
    flux = number * jnp.where(number > 0, left_face, right_face)
    return piece(distribution_table, 2, length - 2) - (
        piece(flux, 1, length - 3) - piece(flux, 0, length - 4)
    )


def transport(padded, along_x_part, along_y_part):
    swept = sweep(padded, courant * along_x_part[:, None, None], 1)
    widened = jnp.pad(swept, ((0, 0), (0, 0), (2, 2)))
    return sweep(widened, courant * along_y_part[:, None, None], 2)


def macroscopic_moments(advected_distribution, along_x_part, along_y_part, along_z_part):
    magnitude_squares = (
        along_x_part * along_x_part + along_y_part * along_y_part + along_z_part * along_z_part
    )
    ones = jnp.ones_like(along_x_part)
    table = quad_weight() * jnp.stack(
        [ones, along_x_part, along_y_part, along_z_part, magnitude_squares]
    )
    local = jnp.einsum("kv,vrc->krc", table, advected_distribution, precision=lax.Precision.HIGHEST)
    integral_totals = lax.psum(local, "vel")
    particle_concentration = integral_totals[0]
    average_drift_x = integral_totals[1] / particle_concentration
    average_drift_y = integral_totals[2] / particle_concentration
    average_drift_z = integral_totals[3] / particle_concentration
    kelvin_level = (
        integral_totals[4] / particle_concentration
        - (
            average_drift_x * average_drift_x
            + average_drift_y * average_drift_y
            + average_drift_z * average_drift_z
        )
    ) / 3.0
    rel_x = along_x_part[:, None, None] - average_drift_x[None]
    rel_y = along_y_part[:, None, None] - average_drift_y[None]
    rel_z = along_z_part[:, None, None] - average_drift_z[None]
    scaled = (
        0.5
        * quad_weight()
        * (rel_x * rel_x + rel_y * rel_y + rel_z * rel_z)
        * advected_distribution
    )
    local_heat = jnp.stack(
        [
            jnp.sum(rel_x * scaled, axis=0),
            jnp.sum(rel_y * scaled, axis=0),
            jnp.sum(rel_z * scaled, axis=0),
        ]
    )
    conductive_transfer = lax.psum(local_heat, "vel")
    return (
        particle_concentration,
        average_drift_x,
        average_drift_y,
        average_drift_z,
        kelvin_level,
        conductive_transfer,
    )


def approach_increment(
    advected_distribution, kind_labels, along_x_part, along_y_part, along_z_part
):
    (
        particle_concentration,
        average_drift_x,
        average_drift_y,
        average_drift_z,
        kelvin_level,
        conductive_transfer,
    ) = macroscopic_moments(advected_distribution, along_x_part, along_y_part, along_z_part)
    rel_x = along_x_part[:, None, None] - average_drift_x[None]
    rel_y = along_y_part[:, None, None] - average_drift_y[None]
    rel_z = along_z_part[:, None, None] - average_drift_z[None]
    relative_magnitude_square = rel_x * rel_x + rel_y * rel_y + rel_z * rel_z
    stress_scalar_grid = particle_concentration * kelvin_level
    gaussian_local_balance = (
        particle_concentration
        * kelvin_level ** (-1.5)
        * jnp.exp(-relative_magnitude_square / (2.0 * kelvin_level))
    )
    conductive_vector_slot = (
        rel_x * conductive_transfer[0]
        + rel_y * conductive_transfer[1]
        + rel_z * conductive_transfer[2]
    )
    corrected_goal_distribution = gaussian_local_balance * (
        1.0
        + (1.0 - diffusivity_ratio)
        * conductive_vector_slot
        * (relative_magnitude_square / kelvin_level - 5.0)
        / (5.0 * stress_scalar_grid * kelvin_level)
    )
    approach_rate = (
        encounter_rate * particle_concentration * kelvin_level ** (1.0 - power_law_index)
    )
    relaxed = advected_distribution + approach_rate * (
        corrected_goal_distribution - advected_distribution
    )
    magnitude_squares = (
        along_x_part * along_x_part + along_y_part * along_y_part + along_z_part * along_z_part
    )[:, None, None]
    wall_distribution = (
        particle_concentration
        * wall_kelvin ** (-1.5)
        * jnp.exp(-magnitude_squares / (2.0 * wall_kelvin))
    )
    inflow_magnitude_square = (
        (along_x_part - inflow_speed) ** 2
        + along_y_part * along_y_part
        + along_z_part * along_z_part
    )[:, None, None]
    inflow_distribution = (
        inflow_concentration
        * inflow_kelvin ** (-1.5)
        * jnp.exp(-inflow_magnitude_square / (2.0 * inflow_kelvin))
    )
    revised_distribution = jnp.where(
        kind_labels == 1,
        wall_distribution,
        jnp.where(kind_labels == 2, inflow_distribution, relaxed),
    )
    return (revised_distribution, kelvin_level)


def per_device(initial, site_kind):
    amount = initial.shape[0]
    along_x_part, along_y_part, along_z_part = speeds(lax.axis_index("vel") * amount, amount)
    distribution_table = initial
    kelvin_level = jnp.zeros(site_kind.shape, jnp.float32)
    for section in range(STEPS):
        padded = with_halo(distribution_table, (("space", 1),), 2)
        advected_distribution = transport(padded, along_x_part, along_y_part)
        distribution_table, kelvin_level = approach_increment(
            advected_distribution, site_kind, along_x_part, along_y_part, along_z_part
        )
    return (distribution_table, kelvin_level)


def solution(mesh):
    return jax.shard_map(
        per_device,
        mesh=mesh,
        in_specs=(P("vel", "space", None), P("space", None)),
        out_specs=(P("vel", "space", None), P("space", None)),
        check_vma=False,
    )
```

profile of v0, /device:TPU:6, one launch (start us, length us, event | category | flops | bytes accessed | tf_op | source)
XLA Modules:
  0.0 373.0 jit_solution(16900406047952305739)
XLA Ops:
  0.6 1.6 copy.19
  2.2 1.3 fusion.116
  3.5 8.9 %collective-permute-start.1 = (f32[864,2,128]{2,0,1:T(8,128)}, f32[864,2,128]{2,0,1:T(8,128)}, u32[]{:S(2)}, u32[]{:S(2)}) collective-permute-start(f32[864,2,128]{2,0,1:T(8,128)} %get-tuple-element.21), channel_id=1, source_target_pairs={{1,0},{2,1},{3,2},{4,3},{5,4},{6,5},{7,6},{8,7},{9,8},{10,9},{11,1... | collective-permute-start | bytes 2654216 | tf_op jit(solution)/shard_map/ppermute | solution.py:31
  12.5 1.9 collective-permute-start
  14.4 0.1 multiply_add_fusion
  14.5 0.1 fusion.96
  14.6 0.6 add_multiply_fusion.1
  15.2 0.6 broadcast.950
  15.8 1.3 stack.36
  17.1 0.0 copy-start.5
  17.2 0.0 copy-start.7
  17.2 0.6 multiply_exponential_fusion
  17.9 0.0 copy-start.17
  17.9 1.3 broadcast_compare_fusion.3
  19.2 19.5 %collective-permute-done = f32[864,2,128]{2,0,1:T(8,128)} collective-permute-done((f32[864,2,128]{2,0,1:T(8,128)}, f32[864,2,128]{2,0,1:T(8,128)}, u32[]{:S(2)}, u32[]{:S(2)}) %collective-permute-start) | collective-permute-done | bytes 884768 | tf_op jit(solution)/shard_map/ppermute | solution.py:28
  38.6 1.2 constant_dynamic-update-slice_fusion.2
  39.8 0.0 copy-done
  39.9 0.1 constant_dynamic-update-slice_fusion.1
  40.0 0.0 collective-permute-done.1
  40.0 1.2 constant_dynamic-update-slice_fusion
  41.2 0.2 slice_subtract_fusion.1
  41.4 0.0 copy-start.9
  41.5 1.1 minimum_multiply_fusion.3
  42.7 2.0 fusion.16
  44.7 0.2 fusion.71
  44.9 1.9 fusion.3
  46.8 2.4 minimum_multiply_fusion.1
  49.2 2.6 fusion.2
  51.8 0.5 fusion.70
  52.4 0.2 copy-done.1
  52.6 0.9 fusion.74
  53.5 89.8 %psum.28 = f32[5,4,128]{2,0,1:T(8,128)S(1)} all-reduce(f32[5,4,128]{2,0,1:T(8,128)S(1)} %fusion.74), channel_id=1, replica_groups=mesh['vel'=16,'space'=16] {'vel'}, use_global_device_ids=true, to_apply=%region_0.1 | all-reduce | flops 2560 | bytes 20480 | tf_op jit(solution)/shard_map/psum | solution.py:88
  143.4 1.1 fusion.20
  144.6 38.9 %psum.29 = f32[3,4,128]{2,1,0:T(4,128)S(1)} all-reduce(f32[3,4,128]{2,1,0:T(4,128)S(1)} %pad_maximum_fusion.5), channel_id=1, replica_groups=mesh['vel'=16,'space'=16] {'vel'}, use_global_device_ids=true, to_apply=%region_4.5 | all-reduce | flops 1536 | bytes 12288 | tf_op jit(solution)/shard_map/psum | solution.py:117
  183.5 0.0 copy-done.2
  183.5 0.0 copy-done.19
  183.5 0.0 copy-done.20
  183.5 4.3 %fusion.42 = f32[864,4,128]{2,0,1:T(8,128)S(1)} fusion(f32[864,4,128]{2,0,1:T(8,128)S(1)} %fusion.70, f32[4,128]{1,0:T(4,128)S(1)} %bitcast.109, f32[4,128]{1,0:T(4,128)S(1)} %bitcast.115, f32[4,128]{1,0:T(4,128)S(1)} %get-tuple-element.37, f32[4,128]{1,0:T(4,128)S(1)} %get-tuple-element.38, f32[4,128]{1,0:T(4,128)S(1)} %get-tuple-element.36, ...), kind=kLoop, calls=%fused_computation.87 | loop fusion | flops 12828672 | bytes 3581824 | tf_op jit(solution)/shard_map/jit(_where)/select_n | solution.py:185
  187.8 0.1 fusion.115
  187.9 1.9 collective-permute-start.2
  189.8 8.4 %collective-permute-start.3 = (f32[864,2,128]{2,0,1:T(8,128)S(1)}, f32[864,2,128]{2,0,1:T(8,128)S(1)}, u32[]{:S(2)}, u32[]{:S(2)}) collective-permute-start(f32[864,2,128]{2,0,1:T(8,128)S(1)} %get-tuple-element.20), channel_id=1, source_target_pairs={{1,0},{2,1},{3,2},{4,3},{5,4},{6,5},{7,6},{8,7},{9,8},{10,9},{11,1... | collective-permute-start | bytes 2654216 | tf_op jit(solution)/shard_map/ppermute | solution.py:31
  198.3 35.9 %collective-permute-done.2 = f32[864,2,128]{2,0,1:T(8,128)S(1)} collective-permute-done((f32[864,2,128]{2,0,1:T(8,128)S(1)}, f32[864,2,128]{2,0,1:T(8,128)S(1)}, u32[]{:S(2)}, u32[]{:S(2)}) %collective-permute-start.2) | collective-permute-done | bytes 884768 | tf_op jit(solution)/shard_map/ppermute | solution.py:28
  234.2 0.0 collective-permute-done.3
  234.2 0.2 pad_maximum_fusion
  234.4 0.2 slice_subtract_fusion
  234.7 0.0 copy-start.16
  234.7 1.1 minimum_multiply_fusion.2
  235.9 1.0 fusion.12
  236.9 3.8 %fusion.69 = f32[864,4,128]{2,0,1:T(8,128)S(1)} fusion(f32[864,5,128]{2,0,1:T(8,128)S(1)} %fusion.12, f32[864,4,128]{2,0,1:T(8,128)S(1)} %fusion.70, f32[4,128]{1,0:T(4,128)S(1)} %bitcast.110, f32[4,128]{1,0:T(4,128)S(1)} %bitcast.116, f32[4,128]{1,0:T(4,128)S(1)} %get-tuple-element.37, f32[4,128]{1,0:T(4,128)S(1)} %get-tuple-element.38, ...), kind=kLoop, calls=%fused_computation.116 | loop fusion | flops 13713408 | bytes 7120768 | tf_op jit(solution)/shard_map/sub | solution.py:68
  240.7 1.9 fusion.8
  242.6 0.0 copy-start.4
  242.6 0.0 copy-start.6
  242.6 0.0 copy-start.8
  242.6 0.0 copy-start.18
  242.6 2.4 minimum_multiply_fusion
  245.1 2.6 fusion.7
  247.7 0.5 fusion.68
  248.2 0.9 fusion.72
  249.1 76.5 %psum.30 = f32[5,4,128]{2,1,0:T(4,128)S(1)} all-reduce(f32[5,4,128]{2,1,0:T(4,128)S(1)} %copy.20), channel_id=1, replica_groups=mesh['vel'=16,'space'=16] {'vel'}, use_global_device_ids=true, to_apply=%region_5.6 | all-reduce | flops 2560 | bytes 20480 | tf_op jit(solution)/shard_map/psum | solution.py:88
  325.6 0.6 fusion.109
  326.3 1.1 fusion.45
  327.5 38.9 %psum.31 = f32[3,4,128]{2,1,0:T(4,128)S(1)} all-reduce(f32[3,4,128]{2,1,0:T(4,128)S(1)} %pad_maximum_fusion.6), channel_id=1, replica_groups=mesh['vel'=16,'space'=16] {'vel'}, use_global_device_ids=true, to_apply=%region_9.10 | all-reduce | flops 1536 | bytes 12288 | tf_op jit(solution)/shard_map/psum | solution.py:117
  366.4 4.3 %fusion.67 = f32[864,4,128]{2,0,1:T(8,128)S(1)} fusion(f32[864,4,128]{2,0,1:T(8,128)S(1)} %fusion.68, f32[4,128]{1,0:T(4,128)S(1)} %bitcast.119, f32[4,128]{1,0:T(4,128)S(1)} %bitcast.121, f32[4,128]{1,0:T(4,128)S(1)} %get-tuple-element.34, f32[4,128]{1,0:T(4,128)S(1)} %get-tuple-element.35, f32[4,128]{1,0:T(4,128)S(1)} %get-tuple-element.33, ...), kind=kLoop, calls=%fused_computation.112 | loop fusion | flops 12828672 | bytes 3581824 | tf_op jit(solution)/shard_map/jit(_where)/select_n | solution.py:185
  370.6 2.3 copy.28
  (43 shorter events, 0.3 us)
Async XLA Ops:
  3.5 36.3 %copy-start = (f32[864,4,128]{2,1,0:T(4,128)S(1)}, f32[864,4,128]{2,1,0:T(4,128)}, u32[]{:S(2)}) copy-start(f32[864,4,128]{2,1,0:T(4,128)} %param.2) | copy-start | bytes 5308420
  3.5 36.4 %collective-permute-start.1 = (f32[864,2,128]{2,0,1:T(8,128)}, f32[864,2,128]{2,0,1:T(8,128)}, u32[]{:S(2)}, u32[]{:S(2)}) collective-permute-start(f32[864,2,128]{2,0,1:T(8,128)} %get-tuple-element.21), channel_id=1, source_target_pairs={{1,0},{2,1},{3,2},{4,3},{5,4},{6,5},{7,6},{8,7},{9,8},{10,9},{11,1... | collective-permute-start | bytes 2654216 | tf_op jit(solution)/shard_map/ppermute | solution.py:31
  12.5 26.1 %collective-permute-start = (f32[864,2,128]{2,0,1:T(8,128)}, f32[864,2,128]{2,0,1:T(8,128)}, u32[]{:S(2)}, u32[]{:S(2)}) collective-permute-start(f32[864,2,128]{2,0,1:T(8,128)} %get-tuple-element.22), channel_id=1, source_target_pairs={{0,1},{1,2},{2,3},{3,4},{4,5},{5,6},{6,7},{7,8},{8,9},{9,10},{10,1... | collective-permute-start | bytes 2654216 | tf_op jit(solution)/shard_map/ppermute | solution.py:28
  17.1 32.1 %copy-start.3 = (f32[864]{0:T(1024)}, f32[864]{0:T(1024)S(1)}, u32[]{:S(2)}) copy-start(f32[864]{0:T(1024)S(1)} %get-tuple-element.51) | copy-start | bytes 10372
  17.1 32.1 %copy-start.5 = (f32[864]{0:T(1024)}, f32[864]{0:T(1024)S(1)}, u32[]{:S(2)}) copy-start(f32[864]{0:T(1024)S(1)} %get-tuple-element.52) | copy-start | bytes 10372
  17.2 25.5 %copy-start.13 = (f32[864]{0:T(1024)}, f32[864]{0:T(1024)S(1)}, u32[]{:S(2)}) copy-start(f32[864]{0:T(1024)S(1)} %get-tuple-element.62) | copy-start | bytes 10372
  17.2 32.1 %copy-start.7 = (f32[864]{0:T(1024)}, f32[864]{0:T(1024)S(1)}, u32[]{:S(2)}) copy-start(f32[864]{0:T(1024)S(1)} %get-tuple-element.61) | copy-start | bytes 10372
  17.8 24.8 %copy-start.15 = (pred[864]{0:T(1024)(128)(4,1)}, pred[864]{0:T(1024)(128)(4,1)S(1)}, u32[]{:S(2)}) copy-start(pred[864]{0:T(1024)(128)(4,1)S(1)} %get-tuple-element.60) | copy-start | bytes 2596
  17.9 31.4 %copy-start.17 = (pred[864]{0:T(1024)(128)(4,1)}, pred[864]{0:T(1024)(128)(4,1)S(1)}, u32[]{:S(2)}) copy-start(pred[864]{0:T(1024)(128)(4,1)S(1)} %get-tuple-element.59) | copy-start | bytes 2596
  41.4 1.2 copy-start.9
  41.5 1.2 copy-start.11
  51.8 0.7 copy-start.1
  52.6 130.9 %copy-start.2 = (f32[864]{0:T(1024)S(1)}, f32[864]{0:T(1024)}, u32[]{:S(2)}) copy-start(f32[864]{0:T(1024)} %get-tuple-element.50) | copy-start | bytes 10372
  52.6 130.9 %copy-start.19 = (pred[4,128]{1,0:T(4,128)(4,1)S(1)}, pred[4,128]{1,0:T(4,128)(4,1)}, u32[]{:S(2)}) copy-start(pred[4,128]{1,0:T(4,128)(4,1)} %get-tuple-element.45) | copy-start | bytes 1540
  52.6 130.9 %copy-start.20 = (pred[4,128]{1,0:T(4,128)(4,1)S(1)}, pred[4,128]{1,0:T(4,128)(4,1)}, u32[]{:S(2)}) copy-start(pred[4,128]{1,0:T(4,128)(4,1)} %get-tuple-element.46) | copy-start | bytes 1540
  187.9 46.3 %collective-permute-start.2 = (f32[864,2,128]{2,0,1:T(8,128)S(1)}, f32[864,2,128]{2,0,1:T(8,128)S(1)}, u32[]{:S(2)}, u32[]{:S(2)}) collective-permute-start(f32[864,2,128]{2,0,1:T(8,128)S(1)} %get-tuple-element.19), channel_id=1, source_target_pairs={{0,1},{1,2},{2,3},{3,4},{4,5},{5,6},{6,7},{7,8},{8,9},{9,10},{10,1... | collective-permute-start | bytes 2654216 | tf_op jit(solution)/shard_map/ppermute | solution.py:28
  189.8 44.3 %collective-permute-start.3 = (f32[864,2,128]{2,0,1:T(8,128)S(1)}, f32[864,2,128]{2,0,1:T(8,128)S(1)}, u32[]{:S(2)}, u32[]{:S(2)}) collective-permute-start(f32[864,2,128]{2,0,1:T(8,128)S(1)} %get-tuple-element.20), channel_id=1, source_target_pairs={{1,0},{2,1},{3,2},{4,3},{5,4},{6,5},{7,6},{8,7},{9,8},{10,9},{11,1... | collective-permute-start | bytes 2654216 | tf_op jit(solution)/shard_map/ppermute | solution.py:31
  234.6 1.2 copy-start.10
  234.6 1.2 copy-start.12
  234.7 1.2 copy-start.14
  234.7 1.2 copy-start.16
  242.6 2.5 copy-start.4
  242.6 2.5 copy-start.6
  242.6 2.5 copy-start.8
  242.6 2.5 copy-start.18
where the time goes:
time: 373 us
  blocking collectives  244 us (65%)
  waiting for transfers between devices  55.3 us (15%)
  other arithmetic  39.1 us (10%)
  starting transfers between devices  21.2 us (6%)
  local copies, waits for them, and re-layouts  10.1 us (3%)
    psum x2, blocking collectives, macroscopic_moments(): integral_totals = lax.psum(local, 'vel')  166 us
    psum x2, blocking collectives, macroscopic_moments(): conductive_transfer = lax.psum(local_heat, 'vel')  77.8 us
    ppermute x2, waiting for transfers between devices, with_halo(): lax.ppermute(lax.slice_in_dim(block, block.shape[dim] - width, None, axis...  55.3 us
    ppermute x2, starting transfers between devices, with_halo(): lax.ppermute(lax.slice_in_dim(block, 0, width, axis=dim), axis, backward)  17.4 us
    select_n x2, other arithmetic, approach_increment(): jnp.where(kind_labels == 1, wall_distribution, jnp.where(kind_labels == 2...  8.54 us
    mul x4, other arithmetic, sweep(): flux = number * jnp.where(number > 0, left_face, right_face)  8.15 us
  transfers between devices with their start and end apart: 4, of which 2 were waited for; matrix products, arithmetic and copies ran while one was open for 2% of the time, Pallas kernels for 0%

commit v1 on v0

--- a/solution.py
+++ b/solution.py
@@ -76,45 +76,83 @@
     return sweep(widened, courant * along_y_part[:, None, None], 2)
 
 
+def xor_tree(values):
+    while len(values) > 1:
+        values = [values[2 * j] + values[2 * j + 1] for j in range(len(values) // 2)]
+    return values[0]
+
+
+def vel_sum(local):
+    count = lax.axis_size("vel")
+    if count & (count - 1):
+        return lax.psum(local, "vel")
+    bits = count.bit_length() - 1
+    low = 0
+    while low < bits:
+        width = min(2, bits - low)
+        values = [local]
+        for member in range(1, 1 << width):
+            mask = member << low
+            values.append(lax.ppermute(local, "vel", [(i, i ^ mask) for i in range(count)]))
+        local = xor_tree(values)
+        low += width
+    return local
+
+
 def macroscopic_moments(advected_distribution, along_x_part, along_y_part, along_z_part):
     magnitude_squares = (
         along_x_part * along_x_part + along_y_part * along_y_part + along_z_part * along_z_part
     )
     ones = jnp.ones_like(along_x_part)
     table = quad_weight() * jnp.stack(
-        [ones, along_x_part, along_y_part, along_z_part, magnitude_squares]
+        [
+            ones,
+            along_x_part,
+            along_y_part,
+            along_z_part,
+            magnitude_squares,
+            along_x_part * along_x_part,
+            along_y_part * along_y_part,
+            along_z_part * along_z_part,
+            along_x_part * along_y_part,
+            along_x_part * along_z_part,
+            along_y_part * along_z_part,
+            along_x_part * magnitude_squares,
+            along_y_part * magnitude_squares,
+            along_z_part * magnitude_squares,
+            jnp.zeros_like(along_x_part),
+            jnp.zeros_like(along_x_part),
+        ]
     )
     local = jnp.einsum("kv,vrc->krc", table, advected_distribution, precision=lax.Precision.HIGHEST)
-    integral_totals = lax.psum(local, "vel")
-    particle_concentration = integral_totals[0]
-    average_drift_x = integral_totals[1] / particle_concentration
-    average_drift_y = integral_totals[2] / particle_concentration
-    average_drift_z = integral_totals[3] / particle_concentration
-    kelvin_level = (
-        integral_totals[4] / particle_concentration
-        - (
-            average_drift_x * average_drift_x
-            + average_drift_y * average_drift_y
-            + average_drift_z * average_drift_z
-        )
-    ) / 3.0
-    rel_x = along_x_part[:, None, None] - average_drift_x[None]
-    rel_y = along_y_part[:, None, None] - average_drift_y[None]
-    rel_z = along_z_part[:, None, None] - average_drift_z[None]
-    scaled = (
-        0.5
-        * quad_weight()
-        * (rel_x * rel_x + rel_y * rel_y + rel_z * rel_z)
-        * advected_distribution
-    )
-    local_heat = jnp.stack(
+    totals = vel_sum(local)
+    particle_concentration = totals[0]
+    average_drift_x = totals[1] / particle_concentration
+    average_drift_y = totals[2] / particle_concentration
+    average_drift_z = totals[3] / particle_concentration
+    energy = totals[4]
+    drift_square = (
+        average_drift_x * average_drift_x
+        + average_drift_y * average_drift_y
+        + average_drift_z * average_drift_z
+    )
+    kelvin_level = (energy / particle_concentration - drift_square) / 3.0
+    xx, yy, zz, xy, xz, yz = (totals[k] for k in range(5, 11))
+    drift = (average_drift_x, average_drift_y, average_drift_z)
+    second = ((xx, xy, xz), (xy, yy, yz), (xz, yz, zz))
+    common = 2.0 * particle_concentration * drift_square
+    conductive_transfer = jnp.stack(
         [
-            jnp.sum(rel_x * scaled, axis=0),
-            jnp.sum(rel_y * scaled, axis=0),
-            jnp.sum(rel_z * scaled, axis=0),
+            0.5
+            * (
+                totals[11 + i]
+                - 2.0 * (drift[0] * second[i][0] + drift[1] * second[i][1] + drift[2] * second[i][2])
+                - drift[i] * energy
+                + drift[i] * common
+            )
+            for i in range(3)
         ]
     )
-    conductive_transfer = lax.psum(local_heat, "vel")
     return (
         particle_concentration,
         average_drift_x,

time: 373 us -> 164 us (0.44)
  blocking collectives: 244 us -> 0 us
  starting transfers between devices: 21.2 us -> 47.8 us
  waiting for transfers between devices: 55.3 us -> 66.8 us
  other arithmetic: 39.1 us -> 31.1 us
    psum x4 -> x0, blocking collectives: 244 us -> none  [the longest x2 166 us: macroscopic_moments(): integral_totals = lax.psum(local, 'vel')]
    ppermute x0 -> x12, starting transfers between devices: none -> 26.7 us  [vel_sum(): lax.ppermute(local, 'vel', [(i, i ^ mask) for i in range(count)])]
    ppermute x2, waiting for transfers between devices: 55.3 us -> 39.8 us  [with_halo(): lax.ppermute(lax.slice_in_dim(block, block.shape[dim] - width, None, axis...]
    ppermute x0 -> x12, waiting for transfers between devices: none -> 14.1 us  [vel_sum(): lax.ppermute(local, 'vel', [(i, i ^ mask) for i in range(count)])]
    ppermute x2, waiting for transfers between devices: 0.01 us -> 12.9 us  [with_halo(): lax.ppermute(lax.slice_in_dim(block, 0, width, axis=dim), axis, backward)]
    sub x4 -> x2, other arithmetic: 5.06 us -> 0.44 us  [sweep(): piece(distribution_table, 2, length - 2)]
  transfers between devices with their start and end apart: 4 -> 16, of which waited for: 2 -> 11; matrix products, arithmetic and copies ran while one was open for 2% -> 6% of each run, Pallas kernels for 0% -> 0%
where the time goes in v1:
time: 164 us; the launch traced here: 161 us
  waiting for transfers between devices  66.8 us (41%)
  starting transfers between devices  47.8 us (29%)
  other arithmetic  31.1 us (19%)
  local copies, waits for them, and re-layouts  11.3 us (7%)
  matrix products  2.59 us (2%)
    ppermute x2, waiting for transfers between devices, with_halo(): lax.ppermute(lax.slice_in_dim(block, block.shape[dim] - width, None, axis...  39.8 us
    ppermute x12, starting transfers between devices, vel_sum(): lax.ppermute(local, 'vel', [(i, i ^ mask) for i in range(count)])  26.7 us
    ppermute x2, starting transfers between devices, with_halo(): lax.ppermute(lax.slice_in_dim(block, 0, width, axis=dim), axis, backward)  17.3 us
    ppermute x12, waiting for transfers between devices, vel_sum(): lax.ppermute(local, 'vel', [(i, i ^ mask) for i in range(count)])  14.1 us
    ppermute x2, waiting for transfers between devices, with_halo(): lax.ppermute(lax.slice_in_dim(block, 0, width, axis=dim), axis, backward)  12.9 us
    mul x4, other arithmetic, sweep(): flux = number * jnp.where(number > 0, left_face, right_face)  8.14 us
    mul x4, other arithmetic, minmod(): 0.5 * (jnp.sign(left) + jnp.sign(right))  7.11 us
    select_n x2, other arithmetic, approach_increment(): jnp.where(kind_labels == 1, wall_distribution, jnp.where(kind_labels == 2...  5.31 us
  transfers between devices with their start and end apart: 16, of which 11 were waited for; matrix products, arithmetic and copies ran while one was open for 6% of the time, Pallas kernels for 0%

profile of v1, /device:TPU:6, one launch (start us, length us, event | category | flops | bytes accessed | tf_op | source)
XLA Modules:
  0.0 160.6 jit_solution(493763814259107215)
XLA Ops:
  0.6 1.6 copy.90
  2.2 0.0 copy-start
  2.2 1.3 fusion.159
  3.6 1.9 %collective-permute-start = (f32[864,2,128]{2,0,1:T(8,128)}, f32[864,2,128]{2,0,1:T(8,128)}, u32[]{:S(2)}, u32[]{:S(2)}) collective-permute-start(f32[864,2,128]{2,0,1:T(8,128)} %get-tuple-element.19), channel_id=1, source_target_pairs={{0,1},{1,2},{2,3},{3,4},{4,5},{5,6},{6,7},{7,8},{8,9},{9,10},{10,1... | collective-permute-start | bytes 2654216 | tf_op jit(solution)/shard_map/ppermute | solution.py:28
  5.5 8.8 %collective-permute-start.1 = (f32[864,2,128]{2,0,1:T(8,128)}, f32[864,2,128]{2,0,1:T(8,128)}, u32[]{:S(2)}, u32[]{:S(2)}) collective-permute-start(f32[864,2,128]{2,0,1:T(8,128)} %get-tuple-element.18), channel_id=1, source_target_pairs={{1,0},{2,1},{3,2},{4,3},{5,4},{6,5},{7,6},{8,7},{9,8},{10,9},{11,1... | collective-permute-start | bytes 2654216 | tf_op jit(solution)/shard_map/ppermute | solution.py:31
  14.3 0.1 fusion.86
  14.4 0.7 add_add_fusion.4
  15.1 0.7 fusion.147
  15.7 0.7 fusion.149
  16.4 0.7 fusion.151
  17.1 0.7 fusion.153
  17.8 0.6 fusion.155
  18.4 0.6 broadcast.1549
  19.0 2.7 %stack.2 = f32[16,864]{1,0:T(8,128)} concatenate(f32[1,864]{1,0:T(1,128)} %broadcast.1549, f32[1,864]{1,0:T(1,128)} %get-tuple-element.53, f32[1,864]{1,0:T(1,128)S(1)} %get-tuple-element.50, f32[1,864]{1,0:T(1,128)S(1)} %get-tuple-element.51, f32[1,864]{1,0:T(1,128)} %get-tuple-element.52, f32[1,864]{1,0:T(1,128)} %get-tuple-element.61, f32[1,864]{1,0:T(1,128)} %fusion.155, ...), dimensions={0} | concatenate | bytes 110592 | tf_op jit(solution)/shard_map/stack | solution.py:107
  21.8 0.7 broadcast_compare_fusion.3
  22.5 5.3 %collective-permute-done = f32[864,2,128]{2,0,1:T(8,128)} collective-permute-done((f32[864,2,128]{2,0,1:T(8,128)}, f32[864,2,128]{2,0,1:T(8,128)}, u32[]{:S(2)}, u32[]{:S(2)}) %collective-permute-start) | collective-permute-done | bytes 884768 | tf_op jit(solution)/shard_map/ppermute | solution.py:28
  27.8 1.2 constant_dynamic-update-slice_fusion.2
  29.0 0.1 constant_dynamic-update-slice_fusion.1
  29.1 12.9 %collective-permute-done.1 = f32[864,2,128]{2,0,1:T(8,128)} collective-permute-done((f32[864,2,128]{2,0,1:T(8,128)}, f32[864,2,128]{2,0,1:T(8,128)}, u32[]{:S(2)}, u32[]{:S(2)}) %collective-permute-start.1) | collective-permute-done | bytes 884768 | tf_op jit(solution)/shard_map/ppermute | solution.py:31
  42.1 1.2 constant_dynamic-update-slice_fusion
  43.3 0.2 slice_subtract_fusion.1
  43.5 1.1 minimum_multiply_fusion.3
  44.7 2.0 %fusion.16 = f32[864,5,128]{2,0,1:T(8,128)S(1)} fusion(f32[864,6,128]{2,0,1:T(8,128)S(1)} %minimum_multiply_fusion.3, f32[864,2,128]{2,0,1:T(8,128)} %collective-permute-done.1, f32[864,4,128]{2,0,1:T(8,128)S(1)} %copy.90, f32[864,2,128]{2,0,1:T(8,128)} %collective-permute-done, f32[864]{0:T(1024)S(1)} %get-tuple-element.48, f32[864]{0:T(1024)S(1)} %get-tuple-element.49, ...), kind=kLoop, calls=%fused_computation.52 | loop fusion | flops 4423680 | bytes 10185696 | tf_op jit(solution)/shard_map/mul | solution.py:67
  46.7 0.2 fusion.61
  46.9 1.9 %fusion.3 = f32[864,4,131]{2,0,1:T(8,128)S(1)} fusion(f32[864,4,128]{2,0,1:T(8,128)S(1)} %fusion.61), kind=kLoop, calls=%fused_computation.11 | loop fusion | flops 452736 | bytes 3580416 | tf_op jit(solution)/shard_map/sub | solution.py:59
  48.8 2.4 %minimum_multiply_fusion.1 = f32[864,4,130]{2,0,1:T(8,128)S(1)} fusion(f32[864,4,131]{2,0,1:T(8,128)S(1)} %fusion.3), kind=kLoop, calls=%fused_computation.24 | loop fusion | flops 3594240 | bytes 5391360 | tf_op jit(solution)/shard_map/mul | solution.py:50
  51.2 2.6 %fusion.2 = f32[864,4,129]{2,0,1:T(8,128)S(1)} fusion(f32[864,4,128]{2,0,1:T(8,128)S(1)} %fusion.61, f32[864,4,130]{2,0,1:T(8,128)S(1)} %minimum_multiply_fusion.1, f32[864]{0:T(1024)S(1)} %get-tuple-element.46, f32[864]{0:T(1024)S(1)} %get-tuple-element.47, f32[864]{0:T(1024)S(1)} %get-tuple-element.56, pred[864]{0:T(1024)(128)(4,1)S(1)} %get-tuple-element.54), kind=kLoop, calls=%fused_computation.10 | loop fusion | flops 2674944 | bytes 7130592 | tf_op jit(solution)/shard_map/mul | solution.py:67
  53.8 1.3 fusion.64
  55.1 10.4 %collective-permute-start.2 = (f32[16,4,128]{2,1,0:T(4,128)S(1)}, f32[16,4,128]{2,1,0:T(4,128)S(1)}, u32[]{:S(2)}, u32[]{:S(2)}) collective-permute-start(f32[16,4,128]{2,1,0:T(4,128)S(1)} %copy.92), channel_id=1, source_target_pairs={{0,16},{16,0},{32,48},{48,32},{64,80},{80,64},{96,112},{112,96},{1... | collective-permute-start | bytes 98312 | tf_op jit(solution)/shard_map/ppermute | solution.py:96
  65.6 2.3 %collective-permute-start.3 = (f32[16,4,128]{2,1,0:T(4,128)S(1)}, f32[16,4,128]{2,1,0:T(4,128)S(1)}, u32[]{:S(2)}, u32[]{:S(2)}) collective-permute-start(f32[16,4,128]{2,1,0:T(4,128)S(1)} %copy.92), channel_id=1, source_target_pairs={{0,32},{16,48},{32,0},{48,16},{64,96},{80,112},{96,64},{112,80},{1... | collective-permute-start | bytes 98312 | tf_op jit(solution)/shard_map/ppermute | solution.py:96
  67.9 1.4 collective-permute-start.4
  69.3 1.4 collective-permute-done.3
  70.7 2.9 %collective-permute-done.4 = f32[16,4,128]{2,1,0:T(4,128)S(1)} collective-permute-done((f32[16,4,128]{2,1,0:T(4,128)S(1)}, f32[16,4,128]{2,1,0:T(4,128)S(1)}, u32[]{:S(2)}, u32[]{:S(2)}) %collective-permute-start.4) | collective-permute-done | bytes 32800 | tf_op jit(solution)/shard_map/ppermute | solution.py:96
  73.6 3.5 %collective-permute-start.6 = (f32[16,4,128]{2,1,0:T(4,128)S(1)}, f32[16,4,128]{2,1,0:T(4,128)S(1)}, u32[]{:S(2)}, u32[]{:S(2)}) collective-permute-start(f32[16,4,128]{2,1,0:T(4,128)S(1)} %add_add_fusion.3), channel_id=1, source_target_pairs={{0,128},{16,144},{32,160},{48,176},{64,192},{80,208},{96,224},{112... | collective-permute-start | bytes 98312 | tf_op jit(solution)/shard_map/ppermute | solution.py:96
  77.1 1.1 collective-permute-start.7
  78.2 1.1 collective-permute-done.6
  79.3 2.9 %collective-permute-done.7 = f32[16,4,128]{2,1,0:T(4,128)S(1)} collective-permute-done((f32[16,4,128]{2,1,0:T(4,128)S(1)}, f32[16,4,128]{2,1,0:T(4,128)S(1)}, u32[]{:S(2)}, u32[]{:S(2)}) %collective-permute-start.7) | collective-permute-done | bytes 32800 | tf_op jit(solution)/shard_map/ppermute | solution.py:96
  82.3 2.7 %fusion.37 = f32[864,4,128]{2,0,1:T(8,128)S(1)} fusion(f32[4,128]{1,0:T(4,128)S(1)} %get-tuple-element.27, f32[4,128]{1,0:T(4,128)S(1)} %get-tuple-element.40, f32[4,128]{1,0:T(4,128)S(1)} %fusion.119, f32[4,128]{1,0:T(4,128)S(1)} %get-tuple-element.34, f32[4,128]{1,0:T(4,128)S(1)} %get-tuple-element.35, f32[4,128]{1,0:T(4,128)S(1)} %get-tuple-element.41, ...), kind=kLoop, calls=%fused_computation.76 | loop fusion | flops 13713408 | bytes 7120768 | tf_op jit(solution)/shard_map/jit(_where)/select_n | solution.py:223
  85.0 0.1 fusion.158
  85.1 1.9 %collective-permute-start.8 = (f32[864,2,128]{2,0,1:T(8,128)S(1)}, f32[864,2,128]{2,0,1:T(8,128)S(1)}, u32[]{:S(2)}, u32[]{:S(2)}) collective-permute-start(f32[864,2,128]{2,0,1:T(8,128)S(1)} %get-tuple-element.16), channel_id=1, source_target_pairs={{0,1},{1,2},{2,3},{3,4},{4,5},{5,6},{6,7},{7,8},{8,9},{9,10},{10,1... | collective-permute-start | bytes 2654216 | tf_op jit(solution)/shard_map/ppermute | solution.py:28
  87.0 8.4 %collective-permute-start.9 = (f32[864,2,128]{2,0,1:T(8,128)S(1)}, f32[864,2,128]{2,0,1:T(8,128)S(1)}, u32[]{:S(2)}, u32[]{:S(2)}) collective-permute-start(f32[864,2,128]{2,0,1:T(8,128)S(1)} %get-tuple-element.17), channel_id=1, source_target_pairs={{1,0},{2,1},{3,2},{4,3},{5,4},{6,5},{7,6},{8,7},{9,8},{10,9},{11,1... | collective-permute-start | bytes 2654216 | tf_op jit(solution)/shard_map/ppermute | solution.py:31
  95.5 34.6 %collective-permute-done.8 = f32[864,2,128]{2,0,1:T(8,128)S(1)} collective-permute-done((f32[864,2,128]{2,0,1:T(8,128)S(1)}, f32[864,2,128]{2,0,1:T(8,128)S(1)}, u32[]{:S(2)}, u32[]{:S(2)}) %collective-permute-start.8) | collective-permute-done | bytes 884768 | tf_op jit(solution)/shard_map/ppermute | solution.py:28
  130.1 0.2 pad_maximum_fusion
  130.3 0.2 slice_subtract_fusion
  130.5 1.1 minimum_multiply_fusion.2
  131.7 1.0 fusion.12
  132.7 0.2 fusion.59
  132.9 1.9 %fusion.8 = f32[864,4,131]{2,0,1:T(8,128)S(1)} fusion(f32[864,4,128]{2,0,1:T(8,128)S(1)} %fusion.59), kind=kLoop, calls=%fused_computation.16 | loop fusion | flops 452736 | bytes 3580416 | tf_op jit(solution)/shard_map/sub | solution.py:59
  134.8 2.4 %minimum_multiply_fusion = f32[864,4,130]{2,0,1:T(8,128)S(1)} fusion(f32[864,4,131]{2,0,1:T(8,128)S(1)} %fusion.8), kind=kLoop, calls=%fused_computation.23 | loop fusion | flops 3594240 | bytes 5391360 | tf_op jit(solution)/shard_map/mul | solution.py:50
  137.2 2.6 %fusion.7 = f32[864,4,129]{2,0,1:T(8,128)S(1)} fusion(f32[864,4,128]{2,0,1:T(8,128)S(1)} %fusion.59, f32[864,4,130]{2,0,1:T(8,128)S(1)} %minimum_multiply_fusion, f32[864]{0:T(1024)S(1)} %get-tuple-element.46, f32[864]{0:T(1024)S(1)} %get-tuple-element.47, f32[864]{0:T(1024)S(1)} %get-tuple-element.56, pred[864]{0:T(1024)(128)(4,1)S(1)} %get-tuple-element.54), kind=kLoop, calls=%fused_computation.15 | loop fusion | flops 2674944 | bytes 7130592 | tf_op jit(solution)/shard_map/mul | solution.py:67
  139.8 1.3 fusion.62
  141.1 0.6 collective-permute-start.10
  141.7 0.7 collective-permute-start.11
  142.4 3.1 %collective-permute-start.12 = (f32[16,4,128]{2,1,0:T(4,128)S(1)}, f32[16,4,128]{2,1,0:T(4,128)S(1)}, u32[]{:S(2)}, u32[]{:S(2)}) collective-permute-start(f32[16,4,128]{2,1,0:T(4,128)S(1)} %copy.96), channel_id=1, source_target_pairs={{0,48},{16,32},{32,16},{48,0},{64,112},{80,96},{96,80},{112,64},{1... | collective-permute-start | bytes 98312 | tf_op jit(solution)/shard_map/ppermute | solution.py:96
  145.6 1.0 collective-permute-done.11
  146.5 1.6 collective-permute-done.12
  148.2 1.6 %collective-permute-start.14 = (f32[16,4,128]{2,1,0:T(4,128)S(1)}, f32[16,4,128]{2,1,0:T(4,128)S(1)}, u32[]{:S(2)}, u32[]{:S(2)}) collective-permute-start(f32[16,4,128]{2,1,0:T(4,128)S(1)} %add_add_fusion.1), channel_id=1, source_target_pairs={{0,128},{16,144},{32,160},{48,176},{64,192},{80,208},{96,224},{112... | collective-permute-start | bytes 98312 | tf_op jit(solution)/shard_map/ppermute | solution.py:96
  149.8 1.0 collective-permute-start.15
  150.8 1.0 collective-permute-start.13
  151.7 1.9 %collective-permute-done.14 = f32[16,4,128]{2,1,0:T(4,128)S(1)} collective-permute-done((f32[16,4,128]{2,1,0:T(4,128)S(1)}, f32[16,4,128]{2,1,0:T(4,128)S(1)}, u32[]{:S(2)}, u32[]{:S(2)}) %collective-permute-start.14) | collective-permute-done | bytes 32800 | tf_op jit(solution)/shard_map/ppermute | solution.py:96
  153.7 1.2 collective-permute-done.15
  155.0 0.6 fusion.144
  155.6 2.6 %fusion.57 = f32[864,4,128]{2,0,1:T(8,128)S(1)} fusion(f32[4,128]{1,0:T(4,128)S(1)} %get-tuple-element.30, f32[4,128]{1,0:T(4,128)S(1)} %get-tuple-element.36, f32[4,128]{1,0:T(4,128)S(1)} %get-tuple-element.29, f32[4,128]{1,0:T(4,128)S(1)} %get-tuple-element.21, f32[4,128]{1,0:T(4,128)S(1)} %get-tuple-element.20, f32[4,128]{1,0:T(4,128)S(1)} %get-tuple-element.37, ...), kind=kLoop, calls=%fused_computation.96 | loop fusion | flops 13713408 | bytes 7120768 | tf_op jit(solution)/shard_map/jit(_where)/select_n | solution.py:223
  158.2 2.3 %copy.99 = f32[864,4,128]{2,1,0:T(4,128)} copy(f32[864,4,128]{2,0,1:T(8,128)S(1)} %fusion.57) | data formatting | bytes 3538944
  (29 shorter events, 0.4 us)
Async XLA Ops:
  2.2 26.8 %copy-start = (f32[864,4,128]{2,1,0:T(4,128)S(1)}, f32[864,4,128]{2,1,0:T(4,128)}, u32[]{:S(2)}) copy-start(f32[864,4,128]{2,1,0:T(4,128)} %param.2) | copy-start | bytes 5308420
  3.6 24.2 %collective-permute-start = (f32[864,2,128]{2,0,1:T(8,128)}, f32[864,2,128]{2,0,1:T(8,128)}, u32[]{:S(2)}, u32[]{:S(2)}) collective-permute-start(f32[864,2,128]{2,0,1:T(8,128)} %get-tuple-element.19), channel_id=1, source_target_pairs={{0,1},{1,2},{2,3},{3,4},{4,5},{5,6},{6,7},{7,8},{8,9},{9,10},{10,1... | collective-permute-start | bytes 2654216 | tf_op jit(solution)/shard_map/ppermute | solution.py:28
  5.5 36.6 %collective-permute-start.1 = (f32[864,2,128]{2,0,1:T(8,128)}, f32[864,2,128]{2,0,1:T(8,128)}, u32[]{:S(2)}, u32[]{:S(2)}) collective-permute-start(f32[864,2,128]{2,0,1:T(8,128)} %get-tuple-element.18), channel_id=1, source_target_pairs={{1,0},{2,1},{3,2},{4,3},{5,4},{6,5},{7,6},{8,7},{9,8},{10,9},{11,1... | collective-permute-start | bytes 2654216 | tf_op jit(solution)/shard_map/ppermute | solution.py:31
  51.2 2.6 %copy-start.1 = (f32[16,864]{1,0:T(8,128)S(1)}, f32[16,864]{1,0:T(8,128)}, u32[]{:S(2)}) copy-start(f32[16,864]{1,0:T(8,128)} %stack.2) | copy-start | bytes 165892
  55.1 14.2 %collective-permute-start.2 = (f32[16,4,128]{2,1,0:T(4,128)S(1)}, f32[16,4,128]{2,1,0:T(4,128)S(1)}, u32[]{:S(2)}, u32[]{:S(2)}) collective-permute-start(f32[16,4,128]{2,1,0:T(4,128)S(1)} %copy.92), channel_id=1, source_target_pairs={{0,16},{16,0},{32,48},{48,32},{64,80},{80,64},{96,112},{112,96},{1... | collective-permute-start | bytes 98312 | tf_op jit(solution)/shard_map/ppermute | solution.py:96
  65.6 5.2 %collective-permute-start.3 = (f32[16,4,128]{2,1,0:T(4,128)S(1)}, f32[16,4,128]{2,1,0:T(4,128)S(1)}, u32[]{:S(2)}, u32[]{:S(2)}) collective-permute-start(f32[16,4,128]{2,1,0:T(4,128)S(1)} %copy.92), channel_id=1, source_target_pairs={{0,32},{16,48},{32,0},{48,16},{64,96},{80,112},{96,64},{112,80},{1... | collective-permute-start | bytes 98312 | tf_op jit(solution)/shard_map/ppermute | solution.py:96
  67.9 5.7 %collective-permute-start.4 = (f32[16,4,128]{2,1,0:T(4,128)S(1)}, f32[16,4,128]{2,1,0:T(4,128)S(1)}, u32[]{:S(2)}, u32[]{:S(2)}) collective-permute-start(f32[16,4,128]{2,1,0:T(4,128)S(1)} %copy.92), channel_id=1, source_target_pairs={{0,48},{16,32},{32,16},{48,0},{64,112},{80,96},{96,80},{112,64},{1... | collective-permute-start | bytes 98312 | tf_op jit(solution)/shard_map/ppermute | solution.py:96
  73.6 5.7 %collective-permute-start.6 = (f32[16,4,128]{2,1,0:T(4,128)S(1)}, f32[16,4,128]{2,1,0:T(4,128)S(1)}, u32[]{:S(2)}, u32[]{:S(2)}) collective-permute-start(f32[16,4,128]{2,1,0:T(4,128)S(1)} %add_add_fusion.3), channel_id=1, source_target_pairs={{0,128},{16,144},{32,160},{48,176},{64,192},{80,208},{96,224},{112... | collective-permute-start | bytes 98312 | tf_op jit(solution)/shard_map/ppermute | solution.py:96
  77.1 5.1 %collective-permute-start.7 = (f32[16,4,128]{2,1,0:T(4,128)S(1)}, f32[16,4,128]{2,1,0:T(4,128)S(1)}, u32[]{:S(2)}, u32[]{:S(2)}) collective-permute-start(f32[16,4,128]{2,1,0:T(4,128)S(1)} %add_add_fusion.3), channel_id=1, source_target_pairs={{0,192},{16,208},{32,224},{48,240},{64,128},{80,144},{96,160},{112... | collective-permute-start | bytes 98312 | tf_op jit(solution)/shard_map/ppermute | solution.py:96
  78.2 4.1 %collective-permute-start.5 = (f32[16,4,128]{2,1,0:T(4,128)S(1)}, f32[16,4,128]{2,1,0:T(4,128)S(1)}, u32[]{:S(2)}, u32[]{:S(2)}) collective-permute-start(f32[16,4,128]{2,1,0:T(4,128)S(1)} %add_add_fusion.3), channel_id=1, source_target_pairs={{0,64},{16,80},{32,96},{48,112},{64,0},{80,16},{96,32},{112,48},{1... | collective-permute-start | bytes 98312 | tf_op jit(solution)/shard_map/ppermute | solution.py:96
  85.1 44.9 %collective-permute-start.8 = (f32[864,2,128]{2,0,1:T(8,128)S(1)}, f32[864,2,128]{2,0,1:T(8,128)S(1)}, u32[]{:S(2)}, u32[]{:S(2)}) collective-permute-start(f32[864,2,128]{2,0,1:T(8,128)S(1)} %get-tuple-element.16), channel_id=1, source_target_pairs={{0,1},{1,2},{2,3},{3,4},{4,5},{5,6},{6,7},{7,8},{8,9},{9,10},{10,1... | collective-permute-start | bytes 2654216 | tf_op jit(solution)/shard_map/ppermute | solution.py:28
  87.0 43.0 %collective-permute-start.9 = (f32[864,2,128]{2,0,1:T(8,128)S(1)}, f32[864,2,128]{2,0,1:T(8,128)S(1)}, u32[]{:S(2)}, u32[]{:S(2)}) collective-permute-start(f32[864,2,128]{2,0,1:T(8,128)S(1)} %get-tuple-element.17), channel_id=1, source_target_pairs={{1,0},{2,1},{3,2},{4,3},{5,4},{6,5},{7,6},{8,7},{9,8},{10,9},{11,1... | collective-permute-start | bytes 2654216 | tf_op jit(solution)/shard_map/ppermute | solution.py:31
  141.1 4.5 %collective-permute-start.10 = (f32[16,4,128]{2,1,0:T(4,128)S(1)}, f32[16,4,128]{2,1,0:T(4,128)S(1)}, u32[]{:S(2)}, u32[]{:S(2)}) collective-permute-start(f32[16,4,128]{2,1,0:T(4,128)S(1)} %copy.96), channel_id=1, source_target_pairs={{0,16},{16,0},{32,48},{48,32},{64,80},{80,64},{96,112},{112,96},{1... | collective-permute-start | bytes 98312 | tf_op jit(solution)/shard_map/ppermute | solution.py:96
  141.7 4.8 %collective-permute-start.11 = (f32[16,4,128]{2,1,0:T(4,128)S(1)}, f32[16,4,128]{2,1,0:T(4,128)S(1)}, u32[]{:S(2)}, u32[]{:S(2)}) collective-permute-start(f32[16,4,128]{2,1,0:T(4,128)S(1)} %copy.96), channel_id=1, source_target_pairs={{0,32},{16,48},{32,0},{48,16},{64,96},{80,112},{96,64},{112,80},{1... | collective-permute-start | bytes 98312 | tf_op jit(solution)/shard_map/ppermute | solution.py:96
  142.4 5.7 %collective-permute-start.12 = (f32[16,4,128]{2,1,0:T(4,128)S(1)}, f32[16,4,128]{2,1,0:T(4,128)S(1)}, u32[]{:S(2)}, u32[]{:S(2)}) collective-permute-start(f32[16,4,128]{2,1,0:T(4,128)S(1)} %copy.96), channel_id=1, source_target_pairs={{0,48},{16,32},{32,16},{48,0},{64,112},{80,96},{96,80},{112,64},{1... | collective-permute-start | bytes 98312 | tf_op jit(solution)/shard_map/ppermute | solution.py:96
  148.2 5.5 %collective-permute-start.14 = (f32[16,4,128]{2,1,0:T(4,128)S(1)}, f32[16,4,128]{2,1,0:T(4,128)S(1)}, u32[]{:S(2)}, u32[]{:S(2)}) collective-permute-start(f32[16,4,128]{2,1,0:T(4,128)S(1)} %add_add_fusion.1), channel_id=1, source_target_pairs={{0,128},{16,144},{32,160},{48,176},{64,192},{80,208},{96,224},{112... | collective-permute-start | bytes 98312 | tf_op jit(solution)/shard_map/ppermute | solution.py:96
  149.8 5.1 %collective-permute-start.15 = (f32[16,4,128]{2,1,0:T(4,128)S(1)}, f32[16,4,128]{2,1,0:T(4,128)S(1)}, u32[]{:S(2)}, u32[]{:S(2)}) collective-permute-start(f32[16,4,128]{2,1,0:T(4,128)S(1)} %add_add_fusion.1), channel_id=1, source_target_pairs={{0,192},{16,208},{32,224},{48,240},{64,128},{80,144},{96,160},{112... | collective-permute-start | bytes 98312 | tf_op jit(solution)/shard_map/ppermute | solution.py:96
  150.8 4.1 %collective-permute-start.13 = (f32[16,4,128]{2,1,0:T(4,128)S(1)}, f32[16,4,128]{2,1,0:T(4,128)S(1)}, u32[]{:S(2)}, u32[]{:S(2)}) collective-permute-start(f32[16,4,128]{2,1,0:T(4,128)S(1)} %add_add_fusion.1), channel_id=1, source_target_pairs={{0,64},{16,80},{32,96},{48,112},{64,0},{80,16},{96,32},{112,48},{1... | collective-permute-start | bytes 98312 | tf_op jit(solution)/shard_map/ppermute | solution.py:96

commit v2 on v1

--- a/solution.py
+++ b/solution.py
@@ -1,6 +1,7 @@
 import math
 
 import jax
+import numpy as np
 import jax.numpy as jnp
 from jax import lax
 from jax.sharding import PartitionSpec as P
@@ -31,6 +32,39 @@
         high = lax.ppermute(lax.slice_in_dim(block, 0, width, axis=dim), axis, backward)
         block = jnp.concatenate([low, block, high], axis=dim)
     return block
+
+
+def halo_signs(vel_count, amount):
+    spacing = 2.0 * speed_limit / (NVX - 1)
+    signs = []
+    for member in range(vel_count):
+        index = np.arange(member * amount, (member + 1) * amount)
+        along_x_part = np.float32(-speed_limit) + np.float32(spacing) * (index // (NVX * NVX)).astype(np.float32)
+        if np.all(along_x_part > 0):
+            signs.append(1)
+        elif np.all(along_x_part < 0):
+            signs.append(-1)
+        else:
+            return None
+    return signs
+
+
+def with_upwind_halo(block, signs):
+    count = lax.axis_size("space")
+    rows = block.shape[1]
+    forward = [(i, i + 1) for i in range(count - 1)]
+    backward = [(target, source) for source, target in forward]
+    low = lax.ppermute(block[:, rows - 1 :], "space", forward)
+    high = lax.ppermute(block[:, :1], "space", backward)
+    pairs = []
+    for member, sign in enumerate(signs):
+        for source, target in forward if sign > 0 else backward:
+            pairs.append((member * count + source, member * count + target))
+    positive = jnp.asarray(np.array(signs, np.int32))[lax.axis_index("vel")] > 0
+    extra = lax.ppermute(
+        jnp.where(positive, block[:, rows - 2 : rows - 1], block[:, 1:2]), ("vel", "space"), pairs
+    )
+    return jnp.concatenate([extra, low, block, high, extra], axis=1)
 
 
 def speeds(offset, amount):
@@ -233,8 +267,12 @@
     along_x_part, along_y_part, along_z_part = speeds(lax.axis_index("vel") * amount, amount)
     distribution_table = initial
     kelvin_level = jnp.zeros(site_kind.shape, jnp.float32)
+    signs = halo_signs(lax.axis_size("vel"), amount)
     for section in range(STEPS):
-        padded = with_halo(distribution_table, (("space", 1),), 2)
+        if signs is None or distribution_table.shape[1] < 2:
+            padded = with_halo(distribution_table, (("space", 1),), 2)
+        else:
+            padded = with_upwind_halo(distribution_table, signs)
         advected_distribution = transport(padded, along_x_part, along_y_part)
         distribution_table, kelvin_level = approach_increment(
             advected_distribution, site_kind, along_x_part, along_y_part, along_z_part

time: 164 us -> 143 us (0.87); the launches traced: 161 us -> 143 us
  waiting for transfers between devices: 66.8 us -> 51.5 us
  starting transfers between devices: 47.8 us -> 54.6 us
  local copies, waits for them, and re-layouts: 11.3 us -> 5.09 us
  other arithmetic: 31.1 us -> 27.2 us
    ppermute x4 -> x6, waiting for transfers between devices: 52.7 us -> 37.5 us  [the longest x2 16.9 us: with_upwind_halo(): high = lax.ppermute(block[:, :1], 'space', backward)]
    ppermute x12, starting transfers between devices: 26.7 us -> 31.8 us  [vel_sum(): lax.ppermute(local, 'vel', [(i, i ^ mask) for i in range(count)])]
    another operation x1, local copies, waits for them, and re-layouts: 2.69 us -> 0.11 us  [macroscopic_moments(): jnp.stack([ones, along_x_part, along_y_part, along_z_part, magnitude_squa...]
    ppermute x4 -> x6, starting transfers between devices: 21.1 us -> 22.8 us  [the longest x2 11.7 us: with_upwind_halo(): high = lax.ppermute(block[:, :1], 'space', backward)]
  transfers between devices with their start and end apart: 16 -> 18, of which waited for: 11 -> 14; matrix products, arithmetic and copies ran while one was open for 6% -> 1% of each run, Pallas kernels for 0% -> 0%
where the time goes in v2:
time: 143 us
  starting transfers between devices  54.6 us (38%)
  waiting for transfers between devices  51.5 us (36%)
  other arithmetic  27.2 us (19%)
  local copies, waits for them, and re-layouts  5.09 us (4%)
  matrix products  2.58 us (2%)
  between operations  1.64 us (1%)
    ppermute x12, starting transfers between devices, vel_sum(): lax.ppermute(local, 'vel', [(i, i ^ mask) for i in range(count)])  31.8 us
    ppermute x2, waiting for transfers between devices, with_upwind_halo(): high = lax.ppermute(block[:, :1], 'space', backward)  16.9 us
    ppermute x12, waiting for transfers between devices, vel_sum(): lax.ppermute(local, 'vel', [(i, i ^ mask) for i in range(count)])  14 us
    ppermute x2, waiting for transfers between devices, with_upwind_halo(): lax.ppermute(jnp.where(positive, block[:, rows - 2:rows - 1], block[:, 1:...  12.4 us
    ppermute x2, starting transfers between devices, with_upwind_halo(): high = lax.ppermute(block[:, :1], 'space', backward)  11.7 us
    ppermute x2, waiting for transfers between devices, with_upwind_halo(): low = lax.ppermute(block[:, rows - 1:], 'space', forward)  8.19 us
    mul x4, other arithmetic, sweep(): flux = number * jnp.where(number > 0, left_face, right_face)  7.28 us
    ppermute x2, starting transfers between devices, with_upwind_halo(): lax.ppermute(jnp.where(positive, block[:, rows - 2:rows - 1], block[:, 1:...  7.27 us
  transfers between devices with their start and end apart: 18, of which 14 were waited for; matrix products, arithmetic and copies ran while one was open for 1% of the time, Pallas kernels for 0%

profile of v2, /device:TPU:6, one launch (start us, length us, event | category | flops | bytes accessed | tf_op | source)
XLA Modules:
  0.0 142.7 jit_solution(6889574623562018350)
XLA Ops:
  0.6 1.6 %copy.98 = f32[864,4,128]{2,0,1:T(8,128)S(1)} copy(f32[864,4,128]{2,1,0:T(4,128)} %param.4) | data formatting | bytes 3538944 | tf_op args[0]
  2.3 0.6 dynamic_slice.6
  3.5 1.1 fusion.159
  4.6 1.9 %collective-permute-start = (f32[864,1,128]{2,0,1:T(8,128)}, f32[864,1,128]{2,0,1:T(8,128)S(1)}, u32[]{:S(2)}, u32[]{:S(2)}) collective-permute-start(f32[864,1,128]{2,0,1:T(8,128)} %get-tuple-element.19), channel_id=1, source_target_pairs={{0,1},{1,2},{2,3},{3,4},{4,5},{5,6},{6,7},{7,8},{8,9},{9,10},{10,1... | collective-permute-start | bytes 1327112 | tf_op jit(solution)/shard_map/ppermute | solution.py:57
  6.5 8.8 %collective-permute-start.1 = (f32[864,1,128]{2,0,1:T(8,128)}, f32[864,1,128]{2,0,1:T(8,128)S(1)}, u32[]{:S(2)}, u32[]{:S(2)}) collective-permute-start(f32[864,1,128]{2,0,1:T(8,128)} %get-tuple-element.20), channel_id=1, source_target_pairs={{1,0},{2,1},{3,2},{4,3},{5,4},{6,5},{7,6},{8,7},{9,8},{10,9},{11,1... | collective-permute-start | bytes 1327112 | tf_op jit(solution)/shard_map/ppermute | solution.py:58
  15.3 2.6 %collective-permute-start.2 = (f32[864,1,128]{2,0,1:T(8,128)}, f32[864,1,128]{2,0,1:T(8,128)S(1)}, u32[]{:S(2)}, u32[]{:S(2)}) collective-permute-start(f32[864,1,128]{2,0,1:T(8,128)} %get-tuple-element.21), channel_id=1, source_target_pairs={{1,0},{2,1},{3,2},{4,3},{5,4},{6,5},{7,6},{8,7},{9,8},{10,9},{11,1... | collective-permute-start | bytes 1327112 | tf_op jit(solution)/shard_map/ppermute | solution.py:64
  18.1 0.1 fusion.86
  18.1 0.1 add_add_fusion.4
  18.2 0.1 fusion.147
  18.3 0.1 fusion.149
  18.4 0.1 fusion.151
  18.5 0.1 fusion.153
  18.6 0.1 stack.2
  18.8 0.9 collective-permute-done
  19.7 5.3 %collective-permute-done.1 = f32[864,1,128]{2,0,1:T(8,128)S(1)} collective-permute-done((f32[864,1,128]{2,0,1:T(8,128)}, f32[864,1,128]{2,0,1:T(8,128)S(1)}, u32[]{:S(2)}, u32[]{:S(2)}) %collective-permute-start.1) | collective-permute-done | bytes 442400 | tf_op jit(solution)/shard_map/ppermute | solution.py:58
  25.0 5.9 %collective-permute-done.2 = f32[864,1,128]{2,0,1:T(8,128)S(1)} collective-permute-done((f32[864,1,128]{2,0,1:T(8,128)}, f32[864,1,128]{2,0,1:T(8,128)S(1)}, u32[]{:S(2)}, u32[]{:S(2)}) %collective-permute-start.2) | collective-permute-done | bytes 442400 | tf_op jit(solution)/shard_map/ppermute | solution.py:64
  30.9 0.3 maximum_subtract_fusion
  31.2 1.1 minimum_multiply_fusion.3
  32.3 1.1 fusion.16
  33.4 0.4 copy-done
  33.8 0.2 fusion.61
  34.0 1.9 %fusion.3 = f32[864,4,131]{2,0,1:T(8,128)S(1)} fusion(f32[864,4,128]{2,0,1:T(8,128)S(1)} %fusion.61), kind=kLoop, calls=%fused_computation.11 | loop fusion | flops 452736 | bytes 3580416 | tf_op jit(solution)/shard_map/sub | solution.py:93
  35.9 2.4 %minimum_multiply_fusion.1 = f32[864,4,130]{2,0,1:T(8,128)S(1)} fusion(f32[864,4,131]{2,0,1:T(8,128)S(1)} %fusion.3), kind=kLoop, calls=%fused_computation.23 | loop fusion | flops 3594240 | bytes 5391360 | tf_op jit(solution)/shard_map/mul | solution.py:84
  38.3 2.6 %fusion.2 = f32[864,4,129]{2,0,1:T(8,128)S(1)} fusion(f32[864,4,128]{2,0,1:T(8,128)S(1)} %fusion.61, f32[864,4,130]{2,0,1:T(8,128)S(1)} %minimum_multiply_fusion.1, f32[864]{0:T(1024)S(1)} %get-tuple-element.48, f32[864]{0:T(1024)S(1)} %get-tuple-element.49, f32[864]{0:T(1024)S(1)} %broadcast_multiply_fusion, pred[864]{0:T(1024)(128)(4,1)S(1)} %broadcast_compare_fusion), kind=kLoop, calls=%fused_computation.10 | loop fusion | flops 2674944 | bytes 7130592 | tf_op jit(solution)/shard_map/mul | solution.py:101
  40.9 1.3 fusion.64
  42.2 13.2 %collective-permute-start.3 = (f32[16,4,128]{2,1,0:T(4,128)S(1)}, f32[16,4,128]{2,1,0:T(4,128)S(1)}, u32[]{:S(2)}, u32[]{:S(2)}) collective-permute-start(f32[16,4,128]{2,1,0:T(4,128)S(1)} %copy.100), channel_id=1, source_target_pairs={{0,16},{16,0},{32,48},{48,32},{64,80},{80,64},{96,112},{112,96},{1... | collective-permute-start | bytes 98312 | tf_op jit(solution)/shard_map/ppermute | solution.py:130
  55.4 0.6 collective-permute-start.4
  55.9 1.9 %collective-permute-start.5 = (f32[16,4,128]{2,1,0:T(4,128)S(1)}, f32[16,4,128]{2,1,0:T(4,128)S(1)}, u32[]{:S(2)}, u32[]{:S(2)}) collective-permute-start(f32[16,4,128]{2,1,0:T(4,128)S(1)} %copy.100), channel_id=1, source_target_pairs={{0,48},{16,32},{32,16},{48,0},{64,112},{80,96},{96,80},{112,64},{1... | collective-permute-start | bytes 98312 | tf_op jit(solution)/shard_map/ppermute | solution.py:130
  57.9 2.5 %collective-permute-done.4 = f32[16,4,128]{2,1,0:T(4,128)S(1)} collective-permute-done((f32[16,4,128]{2,1,0:T(4,128)S(1)}, f32[16,4,128]{2,1,0:T(4,128)S(1)}, u32[]{:S(2)}, u32[]{:S(2)}) %collective-permute-start.4) | collective-permute-done | bytes 32800 | tf_op jit(solution)/shard_map/ppermute | solution.py:130
  60.4 1.3 collective-permute-done.5
  61.7 5.8 %collective-permute-start.7 = (f32[16,4,128]{2,1,0:T(4,128)S(1)}, f32[16,4,128]{2,1,0:T(4,128)S(1)}, u32[]{:S(2)}, u32[]{:S(2)}) collective-permute-start(f32[16,4,128]{2,1,0:T(4,128)S(1)} %add_add_fusion.3), channel_id=1, source_target_pairs={{0,128},{16,144},{32,160},{48,176},{64,192},{80,208},{96,224},{112... | collective-permute-start | bytes 98312 | tf_op jit(solution)/shard_map/ppermute | solution.py:130
  67.5 0.1 collective-permute-start.8
  67.6 0.6 collective-permute-start.6
  68.2 1.2 collective-permute-done.7
  69.4 3.2 %collective-permute-done.8 = f32[16,4,128]{2,1,0:T(4,128)S(1)} collective-permute-done((f32[16,4,128]{2,1,0:T(4,128)S(1)}, f32[16,4,128]{2,1,0:T(4,128)S(1)}, u32[]{:S(2)}, u32[]{:S(2)}) %collective-permute-start.8) | collective-permute-done | bytes 32800 | tf_op jit(solution)/shard_map/ppermute | solution.py:130
  72.7 2.7 %fusion.37 = f32[864,4,128]{2,0,1:T(8,128)S(1)} fusion(f32[4,128]{1,0:T(4,128)S(1)} %get-tuple-element.29, f32[4,128]{1,0:T(4,128)S(1)} %get-tuple-element.42, f32[4,128]{1,0:T(4,128)S(1)} %fusion.119, f32[4,128]{1,0:T(4,128)S(1)} %get-tuple-element.36, f32[4,128]{1,0:T(4,128)S(1)} %get-tuple-element.37, f32[4,128]{1,0:T(4,128)S(1)} %get-tuple-element.43, ...), kind=kLoop, calls=%fused_computation.71 | loop fusion | flops 13713408 | bytes 7120768 | tf_op jit(solution)/shard_map/jit(_where)/select_n | solution.py:257
  75.4 0.1 fusion.158
  75.5 2.8 %collective-permute-start.10 = (f32[864,1,128]{2,0,1:T(8,128)S(1)}, f32[864,1,128]{2,0,1:T(8,128)S(1)}, u32[]{:S(2)}, u32[]{:S(2)}) collective-permute-start(f32[864,1,128]{2,0,1:T(8,128)S(1)} %get-tuple-element.18), channel_id=1, source_target_pairs={{1,0},{2,1},{3,2},{4,3},{5,4},{6,5},{7,6},{8,7},{9,8},{10,9},{11,1... | collective-permute-start | bytes 1327112 | tf_op jit(solution)/shard_map/ppermute | solution.py:58
  78.4 4.7 %collective-permute-start.11 = (f32[864,1,128]{2,0,1:T(8,128)S(1)}, f32[864,1,128]{2,0,1:T(8,128)S(1)}, u32[]{:S(2)}, u32[]{:S(2)}) collective-permute-start(f32[864,1,128]{2,0,1:T(8,128)S(1)} %get-tuple-element.17), channel_id=1, source_target_pairs={{1,0},{2,1},{3,2},{4,3},{5,4},{6,5},{7,6},{8,7},{9,8},{10,9},{11,1... | collective-permute-start | bytes 1327112 | tf_op jit(solution)/shard_map/ppermute | solution.py:64
  83.1 1.9 %collective-permute-start.9 = (f32[864,1,128]{2,0,1:T(8,128)S(1)}, f32[864,1,128]{2,0,1:T(8,128)S(1)}, u32[]{:S(2)}, u32[]{:S(2)}) collective-permute-start(f32[864,1,128]{2,0,1:T(8,128)S(1)} %get-tuple-element.16), channel_id=1, source_target_pairs={{0,1},{1,2},{2,3},{3,4},{4,5},{5,6},{6,7},{7,8},{8,9},{9,10},{10,1... | collective-permute-start | bytes 1327112 | tf_op jit(solution)/shard_map/ppermute | solution.py:57
  85.0 11.6 %collective-permute-done.10 = f32[864,1,128]{2,0,1:T(8,128)S(1)} collective-permute-done((f32[864,1,128]{2,0,1:T(8,128)S(1)}, f32[864,1,128]{2,0,1:T(8,128)S(1)}, u32[]{:S(2)}, u32[]{:S(2)}) %collective-permute-start.10) | collective-permute-done | bytes 442400 | tf_op jit(solution)/shard_map/ppermute | solution.py:58
  96.6 6.6 %collective-permute-done.11 = f32[864,1,128]{2,0,1:T(8,128)S(1)} collective-permute-done((f32[864,1,128]{2,0,1:T(8,128)S(1)}, f32[864,1,128]{2,0,1:T(8,128)S(1)}, u32[]{:S(2)}, u32[]{:S(2)}) %collective-permute-start.11) | collective-permute-done | bytes 442400 | tf_op jit(solution)/shard_map/ppermute | solution.py:64
  103.1 7.3 %collective-permute-done.9 = f32[864,1,128]{2,0,1:T(8,128)S(1)} collective-permute-done((f32[864,1,128]{2,0,1:T(8,128)S(1)}, f32[864,1,128]{2,0,1:T(8,128)S(1)}, u32[]{:S(2)}, u32[]{:S(2)}) %collective-permute-start.9) | collective-permute-done | bytes 442400 | tf_op jit(solution)/shard_map/ppermute | solution.py:57
  110.4 0.3 maximum_subtract_fusion.1
  110.7 1.1 minimum_multiply_fusion.2
  111.9 1.1 fusion.12
  113.0 0.2 fusion.59
  113.2 1.9 %fusion.8 = f32[864,4,131]{2,0,1:T(8,128)S(1)} fusion(f32[864,4,128]{2,0,1:T(8,128)S(1)} %fusion.59), kind=kLoop, calls=%fused_computation.16 | loop fusion | flops 452736 | bytes 3580416 | tf_op jit(solution)/shard_map/sub | solution.py:93
  115.1 2.4 %minimum_multiply_fusion = f32[864,4,130]{2,0,1:T(8,128)S(1)} fusion(f32[864,4,131]{2,0,1:T(8,128)S(1)} %fusion.8), kind=kLoop, calls=%fused_computation.22 | loop fusion | flops 3594240 | bytes 5391360 | tf_op jit(solution)/shard_map/mul | solution.py:84
  117.5 2.6 %fusion.7 = f32[864,4,129]{2,0,1:T(8,128)S(1)} fusion(f32[864,4,128]{2,0,1:T(8,128)S(1)} %fusion.59, f32[864,4,130]{2,0,1:T(8,128)S(1)} %minimum_multiply_fusion, f32[864]{0:T(1024)S(1)} %get-tuple-element.48, f32[864]{0:T(1024)S(1)} %get-tuple-element.49, f32[864]{0:T(1024)S(1)} %broadcast_multiply_fusion, pred[864]{0:T(1024)(128)(4,1)S(1)} %broadcast_compare_fusion), kind=kLoop, calls=%fused_computation.15 | loop fusion | flops 2674944 | bytes 7130592 | tf_op jit(solution)/shard_map/mul | solution.py:101
  120.1 1.3 fusion.62
  121.4 0.1 collective-permute-start.12
  121.5 0.1 collective-permute-start.13
  121.6 4.3 %collective-permute-start.14 = (f32[16,4,128]{2,1,0:T(4,128)S(1)}, f32[16,4,128]{2,1,0:T(4,128)S(1)}, u32[]{:S(2)}, u32[]{:S(2)}) collective-permute-start(f32[16,4,128]{2,1,0:T(4,128)S(1)} %copy.104), channel_id=1, source_target_pairs={{0,48},{16,32},{32,16},{48,0},{64,112},{80,96},{96,80},{112,64},{1... | collective-permute-start | bytes 98312 | tf_op jit(solution)/shard_map/ppermute | solution.py:130
  125.9 0.5 collective-permute-done.13
  126.4 1.7 %collective-permute-done.14 = f32[16,4,128]{2,1,0:T(4,128)S(1)} collective-permute-done((f32[16,4,128]{2,1,0:T(4,128)S(1)}, f32[16,4,128]{2,1,0:T(4,128)S(1)}, u32[]{:S(2)}, u32[]{:S(2)}) %collective-permute-start.14) | collective-permute-done | bytes 32800 | tf_op jit(solution)/shard_map/ppermute | solution.py:130
  128.1 3.7 %collective-permute-start.16 = (f32[16,4,128]{2,1,0:T(4,128)S(1)}, f32[16,4,128]{2,1,0:T(4,128)S(1)}, u32[]{:S(2)}, u32[]{:S(2)}) collective-permute-start(f32[16,4,128]{2,1,0:T(4,128)S(1)} %add_add_fusion.1), channel_id=1, source_target_pairs={{0,128},{16,144},{32,160},{48,176},{64,192},{80,208},{96,224},{112... | collective-permute-start | bytes 98312 | tf_op jit(solution)/shard_map/ppermute | solution.py:130
  131.8 0.8 collective-permute-start.17
  132.6 0.8 collective-permute-start.15
  133.4 0.3 collective-permute-done.16
  133.7 3.2 %collective-permute-done.17 = f32[16,4,128]{2,1,0:T(4,128)S(1)} collective-permute-done((f32[16,4,128]{2,1,0:T(4,128)S(1)}, f32[16,4,128]{2,1,0:T(4,128)S(1)}, u32[]{:S(2)}, u32[]{:S(2)}) %collective-permute-start.17) | collective-permute-done | bytes 32800 | tf_op jit(solution)/shard_map/ppermute | solution.py:130
  137.0 0.6 fusion.144
  137.6 2.7 %fusion.57 = f32[864,4,128]{2,0,1:T(8,128)S(1)} fusion(f32[4,128]{1,0:T(4,128)S(1)} %get-tuple-element.32, f32[4,128]{1,0:T(4,128)S(1)} %get-tuple-element.38, f32[4,128]{1,0:T(4,128)S(1)} %get-tuple-element.31, f32[4,128]{1,0:T(4,128)S(1)} %get-tuple-element.23, f32[4,128]{1,0:T(4,128)S(1)} %get-tuple-element.22, f32[4,128]{1,0:T(4,128)S(1)} %get-tuple-element.39, ...), kind=kLoop, calls=%fused_computation.91 | loop fusion | flops 13713408 | bytes 7120768 | tf_op jit(solution)/shard_map/jit(_where)/select_n | solution.py:257
  140.3 2.3 %copy.107 = f32[864,4,128]{2,1,0:T(4,128)} copy(f32[864,4,128]{2,0,1:T(8,128)S(1)} %fusion.57) | data formatting | bytes 3538944
  (34 shorter events, 0.5 us)
Async XLA Ops:
  0.6 1.6 %copy-start.2 = (s32[16]{0:T(128)S(1)}, s32[16]{0:T(128)}, u32[]{:S(2)}) copy-start(s32[16]{0:T(128)} %constant.97.clone) | copy-start | bytes 196
  2.2 16.6 %copy-start.1 = (s32[4,128]{1,0:T(4,128)S(1)}, s32[4,128]{1,0:T(4,128)}, u32[]{:S(2)}) copy-start(s32[4,128]{1,0:T(4,128)} %param.5) | copy-start | bytes 6148
  4.6 15.1 %collective-permute-start = (f32[864,1,128]{2,0,1:T(8,128)}, f32[864,1,128]{2,0,1:T(8,128)S(1)}, u32[]{:S(2)}, u32[]{:S(2)}) collective-permute-start(f32[864,1,128]{2,0,1:T(8,128)} %get-tuple-element.19), channel_id=1, source_target_pairs={{0,1},{1,2},{2,3},{3,4},{4,5},{5,6},{6,7},{7,8},{8,9},{9,10},{10,1... | collective-permute-start | bytes 1327112 | tf_op jit(solution)/shard_map/ppermute | solution.py:57
  6.5 18.5 %collective-permute-start.1 = (f32[864,1,128]{2,0,1:T(8,128)}, f32[864,1,128]{2,0,1:T(8,128)S(1)}, u32[]{:S(2)}, u32[]{:S(2)}) collective-permute-start(f32[864,1,128]{2,0,1:T(8,128)} %get-tuple-element.20), channel_id=1, source_target_pairs={{1,0},{2,1},{3,2},{4,3},{5,4},{6,5},{7,6},{8,7},{9,8},{10,9},{11,1... | collective-permute-start | bytes 1327112 | tf_op jit(solution)/shard_map/ppermute | solution.py:58
  15.3 15.5 %collective-permute-start.2 = (f32[864,1,128]{2,0,1:T(8,128)}, f32[864,1,128]{2,0,1:T(8,128)S(1)}, u32[]{:S(2)}, u32[]{:S(2)}) collective-permute-start(f32[864,1,128]{2,0,1:T(8,128)} %get-tuple-element.21), channel_id=1, source_target_pairs={{1,0},{2,1},{3,2},{4,3},{5,4},{6,5},{7,6},{8,7},{9,8},{10,9},{11,1... | collective-permute-start | bytes 1327112 | tf_op jit(solution)/shard_map/ppermute | solution.py:64
  32.3 1.5 %copy-start = (f32[864,4,128]{2,1,0:T(4,128)S(1)}, f32[864,4,128]{2,1,0:T(4,128)}, u32[]{:S(2)}) copy-start(f32[864,4,128]{2,1,0:T(4,128)} %param.4) | copy-start | bytes 5308420
  42.2 15.7 %collective-permute-start.3 = (f32[16,4,128]{2,1,0:T(4,128)S(1)}, f32[16,4,128]{2,1,0:T(4,128)S(1)}, u32[]{:S(2)}, u32[]{:S(2)}) collective-permute-start(f32[16,4,128]{2,1,0:T(4,128)S(1)} %copy.100), channel_id=1, source_target_pairs={{0,16},{16,0},{32,48},{48,32},{64,80},{80,64},{96,112},{112,96},{1... | collective-permute-start | bytes 98312 | tf_op jit(solution)/shard_map/ppermute | solution.py:130
  55.4 5.0 %collective-permute-start.4 = (f32[16,4,128]{2,1,0:T(4,128)S(1)}, f32[16,4,128]{2,1,0:T(4,128)S(1)}, u32[]{:S(2)}, u32[]{:S(2)}) collective-permute-start(f32[16,4,128]{2,1,0:T(4,128)S(1)} %copy.100), channel_id=1, source_target_pairs={{0,32},{16,48},{32,0},{48,16},{64,96},{80,112},{96,64},{112,80},{1... | collective-permute-start | bytes 98312 | tf_op jit(solution)/shard_map/ppermute | solution.py:130
  55.9 5.7 %collective-permute-start.5 = (f32[16,4,128]{2,1,0:T(4,128)S(1)}, f32[16,4,128]{2,1,0:T(4,128)S(1)}, u32[]{:S(2)}, u32[]{:S(2)}) collective-permute-start(f32[16,4,128]{2,1,0:T(4,128)S(1)} %copy.100), channel_id=1, source_target_pairs={{0,48},{16,32},{32,16},{48,0},{64,112},{80,96},{96,80},{112,64},{1... | collective-permute-start | bytes 98312 | tf_op jit(solution)/shard_map/ppermute | solution.py:130
  61.7 7.7 %collective-permute-start.7 = (f32[16,4,128]{2,1,0:T(4,128)S(1)}, f32[16,4,128]{2,1,0:T(4,128)S(1)}, u32[]{:S(2)}, u32[]{:S(2)}) collective-permute-start(f32[16,4,128]{2,1,0:T(4,128)S(1)} %add_add_fusion.3), channel_id=1, source_target_pairs={{0,128},{16,144},{32,160},{48,176},{64,192},{80,208},{96,224},{112... | collective-permute-start | bytes 98312 | tf_op jit(solution)/shard_map/ppermute | solution.py:130
  67.5 5.1 %collective-permute-start.8 = (f32[16,4,128]{2,1,0:T(4,128)S(1)}, f32[16,4,128]{2,1,0:T(4,128)S(1)}, u32[]{:S(2)}, u32[]{:S(2)}) collective-permute-start(f32[16,4,128]{2,1,0:T(4,128)S(1)} %add_add_fusion.3), channel_id=1, source_target_pairs={{0,192},{16,208},{32,224},{48,240},{64,128},{80,144},{96,160},{112... | collective-permute-start | bytes 98312 | tf_op jit(solution)/shard_map/ppermute | solution.py:130
  67.6 5.0 %collective-permute-start.6 = (f32[16,4,128]{2,1,0:T(4,128)S(1)}, f32[16,4,128]{2,1,0:T(4,128)S(1)}, u32[]{:S(2)}, u32[]{:S(2)}) collective-permute-start(f32[16,4,128]{2,1,0:T(4,128)S(1)} %add_add_fusion.3), channel_id=1, source_target_pairs={{0,64},{16,80},{32,96},{48,112},{64,0},{80,16},{96,32},{112,48},{1... | collective-permute-start | bytes 98312 | tf_op jit(solution)/shard_map/ppermute | solution.py:130
  75.5 21.1 %collective-permute-start.10 = (f32[864,1,128]{2,0,1:T(8,128)S(1)}, f32[864,1,128]{2,0,1:T(8,128)S(1)}, u32[]{:S(2)}, u32[]{:S(2)}) collective-permute-start(f32[864,1,128]{2,0,1:T(8,128)S(1)} %get-tuple-element.18), channel_id=1, source_target_pairs={{1,0},{2,1},{3,2},{4,3},{5,4},{6,5},{7,6},{8,7},{9,8},{10,9},{11,1... | collective-permute-start | bytes 1327112 | tf_op jit(solution)/shard_map/ppermute | solution.py:58
  78.4 24.8 %collective-permute-start.11 = (f32[864,1,128]{2,0,1:T(8,128)S(1)}, f32[864,1,128]{2,0,1:T(8,128)S(1)}, u32[]{:S(2)}, u32[]{:S(2)}) collective-permute-start(f32[864,1,128]{2,0,1:T(8,128)S(1)} %get-tuple-element.17), channel_id=1, source_target_pairs={{1,0},{2,1},{3,2},{4,3},{5,4},{6,5},{7,6},{8,7},{9,8},{10,9},{11,1... | collective-permute-start | bytes 1327112 | tf_op jit(solution)/shard_map/ppermute | solution.py:64
  83.1 27.4 %collective-permute-start.9 = (f32[864,1,128]{2,0,1:T(8,128)S(1)}, f32[864,1,128]{2,0,1:T(8,128)S(1)}, u32[]{:S(2)}, u32[]{:S(2)}) collective-permute-start(f32[864,1,128]{2,0,1:T(8,128)S(1)} %get-tuple-element.16), channel_id=1, source_target_pairs={{0,1},{1,2},{2,3},{3,4},{4,5},{5,6},{6,7},{7,8},{8,9},{9,10},{10,1... | collective-permute-start | bytes 1327112 | tf_op jit(solution)/shard_map/ppermute | solution.py:57
  121.4 4.5 %collective-permute-start.12 = (f32[16,4,128]{2,1,0:T(4,128)S(1)}, f32[16,4,128]{2,1,0:T(4,128)S(1)}, u32[]{:S(2)}, u32[]{:S(2)}) collective-permute-start(f32[16,4,128]{2,1,0:T(4,128)S(1)} %copy.104), channel_id=1, source_target_pairs={{0,16},{16,0},{32,48},{48,32},{64,80},{80,64},{96,112},{112,96},{1... | collective-permute-start | bytes 98312 | tf_op jit(solution)/shard_map/ppermute | solution.py:130
  121.5 4.9 %collective-permute-start.13 = (f32[16,4,128]{2,1,0:T(4,128)S(1)}, f32[16,4,128]{2,1,0:T(4,128)S(1)}, u32[]{:S(2)}, u32[]{:S(2)}) collective-permute-start(f32[16,4,128]{2,1,0:T(4,128)S(1)} %copy.104), channel_id=1, source_target_pairs={{0,32},{16,48},{32,0},{48,16},{64,96},{80,112},{96,64},{112,80},{1... | collective-permute-start | bytes 98312 | tf_op jit(solution)/shard_map/ppermute | solution.py:130
  121.6 6.5 %collective-permute-start.14 = (f32[16,4,128]{2,1,0:T(4,128)S(1)}, f32[16,4,128]{2,1,0:T(4,128)S(1)}, u32[]{:S(2)}, u32[]{:S(2)}) collective-permute-start(f32[16,4,128]{2,1,0:T(4,128)S(1)} %copy.104), channel_id=1, source_target_pairs={{0,48},{16,32},{32,16},{48,0},{64,112},{80,96},{96,80},{112,64},{1... | collective-permute-start | bytes 98312 | tf_op jit(solution)/shard_map/ppermute | solution.py:130
  128.1 5.6 %collective-permute-start.16 = (f32[16,4,128]{2,1,0:T(4,128)S(1)}, f32[16,4,128]{2,1,0:T(4,128)S(1)}, u32[]{:S(2)}, u32[]{:S(2)}) collective-permute-start(f32[16,4,128]{2,1,0:T(4,128)S(1)} %add_add_fusion.1), channel_id=1, source_target_pairs={{0,128},{16,144},{32,160},{48,176},{64,192},{80,208},{96,224},{112... | collective-permute-start | bytes 98312 | tf_op jit(solution)/shard_map/ppermute | solution.py:130
  131.8 5.1 %collective-permute-start.17 = (f32[16,4,128]{2,1,0:T(4,128)S(1)}, f32[16,4,128]{2,1,0:T(4,128)S(1)}, u32[]{:S(2)}, u32[]{:S(2)}) collective-permute-start(f32[16,4,128]{2,1,0:T(4,128)S(1)} %add_add_fusion.1), channel_id=1, source_target_pairs={{0,192},{16,208},{32,224},{48,240},{64,128},{80,144},{96,160},{112... | collective-permute-start | bytes 98312 | tf_op jit(solution)/shard_map/ppermute | solution.py:130
  132.6 4.3 %collective-permute-start.15 = (f32[16,4,128]{2,1,0:T(4,128)S(1)}, f32[16,4,128]{2,1,0:T(4,128)S(1)}, u32[]{:S(2)}, u32[]{:S(2)}) collective-permute-start(f32[16,4,128]{2,1,0:T(4,128)S(1)} %add_add_fusion.1), channel_id=1, source_target_pairs={{0,64},{16,80},{32,96},{48,112},{64,0},{80,16},{96,32},{112,48},{1... | collective-permute-start | bytes 98312 | tf_op jit(solution)/shard_map/ppermute | solution.py:130

commit v3 on v2

--- a/solution.py
+++ b/solution.py
@@ -5,6 +5,7 @@
 import jax.numpy as jnp
 from jax import lax
 from jax.sharding import PartitionSpec as P
+
 
 NVX = 24
 STEPS = 2
@@ -133,7 +134,7 @@
     return local
 
 
-def macroscopic_moments(advected_distribution, along_x_part, along_y_part, along_z_part):
+def moment_totals(advected_distribution, along_x_part, along_y_part, along_z_part):
     magnitude_squares = (
         along_x_part * along_x_part + along_y_part * along_y_part + along_z_part * along_z_part
     )
@@ -159,7 +160,10 @@
         ]
     )
     local = jnp.einsum("kv,vrc->krc", table, advected_distribution, precision=lax.Precision.HIGHEST)
-    totals = vel_sum(local)
+    return vel_sum(local)
+
+
+def derived_moments(totals):
     particle_concentration = totals[0]
     average_drift_x = totals[1] / particle_concentration
     average_drift_y = totals[2] / particle_concentration
@@ -198,7 +202,7 @@
 
 
 def approach_increment(
-    advected_distribution, kind_labels, along_x_part, along_y_part, along_z_part
+    advected_distribution, kind_labels, along_x_part, along_y_part, along_z_part, totals
 ):
     (
         particle_concentration,
@@ -207,7 +211,7 @@
         average_drift_z,
         kelvin_level,
         conductive_transfer,
-    ) = macroscopic_moments(advected_distribution, along_x_part, along_y_part, along_z_part)
+    ) = derived_moments(totals)
     rel_x = along_x_part[:, None, None] - average_drift_x[None]
     rel_y = along_y_part[:, None, None] - average_drift_y[None]
     rel_z = along_z_part[:, None, None] - average_drift_z[None]
@@ -267,17 +271,53 @@
     along_x_part, along_y_part, along_z_part = speeds(lax.axis_index("vel") * amount, amount)
     distribution_table = initial
     kelvin_level = jnp.zeros(site_kind.shape, jnp.float32)
+    rows = distribution_table.shape[1]
     signs = halo_signs(lax.axis_size("vel"), amount)
+    if signs is None or rows < 2:
+        for _ in range(STEPS):
+            padded = with_halo(distribution_table, (("space", 1),), 2)
+            advected_distribution = transport(padded, along_x_part, along_y_part)
+            totals = moment_totals(advected_distribution, along_x_part, along_y_part, along_z_part)
+            distribution_table, kelvin_level = approach_increment(
+                advected_distribution, site_kind, along_x_part, along_y_part, along_z_part, totals
+            )
+        return (distribution_table, kelvin_level)
+    count = lax.axis_size("space")
+    place = lax.axis_index("space") * rows + jnp.arange(rows + 4) - 2
+    positive = jnp.asarray(np.array(signs, np.int32))[lax.axis_index("vel")] > 0
+    slot = jnp.arange(rows + 4)
+    keep = (place >= 0) & (place < count * rows)
+    keep = keep & jnp.where(positive, slot != rows + 3, slot != 0)
+    padded_kinds = with_upwind_halo(site_kind.astype(jnp.float32)[None], signs)[0]
+    padded = with_upwind_halo(distribution_table, signs)
     for section in range(STEPS):
-        if signs is None or distribution_table.shape[1] < 2:
-            padded = with_halo(distribution_table, (("space", 1),), 2)
-        else:
-            padded = with_upwind_halo(distribution_table, signs)
-        advected_distribution = transport(padded, along_x_part, along_y_part)
-        distribution_table, kelvin_level = approach_increment(
-            advected_distribution, site_kind, along_x_part, along_y_part, along_z_part
+        distribution_table, kelvin_level, padded = upwind_step(
+            section, padded, padded_kinds, keep, site_kind, signs, along_x_part, along_y_part, along_z_part
         )
     return (distribution_table, kelvin_level)
+
+
+def upwind_step(section, padded, padded_kinds, keep, site_kind, signs, along_x_part, along_y_part, along_z_part):
+    distribution_table = kelvin_level = None
+    advected_distribution = transport(padded, along_x_part, along_y_part)
+    if section + 1 < STEPS:
+        advected_padded = with_upwind_halo(advected_distribution, signs)
+    totals = moment_totals(advected_distribution, along_x_part, along_y_part, along_z_part)
+    if section + 1 < STEPS:
+        revised, _ = approach_increment(
+            advected_padded,
+            padded_kinds.astype(jnp.int32),
+            along_x_part,
+            along_y_part,
+            along_z_part,
+            with_upwind_halo(totals, signs),
+        )
+        padded = jnp.where(keep[None, :, None], revised, 0.0)
+    else:
+        distribution_table, kelvin_level = approach_increment(
+            advected_distribution, site_kind, along_x_part, along_y_part, along_z_part, totals
+        )
+    return distribution_table, kelvin_level, padded
 
 
 def solution(mesh):

time: 143 us -> 168 us (1.17)
  starting transfers between devices: 54.6 us -> 88 us
  waiting for transfers between devices: 51.5 us -> 32.1 us
  other arithmetic: 27.2 us -> 35.6 us
  local copies, waits for them, and re-layouts: 5.09 us -> 7.46 us
    ppermute x2 -> x4, waiting for transfers between devices: 16.9 us -> 0.01 us  [with_upwind_halo(): high = lax.ppermute(block[:, :1], 'space', backward)]
    ppermute x2 -> x4, starting transfers between devices: 11.7 us -> 27.4 us  [with_upwind_halo(): high = lax.ppermute(block[:, :1], 'space', backward)]
    ppermute x2 -> x4, starting transfers between devices: 7.27 us -> 23 us  [with_upwind_halo(): lax.ppermute(jnp.where(positive, block[:, rows - 2:rows - 1], block[:, 1:...]
    select_n x0 -> x1, other arithmetic: none -> 9.6 us  [upwind_step(): padded = jnp.where(keep[None, :, None], revised, 0.0)]
    ppermute x2 -> x4, waiting for transfers between devices: 12.4 us -> 7.49 us  [with_upwind_halo(): lax.ppermute(jnp.where(positive, block[:, rows - 2:rows - 1], block[:, 1:...]
    ppermute x2 -> x4, starting transfers between devices: 3.83 us -> 8.17 us  [with_upwind_halo(): low = lax.ppermute(block[:, rows - 1:], 'space', forward)]
    ppermute x12, waiting for transfers between devices: 14 us -> 16.7 us  [vel_sum(): lax.ppermute(local, 'vel', [(i, i ^ mask) for i in range(count)])]
    select_n x2 -> x1, other arithmetic: 5.35 us -> 2.67 us  [approach_increment(): jnp.where(kind_labels == 1, wall_distribution, jnp.where(kind_labels == 2...]
  transfers between devices with their start and end apart: 18 -> 24, of which waited for: 14 -> 10; matrix products, arithmetic and copies ran while one was open for 1% -> 8% of each run, Pallas kernels for 0% -> 0%
where the time goes in v3:
time: 168 us; the launch traced here: 167 us
  starting transfers between devices  88 us (52%)
  other arithmetic  35.6 us (21%)
  waiting for transfers between devices  32.1 us (19%)
  local copies, waits for them, and re-layouts  7.46 us (4%)
  matrix products  2.25 us (1%)
  between operations  1.8 us (1%)
    ppermute x12, starting transfers between devices, vel_sum(): lax.ppermute(local, 'vel', [(i, i ^ mask) for i in range(count)])  29.4 us
    ppermute x4, starting transfers between devices, with_upwind_halo(): high = lax.ppermute(block[:, :1], 'space', backward)  27.4 us
    ppermute x4, starting transfers between devices, with_upwind_halo(): lax.ppermute(jnp.where(positive, block[:, rows - 2:rows - 1], block[:, 1:...  23 us
    ppermute x12, waiting for transfers between devices, vel_sum(): lax.ppermute(local, 'vel', [(i, i ^ mask) for i in range(count)])  16.7 us
    select_n x1, other arithmetic, upwind_step(): padded = jnp.where(keep[None, :, None], revised, 0.0)  9.6 us
    ppermute x4, starting transfers between devices, with_upwind_halo(): low = lax.ppermute(block[:, rows - 1:], 'space', forward)  8.17 us
    ppermute x4, waiting for transfers between devices, with_upwind_halo(): low = lax.ppermute(block[:, rows - 1:], 'space', forward)  7.84 us
    ppermute x4, waiting for transfers between devices, with_upwind_halo(): lax.ppermute(jnp.where(positive, block[:, rows - 2:rows - 1], block[:, 1:...  7.49 us
  transfers between devices with their start and end apart: 24, of which 10 were waited for; matrix products, arithmetic and copies ran while one was open for 8% of the time, Pallas kernels for 0%

profile of v3, /device:TPU:6, one launch (start us, length us, event | category | flops | bytes accessed | tf_op | source)
XLA Modules:
  0.0 167.2 jit_solution(1367443163406258613)
XLA Ops:
  0.7 1.6 copy.85
  2.3 0.6 dynamic_slice.15
  3.5 1.1 fusion.161
  4.6 8.8 %collective-permute-start.5 = (f32[864,1,128]{2,0,1:T(8,128)}, f32[864,1,128]{2,0,1:T(8,128)S(1)}, u32[]{:S(2)}, u32[]{:S(2)}) collective-permute-start(f32[864,1,128]{2,0,1:T(8,128)} %get-tuple-element.21), channel_id=1, source_target_pairs={{1,0},{2,1},{3,2},{4,3},{5,4},{6,5},{7,6},{8,7},{9,8},{10,9},{11,1... | collective-permute-start | bytes 1327112 | tf_op jit(solution)/shard_map/ppermute | solution.py:65
  13.4 2.6 %collective-permute-start.4 = (f32[864,1,128]{2,0,1:T(8,128)}, f32[864,1,128]{2,0,1:T(8,128)S(1)}, u32[]{:S(2)}, u32[]{:S(2)}) collective-permute-start(f32[864,1,128]{2,0,1:T(8,128)} %get-tuple-element.20), channel_id=1, source_target_pairs={{1,0},{2,1},{3,2},{4,3},{5,4},{6,5},{7,6},{8,7},{9,8},{10,9},{11,1... | collective-permute-start | bytes 1327112 | tf_op jit(solution)/shard_map/ppermute | solution.py:59
  16.0 1.9 %collective-permute-start.3 = (f32[864,1,128]{2,0,1:T(8,128)}, f32[864,1,128]{2,0,1:T(8,128)S(1)}, u32[]{:S(2)}, u32[]{:S(2)}) collective-permute-start(f32[864,1,128]{2,0,1:T(8,128)} %get-tuple-element.19), channel_id=1, source_target_pairs={{0,1},{1,2},{2,3},{3,4},{4,5},{5,6},{6,7},{7,8},{8,9},{9,10},{10,1... | collective-permute-start | bytes 1327112 | tf_op jit(solution)/shard_map/ppermute | solution.py:58
  18.0 8.4 %collective-permute-start = (f32[1,1,128]{2,1,0:T(1,128)S(1)}, f32[1,1,128]{2,1,0:T(1,128)S(1)}, u32[]{:S(2)}, u32[]{:S(2)}) collective-permute-start(f32[1,1,128]{2,1,0:T(1,128)S(1)} %get-tuple-element.51), channel_id=1, source_target_pairs={{1,0},{2,1},{3,2},{4,3},{5,4},{6,5},{7,6},{8,7},{9,8},{10,9},{11,1... | collective-permute-start | bytes 1544 | tf_op jit(solution)/shard_map/ppermute | solution.py:65
  26.4 1.9 %collective-permute-start.1 = (f32[1,1,128]{2,1,0:T(1,128)S(1)}, f32[1,1,128]{2,1,0:T(1,128)S(1)}, u32[]{:S(2)}, u32[]{:S(2)}) collective-permute-start(f32[1,1,128]{2,1,0:T(1,128)S(1)} %get-tuple-element.50), channel_id=1, source_target_pairs={{0,1},{1,2},{2,3},{3,4},{4,5},{5,6},{6,7},{7,8},{8,9},{9,10},{10,1... | collective-permute-start | bytes 1544 | tf_op jit(solution)/shard_map/ppermute | solution.py:58
  28.6 0.1 fusion.156
  28.7 0.1 fusion.150
  29.0 0.1 stack.2
  29.3 8.4 %collective-permute-start.2 = (f32[1,1,128]{2,1,0:T(1,128)S(1)}, f32[1,1,128]{2,1,0:T(1,128)S(1)}, u32[]{:S(2)}, u32[]{:S(2)}) collective-permute-start(f32[1,1,128]{2,1,0:T(1,128)S(1)} %get-tuple-element.49), channel_id=1, source_target_pairs={{1,0},{2,1},{3,2},{4,3},{5,4},{6,5},{7,6},{8,7},{9,8},{10,9},{11,1... | collective-permute-start | bytes 1544 | tf_op jit(solution)/shard_map/ppermute | solution.py:59
  37.8 0.3 maximum_subtract_fusion
  38.1 1.1 minimum_multiply_fusion.3
  39.3 1.1 fusion.37
  40.3 0.4 copy-done
  40.7 0.2 fusion.62
  40.9 1.9 %fusion.23 = f32[864,4,131]{2,0,1:T(8,128)S(1)} fusion(f32[864,4,128]{2,0,1:T(8,128)S(1)} %fusion.62), kind=kLoop, calls=%fused_computation.37 | loop fusion | flops 452736 | bytes 3580416 | tf_op jit(solution)/shard_map/sub | solution.py:94
  42.8 2.4 %minimum_multiply_fusion.1 = f32[864,4,130]{2,0,1:T(8,128)S(1)} fusion(f32[864,4,131]{2,0,1:T(8,128)S(1)} %fusion.23), kind=kLoop, calls=%fused_computation.50 | loop fusion | flops 3594240 | bytes 5391360 | tf_op jit(solution)/shard_map/mul | solution.py:85
  45.2 2.6 %fusion.22 = f32[864,4,129]{2,0,1:T(8,128)S(1)} fusion(f32[864,4,128]{2,0,1:T(8,128)S(1)} %fusion.62, f32[864,4,130]{2,0,1:T(8,128)S(1)} %minimum_multiply_fusion.1, f32[864]{0:T(1024)S(1)} %get-tuple-element.56, f32[864]{0:T(1024)S(1)} %get-tuple-element.57, f32[864]{0:T(1024)S(1)} %broadcast_multiply_fusion, pred[864]{0:T(1024)(128)(4,1)S(1)} %broadcast_compare_fusion), kind=kLoop, calls=%fused_computation.36 | loop fusion | flops 2674944 | bytes 7130592 | tf_op jit(solution)/shard_map/mul | solution.py:102
  47.8 0.5 fusion.61
  48.4 1.0 fusion.65
  49.3 7.0 %collective-permute-start.7 = (f32[16,4,128]{2,1,0:T(4,128)S(1)}, f32[16,4,128]{2,1,0:T(4,128)S(1)}, u32[]{:S(2)}, u32[]{:S(2)}) collective-permute-start(f32[16,4,128]{2,1,0:T(4,128)S(1)} %copy.87), channel_id=1, source_target_pairs={{0,32},{16,48},{32,0},{48,16},{64,96},{80,112},{96,64},{112,80},{1... | collective-permute-start | bytes 98312 | tf_op jit(solution)/shard_map/ppermute | solution.py:131
  56.3 2.2 %collective-permute-start.8 = (f32[16,4,128]{2,1,0:T(4,128)S(1)}, f32[16,4,128]{2,1,0:T(4,128)S(1)}, u32[]{:S(2)}, u32[]{:S(2)}) collective-permute-start(f32[16,4,128]{2,1,0:T(4,128)S(1)} %copy.87), channel_id=1, source_target_pairs={{0,48},{16,32},{32,16},{48,0},{64,112},{80,96},{96,80},{112,64},{1... | collective-permute-start | bytes 98312 | tf_op jit(solution)/shard_map/ppermute | solution.py:131
  58.6 3.5 %collective-permute-done.8 = f32[16,4,128]{2,1,0:T(4,128)S(1)} collective-permute-done((f32[16,4,128]{2,1,0:T(4,128)S(1)}, f32[16,4,128]{2,1,0:T(4,128)S(1)}, u32[]{:S(2)}, u32[]{:S(2)}) %collective-permute-start.8) | collective-permute-done | bytes 32800 | tf_op jit(solution)/shard_map/ppermute | solution.py:131
  62.1 0.4 collective-permute-done.6
  62.5 4.8 %collective-permute-start.10 = (f32[16,4,128]{2,1,0:T(4,128)S(1)}, f32[16,4,128]{2,1,0:T(4,128)S(1)}, u32[]{:S(2)}, u32[]{:S(2)}) collective-permute-start(f32[16,4,128]{2,1,0:T(4,128)S(1)} %add_add_fusion.3), channel_id=1, source_target_pairs={{0,128},{16,144},{32,160},{48,176},{64,192},{80,208},{96,224},{112... | collective-permute-start | bytes 98312 | tf_op jit(solution)/shard_map/ppermute | solution.py:131
  67.3 0.7 collective-permute-start.9
  67.9 1.5 collective-permute-done.10
  69.5 2.9 %collective-permute-done.11 = f32[16,4,128]{2,1,0:T(4,128)S(1)} collective-permute-done((f32[16,4,128]{2,1,0:T(4,128)S(1)}, f32[16,4,128]{2,1,0:T(4,128)S(1)}, u32[]{:S(2)}, u32[]{:S(2)}) %collective-permute-start.11) | collective-permute-done | bytes 32800 | tf_op jit(solution)/shard_map/ppermute | solution.py:131
  72.4 3.9 %collective-permute-start.12 = (f32[16,1,128]{2,1,0:T(1,128)S(1)}, f32[16,1,128]{2,1,0:T(1,128)S(1)}, u32[]{:S(2)}, u32[]{:S(2)}) collective-permute-start(f32[16,1,128]{2,1,0:T(1,128)S(1)} %get-tuple-element.40), channel_id=1, source_target_pairs={{1,0},{2,1},{3,2},{4,3},{5,4},{6,5},{7,6},{8,7},{9,8},{10,9},{11,1... | collective-permute-start | bytes 24584 | tf_op jit(solution)/shard_map/ppermute | solution.py:65
  76.3 1.9 %collective-permute-start.13 = (f32[16,1,128]{2,1,0:T(1,128)S(1)}, f32[16,1,128]{2,1,0:T(1,128)S(1)}, u32[]{:S(2)}, u32[]{:S(2)}) collective-permute-start(f32[16,1,128]{2,1,0:T(1,128)S(1)} %get-tuple-element.39), channel_id=1, source_target_pairs={{0,1},{1,2},{2,3},{3,4},{4,5},{5,6},{6,7},{7,8},{8,9},{9,10},{10,1... | collective-permute-start | bytes 24584 | tf_op jit(solution)/shard_map/ppermute | solution.py:58
  78.3 8.4 %collective-permute-start.14 = (f32[16,1,128]{2,1,0:T(1,128)S(1)}, f32[16,1,128]{2,1,0:T(1,128)S(1)}, u32[]{:S(2)}, u32[]{:S(2)}) collective-permute-start(f32[16,1,128]{2,1,0:T(1,128)S(1)} %get-tuple-element.38), channel_id=1, source_target_pairs={{1,0},{2,1},{3,2},{4,3},{5,4},{6,5},{7,6},{8,7},{9,8},{10,9},{11,1... | collective-permute-start | bytes 24584 | tf_op jit(solution)/shard_map/ppermute | solution.py:59
  86.7 0.9 fusion.160
  87.6 1.9 %collective-permute-start.15 = (f32[864,1,128]{2,0,1:T(8,128)}, f32[864,1,128]{2,0,1:T(8,128)S(1)}, u32[]{:S(2)}, u32[]{:S(2)}) collective-permute-start(f32[864,1,128]{2,0,1:T(8,128)} %get-tuple-element.18), channel_id=1, source_target_pairs={{1,0},{2,1},{3,2},{4,3},{5,4},{6,5},{7,6},{8,7},{9,8},{10,9},{11,1... | collective-permute-start | bytes 1327112 | tf_op jit(solution)/shard_map/ppermute | solution.py:65
  89.5 2.4 %collective-permute-start.16 = (f32[864,1,128]{2,0,1:T(8,128)S(1)}, f32[864,1,128]{2,0,1:T(8,128)}, u32[]{:S(2)}, u32[]{:S(2)}) collective-permute-start(f32[864,1,128]{2,0,1:T(8,128)S(1)} %get-tuple-element.17), channel_id=1, source_target_pairs={{0,1},{1,2},{2,3},{3,4},{4,5},{5,6},{6,7},{7,8},{8,9},{9,10},{10,1... | collective-permute-start | bytes 1327112 | tf_op jit(solution)/shard_map/ppermute | solution.py:58
  91.9 8.0 %collective-permute-start.17 = (f32[864,1,128]{2,0,1:T(8,128)S(1)}, f32[864,1,128]{2,0,1:T(8,128)}, u32[]{:S(2)}, u32[]{:S(2)}) collective-permute-start(f32[864,1,128]{2,0,1:T(8,128)S(1)} %get-tuple-element.16), channel_id=1, source_target_pairs={{1,0},{2,1},{3,2},{4,3},{5,4},{6,5},{7,6},{8,7},{9,8},{10,9},{11,1... | collective-permute-start | bytes 1327112 | tf_op jit(solution)/shard_map/ppermute | solution.py:59
  100.1 7.5 %collective-permute-done.15 = f32[864,1,128]{2,0,1:T(8,128)S(1)} collective-permute-done((f32[864,1,128]{2,0,1:T(8,128)}, f32[864,1,128]{2,0,1:T(8,128)S(1)}, u32[]{:S(2)}, u32[]{:S(2)}) %collective-permute-start.15) | collective-permute-done | bytes 442400 | tf_op jit(solution)/shard_map/ppermute | solution.py:65
  107.6 7.8 %collective-permute-done.16 = f32[864,1,128]{2,0,1:T(8,128)} collective-permute-done((f32[864,1,128]{2,0,1:T(8,128)S(1)}, f32[864,1,128]{2,0,1:T(8,128)}, u32[]{:S(2)}, u32[]{:S(2)}) %collective-permute-start.16) | collective-permute-done | bytes 442400 | tf_op jit(solution)/shard_map/ppermute | solution.py:58
  115.4 1.0 constant_dynamic-update-slice_fusion.3
  116.5 0.1 constant_dynamic-update-slice_fusion.2
  116.6 1.0 constant_dynamic-update-slice_fusion.1
  117.7 9.6 %fusion.30 = f32[864,8,128]{2,0,1:T(8,128)S(1)} fusion(f32[864,8,128]{2,0,1:T(8,128)S(1)} %constant_dynamic-update-slice_fusion, f32[8,128]{1,0:T(8,128)S(1)} %get-tuple-element.25, f32[8,128]{1,0:T(8,128)S(1)} %get-tuple-element.43, f32[8,128]{1,0:T(8,128)S(1)} %fusion.86, f32[8,128]{1,0:T(8,128)S(1)} %get-tuple-element.28, ...), kind=kLoop, calls=%fused_computation.49 | loop fusion | flops 26542080 | bytes 7146376 | tf_op jit(solution)/shard_map/jit(_where)/select_n | solution.py:315
  127.3 0.2 slice_subtract_fusion
  127.5 1.1 minimum_multiply_fusion.2
  128.7 1.0 fusion.33
  129.6 0.3 fusion.60
  129.9 1.9 %fusion.28 = f32[864,4,131]{2,0,1:T(8,128)S(1)} fusion(f32[864,4,128]{2,0,1:T(8,128)S(1)} %fusion.60), kind=kLoop, calls=%fused_computation.42 | loop fusion | flops 452736 | bytes 3580416 | tf_op jit(solution)/shard_map/sub | solution.py:94
  131.8 2.4 %minimum_multiply_fusion = f32[864,4,130]{2,0,1:T(8,128)S(1)} fusion(f32[864,4,131]{2,0,1:T(8,128)S(1)} %fusion.28), kind=kLoop, calls=%fused_computation.48 | loop fusion | flops 3594240 | bytes 5391360 | tf_op jit(solution)/shard_map/mul | solution.py:85
  134.2 2.8 %fusion.27 = f32[864,4,129]{2,0,1:T(8,128)S(1)} fusion(f32[864,4,128]{2,0,1:T(8,128)S(1)} %fusion.60, f32[864,4,130]{2,0,1:T(8,128)S(1)} %minimum_multiply_fusion, f32[864]{0:T(1024)S(1)} %get-tuple-element.56, f32[864]{0:T(1024)S(1)} %get-tuple-element.57, f32[864]{0:T(1024)S(1)} %broadcast_multiply_fusion, pred[864]{0:T(1024)(128)(4,1)S(1)} %broadcast_compare_fusion), kind=kLoop, calls=%fused_computation.41 | loop fusion | flops 2674944 | bytes 7130592 | tf_op jit(solution)/shard_map/mul | solution.py:102
  137.0 1.3 fusion.63
  138.3 6.4 %collective-permute-start.19 = (f32[16,4,128]{2,1,0:T(4,128)S(1)}, f32[16,4,128]{2,1,0:T(4,128)S(1)}, u32[]{:S(2)}, u32[]{:S(2)}) collective-permute-start(f32[16,4,128]{2,1,0:T(4,128)S(1)} %copy.91), channel_id=1, source_target_pairs={{0,32},{16,48},{32,0},{48,16},{64,96},{80,112},{96,64},{112,80},{1... | collective-permute-start | bytes 98312 | tf_op jit(solution)/shard_map/ppermute | solution.py:131
  144.7 0.6 collective-permute-start.20
  145.3 0.5 collective-permute-start.18
  145.8 0.9 collective-permute-done.19
  146.6 3.8 %collective-permute-done.20 = f32[16,4,128]{2,1,0:T(4,128)S(1)} collective-permute-done((f32[16,4,128]{2,1,0:T(4,128)S(1)}, f32[16,4,128]{2,1,0:T(4,128)S(1)}, u32[]{:S(2)}, u32[]{:S(2)}) %collective-permute-start.20) | collective-permute-done | bytes 32800 | tf_op jit(solution)/shard_map/ppermute | solution.py:131
  150.5 5.9 %collective-permute-start.22 = (f32[16,4,128]{2,1,0:T(4,128)S(1)}, f32[16,4,128]{2,1,0:T(4,128)S(1)}, u32[]{:S(2)}, u32[]{:S(2)}) collective-permute-start(f32[16,4,128]{2,1,0:T(4,128)S(1)} %add_add_fusion.1), channel_id=1, source_target_pairs={{0,128},{16,144},{32,160},{48,176},{64,192},{80,208},{96,224},{112... | collective-permute-start | bytes 98312 | tf_op jit(solution)/shard_map/ppermute | solution.py:131
  156.4 0.6 collective-permute-start.23
  157.0 0.8 collective-permute-start.21
  157.8 0.5 collective-permute-done.22
  158.3 3.2 %collective-permute-done.23 = f32[16,4,128]{2,1,0:T(4,128)S(1)} collective-permute-done((f32[16,4,128]{2,1,0:T(4,128)S(1)}, f32[16,4,128]{2,1,0:T(4,128)S(1)}, u32[]{:S(2)}, u32[]{:S(2)}) %collective-permute-start.23) | collective-permute-done | bytes 32800 | tf_op jit(solution)/shard_map/ppermute | solution.py:131
  161.6 0.6 fusion.147
  162.2 2.7 %fusion.58 = f32[864,4,128]{2,0,1:T(8,128)S(1)} fusion(f32[4,128]{1,0:T(4,128)S(1)} %get-tuple-element.36, f32[4,128]{1,0:T(4,128)S(1)} %get-tuple-element.45, f32[4,128]{1,0:T(4,128)S(1)} %get-tuple-element.35, f32[4,128]{1,0:T(4,128)S(1)} %get-tuple-element.31, f32[4,128]{1,0:T(4,128)S(1)} %get-tuple-element.30, f32[4,128]{1,0:T(4,128)S(1)} %get-tuple-element.46, ...), kind=kLoop, calls=%fused_computation.92 | loop fusion | flops 13713408 | bytes 7120768 | tf_op jit(solution)/shard_map/jit(_where)/select_n | solution.py:261
  164.9 2.3 %copy.94 = f32[864,4,128]{2,1,0:T(4,128)} copy(f32[864,4,128]{2,0,1:T(8,128)S(1)} %fusion.58) | data formatting | bytes 3538944
  (59 shorter events, 1.1 us)
Async XLA Ops:
  0.6 1.6 copy-start.2
  0.6 17.3 %copy-start.1 = (s32[4,128]{1,0:T(4,128)S(1)}, s32[4,128]{1,0:T(4,128)}, u32[]{:S(2)}) copy-start(s32[4,128]{1,0:T(4,128)} %param.8) | copy-start | bytes 6148
  4.6 24.7 %collective-permute-start.5 = (f32[864,1,128]{2,0,1:T(8,128)}, f32[864,1,128]{2,0,1:T(8,128)S(1)}, u32[]{:S(2)}, u32[]{:S(2)}) collective-permute-start(f32[864,1,128]{2,0,1:T(8,128)} %get-tuple-element.21), channel_id=1, source_target_pairs={{1,0},{2,1},{3,2},{4,3},{5,4},{6,5},{7,6},{8,7},{9,8},{10,9},{11,1... | collective-permute-start | bytes 1327112 | tf_op jit(solution)/shard_map/ppermute | solution.py:65
  13.4 24.3 %collective-permute-start.4 = (f32[864,1,128]{2,0,1:T(8,128)}, f32[864,1,128]{2,0,1:T(8,128)S(1)}, u32[]{:S(2)}, u32[]{:S(2)}) collective-permute-start(f32[864,1,128]{2,0,1:T(8,128)} %get-tuple-element.20), channel_id=1, source_target_pairs={{1,0},{2,1},{3,2},{4,3},{5,4},{6,5},{7,6},{8,7},{9,8},{10,9},{11,1... | collective-permute-start | bytes 1327112 | tf_op jit(solution)/shard_map/ppermute | solution.py:59
  16.0 21.8 %collective-permute-start.3 = (f32[864,1,128]{2,0,1:T(8,128)}, f32[864,1,128]{2,0,1:T(8,128)S(1)}, u32[]{:S(2)}, u32[]{:S(2)}) collective-permute-start(f32[864,1,128]{2,0,1:T(8,128)} %get-tuple-element.19), channel_id=1, source_target_pairs={{0,1},{1,2},{2,3},{3,4},{4,5},{5,6},{6,7},{7,8},{8,9},{9,10},{10,1... | collective-permute-start | bytes 1327112 | tf_op jit(solution)/shard_map/ppermute | solution.py:58
  18.0 40.5 %collective-permute-start = (f32[1,1,128]{2,1,0:T(1,128)S(1)}, f32[1,1,128]{2,1,0:T(1,128)S(1)}, u32[]{:S(2)}, u32[]{:S(2)}) collective-permute-start(f32[1,1,128]{2,1,0:T(1,128)S(1)} %get-tuple-element.51), channel_id=1, source_target_pairs={{1,0},{2,1},{3,2},{4,3},{5,4},{6,5},{7,6},{8,7},{9,8},{10,9},{11,1... | collective-permute-start | bytes 1544 | tf_op jit(solution)/shard_map/ppermute | solution.py:65
  26.4 32.1 %collective-permute-start.1 = (f32[1,1,128]{2,1,0:T(1,128)S(1)}, f32[1,1,128]{2,1,0:T(1,128)S(1)}, u32[]{:S(2)}, u32[]{:S(2)}) collective-permute-start(f32[1,1,128]{2,1,0:T(1,128)S(1)} %get-tuple-element.50), channel_id=1, source_target_pairs={{0,1},{1,2},{2,3},{3,4},{4,5},{5,6},{6,7},{7,8},{8,9},{9,10},{10,1... | collective-permute-start | bytes 1544 | tf_op jit(solution)/shard_map/ppermute | solution.py:58
  29.3 29.2 %collective-permute-start.2 = (f32[1,1,128]{2,1,0:T(1,128)S(1)}, f32[1,1,128]{2,1,0:T(1,128)S(1)}, u32[]{:S(2)}, u32[]{:S(2)}) collective-permute-start(f32[1,1,128]{2,1,0:T(1,128)S(1)} %get-tuple-element.49), channel_id=1, source_target_pairs={{1,0},{2,1},{3,2},{4,3},{5,4},{6,5},{7,6},{8,7},{9,8},{10,9},{11,1... | collective-permute-start | bytes 1544 | tf_op jit(solution)/shard_map/ppermute | solution.py:59
  39.2 1.5 copy-start
  49.3 9.2 %collective-permute-start.7 = (f32[16,4,128]{2,1,0:T(4,128)S(1)}, f32[16,4,128]{2,1,0:T(4,128)S(1)}, u32[]{:S(2)}, u32[]{:S(2)}) collective-permute-start(f32[16,4,128]{2,1,0:T(4,128)S(1)} %copy.87), channel_id=1, source_target_pairs={{0,32},{16,48},{32,0},{48,16},{64,96},{80,112},{96,64},{112,80},{1... | collective-permute-start | bytes 98312 | tf_op jit(solution)/shard_map/ppermute | solution.py:131
  56.3 5.7 %collective-permute-start.8 = (f32[16,4,128]{2,1,0:T(4,128)S(1)}, f32[16,4,128]{2,1,0:T(4,128)S(1)}, u32[]{:S(2)}, u32[]{:S(2)}) collective-permute-start(f32[16,4,128]{2,1,0:T(4,128)S(1)} %copy.87), channel_id=1, source_target_pairs={{0,48},{16,32},{32,16},{48,0},{64,112},{80,96},{96,80},{112,64},{1... | collective-permute-start | bytes 98312 | tf_op jit(solution)/shard_map/ppermute | solution.py:131
  58.5 3.9 %collective-permute-start.6 = (f32[16,4,128]{2,1,0:T(4,128)S(1)}, f32[16,4,128]{2,1,0:T(4,128)S(1)}, u32[]{:S(2)}, u32[]{:S(2)}) collective-permute-start(f32[16,4,128]{2,1,0:T(4,128)S(1)} %copy.87), channel_id=1, source_target_pairs={{0,16},{16,0},{32,48},{48,32},{64,80},{80,64},{96,112},{112,96},{1... | collective-permute-start | bytes 98312 | tf_op jit(solution)/shard_map/ppermute | solution.py:131
  62.5 7.0 %collective-permute-start.10 = (f32[16,4,128]{2,1,0:T(4,128)S(1)}, f32[16,4,128]{2,1,0:T(4,128)S(1)}, u32[]{:S(2)}, u32[]{:S(2)}) collective-permute-start(f32[16,4,128]{2,1,0:T(4,128)S(1)} %add_add_fusion.3), channel_id=1, source_target_pairs={{0,128},{16,144},{32,160},{48,176},{64,192},{80,208},{96,224},{112... | collective-permute-start | bytes 98312 | tf_op jit(solution)/shard_map/ppermute | solution.py:131
  67.3 5.1 %collective-permute-start.11 = (f32[16,4,128]{2,1,0:T(4,128)S(1)}, f32[16,4,128]{2,1,0:T(4,128)S(1)}, u32[]{:S(2)}, u32[]{:S(2)}) collective-permute-start(f32[16,4,128]{2,1,0:T(4,128)S(1)} %add_add_fusion.3), channel_id=1, source_target_pairs={{0,192},{16,208},{32,224},{48,240},{64,128},{80,144},{96,160},{112... | collective-permute-start | bytes 98312 | tf_op jit(solution)/shard_map/ppermute | solution.py:131
  67.3 5.1 %collective-permute-start.9 = (f32[16,4,128]{2,1,0:T(4,128)S(1)}, f32[16,4,128]{2,1,0:T(4,128)S(1)}, u32[]{:S(2)}, u32[]{:S(2)}) collective-permute-start(f32[16,4,128]{2,1,0:T(4,128)S(1)} %add_add_fusion.3), channel_id=1, source_target_pairs={{0,64},{16,80},{32,96},{48,112},{64,0},{80,16},{96,32},{112,48},{1... | collective-permute-start | bytes 98312 | tf_op jit(solution)/shard_map/ppermute | solution.py:131
  72.4 19.5 %collective-permute-start.12 = (f32[16,1,128]{2,1,0:T(1,128)S(1)}, f32[16,1,128]{2,1,0:T(1,128)S(1)}, u32[]{:S(2)}, u32[]{:S(2)}) collective-permute-start(f32[16,1,128]{2,1,0:T(1,128)S(1)} %get-tuple-element.40), channel_id=1, source_target_pairs={{1,0},{2,1},{3,2},{4,3},{5,4},{6,5},{7,6},{8,7},{9,8},{10,9},{11,1... | collective-permute-start | bytes 24584 | tf_op jit(solution)/shard_map/ppermute | solution.py:65
  76.3 23.6 %collective-permute-start.13 = (f32[16,1,128]{2,1,0:T(1,128)S(1)}, f32[16,1,128]{2,1,0:T(1,128)S(1)}, u32[]{:S(2)}, u32[]{:S(2)}) collective-permute-start(f32[16,1,128]{2,1,0:T(1,128)S(1)} %get-tuple-element.39), channel_id=1, source_target_pairs={{0,1},{1,2},{2,3},{3,4},{4,5},{5,6},{6,7},{7,8},{8,9},{9,10},{10,1... | collective-permute-start | bytes 24584 | tf_op jit(solution)/shard_map/ppermute | solution.py:58
  78.3 21.7 %collective-permute-start.14 = (f32[16,1,128]{2,1,0:T(1,128)S(1)}, f32[16,1,128]{2,1,0:T(1,128)S(1)}, u32[]{:S(2)}, u32[]{:S(2)}) collective-permute-start(f32[16,1,128]{2,1,0:T(1,128)S(1)} %get-tuple-element.38), channel_id=1, source_target_pairs={{1,0},{2,1},{3,2},{4,3},{5,4},{6,5},{7,6},{8,7},{9,8},{10,9},{11,1... | collective-permute-start | bytes 24584 | tf_op jit(solution)/shard_map/ppermute | solution.py:59
  87.6 20.0 %collective-permute-start.15 = (f32[864,1,128]{2,0,1:T(8,128)}, f32[864,1,128]{2,0,1:T(8,128)S(1)}, u32[]{:S(2)}, u32[]{:S(2)}) collective-permute-start(f32[864,1,128]{2,0,1:T(8,128)} %get-tuple-element.18), channel_id=1, source_target_pairs={{1,0},{2,1},{3,2},{4,3},{5,4},{6,5},{7,6},{8,7},{9,8},{10,9},{11,1... | collective-permute-start | bytes 1327112 | tf_op jit(solution)/shard_map/ppermute | solution.py:65
  89.5 25.9 %collective-permute-start.16 = (f32[864,1,128]{2,0,1:T(8,128)S(1)}, f32[864,1,128]{2,0,1:T(8,128)}, u32[]{:S(2)}, u32[]{:S(2)}) collective-permute-start(f32[864,1,128]{2,0,1:T(8,128)S(1)} %get-tuple-element.17), channel_id=1, source_target_pairs={{0,1},{1,2},{2,3},{3,4},{4,5},{5,6},{6,7},{7,8},{8,9},{9,10},{10,1... | collective-permute-start | bytes 1327112 | tf_op jit(solution)/shard_map/ppermute | solution.py:58
  91.9 24.7 %collective-permute-start.17 = (f32[864,1,128]{2,0,1:T(8,128)S(1)}, f32[864,1,128]{2,0,1:T(8,128)}, u32[]{:S(2)}, u32[]{:S(2)}) collective-permute-start(f32[864,1,128]{2,0,1:T(8,128)S(1)} %get-tuple-element.16), channel_id=1, source_target_pairs={{1,0},{2,1},{3,2},{4,3},{5,4},{6,5},{7,6},{8,7},{9,8},{10,9},{11,1... | collective-permute-start | bytes 1327112 | tf_op jit(solution)/shard_map/ppermute | solution.py:59
  138.3 8.3 %collective-permute-start.19 = (f32[16,4,128]{2,1,0:T(4,128)S(1)}, f32[16,4,128]{2,1,0:T(4,128)S(1)}, u32[]{:S(2)}, u32[]{:S(2)}) collective-permute-start(f32[16,4,128]{2,1,0:T(4,128)S(1)} %copy.91), channel_id=1, source_target_pairs={{0,32},{16,48},{32,0},{48,16},{64,96},{80,112},{96,64},{112,80},{1... | collective-permute-start | bytes 98312 | tf_op jit(solution)/shard_map/ppermute | solution.py:131
  144.7 5.7 %collective-permute-start.20 = (f32[16,4,128]{2,1,0:T(4,128)S(1)}, f32[16,4,128]{2,1,0:T(4,128)S(1)}, u32[]{:S(2)}, u32[]{:S(2)}) collective-permute-start(f32[16,4,128]{2,1,0:T(4,128)S(1)} %copy.91), channel_id=1, source_target_pairs={{0,48},{16,32},{32,16},{48,0},{64,112},{80,96},{96,80},{112,64},{1... | collective-permute-start | bytes 98312 | tf_op jit(solution)/shard_map/ppermute | solution.py:131
  145.3 5.2 %collective-permute-start.18 = (f32[16,4,128]{2,1,0:T(4,128)S(1)}, f32[16,4,128]{2,1,0:T(4,128)S(1)}, u32[]{:S(2)}, u32[]{:S(2)}) collective-permute-start(f32[16,4,128]{2,1,0:T(4,128)S(1)} %copy.91), channel_id=1, source_target_pairs={{0,16},{16,0},{32,48},{48,32},{64,80},{80,64},{96,112},{112,96},{1... | collective-permute-start | bytes 98312 | tf_op jit(solution)/shard_map/ppermute | solution.py:131
  150.5 7.8 %collective-permute-start.22 = (f32[16,4,128]{2,1,0:T(4,128)S(1)}, f32[16,4,128]{2,1,0:T(4,128)S(1)}, u32[]{:S(2)}, u32[]{:S(2)}) collective-permute-start(f32[16,4,128]{2,1,0:T(4,128)S(1)} %add_add_fusion.1), channel_id=1, source_target_pairs={{0,128},{16,144},{32,160},{48,176},{64,192},{80,208},{96,224},{112... | collective-permute-start | bytes 98312 | tf_op jit(solution)/shard_map/ppermute | solution.py:131
  156.4 5.1 %collective-permute-start.23 = (f32[16,4,128]{2,1,0:T(4,128)S(1)}, f32[16,4,128]{2,1,0:T(4,128)S(1)}, u32[]{:S(2)}, u32[]{:S(2)}) collective-permute-start(f32[16,4,128]{2,1,0:T(4,128)S(1)} %add_add_fusion.1), channel_id=1, source_target_pairs={{0,192},{16,208},{32,224},{48,240},{64,128},{80,144},{96,160},{112... | collective-permute-start | bytes 98312 | tf_op jit(solution)/shard_map/ppermute | solution.py:131
  157.0 4.5 %collective-permute-start.21 = (f32[16,4,128]{2,1,0:T(4,128)S(1)}, f32[16,4,128]{2,1,0:T(4,128)S(1)}, u32[]{:S(2)}, u32[]{:S(2)}) collective-permute-start(f32[16,4,128]{2,1,0:T(4,128)S(1)} %add_add_fusion.1), channel_id=1, source_target_pairs={{0,64},{16,80},{32,96},{48,112},{64,0},{80,16},{96,32},{112,48},{1... | collective-permute-start | bytes 98312 | tf_op jit(solution)/shard_map/ppermute | solution.py:131

commit v4 on v2

--- a/solution.py
+++ b/solution.py
@@ -54,17 +54,25 @@
     rows = block.shape[1]
     forward = [(i, i + 1) for i in range(count - 1)]
     backward = [(target, source) for source, target in forward]
-    low = lax.ppermute(block[:, rows - 1 :], "space", forward)
-    high = lax.ppermute(block[:, :1], "space", backward)
-    pairs = []
+    upwind = []
+    downwind = []
     for member, sign in enumerate(signs):
-        for source, target in forward if sign > 0 else backward:
-            pairs.append((member * count + source, member * count + target))
+        for source, target in forward:
+            pair = (member * count + source, member * count + target)
+            (upwind if sign > 0 else downwind).append(pair)
+        for source, target in backward:
+            pair = (member * count + source, member * count + target)
+            (downwind if sign > 0 else upwind).append(pair)
     positive = jnp.asarray(np.array(signs, np.int32))[lax.axis_index("vel")] > 0
-    extra = lax.ppermute(
-        jnp.where(positive, block[:, rows - 2 : rows - 1], block[:, 1:2]), ("vel", "space"), pairs
-    )
-    return jnp.concatenate([extra, low, block, high, extra], axis=1)
+    wide = lax.ppermute(
+        jnp.where(positive, block[:, rows - 2 :], block[:, :2]), ("vel", "space"), upwind
+    )
+    narrow = lax.ppermute(
+        jnp.where(positive, block[:, :1], block[:, rows - 1 :]), ("vel", "space"), downwind
+    )
+    low = jnp.where(positive, wide, jnp.concatenate([narrow, narrow], axis=1))
+    high = jnp.where(positive, jnp.concatenate([narrow, narrow], axis=1), wide)
+    return jnp.concatenate([low, block, high], axis=1)
 
 
 def speeds(offset, amount):

time: 143 us -> 148 us (1.035)
  waiting for transfers between devices: 51.5 us -> 57.1 us
  starting transfers between devices: 54.6 us -> 51.9 us
  other arithmetic: 27.2 us -> 28.7 us
    ppermute x6 -> x4, starting transfers between devices: 22.8 us -> 17 us  [the longest x2 13.1 us: with_upwind_halo(): lax.ppermute(jnp.where(positive, block[:, rows - 2:], block[:, :2]), ('ve...]
    ppermute x6 -> x4, waiting for transfers between devices: 37.5 us -> 42.6 us  [the longest x2 31.6 us: with_upwind_halo(): lax.ppermute(jnp.where(positive, block[:, :1], block[:, rows - 1:]), ('ve...]
    ppermute x12, starting transfers between devices: 31.8 us -> 34.9 us  [vel_sum(): lax.ppermute(local, 'vel', [(i, i ^ mask) for i in range(count)])]
    select_n x0 -> x6, other arithmetic: none -> 2.44 us  [the longest x2 1.4 us: with_upwind_halo(): low = jnp.where(positive, wide, jnp.concatenate([narrow, narrow], axis=1))]
    unnamed x8 -> x10, local copies, waits for them, and re-layouts: 4.35 us -> 4.46 us
  transfers between devices with their start and end apart: 18 -> 16, of which waited for: 14 -> 11; matrix products, arithmetic and copies ran while one was open for 1% -> 1% of each run, Pallas kernels for 0% -> 0%
where the time goes in v4:
time: 148 us; the launch traced here: 147 us
  waiting for transfers between devices  57.1 us (39%)
  starting transfers between devices  51.9 us (35%)
  other arithmetic  28.7 us (19%)
  local copies, waits for them, and re-layouts  5.26 us (4%)
  matrix products  2.62 us (2%)
  between operations  1.68 us (1%)
    ppermute x12, starting transfers between devices, vel_sum(): lax.ppermute(local, 'vel', [(i, i ^ mask) for i in range(count)])  34.9 us
    ppermute x2, waiting for transfers between devices, with_upwind_halo(): lax.ppermute(jnp.where(positive, block[:, :1], block[:, rows - 1:]), ('ve...  31.6 us
    ppermute x12, waiting for transfers between devices, vel_sum(): lax.ppermute(local, 'vel', [(i, i ^ mask) for i in range(count)])  14.5 us
    ppermute x2, starting transfers between devices, with_upwind_halo(): lax.ppermute(jnp.where(positive, block[:, rows - 2:], block[:, :2]), ('ve...  13.1 us
    ppermute x2, waiting for transfers between devices, with_upwind_halo(): lax.ppermute(jnp.where(positive, block[:, rows - 2:], block[:, :2]), ('ve...  11 us
    mul x4, other arithmetic, sweep(): flux = number * jnp.where(number > 0, left_face, right_face)  7.15 us
    mul x4, other arithmetic, minmod(): 0.5 * (jnp.sign(left) + jnp.sign(right))  7.11 us
    select_n x2, other arithmetic, approach_increment(): jnp.where(kind_labels == 1, wall_distribution, jnp.where(kind_labels == 2...  5.36 us
  transfers between devices with their start and end apart: 16, of which 11 were waited for; matrix products, arithmetic and copies ran while one was open for 1% of the time, Pallas kernels for 0%

profile of v4, /device:TPU:6, one launch (start us, length us, event | category | flops | bytes accessed | tf_op | source)
XLA Modules:
  0.0 147.2 jit_solution(15009518061475355926)
XLA Ops:
  0.6 1.6 %copy.96 = f32[864,4,128]{2,0,1:T(8,128)S(1)} copy(f32[864,4,128]{2,1,0:T(4,128)} %param.4) | data formatting | bytes 3538944 | tf_op args[0]
  2.3 0.6 dynamic_slice.6
  3.5 0.8 slice_select_fusion.3
  4.3 1.9 %collective-permute-start.1 = (f32[864,1,128]{2,0,1:T(8,128)}, f32[864,1,128]{2,0,1:T(8,128)S(1)}, u32[]{:S(2)}, u32[]{:S(2)}) collective-permute-start(f32[864,1,128]{2,0,1:T(8,128)} %slice_select_fusion.3), channel_id=1, source_target_pairs={{0,1},{1,2},{2,3},{3,4},{4,5},{5,6},{6,7},{7,8},{8,9},{9,10},{10,1... | collective-permute-start | bytes 1327112 | tf_op jit(solution)/shard_map/ppermute | solution.py:70
  6.2 0.1 slice_select_fusion.1
  6.3 8.8 %collective-permute-start = (f32[864,2,128]{2,0,1:T(8,128)S(1)}, f32[864,2,128]{2,0,1:T(8,128)}, u32[]{:S(2)}, u32[]{:S(2)}) collective-permute-start(f32[864,2,128]{2,0,1:T(8,128)S(1)} %slice_select_fusion.1), channel_id=1, source_target_pairs={{1,0},{2,1},{3,2},{4,3},{5,4},{6,5},{7,6},{8,7},{9,8},{10,9},{11,1... | collective-permute-start | bytes 2654216 | tf_op jit(solution)/shard_map/ppermute | solution.py:67
  15.2 0.1 fusion.86
  15.3 0.1 add_add_fusion.4
  15.3 0.1 fusion.147
  15.4 0.1 fusion.149
  15.5 0.1 fusion.151
  15.6 0.1 fusion.153
  15.7 0.1 fusion.155
  15.8 0.1 stack.2
  16.0 3.4 %collective-permute-done.1 = f32[864,1,128]{2,0,1:T(8,128)S(1)} collective-permute-done((f32[864,1,128]{2,0,1:T(8,128)}, f32[864,1,128]{2,0,1:T(8,128)S(1)}, u32[]{:S(2)}, u32[]{:S(2)}) %collective-permute-start.1) | collective-permute-done | bytes 442400 | tf_op jit(solution)/shard_map/ppermute | solution.py:70
  19.5 11.0 %collective-permute-done = f32[864,2,128]{2,0,1:T(8,128)} collective-permute-done((f32[864,2,128]{2,0,1:T(8,128)S(1)}, f32[864,2,128]{2,0,1:T(8,128)}, u32[]{:S(2)}, u32[]{:S(2)}) %collective-permute-start) | collective-permute-done | bytes 884768 | tf_op jit(solution)/shard_map/ppermute | solution.py:67
  30.5 1.3 broadcast_select_fusion.3
  31.8 0.3 pad_maximum_fusion
  32.0 0.2 slice_subtract_fusion.1
  32.2 1.1 minimum_multiply_fusion.3
  33.4 1.0 fusion.16
  34.4 0.4 copy-done
  34.9 0.2 fusion.61
  35.1 1.9 %fusion.3 = f32[864,4,131]{2,0,1:T(8,128)S(1)} fusion(f32[864,4,128]{2,0,1:T(8,128)S(1)} %fusion.61), kind=kLoop, calls=%fused_computation.11 | loop fusion | flops 452736 | bytes 3580416 | tf_op jit(solution)/shard_map/sub | solution.py:101
  37.0 2.4 %minimum_multiply_fusion.1 = f32[864,4,130]{2,0,1:T(8,128)S(1)} fusion(f32[864,4,131]{2,0,1:T(8,128)S(1)} %fusion.3), kind=kLoop, calls=%fused_computation.25 | loop fusion | flops 3594240 | bytes 5391360 | tf_op jit(solution)/shard_map/mul | solution.py:92
  39.4 2.6 %fusion.2 = f32[864,4,129]{2,0,1:T(8,128)S(1)} fusion(f32[864,4,128]{2,0,1:T(8,128)S(1)} %fusion.61, f32[864,4,130]{2,0,1:T(8,128)S(1)} %minimum_multiply_fusion.1, f32[864]{0:T(1024)S(1)} %get-tuple-element.45, f32[864]{0:T(1024)S(1)} %get-tuple-element.48, f32[864]{0:T(1024)S(1)} %get-tuple-element.49, pred[864]{0:T(1024)(128)(4,1)S(1)} %broadcast_compare_fusion), kind=kLoop, calls=%fused_computation.10 | loop fusion | flops 2674944 | bytes 7130592 | tf_op jit(solution)/shard_map/mul | solution.py:109
  42.0 1.3 fusion.64
  43.3 13.2 %collective-permute-start.2 = (f32[16,4,128]{2,1,0:T(4,128)S(1)}, f32[16,4,128]{2,1,0:T(4,128)S(1)}, u32[]{:S(2)}, u32[]{:S(2)}) collective-permute-start(f32[16,4,128]{2,1,0:T(4,128)S(1)} %copy.98), channel_id=1, source_target_pairs={{0,16},{16,0},{32,48},{48,32},{64,80},{80,64},{96,112},{112,96},{1... | collective-permute-start | bytes 98312 | tf_op jit(solution)/shard_map/ppermute | solution.py:138
  56.5 0.6 collective-permute-start.3
  57.0 1.9 %collective-permute-start.4 = (f32[16,4,128]{2,1,0:T(4,128)S(1)}, f32[16,4,128]{2,1,0:T(4,128)S(1)}, u32[]{:S(2)}, u32[]{:S(2)}) collective-permute-start(f32[16,4,128]{2,1,0:T(4,128)S(1)} %copy.98), channel_id=1, source_target_pairs={{0,48},{16,32},{32,16},{48,0},{64,112},{80,96},{96,80},{112,64},{1... | collective-permute-start | bytes 98312 | tf_op jit(solution)/shard_map/ppermute | solution.py:138
  59.0 2.8 %collective-permute-done.3 = f32[16,4,128]{2,1,0:T(4,128)S(1)} collective-permute-done((f32[16,4,128]{2,1,0:T(4,128)S(1)}, f32[16,4,128]{2,1,0:T(4,128)S(1)}, u32[]{:S(2)}, u32[]{:S(2)}) %collective-permute-start.3) | collective-permute-done | bytes 32800 | tf_op jit(solution)/shard_map/ppermute | solution.py:138
  61.8 0.9 collective-permute-done.4
  62.8 4.7 %collective-permute-start.6 = (f32[16,4,128]{2,1,0:T(4,128)S(1)}, f32[16,4,128]{2,1,0:T(4,128)S(1)}, u32[]{:S(2)}, u32[]{:S(2)}) collective-permute-start(f32[16,4,128]{2,1,0:T(4,128)S(1)} %add_add_fusion.3), channel_id=1, source_target_pairs={{0,128},{16,144},{32,160},{48,176},{64,192},{80,208},{96,224},{112... | collective-permute-start | bytes 98312 | tf_op jit(solution)/shard_map/ppermute | solution.py:138
  67.5 0.7 collective-permute-start.5
  68.2 1.3 collective-permute-done.6
  69.4 3.2 %collective-permute-done.7 = f32[16,4,128]{2,1,0:T(4,128)S(1)} collective-permute-done((f32[16,4,128]{2,1,0:T(4,128)S(1)}, f32[16,4,128]{2,1,0:T(4,128)S(1)}, u32[]{:S(2)}, u32[]{:S(2)}) %collective-permute-start.7) | collective-permute-done | bytes 32800 | tf_op jit(solution)/shard_map/ppermute | solution.py:138
  72.7 2.7 %fusion.37 = f32[864,4,128]{2,0,1:T(8,128)S(1)} fusion(f32[4,128]{1,0:T(4,128)S(1)} %get-tuple-element.27, f32[4,128]{1,0:T(4,128)S(1)} %get-tuple-element.40, f32[4,128]{1,0:T(4,128)S(1)} %fusion.119, f32[4,128]{1,0:T(4,128)S(1)} %get-tuple-element.34, f32[4,128]{1,0:T(4,128)S(1)} %get-tuple-element.35, f32[4,128]{1,0:T(4,128)S(1)} %get-tuple-element.41, ...), kind=kLoop, calls=%fused_computation.77 | loop fusion | flops 13713408 | bytes 7120768 | tf_op jit(solution)/shard_map/jit(_where)/select_n | solution.py:265
  75.4 0.1 slice_select_fusion
  75.5 4.3 %collective-permute-start.8 = (f32[864,2,128]{2,0,1:T(8,128)S(1)}, f32[864,2,128]{2,0,1:T(8,128)S(1)}, u32[]{:S(2)}, u32[]{:S(2)}) collective-permute-start(f32[864,2,128]{2,0,1:T(8,128)S(1)} %slice_select_fusion), channel_id=1, source_target_pairs={{1,0},{2,1},{3,2},{4,3},{5,4},{6,5},{7,6},{8,7},{9,8},{10,9},{11,1... | collective-permute-start | bytes 2654216 | tf_op jit(solution)/shard_map/ppermute | solution.py:67
  79.9 1.9 %collective-permute-start.9 = (f32[864,1,128]{2,0,1:T(8,128)S(1)}, f32[864,1,128]{2,0,1:T(8,128)S(1)}, u32[]{:S(2)}, u32[]{:S(2)}) collective-permute-start(f32[864,1,128]{2,0,1:T(8,128)S(1)} %slice_select_fusion.2), channel_id=1, source_target_pairs={{0,1},{1,2},{2,3},{3,4},{4,5},{5,6},{6,7},{7,8},{8,9},{9,10},{10,1... | collective-permute-start | bytes 1327112 | tf_op jit(solution)/shard_map/ppermute | solution.py:70
  81.8 28.2 %collective-permute-done.9 = f32[864,1,128]{2,0,1:T(8,128)S(1)} collective-permute-done((f32[864,1,128]{2,0,1:T(8,128)S(1)}, f32[864,1,128]{2,0,1:T(8,128)S(1)}, u32[]{:S(2)}, u32[]{:S(2)}) %collective-permute-start.9) | collective-permute-done | bytes 442400 | tf_op jit(solution)/shard_map/ppermute | solution.py:70
  110.1 0.1 broadcast_select_fusion.1
  110.2 0.2 pad_maximum_fusion.1
  110.5 0.2 slice_subtract_fusion
  110.7 1.1 minimum_multiply_fusion.2
  111.8 1.0 fusion.12
  112.8 0.3 fusion.59
  113.1 1.9 %fusion.8 = f32[864,4,131]{2,0,1:T(8,128)S(1)} fusion(f32[864,4,128]{2,0,1:T(8,128)S(1)} %fusion.59), kind=kLoop, calls=%fused_computation.16 | loop fusion | flops 452736 | bytes 3580416 | tf_op jit(solution)/shard_map/sub | solution.py:101
  115.0 2.4 %minimum_multiply_fusion = f32[864,4,130]{2,0,1:T(8,128)S(1)} fusion(f32[864,4,131]{2,0,1:T(8,128)S(1)} %fusion.8), kind=kLoop, calls=%fused_computation.24 | loop fusion | flops 3594240 | bytes 5391360 | tf_op jit(solution)/shard_map/mul | solution.py:92
  117.4 2.6 %fusion.7 = f32[864,4,129]{2,0,1:T(8,128)S(1)} fusion(f32[864,4,128]{2,0,1:T(8,128)S(1)} %fusion.59, f32[864,4,130]{2,0,1:T(8,128)S(1)} %minimum_multiply_fusion, f32[864]{0:T(1024)S(1)} %get-tuple-element.45, f32[864]{0:T(1024)S(1)} %get-tuple-element.48, f32[864]{0:T(1024)S(1)} %get-tuple-element.49, pred[864]{0:T(1024)(128)(4,1)S(1)} %broadcast_compare_fusion), kind=kLoop, calls=%fused_computation.15 | loop fusion | flops 2674944 | bytes 7130592 | tf_op jit(solution)/shard_map/mul | solution.py:109
  120.0 1.3 fusion.62
  121.3 0.3 collective-permute-start.10
  121.6 1.2 collective-permute-start.11
  122.8 3.2 %collective-permute-start.12 = (f32[16,4,128]{2,1,0:T(4,128)S(1)}, f32[16,4,128]{2,1,0:T(4,128)S(1)}, u32[]{:S(2)}, u32[]{:S(2)}) collective-permute-start(f32[16,4,128]{2,1,0:T(4,128)S(1)} %copy.102), channel_id=1, source_target_pairs={{0,48},{16,32},{32,16},{48,0},{64,112},{80,96},{96,80},{112,64},{1... | collective-permute-start | bytes 98312 | tf_op jit(solution)/shard_map/ppermute | solution.py:138
  126.0 0.5 collective-permute-done.11
  126.5 2.0 %collective-permute-done.12 = f32[16,4,128]{2,1,0:T(4,128)S(1)} collective-permute-done((f32[16,4,128]{2,1,0:T(4,128)S(1)}, f32[16,4,128]{2,1,0:T(4,128)S(1)}, u32[]{:S(2)}, u32[]{:S(2)}) %collective-permute-start.12) | collective-permute-done | bytes 32800 | tf_op jit(solution)/shard_map/ppermute | solution.py:138
  128.5 7.9 %collective-permute-start.14 = (f32[16,4,128]{2,1,0:T(4,128)S(1)}, f32[16,4,128]{2,1,0:T(4,128)S(1)}, u32[]{:S(2)}, u32[]{:S(2)}) collective-permute-start(f32[16,4,128]{2,1,0:T(4,128)S(1)} %add_add_fusion.1), channel_id=1, source_target_pairs={{0,128},{16,144},{32,160},{48,176},{64,192},{80,208},{96,224},{112... | collective-permute-start | bytes 98312 | tf_op jit(solution)/shard_map/ppermute | solution.py:138
  136.4 0.6 collective-permute-start.15
  137.0 0.8 collective-permute-start.13
  137.8 0.5 collective-permute-done.14
  138.3 3.2 %collective-permute-done.15 = f32[16,4,128]{2,1,0:T(4,128)S(1)} collective-permute-done((f32[16,4,128]{2,1,0:T(4,128)S(1)}, f32[16,4,128]{2,1,0:T(4,128)S(1)}, u32[]{:S(2)}, u32[]{:S(2)}) %collective-permute-start.15) | collective-permute-done | bytes 32800 | tf_op jit(solution)/shard_map/ppermute | solution.py:138
  141.6 0.6 fusion.144
  142.2 2.7 %fusion.57 = f32[864,4,128]{2,0,1:T(8,128)S(1)} fusion(f32[4,128]{1,0:T(4,128)S(1)} %get-tuple-element.30, f32[4,128]{1,0:T(4,128)S(1)} %get-tuple-element.36, f32[4,128]{1,0:T(4,128)S(1)} %get-tuple-element.29, f32[4,128]{1,0:T(4,128)S(1)} %get-tuple-element.21, f32[4,128]{1,0:T(4,128)S(1)} %get-tuple-element.20, f32[4,128]{1,0:T(4,128)S(1)} %get-tuple-element.37, ...), kind=kLoop, calls=%fused_computation.97 | loop fusion | flops 13713408 | bytes 7120768 | tf_op jit(solution)/shard_map/jit(_where)/select_n | solution.py:265
  144.9 2.3 %copy.105 = f32[864,4,128]{2,1,0:T(4,128)} copy(f32[864,4,128]{2,0,1:T(8,128)S(1)} %fusion.57) | data formatting | bytes 3538944
  (39 shorter events, 0.6 us)
Async XLA Ops:
  0.6 1.6 %copy-start.2 = (s32[16]{0:T(128)S(1)}, s32[16]{0:T(128)}, u32[]{:S(2)}) copy-start(s32[16]{0:T(128)} %constant.97.clone) | copy-start | bytes 196
  2.2 13.8 %copy-start.1 = (s32[4,128]{1,0:T(4,128)S(1)}, s32[4,128]{1,0:T(4,128)}, u32[]{:S(2)}) copy-start(s32[4,128]{1,0:T(4,128)} %param.5) | copy-start | bytes 6148
  4.3 15.1 %collective-permute-start.1 = (f32[864,1,128]{2,0,1:T(8,128)}, f32[864,1,128]{2,0,1:T(8,128)S(1)}, u32[]{:S(2)}, u32[]{:S(2)}) collective-permute-start(f32[864,1,128]{2,0,1:T(8,128)} %slice_select_fusion.3), channel_id=1, source_target_pairs={{0,1},{1,2},{2,3},{3,4},{4,5},{5,6},{6,7},{7,8},{8,9},{9,10},{10,1... | collective-permute-start | bytes 1327112 | tf_op jit(solution)/shard_map/ppermute | solution.py:70
  6.3 24.1 %collective-permute-start = (f32[864,2,128]{2,0,1:T(8,128)S(1)}, f32[864,2,128]{2,0,1:T(8,128)}, u32[]{:S(2)}, u32[]{:S(2)}) collective-permute-start(f32[864,2,128]{2,0,1:T(8,128)S(1)} %slice_select_fusion.1), channel_id=1, source_target_pairs={{1,0},{2,1},{3,2},{4,3},{5,4},{6,5},{7,6},{8,7},{9,8},{10,9},{11,1... | collective-permute-start | bytes 2654216 | tf_op jit(solution)/shard_map/ppermute | solution.py:67
  33.4 1.5 %copy-start = (f32[864,4,128]{2,1,0:T(4,128)S(1)}, f32[864,4,128]{2,1,0:T(4,128)}, u32[]{:S(2)}) copy-start(f32[864,4,128]{2,1,0:T(4,128)} %param.4) | copy-start | bytes 5308420
  43.3 15.7 %collective-permute-start.2 = (f32[16,4,128]{2,1,0:T(4,128)S(1)}, f32[16,4,128]{2,1,0:T(4,128)S(1)}, u32[]{:S(2)}, u32[]{:S(2)}) collective-permute-start(f32[16,4,128]{2,1,0:T(4,128)S(1)} %copy.98), channel_id=1, source_target_pairs={{0,16},{16,0},{32,48},{48,32},{64,80},{80,64},{96,112},{112,96},{1... | collective-permute-start | bytes 98312 | tf_op jit(solution)/shard_map/ppermute | solution.py:138
  56.5 5.3 %collective-permute-start.3 = (f32[16,4,128]{2,1,0:T(4,128)S(1)}, f32[16,4,128]{2,1,0:T(4,128)S(1)}, u32[]{:S(2)}, u32[]{:S(2)}) collective-permute-start(f32[16,4,128]{2,1,0:T(4,128)S(1)} %copy.98), channel_id=1, source_target_pairs={{0,32},{16,48},{32,0},{48,16},{64,96},{80,112},{96,64},{112,80},{1... | collective-permute-start | bytes 98312 | tf_op jit(solution)/shard_map/ppermute | solution.py:138
  57.0 5.7 %collective-permute-start.4 = (f32[16,4,128]{2,1,0:T(4,128)S(1)}, f32[16,4,128]{2,1,0:T(4,128)S(1)}, u32[]{:S(2)}, u32[]{:S(2)}) collective-permute-start(f32[16,4,128]{2,1,0:T(4,128)S(1)} %copy.98), channel_id=1, source_target_pairs={{0,48},{16,32},{32,16},{48,0},{64,112},{80,96},{96,80},{112,64},{1... | collective-permute-start | bytes 98312 | tf_op jit(solution)/shard_map/ppermute | solution.py:138
  62.8 6.7 %collective-permute-start.6 = (f32[16,4,128]{2,1,0:T(4,128)S(1)}, f32[16,4,128]{2,1,0:T(4,128)S(1)}, u32[]{:S(2)}, u32[]{:S(2)}) collective-permute-start(f32[16,4,128]{2,1,0:T(4,128)S(1)} %add_add_fusion.3), channel_id=1, source_target_pairs={{0,128},{16,144},{32,160},{48,176},{64,192},{80,208},{96,224},{112... | collective-permute-start | bytes 98312 | tf_op jit(solution)/shard_map/ppermute | solution.py:138
  67.5 5.1 %collective-permute-start.7 = (f32[16,4,128]{2,1,0:T(4,128)S(1)}, f32[16,4,128]{2,1,0:T(4,128)S(1)}, u32[]{:S(2)}, u32[]{:S(2)}) collective-permute-start(f32[16,4,128]{2,1,0:T(4,128)S(1)} %add_add_fusion.3), channel_id=1, source_target_pairs={{0,192},{16,208},{32,224},{48,240},{64,128},{80,144},{96,160},{112... | collective-permute-start | bytes 98312 | tf_op jit(solution)/shard_map/ppermute | solution.py:138
  67.5 5.1 %collective-permute-start.5 = (f32[16,4,128]{2,1,0:T(4,128)S(1)}, f32[16,4,128]{2,1,0:T(4,128)S(1)}, u32[]{:S(2)}, u32[]{:S(2)}) collective-permute-start(f32[16,4,128]{2,1,0:T(4,128)S(1)} %add_add_fusion.3), channel_id=1, source_target_pairs={{0,64},{16,80},{32,96},{48,112},{64,0},{80,16},{96,32},{112,48},{1... | collective-permute-start | bytes 98312 | tf_op jit(solution)/shard_map/ppermute | solution.py:138
  75.5 34.6 %collective-permute-start.8 = (f32[864,2,128]{2,0,1:T(8,128)S(1)}, f32[864,2,128]{2,0,1:T(8,128)S(1)}, u32[]{:S(2)}, u32[]{:S(2)}) collective-permute-start(f32[864,2,128]{2,0,1:T(8,128)S(1)} %slice_select_fusion), channel_id=1, source_target_pairs={{1,0},{2,1},{3,2},{4,3},{5,4},{6,5},{7,6},{8,7},{9,8},{10,9},{11,1... | collective-permute-start | bytes 2654216 | tf_op jit(solution)/shard_map/ppermute | solution.py:67
  79.9 30.1 %collective-permute-start.9 = (f32[864,1,128]{2,0,1:T(8,128)S(1)}, f32[864,1,128]{2,0,1:T(8,128)S(1)}, u32[]{:S(2)}, u32[]{:S(2)}) collective-permute-start(f32[864,1,128]{2,0,1:T(8,128)S(1)} %slice_select_fusion.2), channel_id=1, source_target_pairs={{0,1},{1,2},{2,3},{3,4},{4,5},{5,6},{6,7},{7,8},{8,9},{9,10},{10,1... | collective-permute-start | bytes 1327112 | tf_op jit(solution)/shard_map/ppermute | solution.py:70
  121.3 4.7 %collective-permute-start.10 = (f32[16,4,128]{2,1,0:T(4,128)S(1)}, f32[16,4,128]{2,1,0:T(4,128)S(1)}, u32[]{:S(2)}, u32[]{:S(2)}) collective-permute-start(f32[16,4,128]{2,1,0:T(4,128)S(1)} %copy.102), channel_id=1, source_target_pairs={{0,16},{16,0},{32,48},{48,32},{64,80},{80,64},{96,112},{112,96},{1... | collective-permute-start | bytes 98312 | tf_op jit(solution)/shard_map/ppermute | solution.py:138
  121.6 4.9 %collective-permute-start.11 = (f32[16,4,128]{2,1,0:T(4,128)S(1)}, f32[16,4,128]{2,1,0:T(4,128)S(1)}, u32[]{:S(2)}, u32[]{:S(2)}) collective-permute-start(f32[16,4,128]{2,1,0:T(4,128)S(1)} %copy.102), channel_id=1, source_target_pairs={{0,32},{16,48},{32,0},{48,16},{64,96},{80,112},{96,64},{112,80},{1... | collective-permute-start | bytes 98312 | tf_op jit(solution)/shard_map/ppermute | solution.py:138
  122.8 5.7 %collective-permute-start.12 = (f32[16,4,128]{2,1,0:T(4,128)S(1)}, f32[16,4,128]{2,1,0:T(4,128)S(1)}, u32[]{:S(2)}, u32[]{:S(2)}) collective-permute-start(f32[16,4,128]{2,1,0:T(4,128)S(1)} %copy.102), channel_id=1, source_target_pairs={{0,48},{16,32},{32,16},{48,0},{64,112},{80,96},{96,80},{112,64},{1... | collective-permute-start | bytes 98312 | tf_op jit(solution)/shard_map/ppermute | solution.py:138
  128.5 9.8 %collective-permute-start.14 = (f32[16,4,128]{2,1,0:T(4,128)S(1)}, f32[16,4,128]{2,1,0:T(4,128)S(1)}, u32[]{:S(2)}, u32[]{:S(2)}) collective-permute-start(f32[16,4,128]{2,1,0:T(4,128)S(1)} %add_add_fusion.1), channel_id=1, source_target_pairs={{0,128},{16,144},{32,160},{48,176},{64,192},{80,208},{96,224},{112... | collective-permute-start | bytes 98312 | tf_op jit(solution)/shard_map/ppermute | solution.py:138
  136.4 5.1 %collective-permute-start.15 = (f32[16,4,128]{2,1,0:T(4,128)S(1)}, f32[16,4,128]{2,1,0:T(4,128)S(1)}, u32[]{:S(2)}, u32[]{:S(2)}) collective-permute-start(f32[16,4,128]{2,1,0:T(4,128)S(1)} %add_add_fusion.1), channel_id=1, source_target_pairs={{0,192},{16,208},{32,224},{48,240},{64,128},{80,144},{96,160},{112... | collective-permute-start | bytes 98312 | tf_op jit(solution)/shard_map/ppermute | solution.py:138
  137.0 4.5 %collective-permute-start.13 = (f32[16,4,128]{2,1,0:T(4,128)S(1)}, f32[16,4,128]{2,1,0:T(4,128)S(1)}, u32[]{:S(2)}, u32[]{:S(2)}) collective-permute-start(f32[16,4,128]{2,1,0:T(4,128)S(1)} %add_add_fusion.1), channel_id=1, source_target_pairs={{0,64},{16,80},{32,96},{48,112},{64,0},{80,16},{96,32},{112,48},{1... | collective-permute-start | bytes 98312 | tf_op jit(solution)/shard_map/ppermute | solution.py:138

commit v5 on v2

--- a/solution.py
+++ b/solution.py
@@ -1,9 +1,12 @@
 import math
+import os
 
 import jax
 import numpy as np
 import jax.numpy as jnp
 from jax import lax
+from jax.experimental import pallas as pl
+from jax.experimental.pallas import tpu as pltpu
 from jax.sharding import PartitionSpec as P
 
 NVX = 24
@@ -104,10 +107,69 @@
     )
 
 
+def kernel_minmod(left, right):
+    both_up = (left > 0) & (right > 0)
+    both_down = (left < 0) & (right < 0)
+    return jnp.where(
+        both_up, jnp.minimum(left, right), jnp.where(both_down, jnp.maximum(left, right), 0.0)
+    )
+
+
+def face_flux(number, lower, upper, lower_slope, upper_slope):
+    return number * jnp.where(
+        number > 0,
+        lower + 0.5 * (1.0 - number) * lower_slope,
+        upper - 0.5 * (1.0 + number) * upper_slope,
+    )
+
+
+def transport_kernel(number_x_ref, number_y_ref, padded_ref, out_ref):
+    number_x = number_x_ref[...]
+    number_y = number_y_ref[...]
+    depth = padded_ref.shape[0]
+    values = [padded_ref[k] for k in range(depth)]
+    jumps = [values[k + 1] - values[k] for k in range(depth - 1)]
+    slopes = {k: kernel_minmod(jumps[k - 1], jumps[k]) for k in range(1, depth - 1)}
+    flux = {
+        k: face_flux(number_x, values[k], values[k + 1], slopes[k], slopes[k + 1])
+        for k in range(1, depth - 2)
+    }
+    width = values[0].shape[-1]
+    lane = lax.broadcasted_iota(jnp.int32, values[0].shape, 1)
+    first = lane == 0
+    last = lane == width - 1
+    for k in range(2, depth - 2):
+        swept = values[k] - (flux[k] - flux[k - 1])
+        before = jnp.where(first, 0.0, pltpu.roll(swept, 1, 1))
+        after = jnp.where(last, 0.0, pltpu.roll(swept, width - 1, 1))
+        slope = kernel_minmod(swept - before, after - swept)
+        slope_before = jnp.where(first, 0.0, pltpu.roll(slope, 1, 1))
+        slope_after = jnp.where(last, 0.0, pltpu.roll(slope, width - 1, 1))
+        flux_after = face_flux(number_y, swept, after, slope, slope_after)
+        flux_before = face_flux(number_y, before, swept, slope_before, slope)
+        out_ref[k - 2] = swept - (flux_after - flux_before)
+
+
 def transport(padded, along_x_part, along_y_part):
-    swept = sweep(padded, courant * along_x_part[:, None, None], 1)
-    widened = jnp.pad(swept, ((0, 0), (0, 0), (2, 2)))
-    return sweep(widened, courant * along_y_part[:, None, None], 2)
+    amount, depth, width = padded.shape
+    rows = depth - 4
+    block = 96 if amount % 96 == 0 else amount
+    number_x = (courant * along_x_part)[:, None]
+    number_y = (courant * along_y_part)[:, None]
+    stacked = jnp.transpose(padded, (1, 0, 2))
+    swept = pl.pallas_call(
+        transport_kernel,
+        grid=(amount // block,),
+        in_specs=[
+            pl.BlockSpec((block, 1), lambda i: (i, 0)),
+            pl.BlockSpec((block, 1), lambda i: (i, 0)),
+            pl.BlockSpec((depth, block, width), lambda i: (0, i, 0)),
+        ],
+        out_specs=pl.BlockSpec((rows, block, width), lambda i: (0, i, 0)),
+        out_shape=jax.ShapeDtypeStruct((rows, amount, width), padded.dtype),
+        interpret=os.environ.get("SOLUTION_INTERPRET") == "1",
+    )(number_x, number_y, stacked)
+    return jnp.transpose(swept, (1, 0, 2))
 
 
 def xor_tree(values):

time: 143 us -> 164 us (1.15)
  Pallas kernels: 0 us -> 18.7 us
  other arithmetic: 27.2 us -> 16.8 us
  local copies, waits for them, and re-layouts: 5.09 us -> 14.8 us
  matrix products: 2.58 us -> 5.13 us
  waiting for transfers between devices: 51.5 us -> 49.4 us
  starting transfers between devices: 54.6 us -> 56.3 us
    pallas_call x0 -> x2, Pallas kernels: none -> 18.7 us  [transport(): pl.pallas_call(transport_kernel, grid=(amount // block,), in_specs=[pl.Bl...]
    ppermute x2, waiting for transfers between devices: 16.9 us -> 0.01 us  [with_upwind_halo(): high = lax.ppermute(block[:, :1], 'space', backward)]
    mul x12 -> x2, other arithmetic: 14.5 us -> 1.61 us  [the longest x1 0.82 us: transport(): number_y = (courant * along_y_part)[:, None]]
    ppermute x2, waiting for transfers between devices: 8.19 us -> 20.9 us  [with_upwind_halo(): low = lax.ppermute(block[:, rows - 1:], 'space', forward)]
    unnamed x8 -> x19, local copies, waits for them, and re-layouts: 4.35 us -> 12.1 us
    ppermute x12, starting transfers between devices: 31.8 us -> 24.2 us  [vel_sum(): lax.ppermute(local, 'vel', [(i, i ^ mask) for i in range(count)])]
    ppermute x2, starting transfers between devices: 11.7 us -> 17.4 us  [with_upwind_halo(): high = lax.ppermute(block[:, :1], 'space', backward)]
    sub x6 -> x0, other arithmetic: 4.75 us -> none  [the longest x4 4.35 us: sweep(): piece(distribution_table, 1, length)]
  transfers between devices with their start and end apart: 18 -> 18, of which waited for: 14 -> 12; matrix products, arithmetic and copies ran while one was open for 1% -> 8% of each run, Pallas kernels for 0% -> 0%
where the time goes in v5:
time: 164 us; the launch traced here: 163 us
  starting transfers between devices  56.3 us (34%)
  waiting for transfers between devices  49.4 us (30%)
  Pallas kernels  18.7 us (11%)
  other arithmetic  16.8 us (10%)
  local copies, waits for them, and re-layouts  14.8 us (9%)
  matrix products  5.13 us (3%)
    ppermute x12, starting transfers between devices, vel_sum(): lax.ppermute(local, 'vel', [(i, i ^ mask) for i in range(count)])  24.2 us
    ppermute x2, waiting for transfers between devices, with_upwind_halo(): low = lax.ppermute(block[:, rows - 1:], 'space', forward)  20.9 us
    pallas_call x2, Pallas kernels, transport(): pl.pallas_call(transport_kernel, grid=(amount // block,), in_specs=[pl.Bl...  18.7 us
    ppermute x2, starting transfers between devices, with_upwind_halo(): high = lax.ppermute(block[:, :1], 'space', backward)  17.4 us
    ppermute x2, waiting for transfers between devices, with_upwind_halo(): lax.ppermute(jnp.where(positive, block[:, rows - 2:rows - 1], block[:, 1:...  15.2 us
    ppermute x12, waiting for transfers between devices, vel_sum(): lax.ppermute(local, 'vel', [(i, i ^ mask) for i in range(count)])  13.4 us
    unnamed x19, local copies, waits for them, and re-layouts  12.1 us
    ppermute x2, starting transfers between devices, with_upwind_halo(): lax.ppermute(jnp.where(positive, block[:, rows - 2:rows - 1], block[:, 1:...  10.9 us
  transfers between devices with their start and end apart: 18, of which 12 were waited for; matrix products, arithmetic and copies ran while one was open for 8% of the time, Pallas kernels for 0%

profile of v5, /device:TPU:6, one launch (start us, length us, event | category | flops | bytes accessed | tf_op | source)
XLA Modules:
  0.0 162.8 jit_solution(12546578753441672277)
XLA Ops:
  0.6 1.6 copy.54
  2.3 0.6 dynamic_slice.6
  3.5 1.0 fusion.141
  4.5 8.8 %collective-permute-start.2 = (f32[864,1,128]{2,0,1:T(8,128)S(1)}, f32[864,1,128]{2,0,1:T(8,128)}, u32[]{:S(2)}, u32[]{:S(2)}) collective-permute-start(f32[864,1,128]{2,0,1:T(8,128)S(1)} %get-tuple-element.19), channel_id=1, source_target_pairs={{1,0},{2,1},{3,2},{4,3},{5,4},{6,5},{7,6},{8,7},{9,8},{10,9},{11,1... | collective-permute-start | bytes 1327112 | tf_op jit(solution)/shard_map/ppermute | solution.py:61
  13.3 1.9 %collective-permute-start.1 = (f32[864,1,128]{2,0,1:T(8,128)}, f32[864,1,128]{2,0,1:T(8,128)}, u32[]{:S(2)}, u32[]{:S(2)}) collective-permute-start(f32[864,1,128]{2,0,1:T(8,128)} %get-tuple-element.20), channel_id=1, source_target_pairs={{0,1},{1,2},{2,3},{3,4},{4,5},{5,6},{6,7},{7,8},{8,9},{9,10},{10,1... | collective-permute-start | bytes 1327112 | tf_op jit(solution)/shard_map/ppermute | solution.py:60
  15.3 8.4 %collective-permute-start = (f32[864,1,128]{2,0,1:T(8,128)}, f32[864,1,128]{2,0,1:T(8,128)S(1)}, u32[]{:S(2)}, u32[]{:S(2)}) collective-permute-start(f32[864,1,128]{2,0,1:T(8,128)} %get-tuple-element.21), channel_id=1, source_target_pairs={{1,0},{2,1},{3,2},{4,3},{5,4},{6,5},{7,6},{8,7},{9,8},{10,9},{11,1... | collective-permute-start | bytes 1327112 | tf_op jit(solution)/shard_map/ppermute | solution.py:67
  23.7 0.1 fusion.131
  23.8 0.1 fusion.137
  23.9 0.1 fusion.135
  24.0 0.1 fusion.133
  24.1 0.1 add_add_fusion.4
  24.1 0.1 fusion.72
  24.2 0.1 fusion.66
  24.3 0.2 copy.53
  24.5 0.8 broadcast_multiply_fusion.number_y_ref
  25.3 0.2 copy.50
  25.5 0.1 fusion.139
  25.6 0.1 stack.2
  25.8 0.8 broadcast_multiply_fusion.1.number_x_ref
  26.6 10.6 %collective-permute-done = f32[864,1,128]{2,0,1:T(8,128)S(1)} collective-permute-done((f32[864,1,128]{2,0,1:T(8,128)}, f32[864,1,128]{2,0,1:T(8,128)S(1)}, u32[]{:S(2)}, u32[]{:S(2)}) %collective-permute-start) | collective-permute-done | bytes 442400 | tf_op jit(solution)/shard_map/ppermute | solution.py:67
  37.2 0.8 constant_dynamic-update-slice_fusion.4
  38.0 6.7 %collective-permute-done.1 = f32[864,1,128]{2,0,1:T(8,128)} collective-permute-done((f32[864,1,128]{2,0,1:T(8,128)}, f32[864,1,128]{2,0,1:T(8,128)}, u32[]{:S(2)}, u32[]{:S(2)}) %collective-permute-start.1) | collective-permute-done | bytes 442400 | tf_op jit(solution)/shard_map/ppermute | solution.py:60
  44.7 1.8 %constant_dynamic-update-slice_fusion.3 = f32[864,8,128]{2,0,1:T(8,128)} fusion(f32[864,8,128]{2,0,1:T(8,128)} %constant_dynamic-update-slice_fusion.4, f32[864,1,128]{2,0,1:T(8,128)} %collective-permute-done.1), kind=kLoop, calls=%fused_computation.73 | loop fusion | bytes 884736
  46.5 1.3 constant_dynamic-update-slice_fusion.2
  47.9 1.8 %constant_dynamic-update-slice_fusion.1 = f32[864,8,128]{2,0,1:T(8,128)} fusion(f32[864,8,128]{2,0,1:T(8,128)} %constant_dynamic-update-slice_fusion.2, f32[864,1,128]{2,0,1:T(8,128)} %collective-permute-done.2), kind=kLoop, calls=%fused_computation.71 | loop fusion | bytes 884736
  49.7 0.8 constant_dynamic-update-slice_fusion
  50.5 9.3 %shard_map.59 = f32[4,864,128]{2,1,0:T(8,128)} custom-call(f32[864,1]{1,0:T(8,128)} %broadcast_multiply_fusion.1.number_x_ref, f32[864,1]{1,0:T(8,128)} %broadcast_multiply_fusion.number_y_ref, f32[8,864,128]{2,1,0:T(8,128)} %bitcast.2.padded_ref), custom_call_target="tpu_custom_call" | custom-call | tf_op jit(solution)/shard_map/pallas_call | solution.py:160
  59.8 2.6 %fusion.42 = f32[16,4,128]{2,0,1:T(8,128)S(1)} fusion(f32[4,864,128]{2,1,0:T(8,128)} %shard_map.59, f32[16,864]{1,0:T(8,128)S(1)} %stack.2), kind=kOutput, calls=%fused_computation.54 | convolution fusion | flops 84948480 | bytes 1857536 | tf_op jit(solution)/shard_map/kv,vrc->krc/dot_general | solution.py:223
  62.4 0.6 collective-permute-start.4
  63.0 3.9 %collective-permute-start.5 = (f32[16,4,128]{2,1,0:T(4,128)S(1)}, f32[16,4,128]{2,1,0:T(4,128)S(1)}, u32[]{:S(2)}, u32[]{:S(2)}) collective-permute-start(f32[16,4,128]{2,1,0:T(4,128)S(1)} %copy.60), channel_id=1, source_target_pairs={{0,48},{16,32},{32,16},{48,0},{64,112},{80,96},{96,80},{112,64},{1... | collective-permute-start | bytes 98312 | tf_op jit(solution)/shard_map/ppermute | solution.py:192
  66.9 0.4 collective-permute-done.4
  67.3 1.8 %collective-permute-done.5 = f32[16,4,128]{2,1,0:T(4,128)S(1)} collective-permute-done((f32[16,4,128]{2,1,0:T(4,128)S(1)}, f32[16,4,128]{2,1,0:T(4,128)S(1)}, u32[]{:S(2)}, u32[]{:S(2)}) %collective-permute-start.5) | collective-permute-done | bytes 32800 | tf_op jit(solution)/shard_map/ppermute | solution.py:192
  69.2 5.2 %collective-permute-start.8 = (f32[16,4,128]{2,1,0:T(4,128)S(1)}, f32[16,4,128]{2,1,0:T(4,128)S(1)}, u32[]{:S(2)}, u32[]{:S(2)}) collective-permute-start(f32[16,4,128]{2,1,0:T(4,128)S(1)} %add_add_fusion.3), channel_id=1, source_target_pairs={{0,192},{16,208},{32,224},{48,240},{64,128},{80,144},{96,160},{112... | collective-permute-start | bytes 98312 | tf_op jit(solution)/shard_map/ppermute | solution.py:192
  74.4 0.3 collective-permute-start.7
  74.7 0.7 collective-permute-start.6
  75.4 0.9 collective-permute-done.8
  76.3 3.5 %collective-permute-done.7 = f32[16,4,128]{2,1,0:T(4,128)S(1)} collective-permute-done((f32[16,4,128]{2,1,0:T(4,128)S(1)}, f32[16,4,128]{2,1,0:T(4,128)S(1)}, u32[]{:S(2)}, u32[]{:S(2)}) %collective-permute-start.7) | collective-permute-done | bytes 32800 | tf_op jit(solution)/shard_map/ppermute | solution.py:192
  79.9 4.3 %fusion.19 = f32[864,4,128]{2,0,1:T(8,128)S(1)} fusion(f32[4,864,128]{2,1,0:T(8,128)S(1)} %copy-done, f32[4,128]{1,0:T(4,128)S(1)} %get-tuple-element.29, f32[4,128]{1,0:T(4,128)S(1)} %get-tuple-element.42, f32[4,128]{1,0:T(4,128)S(1)} %fusion.103, f32[4,128]{1,0:T(4,128)S(1)} %get-tuple-element.36, f32[4,128]{1,0:T(4,128)S(1)} %get-tuple-element.37, ...), kind=kLoop, calls=%fused_computation.31 | loop fusion | flops 12828672 | bytes 3581824 | tf_op jit(solution)/shard_map/jit(_where)/select_n | solution.py:319
  84.2 0.1 fusion.140
  84.3 2.4 %collective-permute-start.9 = (f32[864,1,128]{2,0,1:T(8,128)S(1)}, f32[864,1,128]{2,0,1:T(8,128)S(1)}, u32[]{:S(2)}, u32[]{:S(2)}) collective-permute-start(f32[864,1,128]{2,0,1:T(8,128)S(1)} %get-tuple-element.18), channel_id=1, source_target_pairs={{1,0},{2,1},{3,2},{4,3},{5,4},{6,5},{7,6},{8,7},{9,8},{10,9},{11,1... | collective-permute-start | bytes 1327112 | tf_op jit(solution)/shard_map/ppermute | solution.py:67
  86.8 1.9 %collective-permute-start.10 = (f32[864,1,128]{2,0,1:T(8,128)S(1)}, f32[864,1,128]{2,0,1:T(8,128)S(1)}, u32[]{:S(2)}, u32[]{:S(2)}) collective-permute-start(f32[864,1,128]{2,0,1:T(8,128)S(1)} %get-tuple-element.17), channel_id=1, source_target_pairs={{0,1},{1,2},{2,3},{3,4},{4,5},{5,6},{6,7},{7,8},{8,9},{9,10},{10,1... | collective-permute-start | bytes 1327112 | tf_op jit(solution)/shard_map/ppermute | solution.py:60
  88.7 8.6 %collective-permute-start.11 = (f32[864,1,128]{2,0,1:T(8,128)S(1)}, f32[864,1,128]{2,0,1:T(8,128)S(1)}, u32[]{:S(2)}, u32[]{:S(2)}) collective-permute-start(f32[864,1,128]{2,0,1:T(8,128)S(1)} %get-tuple-element.16), channel_id=1, source_target_pairs={{1,0},{2,1},{3,2},{4,3},{5,4},{6,5},{7,6},{8,7},{9,8},{10,9},{11,1... | collective-permute-start | bytes 1327112 | tf_op jit(solution)/shard_map/ppermute | solution.py:61
  97.3 4.6 %collective-permute-done.9 = f32[864,1,128]{2,0,1:T(8,128)S(1)} collective-permute-done((f32[864,1,128]{2,0,1:T(8,128)S(1)}, f32[864,1,128]{2,0,1:T(8,128)S(1)}, u32[]{:S(2)}, u32[]{:S(2)}) %collective-permute-start.9) | collective-permute-done | bytes 442400 | tf_op jit(solution)/shard_map/ppermute | solution.py:67
  101.9 0.8 constant_dynamic-update-slice_fusion.9
  102.7 14.1 %collective-permute-done.10 = f32[864,1,128]{2,0,1:T(8,128)S(1)} collective-permute-done((f32[864,1,128]{2,0,1:T(8,128)S(1)}, f32[864,1,128]{2,0,1:T(8,128)S(1)}, u32[]{:S(2)}, u32[]{:S(2)}) %collective-permute-start.10) | collective-permute-done | bytes 442400 | tf_op jit(solution)/shard_map/ppermute | solution.py:60
  116.8 0.8 constant_dynamic-update-slice_fusion.8
  117.6 4.1 %constant_dynamic-update-slice_fusion.7 = f32[864,8,128]{2,0,1:T(8,128)} fusion(f32[864,8,128]{2,0,1:T(8,128)} %constant_dynamic-update-slice_fusion.8, f32[4,128]{1,0:T(4,128)S(1)} %get-tuple-element.29, f32[4,128]{1,0:T(4,128)S(1)} %get-tuple-element.42, f32[4,128]{1,0:T(4,128)S(1)} %fusion.103, f32[4,128]{1,0:T(4,128)S(1)} %get-tuple-element.36, ...), kind=kLoop, calls=%fused_computation.77 | loop fusion | flops 12828672 | bytes 3581824
  121.7 0.8 constant_dynamic-update-slice_fusion.6
  122.5 0.8 constant_dynamic-update-slice_fusion.5
  123.3 9.3 %shard_map.60 = f32[4,864,128]{2,1,0:T(8,128)} custom-call(f32[864,1]{1,0:T(8,128)} %broadcast_multiply_fusion.1.number_x_ref, f32[864,1]{1,0:T(8,128)} %broadcast_multiply_fusion.number_y_ref, f32[8,864,128]{2,1,0:T(8,128)} %bitcast.16.padded_ref), custom_call_target="tpu_custom_call" | custom-call | tf_op jit(solution)/shard_map/pallas_call | solution.py:160
  132.7 2.6 %fusion.40 = f32[16,4,128]{2,0,1:T(8,128)S(1)} fusion(f32[4,864,128]{2,1,0:T(8,128)} %shard_map.60, f32[16,864]{1,0:T(8,128)S(1)} %stack.2), kind=kOutput, calls=%fused_computation.52 | convolution fusion | flops 84948480 | bytes 1857536 | tf_op jit(solution)/shard_map/kv,vrc->krc/dot_general | solution.py:223
  135.3 0.1 collective-permute-start.13
  135.4 0.1 collective-permute-start.12
  135.5 4.3 %collective-permute-start.14 = (f32[16,4,128]{2,1,0:T(4,128)S(1)}, f32[16,4,128]{2,1,0:T(4,128)S(1)}, u32[]{:S(2)}, u32[]{:S(2)}) collective-permute-start(f32[16,4,128]{2,1,0:T(4,128)S(1)} %copy.64), channel_id=1, source_target_pairs={{0,48},{16,32},{32,16},{48,0},{64,112},{80,96},{96,80},{112,64},{1... | collective-permute-start | bytes 98312 | tf_op jit(solution)/shard_map/ppermute | solution.py:192
  139.7 0.4 collective-permute-done.13
  140.2 1.8 %collective-permute-done.14 = f32[16,4,128]{2,1,0:T(4,128)S(1)} collective-permute-done((f32[16,4,128]{2,1,0:T(4,128)S(1)}, f32[16,4,128]{2,1,0:T(4,128)S(1)}, u32[]{:S(2)}, u32[]{:S(2)}) %collective-permute-start.14) | collective-permute-done | bytes 32800 | tf_op jit(solution)/shard_map/ppermute | solution.py:192
  142.0 8.1 %collective-permute-start.17 = (f32[16,4,128]{2,1,0:T(4,128)S(1)}, f32[16,4,128]{2,1,0:T(4,128)S(1)}, u32[]{:S(2)}, u32[]{:S(2)}) collective-permute-start(f32[16,4,128]{2,1,0:T(4,128)S(1)} %add_add_fusion.1), channel_id=1, source_target_pairs={{0,192},{16,208},{32,224},{48,240},{64,128},{80,144},{96,160},{112... | collective-permute-start | bytes 98312 | tf_op jit(solution)/shard_map/ppermute | solution.py:192
  150.1 0.8 collective-permute-start.16
  150.9 0.1 collective-permute-start.15
  151.1 0.9 collective-permute-done.17
  152.0 3.5 %collective-permute-done.16 = f32[16,4,128]{2,1,0:T(4,128)S(1)} collective-permute-done((f32[16,4,128]{2,1,0:T(4,128)S(1)}, f32[16,4,128]{2,1,0:T(4,128)S(1)}, u32[]{:S(2)}, u32[]{:S(2)}) %collective-permute-start.16) | collective-permute-done | bytes 32800 | tf_op jit(solution)/shard_map/ppermute | solution.py:192
  155.5 0.6 fusion.128
  156.2 4.3 %fusion.39 = f32[864,4,128]{2,0,1:T(8,128)S(1)} fusion(f32[4,864,128]{2,1,0:T(8,128)S(1)} %copy-done.1, f32[4,128]{1,0:T(4,128)S(1)} %get-tuple-element.32, f32[4,128]{1,0:T(4,128)S(1)} %get-tuple-element.38, f32[4,128]{1,0:T(4,128)S(1)} %get-tuple-element.31, f32[4,128]{1,0:T(4,128)S(1)} %get-tuple-element.23, f32[4,128]{1,0:T(4,128)S(1)} %get-tuple-element.22, ...), kind=kLoop, calls=%fused_computation.51 | loop fusion | flops 12828672 | bytes 3581824 | tf_op jit(solution)/shard_map/jit(_where)/select_n | solution.py:319
  160.5 2.3 %copy.67 = f32[864,4,128]{2,1,0:T(4,128)} copy(f32[864,4,128]{2,0,1:T(8,128)S(1)} %fusion.39) | data formatting | bytes 3538944
  (35 shorter events, 0.3 us)
Async XLA Ops:
  0.6 1.6 copy-start.4
  2.2 22.0 %copy-start.3 = (s32[4,128]{1,0:T(4,128)S(1)}, s32[4,128]{1,0:T(4,128)}, u32[]{:S(2)}) copy-start(s32[4,128]{1,0:T(4,128)} %param.5) | copy-start | bytes 6148
  4.5 43.3 %collective-permute-start.2 = (f32[864,1,128]{2,0,1:T(8,128)S(1)}, f32[864,1,128]{2,0,1:T(8,128)}, u32[]{:S(2)}, u32[]{:S(2)}) collective-permute-start(f32[864,1,128]{2,0,1:T(8,128)S(1)} %get-tuple-element.19), channel_id=1, source_target_pairs={{1,0},{2,1},{3,2},{4,3},{5,4},{6,5},{7,6},{8,7},{9,8},{10,9},{11,1... | collective-permute-start | bytes 1327112 | tf_op jit(solution)/shard_map/ppermute | solution.py:61
  13.3 31.4 %collective-permute-start.1 = (f32[864,1,128]{2,0,1:T(8,128)}, f32[864,1,128]{2,0,1:T(8,128)}, u32[]{:S(2)}, u32[]{:S(2)}) collective-permute-start(f32[864,1,128]{2,0,1:T(8,128)} %get-tuple-element.20), channel_id=1, source_target_pairs={{0,1},{1,2},{2,3},{3,4},{4,5},{5,6},{6,7},{7,8},{8,9},{9,10},{10,1... | collective-permute-start | bytes 1327112 | tf_op jit(solution)/shard_map/ppermute | solution.py:60
  15.3 21.9 %collective-permute-start = (f32[864,1,128]{2,0,1:T(8,128)}, f32[864,1,128]{2,0,1:T(8,128)S(1)}, u32[]{:S(2)}, u32[]{:S(2)}) collective-permute-start(f32[864,1,128]{2,0,1:T(8,128)} %get-tuple-element.21), channel_id=1, source_target_pairs={{1,0},{2,1},{3,2},{4,3},{5,4},{6,5},{7,6},{8,7},{9,8},{10,9},{11,1... | collective-permute-start | bytes 1327112 | tf_op jit(solution)/shard_map/ppermute | solution.py:67
  25.3 21.2 %copy-start.2 = (f32[864,4,128]{2,1,0:T(4,128)S(1)}, f32[864,4,128]{2,1,0:T(4,128)}, u32[]{:S(2)}) copy-start(f32[864,4,128]{2,1,0:T(4,128)} %param.4) | copy-start | bytes 5308420
  59.8 20.1 %copy-start = (f32[4,864,128]{2,1,0:T(8,128)S(1)}, f32[4,864,128]{2,1,0:T(8,128)}, u32[]{:S(2)}) copy-start(f32[4,864,128]{2,1,0:T(8,128)} %shard_map.59) | copy-start | bytes 5308420
  62.4 4.9 %collective-permute-start.4 = (f32[16,4,128]{2,1,0:T(4,128)S(1)}, f32[16,4,128]{2,1,0:T(4,128)S(1)}, u32[]{:S(2)}, u32[]{:S(2)}) collective-permute-start(f32[16,4,128]{2,1,0:T(4,128)S(1)} %copy.60), channel_id=1, source_target_pairs={{0,32},{16,48},{32,0},{48,16},{64,96},{80,112},{96,64},{112,80},{1... | collective-permute-start | bytes 98312 | tf_op jit(solution)/shard_map/ppermute | solution.py:192
  63.0 4.3 %collective-permute-start.3 = (f32[16,4,128]{2,1,0:T(4,128)S(1)}, f32[16,4,128]{2,1,0:T(4,128)S(1)}, u32[]{:S(2)}, u32[]{:S(2)}) collective-permute-start(f32[16,4,128]{2,1,0:T(4,128)S(1)} %copy.60), channel_id=1, source_target_pairs={{0,16},{16,0},{32,48},{48,32},{64,80},{80,64},{96,112},{112,96},{1... | collective-permute-start | bytes 98312 | tf_op jit(solution)/shard_map/ppermute | solution.py:192
  63.0 6.1 %collective-permute-start.5 = (f32[16,4,128]{2,1,0:T(4,128)S(1)}, f32[16,4,128]{2,1,0:T(4,128)S(1)}, u32[]{:S(2)}, u32[]{:S(2)}) collective-permute-start(f32[16,4,128]{2,1,0:T(4,128)S(1)} %copy.60), channel_id=1, source_target_pairs={{0,48},{16,32},{32,16},{48,0},{64,112},{80,96},{96,80},{112,64},{1... | collective-permute-start | bytes 98312 | tf_op jit(solution)/shard_map/ppermute | solution.py:192
  69.2 7.1 %collective-permute-start.8 = (f32[16,4,128]{2,1,0:T(4,128)S(1)}, f32[16,4,128]{2,1,0:T(4,128)S(1)}, u32[]{:S(2)}, u32[]{:S(2)}) collective-permute-start(f32[16,4,128]{2,1,0:T(4,128)S(1)} %add_add_fusion.3), channel_id=1, source_target_pairs={{0,192},{16,208},{32,224},{48,240},{64,128},{80,144},{96,160},{112... | collective-permute-start | bytes 98312 | tf_op jit(solution)/shard_map/ppermute | solution.py:192
  74.4 5.4 %collective-permute-start.7 = (f32[16,4,128]{2,1,0:T(4,128)S(1)}, f32[16,4,128]{2,1,0:T(4,128)S(1)}, u32[]{:S(2)}, u32[]{:S(2)}) collective-permute-start(f32[16,4,128]{2,1,0:T(4,128)S(1)} %add_add_fusion.3), channel_id=1, source_target_pairs={{0,128},{16,144},{32,160},{48,176},{64,192},{80,208},{96,224},{112... | collective-permute-start | bytes 98312 | tf_op jit(solution)/shard_map/ppermute | solution.py:192
  74.7 5.1 %collective-permute-start.6 = (f32[16,4,128]{2,1,0:T(4,128)S(1)}, f32[16,4,128]{2,1,0:T(4,128)S(1)}, u32[]{:S(2)}, u32[]{:S(2)}) collective-permute-start(f32[16,4,128]{2,1,0:T(4,128)S(1)} %add_add_fusion.3), channel_id=1, source_target_pairs={{0,64},{16,80},{32,96},{48,112},{64,0},{80,16},{96,32},{112,48},{1... | collective-permute-start | bytes 98312 | tf_op jit(solution)/shard_map/ppermute | solution.py:192
  84.3 17.6 %collective-permute-start.9 = (f32[864,1,128]{2,0,1:T(8,128)S(1)}, f32[864,1,128]{2,0,1:T(8,128)S(1)}, u32[]{:S(2)}, u32[]{:S(2)}) collective-permute-start(f32[864,1,128]{2,0,1:T(8,128)S(1)} %get-tuple-element.18), channel_id=1, source_target_pairs={{1,0},{2,1},{3,2},{4,3},{5,4},{6,5},{7,6},{8,7},{9,8},{10,9},{11,1... | collective-permute-start | bytes 1327112 | tf_op jit(solution)/shard_map/ppermute | solution.py:67
  86.8 30.1 %collective-permute-start.10 = (f32[864,1,128]{2,0,1:T(8,128)S(1)}, f32[864,1,128]{2,0,1:T(8,128)S(1)}, u32[]{:S(2)}, u32[]{:S(2)}) collective-permute-start(f32[864,1,128]{2,0,1:T(8,128)S(1)} %get-tuple-element.17), channel_id=1, source_target_pairs={{0,1},{1,2},{2,3},{3,4},{4,5},{5,6},{6,7},{7,8},{8,9},{9,10},{10,1... | collective-permute-start | bytes 1327112 | tf_op jit(solution)/shard_map/ppermute | solution.py:60
  88.7 33.0 %collective-permute-start.11 = (f32[864,1,128]{2,0,1:T(8,128)S(1)}, f32[864,1,128]{2,0,1:T(8,128)S(1)}, u32[]{:S(2)}, u32[]{:S(2)}) collective-permute-start(f32[864,1,128]{2,0,1:T(8,128)S(1)} %get-tuple-element.16), channel_id=1, source_target_pairs={{1,0},{2,1},{3,2},{4,3},{5,4},{6,5},{7,6},{8,7},{9,8},{10,9},{11,1... | collective-permute-start | bytes 1327112 | tf_op jit(solution)/shard_map/ppermute | solution.py:61
  132.7 23.5 %copy-start.1 = (f32[4,864,128]{2,1,0:T(8,128)S(1)}, f32[4,864,128]{2,1,0:T(8,128)}, u32[]{:S(2)}) copy-start(f32[4,864,128]{2,1,0:T(8,128)} %shard_map.60) | copy-start | bytes 5308420
  135.3 4.9 %collective-permute-start.13 = (f32[16,4,128]{2,1,0:T(4,128)S(1)}, f32[16,4,128]{2,1,0:T(4,128)S(1)}, u32[]{:S(2)}, u32[]{:S(2)}) collective-permute-start(f32[16,4,128]{2,1,0:T(4,128)S(1)} %copy.64), channel_id=1, source_target_pairs={{0,32},{16,48},{32,0},{48,16},{64,96},{80,112},{96,64},{112,80},{1... | collective-permute-start | bytes 98312 | tf_op jit(solution)/shard_map/ppermute | solution.py:192
  135.4 4.8 %collective-permute-start.12 = (f32[16,4,128]{2,1,0:T(4,128)S(1)}, f32[16,4,128]{2,1,0:T(4,128)S(1)}, u32[]{:S(2)}, u32[]{:S(2)}) collective-permute-start(f32[16,4,128]{2,1,0:T(4,128)S(1)} %copy.64), channel_id=1, source_target_pairs={{0,16},{16,0},{32,48},{48,32},{64,80},{80,64},{96,112},{112,96},{1... | collective-permute-start | bytes 98312 | tf_op jit(solution)/shard_map/ppermute | solution.py:192
  135.5 6.5 %collective-permute-start.14 = (f32[16,4,128]{2,1,0:T(4,128)S(1)}, f32[16,4,128]{2,1,0:T(4,128)S(1)}, u32[]{:S(2)}, u32[]{:S(2)}) collective-permute-start(f32[16,4,128]{2,1,0:T(4,128)S(1)} %copy.64), channel_id=1, source_target_pairs={{0,48},{16,32},{32,16},{48,0},{64,112},{80,96},{96,80},{112,64},{1... | collective-permute-start | bytes 98312 | tf_op jit(solution)/shard_map/ppermute | solution.py:192
  142.0 10.0 %collective-permute-start.17 = (f32[16,4,128]{2,1,0:T(4,128)S(1)}, f32[16,4,128]{2,1,0:T(4,128)S(1)}, u32[]{:S(2)}, u32[]{:S(2)}) collective-permute-start(f32[16,4,128]{2,1,0:T(4,128)S(1)} %add_add_fusion.1), channel_id=1, source_target_pairs={{0,192},{16,208},{32,224},{48,240},{64,128},{80,144},{96,160},{112... | collective-permute-start | bytes 98312 | tf_op jit(solution)/shard_map/ppermute | solution.py:192
  150.1 5.4 %collective-permute-start.16 = (f32[16,4,128]{2,1,0:T(4,128)S(1)}, f32[16,4,128]{2,1,0:T(4,128)S(1)}, u32[]{:S(2)}, u32[]{:S(2)}) collective-permute-start(f32[16,4,128]{2,1,0:T(4,128)S(1)} %add_add_fusion.1), channel_id=1, source_target_pairs={{0,128},{16,144},{32,160},{48,176},{64,192},{80,208},{96,224},{112... | collective-permute-start | bytes 98312 | tf_op jit(solution)/shard_map/ppermute | solution.py:192
  150.9 4.6 %collective-permute-start.15 = (f32[16,4,128]{2,1,0:T(4,128)S(1)}, f32[16,4,128]{2,1,0:T(4,128)S(1)}, u32[]{:S(2)}, u32[]{:S(2)}) collective-permute-start(f32[16,4,128]{2,1,0:T(4,128)S(1)} %add_add_fusion.1), channel_id=1, source_target_pairs={{0,64},{16,80},{32,96},{48,112},{64,0},{80,16},{96,32},{112,48},{1... | collective-permute-start | bytes 98312 | tf_op jit(solution)/shard_map/ppermute | solution.py:192

commit v6 on v2

--- a/solution.py
+++ b/solution.py
@@ -121,15 +121,17 @@
     if count & (count - 1):
         return lax.psum(local, "vel")
     bits = count.bit_length() - 1
+    groups = []
     low = 0
     while low < bits:
-        width = min(2, bits - low)
+        groups.append((low, min(2, bits - low)))
+        low += 2
+    for low, width in reversed(groups):
         values = [local]
         for member in range(1, 1 << width):
             mask = member << low
             values.append(lax.ppermute(local, "vel", [(i, i ^ mask) for i in range(count)]))
         local = xor_tree(values)
-        low += width
     return local
 
 

time: 143 us -> 143 us (level)
    ppermute x2, waiting for transfers between devices: 16.9 us -> 5.32 us  [with_upwind_halo(): high = lax.ppermute(block[:, :1], 'space', backward)]
    ppermute x2, waiting for transfers between devices: 12.4 us -> 21.6 us  [with_upwind_halo(): lax.ppermute(jnp.where(positive, block[:, rows - 2:rows - 1], block[:, 1:...]
    ppermute x2, starting transfers between devices: 7.27 us -> 9.24 us  [with_upwind_halo(): lax.ppermute(jnp.where(positive, block[:, rows - 2:rows - 1], block[:, 1:...]
where the time goes in v6:
time: 143 us; the launch traced here: 142 us
  starting transfers between devices  55.6 us (39%)
  waiting for transfers between devices  50.4 us (35%)
  other arithmetic  27.2 us (19%)
  local copies, waits for them, and re-layouts  5.09 us (4%)
  matrix products  2.58 us (2%)
  between operations  1.66 us (1%)
    ppermute x12, starting transfers between devices, vel_sum(): lax.ppermute(local, 'vel', [(i, i ^ mask) for i in range(count)])  31.8 us
    ppermute x2, waiting for transfers between devices, with_upwind_halo(): lax.ppermute(jnp.where(positive, block[:, rows - 2:rows - 1], block[:, 1:...  21.6 us
    ppermute x12, waiting for transfers between devices, vel_sum(): lax.ppermute(local, 'vel', [(i, i ^ mask) for i in range(count)])  14.3 us
    ppermute x2, starting transfers between devices, with_upwind_halo(): high = lax.ppermute(block[:, :1], 'space', backward)  10.7 us
    ppermute x2, starting transfers between devices, with_upwind_halo(): lax.ppermute(jnp.where(positive, block[:, rows - 2:rows - 1], block[:, 1:...  9.24 us
    ppermute x2, waiting for transfers between devices, with_upwind_halo(): low = lax.ppermute(block[:, rows - 1:], 'space', forward)  9.08 us
    mul x4, other arithmetic, sweep(): flux = number * jnp.where(number > 0, left_face, right_face)  7.28 us
    mul x4, other arithmetic, minmod(): 0.5 * (jnp.sign(left) + jnp.sign(right))  7.11 us
  transfers between devices with their start and end apart: 18, of which 14 were waited for; matrix products, arithmetic and copies ran while one was open for 1% of the time, Pallas kernels for 0%

profile of v6, /device:TPU:6, one launch (start us, length us, event | category | flops | bytes accessed | tf_op | source)
XLA Modules:
  0.0 142.5 jit_solution(2539595720712169115)
XLA Ops:
  0.6 1.6 %copy.98 = f32[864,4,128]{2,0,1:T(8,128)S(1)} copy(f32[864,4,128]{2,1,0:T(4,128)} %param.4) | data formatting | bytes 3538944 | tf_op args[0]
  2.3 0.6 dynamic_slice.6
  3.5 1.1 fusion.159
  4.6 1.9 %collective-permute-start = (f32[864,1,128]{2,0,1:T(8,128)}, f32[864,1,128]{2,0,1:T(8,128)S(1)}, u32[]{:S(2)}, u32[]{:S(2)}) collective-permute-start(f32[864,1,128]{2,0,1:T(8,128)} %get-tuple-element.19), channel_id=1, source_target_pairs={{0,1},{1,2},{2,3},{3,4},{4,5},{5,6},{6,7},{7,8},{8,9},{9,10},{10,1... | collective-permute-start | bytes 1327112 | tf_op jit(solution)/shard_map/ppermute | solution.py:57
  6.5 8.8 %collective-permute-start.1 = (f32[864,1,128]{2,0,1:T(8,128)}, f32[864,1,128]{2,0,1:T(8,128)S(1)}, u32[]{:S(2)}, u32[]{:S(2)}) collective-permute-start(f32[864,1,128]{2,0,1:T(8,128)} %get-tuple-element.20), channel_id=1, source_target_pairs={{1,0},{2,1},{3,2},{4,3},{5,4},{6,5},{7,6},{8,7},{9,8},{10,9},{11,1... | collective-permute-start | bytes 1327112 | tf_op jit(solution)/shard_map/ppermute | solution.py:58
  15.3 2.6 %collective-permute-start.2 = (f32[864,1,128]{2,0,1:T(8,128)}, f32[864,1,128]{2,0,1:T(8,128)S(1)}, u32[]{:S(2)}, u32[]{:S(2)}) collective-permute-start(f32[864,1,128]{2,0,1:T(8,128)} %get-tuple-element.21), channel_id=1, source_target_pairs={{1,0},{2,1},{3,2},{4,3},{5,4},{6,5},{7,6},{8,7},{9,8},{10,9},{11,1... | collective-permute-start | bytes 1327112 | tf_op jit(solution)/shard_map/ppermute | solution.py:64
  18.1 0.1 fusion.86
  18.1 0.1 add_add_fusion.4
  18.2 0.1 fusion.147
  18.3 0.1 fusion.149
  18.4 0.1 fusion.151
  18.5 0.1 fusion.153
  18.6 0.1 fusion.155
  18.6 0.1 stack.2
  18.8 0.9 collective-permute-done
  19.7 5.3 %collective-permute-done.1 = f32[864,1,128]{2,0,1:T(8,128)S(1)} collective-permute-done((f32[864,1,128]{2,0,1:T(8,128)}, f32[864,1,128]{2,0,1:T(8,128)S(1)}, u32[]{:S(2)}, u32[]{:S(2)}) %collective-permute-start.1) | collective-permute-done | bytes 442400 | tf_op jit(solution)/shard_map/ppermute | solution.py:58
  25.0 5.9 %collective-permute-done.2 = f32[864,1,128]{2,0,1:T(8,128)S(1)} collective-permute-done((f32[864,1,128]{2,0,1:T(8,128)}, f32[864,1,128]{2,0,1:T(8,128)S(1)}, u32[]{:S(2)}, u32[]{:S(2)}) %collective-permute-start.2) | collective-permute-done | bytes 442400 | tf_op jit(solution)/shard_map/ppermute | solution.py:64
  30.9 0.3 maximum_subtract_fusion
  31.2 1.1 minimum_multiply_fusion.3
  32.3 1.1 fusion.16
  33.4 0.4 copy-done
  33.8 0.2 fusion.61
  34.0 1.9 %fusion.3 = f32[864,4,131]{2,0,1:T(8,128)S(1)} fusion(f32[864,4,128]{2,0,1:T(8,128)S(1)} %fusion.61), kind=kLoop, calls=%fused_computation.11 | loop fusion | flops 452736 | bytes 3580416 | tf_op jit(solution)/shard_map/sub | solution.py:93
  35.9 2.4 %minimum_multiply_fusion.1 = f32[864,4,130]{2,0,1:T(8,128)S(1)} fusion(f32[864,4,131]{2,0,1:T(8,128)S(1)} %fusion.3), kind=kLoop, calls=%fused_computation.23 | loop fusion | flops 3594240 | bytes 5391360 | tf_op jit(solution)/shard_map/mul | solution.py:84
  38.3 2.6 %fusion.2 = f32[864,4,129]{2,0,1:T(8,128)S(1)} fusion(f32[864,4,128]{2,0,1:T(8,128)S(1)} %fusion.61, f32[864,4,130]{2,0,1:T(8,128)S(1)} %minimum_multiply_fusion.1, f32[864]{0:T(1024)S(1)} %get-tuple-element.48, f32[864]{0:T(1024)S(1)} %get-tuple-element.49, f32[864]{0:T(1024)S(1)} %broadcast_multiply_fusion, pred[864]{0:T(1024)(128)(4,1)S(1)} %broadcast_compare_fusion), kind=kLoop, calls=%fused_computation.10 | loop fusion | flops 2674944 | bytes 7130592 | tf_op jit(solution)/shard_map/mul | solution.py:101
  40.9 1.3 fusion.64
  42.2 1.7 %collective-permute-start.3 = (f32[16,4,128]{2,1,0:T(4,128)S(1)}, f32[16,4,128]{2,1,0:T(4,128)S(1)}, u32[]{:S(2)}, u32[]{:S(2)}) collective-permute-start(f32[16,4,128]{2,1,0:T(4,128)S(1)} %copy.100), channel_id=1, source_target_pairs={{0,64},{16,80},{32,96},{48,112},{64,0},{80,16},{96,32},{112,48},{1... | collective-permute-start | bytes 98312 | tf_op jit(solution)/shard_map/ppermute | solution.py:133
  43.9 18.2 %collective-permute-start.4 = (f32[16,4,128]{2,1,0:T(4,128)S(1)}, f32[16,4,128]{2,1,0:T(4,128)S(1)}, u32[]{:S(2)}, u32[]{:S(2)}) collective-permute-start(f32[16,4,128]{2,1,0:T(4,128)S(1)} %copy.100), channel_id=1, source_target_pairs={{0,128},{16,144},{32,160},{48,176},{64,192},{80,208},{96,224},{112... | collective-permute-start | bytes 98312 | tf_op jit(solution)/shard_map/ppermute | solution.py:133
  62.1 2.2 %collective-permute-done.4 = f32[16,4,128]{2,1,0:T(4,128)S(1)} collective-permute-done((f32[16,4,128]{2,1,0:T(4,128)S(1)}, f32[16,4,128]{2,1,0:T(4,128)S(1)}, u32[]{:S(2)}, u32[]{:S(2)}) %collective-permute-start.4) | collective-permute-done | bytes 32800 | tf_op jit(solution)/shard_map/ppermute | solution.py:133
  64.3 2.9 %collective-permute-done.5 = f32[16,4,128]{2,1,0:T(4,128)S(1)} collective-permute-done((f32[16,4,128]{2,1,0:T(4,128)S(1)}, f32[16,4,128]{2,1,0:T(4,128)S(1)}, u32[]{:S(2)}, u32[]{:S(2)}) %collective-permute-start.5) | collective-permute-done | bytes 32800 | tf_op jit(solution)/shard_map/ppermute | solution.py:133
  67.2 0.1 collective-permute-start.7
  67.3 1.7 %collective-permute-start.8 = (f32[16,4,128]{2,1,0:T(4,128)S(1)}, f32[16,4,128]{2,1,0:T(4,128)S(1)}, u32[]{:S(2)}, u32[]{:S(2)}) collective-permute-start(f32[16,4,128]{2,1,0:T(4,128)S(1)} %add_add_fusion.3), channel_id=1, source_target_pairs={{0,48},{16,32},{32,16},{48,0},{64,112},{80,96},{96,80},{112,64},{1... | collective-permute-start | bytes 98312 | tf_op jit(solution)/shard_map/ppermute | solution.py:133
  69.0 1.8 %collective-permute-start.6 = (f32[16,4,128]{2,1,0:T(4,128)S(1)}, f32[16,4,128]{2,1,0:T(4,128)S(1)}, u32[]{:S(2)}, u32[]{:S(2)}) collective-permute-start(f32[16,4,128]{2,1,0:T(4,128)S(1)} %add_add_fusion.3), channel_id=1, source_target_pairs={{0,16},{16,0},{32,48},{48,32},{64,80},{80,64},{96,112},{112,96},{1... | collective-permute-start | bytes 98312 | tf_op jit(solution)/shard_map/ppermute | solution.py:133
  70.8 1.3 collective-permute-done.7
  72.1 1.2 collective-permute-done.8
  73.4 2.7 %fusion.37 = f32[864,4,128]{2,0,1:T(8,128)S(1)} fusion(f32[4,128]{1,0:T(4,128)S(1)} %get-tuple-element.29, f32[4,128]{1,0:T(4,128)S(1)} %get-tuple-element.42, f32[4,128]{1,0:T(4,128)S(1)} %fusion.119, f32[4,128]{1,0:T(4,128)S(1)} %get-tuple-element.36, f32[4,128]{1,0:T(4,128)S(1)} %get-tuple-element.37, f32[4,128]{1,0:T(4,128)S(1)} %get-tuple-element.43, ...), kind=kLoop, calls=%fused_computation.71 | loop fusion | flops 13713408 | bytes 7120768 | tf_op jit(solution)/shard_map/jit(_where)/select_n | solution.py:259
  76.0 0.1 fusion.158
  76.1 1.9 %collective-permute-start.10 = (f32[864,1,128]{2,0,1:T(8,128)S(1)}, f32[864,1,128]{2,0,1:T(8,128)S(1)}, u32[]{:S(2)}, u32[]{:S(2)}) collective-permute-start(f32[864,1,128]{2,0,1:T(8,128)S(1)} %get-tuple-element.18), channel_id=1, source_target_pairs={{1,0},{2,1},{3,2},{4,3},{5,4},{6,5},{7,6},{8,7},{9,8},{10,9},{11,1... | collective-permute-start | bytes 1327112 | tf_op jit(solution)/shard_map/ppermute | solution.py:58
  78.1 6.7 %collective-permute-start.11 = (f32[864,1,128]{2,0,1:T(8,128)S(1)}, f32[864,1,128]{2,0,1:T(8,128)S(1)}, u32[]{:S(2)}, u32[]{:S(2)}) collective-permute-start(f32[864,1,128]{2,0,1:T(8,128)S(1)} %get-tuple-element.17), channel_id=1, source_target_pairs={{1,0},{2,1},{3,2},{4,3},{5,4},{6,5},{7,6},{8,7},{9,8},{10,9},{11,1... | collective-permute-start | bytes 1327112 | tf_op jit(solution)/shard_map/ppermute | solution.py:64
  84.7 1.9 %collective-permute-start.9 = (f32[864,1,128]{2,0,1:T(8,128)S(1)}, f32[864,1,128]{2,0,1:T(8,128)S(1)}, u32[]{:S(2)}, u32[]{:S(2)}) collective-permute-start(f32[864,1,128]{2,0,1:T(8,128)S(1)} %get-tuple-element.16), channel_id=1, source_target_pairs={{0,1},{1,2},{2,3},{3,4},{4,5},{5,6},{6,7},{7,8},{8,9},{9,10},{10,1... | collective-permute-start | bytes 1327112 | tf_op jit(solution)/shard_map/ppermute | solution.py:57
  86.7 15.8 %collective-permute-done.11 = f32[864,1,128]{2,0,1:T(8,128)S(1)} collective-permute-done((f32[864,1,128]{2,0,1:T(8,128)S(1)}, f32[864,1,128]{2,0,1:T(8,128)S(1)}, u32[]{:S(2)}, u32[]{:S(2)}) %collective-permute-start.11) | collective-permute-done | bytes 442400 | tf_op jit(solution)/shard_map/ppermute | solution.py:64
  102.4 8.2 %collective-permute-done.9 = f32[864,1,128]{2,0,1:T(8,128)S(1)} collective-permute-done((f32[864,1,128]{2,0,1:T(8,128)S(1)}, f32[864,1,128]{2,0,1:T(8,128)S(1)}, u32[]{:S(2)}, u32[]{:S(2)}) %collective-permute-start.9) | collective-permute-done | bytes 442400 | tf_op jit(solution)/shard_map/ppermute | solution.py:57
  110.7 0.3 maximum_subtract_fusion.1
  111.0 1.1 minimum_multiply_fusion.2
  112.1 1.1 fusion.12
  113.2 0.2 fusion.59
  113.4 1.9 %fusion.8 = f32[864,4,131]{2,0,1:T(8,128)S(1)} fusion(f32[864,4,128]{2,0,1:T(8,128)S(1)} %fusion.59), kind=kLoop, calls=%fused_computation.16 | loop fusion | flops 452736 | bytes 3580416 | tf_op jit(solution)/shard_map/sub | solution.py:93
  115.3 2.4 %minimum_multiply_fusion = f32[864,4,130]{2,0,1:T(8,128)S(1)} fusion(f32[864,4,131]{2,0,1:T(8,128)S(1)} %fusion.8), kind=kLoop, calls=%fused_computation.22 | loop fusion | flops 3594240 | bytes 5391360 | tf_op jit(solution)/shard_map/mul | solution.py:84
  117.7 2.6 %fusion.7 = f32[864,4,129]{2,0,1:T(8,128)S(1)} fusion(f32[864,4,128]{2,0,1:T(8,128)S(1)} %fusion.59, f32[864,4,130]{2,0,1:T(8,128)S(1)} %minimum_multiply_fusion, f32[864]{0:T(1024)S(1)} %get-tuple-element.48, f32[864]{0:T(1024)S(1)} %get-tuple-element.49, f32[864]{0:T(1024)S(1)} %broadcast_multiply_fusion, pred[864]{0:T(1024)(128)(4,1)S(1)} %broadcast_compare_fusion), kind=kLoop, calls=%fused_computation.15 | loop fusion | flops 2674944 | bytes 7130592 | tf_op jit(solution)/shard_map/mul | solution.py:101
  120.3 1.3 fusion.62
  121.6 0.1 collective-permute-start.12
  121.7 3.7 %collective-permute-start.13 = (f32[16,4,128]{2,1,0:T(4,128)S(1)}, f32[16,4,128]{2,1,0:T(4,128)S(1)}, u32[]{:S(2)}, u32[]{:S(2)}) collective-permute-start(f32[16,4,128]{2,1,0:T(4,128)S(1)} %copy.104), channel_id=1, source_target_pairs={{0,128},{16,144},{32,160},{48,176},{64,192},{80,208},{96,224},{112... | collective-permute-start | bytes 98312 | tf_op jit(solution)/shard_map/ppermute | solution.py:133
  125.4 1.0 collective-permute-start.14
  126.4 1.2 collective-permute-done.13
  127.6 2.9 %collective-permute-done.14 = f32[16,4,128]{2,1,0:T(4,128)S(1)} collective-permute-done((f32[16,4,128]{2,1,0:T(4,128)S(1)}, f32[16,4,128]{2,1,0:T(4,128)S(1)}, u32[]{:S(2)}, u32[]{:S(2)}) %collective-permute-start.14) | collective-permute-done | bytes 32800 | tf_op jit(solution)/shard_map/ppermute | solution.py:133
  130.5 0.1 collective-permute-start.16
  130.6 2.0 %collective-permute-start.17 = (f32[16,4,128]{2,1,0:T(4,128)S(1)}, f32[16,4,128]{2,1,0:T(4,128)S(1)}, u32[]{:S(2)}, u32[]{:S(2)}) collective-permute-start(f32[16,4,128]{2,1,0:T(4,128)S(1)} %add_add_fusion.1), channel_id=1, source_target_pairs={{0,48},{16,32},{32,16},{48,0},{64,112},{80,96},{96,80},{112,64},{1... | collective-permute-start | bytes 98312 | tf_op jit(solution)/shard_map/ppermute | solution.py:133
  132.7 1.4 %collective-permute-start.15 = (f32[16,4,128]{2,1,0:T(4,128)S(1)}, f32[16,4,128]{2,1,0:T(4,128)S(1)}, u32[]{:S(2)}, u32[]{:S(2)}) collective-permute-start(f32[16,4,128]{2,1,0:T(4,128)S(1)} %add_add_fusion.1), channel_id=1, source_target_pairs={{0,16},{16,0},{32,48},{48,32},{64,80},{80,64},{96,112},{112,96},{1... | collective-permute-start | bytes 98312 | tf_op jit(solution)/shard_map/ppermute | solution.py:133
  134.1 1.3 collective-permute-done.16
  135.4 1.0 collective-permute-done.17
  136.4 0.3 collective-permute-done.15
  136.8 0.6 fusion.144
  137.4 2.7 %fusion.57 = f32[864,4,128]{2,0,1:T(8,128)S(1)} fusion(f32[4,128]{1,0:T(4,128)S(1)} %get-tuple-element.32, f32[4,128]{1,0:T(4,128)S(1)} %get-tuple-element.38, f32[4,128]{1,0:T(4,128)S(1)} %get-tuple-element.31, f32[4,128]{1,0:T(4,128)S(1)} %get-tuple-element.23, f32[4,128]{1,0:T(4,128)S(1)} %get-tuple-element.22, f32[4,128]{1,0:T(4,128)S(1)} %get-tuple-element.39, ...), kind=kLoop, calls=%fused_computation.91 | loop fusion | flops 13713408 | bytes 7120768 | tf_op jit(solution)/shard_map/jit(_where)/select_n | solution.py:259
  140.1 2.3 %copy.107 = f32[864,4,128]{2,1,0:T(4,128)} copy(f32[864,4,128]{2,0,1:T(8,128)S(1)} %fusion.57) | data formatting | bytes 3538944
  (34 shorter events, 0.5 us)
Async XLA Ops:
  0.6 1.6 %copy-start.2 = (s32[16]{0:T(128)S(1)}, s32[16]{0:T(128)}, u32[]{:S(2)}) copy-start(s32[16]{0:T(128)} %constant.97.clone) | copy-start | bytes 196
  2.2 16.6 %copy-start.1 = (s32[4,128]{1,0:T(4,128)S(1)}, s32[4,128]{1,0:T(4,128)}, u32[]{:S(2)}) copy-start(s32[4,128]{1,0:T(4,128)} %param.5) | copy-start | bytes 6148
  4.6 15.1 %collective-permute-start = (f32[864,1,128]{2,0,1:T(8,128)}, f32[864,1,128]{2,0,1:T(8,128)S(1)}, u32[]{:S(2)}, u32[]{:S(2)}) collective-permute-start(f32[864,1,128]{2,0,1:T(8,128)} %get-tuple-element.19), channel_id=1, source_target_pairs={{0,1},{1,2},{2,3},{3,4},{4,5},{5,6},{6,7},{7,8},{8,9},{9,10},{10,1... | collective-permute-start | bytes 1327112 | tf_op jit(solution)/shard_map/ppermute | solution.py:57
  6.5 18.5 %collective-permute-start.1 = (f32[864,1,128]{2,0,1:T(8,128)}, f32[864,1,128]{2,0,1:T(8,128)S(1)}, u32[]{:S(2)}, u32[]{:S(2)}) collective-permute-start(f32[864,1,128]{2,0,1:T(8,128)} %get-tuple-element.20), channel_id=1, source_target_pairs={{1,0},{2,1},{3,2},{4,3},{5,4},{6,5},{7,6},{8,7},{9,8},{10,9},{11,1... | collective-permute-start | bytes 1327112 | tf_op jit(solution)/shard_map/ppermute | solution.py:58
  15.3 15.5 %collective-permute-start.2 = (f32[864,1,128]{2,0,1:T(8,128)}, f32[864,1,128]{2,0,1:T(8,128)S(1)}, u32[]{:S(2)}, u32[]{:S(2)}) collective-permute-start(f32[864,1,128]{2,0,1:T(8,128)} %get-tuple-element.21), channel_id=1, source_target_pairs={{1,0},{2,1},{3,2},{4,3},{5,4},{6,5},{7,6},{8,7},{9,8},{10,9},{11,1... | collective-permute-start | bytes 1327112 | tf_op jit(solution)/shard_map/ppermute | solution.py:64
  32.3 1.5 %copy-start = (f32[864,4,128]{2,1,0:T(4,128)S(1)}, f32[864,4,128]{2,1,0:T(4,128)}, u32[]{:S(2)}) copy-start(f32[864,4,128]{2,1,0:T(4,128)} %param.4) | copy-start | bytes 5308420
  42.2 19.9 %collective-permute-start.3 = (f32[16,4,128]{2,1,0:T(4,128)S(1)}, f32[16,4,128]{2,1,0:T(4,128)S(1)}, u32[]{:S(2)}, u32[]{:S(2)}) collective-permute-start(f32[16,4,128]{2,1,0:T(4,128)S(1)} %copy.100), channel_id=1, source_target_pairs={{0,64},{16,80},{32,96},{48,112},{64,0},{80,16},{96,32},{112,48},{1... | collective-permute-start | bytes 98312 | tf_op jit(solution)/shard_map/ppermute | solution.py:133
  43.9 20.4 %collective-permute-start.4 = (f32[16,4,128]{2,1,0:T(4,128)S(1)}, f32[16,4,128]{2,1,0:T(4,128)S(1)}, u32[]{:S(2)}, u32[]{:S(2)}) collective-permute-start(f32[16,4,128]{2,1,0:T(4,128)S(1)} %copy.100), channel_id=1, source_target_pairs={{0,128},{16,144},{32,160},{48,176},{64,192},{80,208},{96,224},{112... | collective-permute-start | bytes 98312 | tf_op jit(solution)/shard_map/ppermute | solution.py:133
  62.0 5.1 %collective-permute-start.5 = (f32[16,4,128]{2,1,0:T(4,128)S(1)}, f32[16,4,128]{2,1,0:T(4,128)S(1)}, u32[]{:S(2)}, u32[]{:S(2)}) collective-permute-start(f32[16,4,128]{2,1,0:T(4,128)S(1)} %copy.100), channel_id=1, source_target_pairs={{0,192},{16,208},{32,224},{48,240},{64,128},{80,144},{96,160},{112... | collective-permute-start | bytes 98312 | tf_op jit(solution)/shard_map/ppermute | solution.py:133
  67.2 4.9 %collective-permute-start.7 = (f32[16,4,128]{2,1,0:T(4,128)S(1)}, f32[16,4,128]{2,1,0:T(4,128)S(1)}, u32[]{:S(2)}, u32[]{:S(2)}) collective-permute-start(f32[16,4,128]{2,1,0:T(4,128)S(1)} %add_add_fusion.3), channel_id=1, source_target_pairs={{0,32},{16,48},{32,0},{48,16},{64,96},{80,112},{96,64},{112,80},{1... | collective-permute-start | bytes 98312 | tf_op jit(solution)/shard_map/ppermute | solution.py:133
  67.3 6.0 %collective-permute-start.8 = (f32[16,4,128]{2,1,0:T(4,128)S(1)}, f32[16,4,128]{2,1,0:T(4,128)S(1)}, u32[]{:S(2)}, u32[]{:S(2)}) collective-permute-start(f32[16,4,128]{2,1,0:T(4,128)S(1)} %add_add_fusion.3), channel_id=1, source_target_pairs={{0,48},{16,32},{32,16},{48,0},{64,112},{80,96},{96,80},{112,64},{1... | collective-permute-start | bytes 98312 | tf_op jit(solution)/shard_map/ppermute | solution.py:133
  69.0 4.3 %collective-permute-start.6 = (f32[16,4,128]{2,1,0:T(4,128)S(1)}, f32[16,4,128]{2,1,0:T(4,128)S(1)}, u32[]{:S(2)}, u32[]{:S(2)}) collective-permute-start(f32[16,4,128]{2,1,0:T(4,128)S(1)} %add_add_fusion.3), channel_id=1, source_target_pairs={{0,16},{16,0},{32,48},{48,32},{64,80},{80,64},{96,112},{112,96},{1... | collective-permute-start | bytes 98312 | tf_op jit(solution)/shard_map/ppermute | solution.py:133
  76.1 10.5 %collective-permute-start.10 = (f32[864,1,128]{2,0,1:T(8,128)S(1)}, f32[864,1,128]{2,0,1:T(8,128)S(1)}, u32[]{:S(2)}, u32[]{:S(2)}) collective-permute-start(f32[864,1,128]{2,0,1:T(8,128)S(1)} %get-tuple-element.18), channel_id=1, source_target_pairs={{1,0},{2,1},{3,2},{4,3},{5,4},{6,5},{7,6},{8,7},{9,8},{10,9},{11,1... | collective-permute-start | bytes 1327112 | tf_op jit(solution)/shard_map/ppermute | solution.py:58
  78.1 24.4 %collective-permute-start.11 = (f32[864,1,128]{2,0,1:T(8,128)S(1)}, f32[864,1,128]{2,0,1:T(8,128)S(1)}, u32[]{:S(2)}, u32[]{:S(2)}) collective-permute-start(f32[864,1,128]{2,0,1:T(8,128)S(1)} %get-tuple-element.17), channel_id=1, source_target_pairs={{1,0},{2,1},{3,2},{4,3},{5,4},{6,5},{7,6},{8,7},{9,8},{10,9},{11,1... | collective-permute-start | bytes 1327112 | tf_op jit(solution)/shard_map/ppermute | solution.py:64
  84.7 25.9 %collective-permute-start.9 = (f32[864,1,128]{2,0,1:T(8,128)S(1)}, f32[864,1,128]{2,0,1:T(8,128)S(1)}, u32[]{:S(2)}, u32[]{:S(2)}) collective-permute-start(f32[864,1,128]{2,0,1:T(8,128)S(1)} %get-tuple-element.16), channel_id=1, source_target_pairs={{0,1},{1,2},{2,3},{3,4},{4,5},{5,6},{6,7},{7,8},{8,9},{9,10},{10,1... | collective-permute-start | bytes 1327112 | tf_op jit(solution)/shard_map/ppermute | solution.py:57
  121.6 4.8 %collective-permute-start.12 = (f32[16,4,128]{2,1,0:T(4,128)S(1)}, f32[16,4,128]{2,1,0:T(4,128)S(1)}, u32[]{:S(2)}, u32[]{:S(2)}) collective-permute-start(f32[16,4,128]{2,1,0:T(4,128)S(1)} %copy.104), channel_id=1, source_target_pairs={{0,64},{16,80},{32,96},{48,112},{64,0},{80,16},{96,32},{112,48},{1... | collective-permute-start | bytes 98312 | tf_op jit(solution)/shard_map/ppermute | solution.py:133
  121.7 5.9 %collective-permute-start.13 = (f32[16,4,128]{2,1,0:T(4,128)S(1)}, f32[16,4,128]{2,1,0:T(4,128)S(1)}, u32[]{:S(2)}, u32[]{:S(2)}) collective-permute-start(f32[16,4,128]{2,1,0:T(4,128)S(1)} %copy.104), channel_id=1, source_target_pairs={{0,128},{16,144},{32,160},{48,176},{64,192},{80,208},{96,224},{112... | collective-permute-start | bytes 98312 | tf_op jit(solution)/shard_map/ppermute | solution.py:133
  125.4 5.1 %collective-permute-start.14 = (f32[16,4,128]{2,1,0:T(4,128)S(1)}, f32[16,4,128]{2,1,0:T(4,128)S(1)}, u32[]{:S(2)}, u32[]{:S(2)}) collective-permute-start(f32[16,4,128]{2,1,0:T(4,128)S(1)} %copy.104), channel_id=1, source_target_pairs={{0,192},{16,208},{32,224},{48,240},{64,128},{80,144},{96,160},{112... | collective-permute-start | bytes 98312 | tf_op jit(solution)/shard_map/ppermute | solution.py:133
  130.5 4.9 %collective-permute-start.16 = (f32[16,4,128]{2,1,0:T(4,128)S(1)}, f32[16,4,128]{2,1,0:T(4,128)S(1)}, u32[]{:S(2)}, u32[]{:S(2)}) collective-permute-start(f32[16,4,128]{2,1,0:T(4,128)S(1)} %add_add_fusion.1), channel_id=1, source_target_pairs={{0,32},{16,48},{32,0},{48,16},{64,96},{80,112},{96,64},{112,80},{1... | collective-permute-start | bytes 98312 | tf_op jit(solution)/shard_map/ppermute | solution.py:133
  130.6 5.8 %collective-permute-start.17 = (f32[16,4,128]{2,1,0:T(4,128)S(1)}, f32[16,4,128]{2,1,0:T(4,128)S(1)}, u32[]{:S(2)}, u32[]{:S(2)}) collective-permute-start(f32[16,4,128]{2,1,0:T(4,128)S(1)} %add_add_fusion.1), channel_id=1, source_target_pairs={{0,48},{16,32},{32,16},{48,0},{64,112},{80,96},{96,80},{112,64},{1... | collective-permute-start | bytes 98312 | tf_op jit(solution)/shard_map/ppermute | solution.py:133
  132.7 4.1 %collective-permute-start.15 = (f32[16,4,128]{2,1,0:T(4,128)S(1)}, f32[16,4,128]{2,1,0:T(4,128)S(1)}, u32[]{:S(2)}, u32[]{:S(2)}) collective-permute-start(f32[16,4,128]{2,1,0:T(4,128)S(1)} %add_add_fusion.1), channel_id=1, source_target_pairs={{0,16},{16,0},{32,48},{48,32},{64,80},{80,64},{96,112},{112,96},{1... | collective-permute-start | bytes 98312 | tf_op jit(solution)/shard_map/ppermute | solution.py:133

commit v7 on v6

--- a/solution.py
+++ b/solution.py
@@ -81,7 +81,7 @@
 
 
 def minmod(left, right):
-    return 0.5 * (jnp.sign(left) + jnp.sign(right)) * jnp.minimum(jnp.abs(left), jnp.abs(right))
+    return jnp.maximum(jnp.minimum(left, right), jnp.minimum(jnp.maximum(left, right), 0.0))
 
 
 def sweep(distribution_table, number, along):

time: 143 us -> 138 us (0.965)
  other arithmetic: 27.2 us -> 22.8 us
    mul x4 -> x0, other arithmetic: 7.11 us -> none  [minmod(): 0.5 * (jnp.sign(left) + jnp.sign(right))]
    max x0 -> x4, other arithmetic: none -> 2.65 us  [minmod(): jnp.maximum(jnp.minimum(left, right), jnp.minimum(jnp.maximum(left, right...]
  transfers between devices with their start and end apart: 18 -> 18, of which waited for: 14 -> 15; matrix products, arithmetic and copies ran while one was open for 1% -> 1% of each run, Pallas kernels for 0% -> 0%
where the time goes in v7:
time: 138 us
  starting transfers between devices  55.8 us (40%)
  waiting for transfers between devices  50.2 us (36%)
  other arithmetic  22.8 us (17%)
  local copies, waits for them, and re-layouts  5.09 us (4%)
  matrix products  2.58 us (2%)
  between operations  1.66 us (1%)
    ppermute x12, starting transfers between devices, vel_sum(): lax.ppermute(local, 'vel', [(i, i ^ mask) for i in range(count)])  31.8 us
    ppermute x2, waiting for transfers between devices, with_upwind_halo(): lax.ppermute(jnp.where(positive, block[:, rows - 2:rows - 1], block[:, 1:...  21.2 us
    ppermute x12, waiting for transfers between devices, vel_sum(): lax.ppermute(local, 'vel', [(i, i ^ mask) for i in range(count)])  14.2 us
    ppermute x2, starting transfers between devices, with_upwind_halo(): high = lax.ppermute(block[:, :1], 'space', backward)  10.7 us
    ppermute x2, waiting for transfers between devices, with_upwind_halo(): low = lax.ppermute(block[:, rows - 1:], 'space', forward)  9.51 us
    ppermute x2, starting transfers between devices, with_upwind_halo(): lax.ppermute(jnp.where(positive, block[:, rows - 2:rows - 1], block[:, 1:...  9.27 us
    mul x4, other arithmetic, sweep(): flux = number * jnp.where(number > 0, left_face, right_face)  7.28 us
    select_n x2, other arithmetic, approach_increment(): jnp.where(kind_labels == 1, wall_distribution, jnp.where(kind_labels == 2...  5.35 us
  transfers between devices with their start and end apart: 18, of which 15 were waited for; matrix products, arithmetic and copies ran while one was open for 1% of the time, Pallas kernels for 0%

profile of v7, /device:TPU:6, one launch (start us, length us, event | category | flops | bytes accessed | tf_op | source)
XLA Modules:
  0.0 138.1 jit_solution(16810890568267354469)
XLA Ops:
  0.6 1.6 %copy.98 = f32[864,4,128]{2,0,1:T(8,128)S(1)} copy(f32[864,4,128]{2,1,0:T(4,128)} %param.4) | data formatting | bytes 3538944 | tf_op args[0]
  2.3 0.6 dynamic_slice.6
  3.5 1.1 fusion.159
  4.6 1.9 %collective-permute-start = (f32[864,1,128]{2,0,1:T(8,128)}, f32[864,1,128]{2,0,1:T(8,128)S(1)}, u32[]{:S(2)}, u32[]{:S(2)}) collective-permute-start(f32[864,1,128]{2,0,1:T(8,128)} %get-tuple-element.19), channel_id=1, source_target_pairs={{0,1},{1,2},{2,3},{3,4},{4,5},{5,6},{6,7},{7,8},{8,9},{9,10},{10,1... | collective-permute-start | bytes 1327112 | tf_op jit(solution)/shard_map/ppermute | solution.py:57
  6.5 8.8 %collective-permute-start.1 = (f32[864,1,128]{2,0,1:T(8,128)}, f32[864,1,128]{2,0,1:T(8,128)S(1)}, u32[]{:S(2)}, u32[]{:S(2)}) collective-permute-start(f32[864,1,128]{2,0,1:T(8,128)} %get-tuple-element.20), channel_id=1, source_target_pairs={{1,0},{2,1},{3,2},{4,3},{5,4},{6,5},{7,6},{8,7},{9,8},{10,9},{11,1... | collective-permute-start | bytes 1327112 | tf_op jit(solution)/shard_map/ppermute | solution.py:58
  15.3 2.6 %collective-permute-start.2 = (f32[864,1,128]{2,0,1:T(8,128)}, f32[864,1,128]{2,0,1:T(8,128)S(1)}, u32[]{:S(2)}, u32[]{:S(2)}) collective-permute-start(f32[864,1,128]{2,0,1:T(8,128)} %get-tuple-element.21), channel_id=1, source_target_pairs={{1,0},{2,1},{3,2},{4,3},{5,4},{6,5},{7,6},{8,7},{9,8},{10,9},{11,1... | collective-permute-start | bytes 1327112 | tf_op jit(solution)/shard_map/ppermute | solution.py:64
  18.1 0.1 fusion.86
  18.1 0.1 add_add_fusion.4
  18.2 0.1 fusion.147
  18.3 0.1 fusion.149
  18.4 0.1 fusion.151
  18.5 0.1 fusion.153
  18.6 0.1 stack.2
  18.8 0.9 collective-permute-done
  19.7 5.3 %collective-permute-done.1 = f32[864,1,128]{2,0,1:T(8,128)S(1)} collective-permute-done((f32[864,1,128]{2,0,1:T(8,128)}, f32[864,1,128]{2,0,1:T(8,128)S(1)}, u32[]{:S(2)}, u32[]{:S(2)}) %collective-permute-start.1) | collective-permute-done | bytes 442400 | tf_op jit(solution)/shard_map/ppermute | solution.py:58
  25.0 5.9 %collective-permute-done.2 = f32[864,1,128]{2,0,1:T(8,128)S(1)} collective-permute-done((f32[864,1,128]{2,0,1:T(8,128)}, f32[864,1,128]{2,0,1:T(8,128)S(1)}, u32[]{:S(2)}, u32[]{:S(2)}) %collective-permute-start.2) | collective-permute-done | bytes 442400 | tf_op jit(solution)/shard_map/ppermute | solution.py:64
  30.9 0.3 maximum_subtract_fusion
  31.2 0.3 minimum_maximum_fusion.3
  31.5 1.1 fusion.16
  32.6 0.4 copy-done
  33.0 0.2 fusion.61
  33.2 1.9 %fusion.3 = f32[864,4,131]{2,0,1:T(8,128)S(1)} fusion(f32[864,4,128]{2,0,1:T(8,128)S(1)} %fusion.61), kind=kLoop, calls=%fused_computation.11 | loop fusion | flops 452736 | bytes 3580416 | tf_op jit(solution)/shard_map/sub | solution.py:93
  35.1 1.0 minimum_maximum_fusion.1
  36.1 2.6 %fusion.2 = f32[864,4,129]{2,0,1:T(8,128)S(1)} fusion(f32[864,4,128]{2,0,1:T(8,128)S(1)} %fusion.61, f32[864,4,130]{2,0,1:T(8,128)S(1)} %minimum_maximum_fusion.1, f32[864]{0:T(1024)S(1)} %get-tuple-element.48, f32[864]{0:T(1024)S(1)} %get-tuple-element.49, f32[864]{0:T(1024)S(1)} %broadcast_multiply_fusion, pred[864]{0:T(1024)(128)(4,1)S(1)} %broadcast_compare_fusion), kind=kLoop, calls=%fused_computation.10 | loop fusion | flops 2674944 | bytes 7130592 | tf_op jit(solution)/shard_map/mul | solution.py:101
  38.7 1.3 fusion.64
  40.0 1.7 %collective-permute-start.3 = (f32[16,4,128]{2,1,0:T(4,128)S(1)}, f32[16,4,128]{2,1,0:T(4,128)S(1)}, u32[]{:S(2)}, u32[]{:S(2)}) collective-permute-start(f32[16,4,128]{2,1,0:T(4,128)S(1)} %copy.100), channel_id=1, source_target_pairs={{0,64},{16,80},{32,96},{48,112},{64,0},{80,16},{96,32},{112,48},{1... | collective-permute-start | bytes 98312 | tf_op jit(solution)/shard_map/ppermute | solution.py:133
  41.6 18.2 %collective-permute-start.4 = (f32[16,4,128]{2,1,0:T(4,128)S(1)}, f32[16,4,128]{2,1,0:T(4,128)S(1)}, u32[]{:S(2)}, u32[]{:S(2)}) collective-permute-start(f32[16,4,128]{2,1,0:T(4,128)S(1)} %copy.100), channel_id=1, source_target_pairs={{0,128},{16,144},{32,160},{48,176},{64,192},{80,208},{96,224},{112... | collective-permute-start | bytes 98312 | tf_op jit(solution)/shard_map/ppermute | solution.py:133
  59.9 2.2 %collective-permute-done.4 = f32[16,4,128]{2,1,0:T(4,128)S(1)} collective-permute-done((f32[16,4,128]{2,1,0:T(4,128)S(1)}, f32[16,4,128]{2,1,0:T(4,128)S(1)}, u32[]{:S(2)}, u32[]{:S(2)}) %collective-permute-start.4) | collective-permute-done | bytes 32800 | tf_op jit(solution)/shard_map/ppermute | solution.py:133
  62.1 2.9 %collective-permute-done.5 = f32[16,4,128]{2,1,0:T(4,128)S(1)} collective-permute-done((f32[16,4,128]{2,1,0:T(4,128)S(1)}, f32[16,4,128]{2,1,0:T(4,128)S(1)}, u32[]{:S(2)}, u32[]{:S(2)}) %collective-permute-start.5) | collective-permute-done | bytes 32800 | tf_op jit(solution)/shard_map/ppermute | solution.py:133
  65.0 0.1 collective-permute-start.7
  65.1 1.7 %collective-permute-start.8 = (f32[16,4,128]{2,1,0:T(4,128)S(1)}, f32[16,4,128]{2,1,0:T(4,128)S(1)}, u32[]{:S(2)}, u32[]{:S(2)}) collective-permute-start(f32[16,4,128]{2,1,0:T(4,128)S(1)} %add_add_fusion.3), channel_id=1, source_target_pairs={{0,48},{16,32},{32,16},{48,0},{64,112},{80,96},{96,80},{112,64},{1... | collective-permute-start | bytes 98312 | tf_op jit(solution)/shard_map/ppermute | solution.py:133
  66.8 1.8 %collective-permute-start.6 = (f32[16,4,128]{2,1,0:T(4,128)S(1)}, f32[16,4,128]{2,1,0:T(4,128)S(1)}, u32[]{:S(2)}, u32[]{:S(2)}) collective-permute-start(f32[16,4,128]{2,1,0:T(4,128)S(1)} %add_add_fusion.3), channel_id=1, source_target_pairs={{0,16},{16,0},{32,48},{48,32},{64,80},{80,64},{96,112},{112,96},{1... | collective-permute-start | bytes 98312 | tf_op jit(solution)/shard_map/ppermute | solution.py:133
  68.6 1.3 collective-permute-done.7
  69.9 1.1 collective-permute-done.8
  71.0 0.1 collective-permute-done.6
  71.1 2.7 %fusion.37 = f32[864,4,128]{2,0,1:T(8,128)S(1)} fusion(f32[4,128]{1,0:T(4,128)S(1)} %get-tuple-element.29, f32[4,128]{1,0:T(4,128)S(1)} %get-tuple-element.42, f32[4,128]{1,0:T(4,128)S(1)} %fusion.119, f32[4,128]{1,0:T(4,128)S(1)} %get-tuple-element.36, f32[4,128]{1,0:T(4,128)S(1)} %get-tuple-element.37, f32[4,128]{1,0:T(4,128)S(1)} %get-tuple-element.43, ...), kind=kLoop, calls=%fused_computation.71 | loop fusion | flops 13713408 | bytes 7120768 | tf_op jit(solution)/shard_map/jit(_where)/select_n | solution.py:259
  73.8 0.1 fusion.158
  73.9 1.9 %collective-permute-start.10 = (f32[864,1,128]{2,0,1:T(8,128)S(1)}, f32[864,1,128]{2,0,1:T(8,128)S(1)}, u32[]{:S(2)}, u32[]{:S(2)}) collective-permute-start(f32[864,1,128]{2,0,1:T(8,128)S(1)} %get-tuple-element.18), channel_id=1, source_target_pairs={{1,0},{2,1},{3,2},{4,3},{5,4},{6,5},{7,6},{8,7},{9,8},{10,9},{11,1... | collective-permute-start | bytes 1327112 | tf_op jit(solution)/shard_map/ppermute | solution.py:58
  75.8 6.7 %collective-permute-start.11 = (f32[864,1,128]{2,0,1:T(8,128)S(1)}, f32[864,1,128]{2,0,1:T(8,128)S(1)}, u32[]{:S(2)}, u32[]{:S(2)}) collective-permute-start(f32[864,1,128]{2,0,1:T(8,128)S(1)} %get-tuple-element.17), channel_id=1, source_target_pairs={{1,0},{2,1},{3,2},{4,3},{5,4},{6,5},{7,6},{8,7},{9,8},{10,9},{11,1... | collective-permute-start | bytes 1327112 | tf_op jit(solution)/shard_map/ppermute | solution.py:64
  82.5 2.1 %collective-permute-start.9 = (f32[864,1,128]{2,0,1:T(8,128)S(1)}, f32[864,1,128]{2,0,1:T(8,128)S(1)}, u32[]{:S(2)}, u32[]{:S(2)}) collective-permute-start(f32[864,1,128]{2,0,1:T(8,128)S(1)} %get-tuple-element.16), channel_id=1, source_target_pairs={{0,1},{1,2},{2,3},{3,4},{4,5},{5,6},{6,7},{7,8},{8,9},{9,10},{10,1... | collective-permute-start | bytes 1327112 | tf_op jit(solution)/shard_map/ppermute | solution.py:57
  84.6 15.3 %collective-permute-done.11 = f32[864,1,128]{2,0,1:T(8,128)S(1)} collective-permute-done((f32[864,1,128]{2,0,1:T(8,128)S(1)}, f32[864,1,128]{2,0,1:T(8,128)S(1)}, u32[]{:S(2)}, u32[]{:S(2)}) %collective-permute-start.11) | collective-permute-done | bytes 442400 | tf_op jit(solution)/shard_map/ppermute | solution.py:64
  100.0 8.6 %collective-permute-done.9 = f32[864,1,128]{2,0,1:T(8,128)S(1)} collective-permute-done((f32[864,1,128]{2,0,1:T(8,128)S(1)}, f32[864,1,128]{2,0,1:T(8,128)S(1)}, u32[]{:S(2)}, u32[]{:S(2)}) %collective-permute-start.9) | collective-permute-done | bytes 442400 | tf_op jit(solution)/shard_map/ppermute | solution.py:57
  108.6 0.3 maximum_subtract_fusion.1
  108.9 0.3 minimum_maximum_fusion.2
  109.3 1.1 fusion.12
  110.3 0.2 fusion.59
  110.5 1.9 %fusion.8 = f32[864,4,131]{2,0,1:T(8,128)S(1)} fusion(f32[864,4,128]{2,0,1:T(8,128)S(1)} %fusion.59), kind=kLoop, calls=%fused_computation.16 | loop fusion | flops 452736 | bytes 3580416 | tf_op jit(solution)/shard_map/sub | solution.py:93
  112.4 1.0 minimum_maximum_fusion
  113.4 2.6 %fusion.7 = f32[864,4,129]{2,0,1:T(8,128)S(1)} fusion(f32[864,4,128]{2,0,1:T(8,128)S(1)} %fusion.59, f32[864,4,130]{2,0,1:T(8,128)S(1)} %minimum_maximum_fusion, f32[864]{0:T(1024)S(1)} %get-tuple-element.48, f32[864]{0:T(1024)S(1)} %get-tuple-element.49, f32[864]{0:T(1024)S(1)} %broadcast_multiply_fusion, pred[864]{0:T(1024)(128)(4,1)S(1)} %broadcast_compare_fusion), kind=kLoop, calls=%fused_computation.15 | loop fusion | flops 2674944 | bytes 7130592 | tf_op jit(solution)/shard_map/mul | solution.py:101
  116.0 1.3 fusion.62
  117.3 0.1 collective-permute-start.12
  117.4 3.5 %collective-permute-start.13 = (f32[16,4,128]{2,1,0:T(4,128)S(1)}, f32[16,4,128]{2,1,0:T(4,128)S(1)}, u32[]{:S(2)}, u32[]{:S(2)}) collective-permute-start(f32[16,4,128]{2,1,0:T(4,128)S(1)} %copy.104), channel_id=1, source_target_pairs={{0,128},{16,144},{32,160},{48,176},{64,192},{80,208},{96,224},{112... | collective-permute-start | bytes 98312 | tf_op jit(solution)/shard_map/ppermute | solution.py:133
  120.9 1.2 collective-permute-start.14
  122.1 1.1 collective-permute-done.13
  123.2 2.9 %collective-permute-done.14 = f32[16,4,128]{2,1,0:T(4,128)S(1)} collective-permute-done((f32[16,4,128]{2,1,0:T(4,128)S(1)}, f32[16,4,128]{2,1,0:T(4,128)S(1)}, u32[]{:S(2)}, u32[]{:S(2)}) %collective-permute-start.14) | collective-permute-done | bytes 32800 | tf_op jit(solution)/shard_map/ppermute | solution.py:133
  126.1 0.1 collective-permute-start.16
  126.2 2.0 %collective-permute-start.17 = (f32[16,4,128]{2,1,0:T(4,128)S(1)}, f32[16,4,128]{2,1,0:T(4,128)S(1)}, u32[]{:S(2)}, u32[]{:S(2)}) collective-permute-start(f32[16,4,128]{2,1,0:T(4,128)S(1)} %add_add_fusion.1), channel_id=1, source_target_pairs={{0,48},{16,32},{32,16},{48,0},{64,112},{80,96},{96,80},{112,64},{1... | collective-permute-start | bytes 98312 | tf_op jit(solution)/shard_map/ppermute | solution.py:133
  128.2 1.5 %collective-permute-start.15 = (f32[16,4,128]{2,1,0:T(4,128)S(1)}, f32[16,4,128]{2,1,0:T(4,128)S(1)}, u32[]{:S(2)}, u32[]{:S(2)}) collective-permute-start(f32[16,4,128]{2,1,0:T(4,128)S(1)} %add_add_fusion.1), channel_id=1, source_target_pairs={{0,16},{16,0},{32,48},{48,32},{64,80},{80,64},{96,112},{112,96},{1... | collective-permute-start | bytes 98312 | tf_op jit(solution)/shard_map/ppermute | solution.py:133
  129.7 1.3 collective-permute-done.16
  131.0 1.0 collective-permute-done.17
  132.0 0.3 collective-permute-done.15
  132.4 0.6 fusion.144
  133.0 2.7 %fusion.57 = f32[864,4,128]{2,0,1:T(8,128)S(1)} fusion(f32[4,128]{1,0:T(4,128)S(1)} %get-tuple-element.32, f32[4,128]{1,0:T(4,128)S(1)} %get-tuple-element.38, f32[4,128]{1,0:T(4,128)S(1)} %get-tuple-element.31, f32[4,128]{1,0:T(4,128)S(1)} %get-tuple-element.23, f32[4,128]{1,0:T(4,128)S(1)} %get-tuple-element.22, f32[4,128]{1,0:T(4,128)S(1)} %get-tuple-element.39, ...), kind=kLoop, calls=%fused_computation.91 | loop fusion | flops 13713408 | bytes 7120768 | tf_op jit(solution)/shard_map/jit(_where)/select_n | solution.py:259
  135.7 2.3 %copy.107 = f32[864,4,128]{2,1,0:T(4,128)} copy(f32[864,4,128]{2,0,1:T(8,128)S(1)} %fusion.57) | data formatting | bytes 3538944
  (34 shorter events, 0.5 us)
Async XLA Ops:
  0.6 1.6 %copy-start.2 = (s32[16]{0:T(128)S(1)}, s32[16]{0:T(128)}, u32[]{:S(2)}) copy-start(s32[16]{0:T(128)} %constant.97.clone) | copy-start | bytes 196
  2.2 16.6 %copy-start.1 = (s32[4,128]{1,0:T(4,128)S(1)}, s32[4,128]{1,0:T(4,128)}, u32[]{:S(2)}) copy-start(s32[4,128]{1,0:T(4,128)} %param.5) | copy-start | bytes 6148
  4.6 15.1 %collective-permute-start = (f32[864,1,128]{2,0,1:T(8,128)}, f32[864,1,128]{2,0,1:T(8,128)S(1)}, u32[]{:S(2)}, u32[]{:S(2)}) collective-permute-start(f32[864,1,128]{2,0,1:T(8,128)} %get-tuple-element.19), channel_id=1, source_target_pairs={{0,1},{1,2},{2,3},{3,4},{4,5},{5,6},{6,7},{7,8},{8,9},{9,10},{10,1... | collective-permute-start | bytes 1327112 | tf_op jit(solution)/shard_map/ppermute | solution.py:57
  6.5 18.5 %collective-permute-start.1 = (f32[864,1,128]{2,0,1:T(8,128)}, f32[864,1,128]{2,0,1:T(8,128)S(1)}, u32[]{:S(2)}, u32[]{:S(2)}) collective-permute-start(f32[864,1,128]{2,0,1:T(8,128)} %get-tuple-element.20), channel_id=1, source_target_pairs={{1,0},{2,1},{3,2},{4,3},{5,4},{6,5},{7,6},{8,7},{9,8},{10,9},{11,1... | collective-permute-start | bytes 1327112 | tf_op jit(solution)/shard_map/ppermute | solution.py:58
  15.3 15.5 %collective-permute-start.2 = (f32[864,1,128]{2,0,1:T(8,128)}, f32[864,1,128]{2,0,1:T(8,128)S(1)}, u32[]{:S(2)}, u32[]{:S(2)}) collective-permute-start(f32[864,1,128]{2,0,1:T(8,128)} %get-tuple-element.21), channel_id=1, source_target_pairs={{1,0},{2,1},{3,2},{4,3},{5,4},{6,5},{7,6},{8,7},{9,8},{10,9},{11,1... | collective-permute-start | bytes 1327112 | tf_op jit(solution)/shard_map/ppermute | solution.py:64
  31.5 1.5 %copy-start = (f32[864,4,128]{2,1,0:T(4,128)S(1)}, f32[864,4,128]{2,1,0:T(4,128)}, u32[]{:S(2)}) copy-start(f32[864,4,128]{2,1,0:T(4,128)} %param.4) | copy-start | bytes 5308420
  40.0 19.9 %collective-permute-start.3 = (f32[16,4,128]{2,1,0:T(4,128)S(1)}, f32[16,4,128]{2,1,0:T(4,128)S(1)}, u32[]{:S(2)}, u32[]{:S(2)}) collective-permute-start(f32[16,4,128]{2,1,0:T(4,128)S(1)} %copy.100), channel_id=1, source_target_pairs={{0,64},{16,80},{32,96},{48,112},{64,0},{80,16},{96,32},{112,48},{1... | collective-permute-start | bytes 98312 | tf_op jit(solution)/shard_map/ppermute | solution.py:133
  41.6 20.4 %collective-permute-start.4 = (f32[16,4,128]{2,1,0:T(4,128)S(1)}, f32[16,4,128]{2,1,0:T(4,128)S(1)}, u32[]{:S(2)}, u32[]{:S(2)}) collective-permute-start(f32[16,4,128]{2,1,0:T(4,128)S(1)} %copy.100), channel_id=1, source_target_pairs={{0,128},{16,144},{32,160},{48,176},{64,192},{80,208},{96,224},{112... | collective-permute-start | bytes 98312 | tf_op jit(solution)/shard_map/ppermute | solution.py:133
  59.8 5.1 %collective-permute-start.5 = (f32[16,4,128]{2,1,0:T(4,128)S(1)}, f32[16,4,128]{2,1,0:T(4,128)S(1)}, u32[]{:S(2)}, u32[]{:S(2)}) collective-permute-start(f32[16,4,128]{2,1,0:T(4,128)S(1)} %copy.100), channel_id=1, source_target_pairs={{0,192},{16,208},{32,224},{48,240},{64,128},{80,144},{96,160},{112... | collective-permute-start | bytes 98312 | tf_op jit(solution)/shard_map/ppermute | solution.py:133
  65.0 4.9 %collective-permute-start.7 = (f32[16,4,128]{2,1,0:T(4,128)S(1)}, f32[16,4,128]{2,1,0:T(4,128)S(1)}, u32[]{:S(2)}, u32[]{:S(2)}) collective-permute-start(f32[16,4,128]{2,1,0:T(4,128)S(1)} %add_add_fusion.3), channel_id=1, source_target_pairs={{0,32},{16,48},{32,0},{48,16},{64,96},{80,112},{96,64},{112,80},{1... | collective-permute-start | bytes 98312 | tf_op jit(solution)/shard_map/ppermute | solution.py:133
  65.1 5.9 %collective-permute-start.8 = (f32[16,4,128]{2,1,0:T(4,128)S(1)}, f32[16,4,128]{2,1,0:T(4,128)S(1)}, u32[]{:S(2)}, u32[]{:S(2)}) collective-permute-start(f32[16,4,128]{2,1,0:T(4,128)S(1)} %add_add_fusion.3), channel_id=1, source_target_pairs={{0,48},{16,32},{32,16},{48,0},{64,112},{80,96},{96,80},{112,64},{1... | collective-permute-start | bytes 98312 | tf_op jit(solution)/shard_map/ppermute | solution.py:133
  66.8 4.3 %collective-permute-start.6 = (f32[16,4,128]{2,1,0:T(4,128)S(1)}, f32[16,4,128]{2,1,0:T(4,128)S(1)}, u32[]{:S(2)}, u32[]{:S(2)}) collective-permute-start(f32[16,4,128]{2,1,0:T(4,128)S(1)} %add_add_fusion.3), channel_id=1, source_target_pairs={{0,16},{16,0},{32,48},{48,32},{64,80},{80,64},{96,112},{112,96},{1... | collective-permute-start | bytes 98312 | tf_op jit(solution)/shard_map/ppermute | solution.py:133
  73.9 10.7 %collective-permute-start.10 = (f32[864,1,128]{2,0,1:T(8,128)S(1)}, f32[864,1,128]{2,0,1:T(8,128)S(1)}, u32[]{:S(2)}, u32[]{:S(2)}) collective-permute-start(f32[864,1,128]{2,0,1:T(8,128)S(1)} %get-tuple-element.18), channel_id=1, source_target_pairs={{1,0},{2,1},{3,2},{4,3},{5,4},{6,5},{7,6},{8,7},{9,8},{10,9},{11,1... | collective-permute-start | bytes 1327112 | tf_op jit(solution)/shard_map/ppermute | solution.py:58
  75.8 24.1 %collective-permute-start.11 = (f32[864,1,128]{2,0,1:T(8,128)S(1)}, f32[864,1,128]{2,0,1:T(8,128)S(1)}, u32[]{:S(2)}, u32[]{:S(2)}) collective-permute-start(f32[864,1,128]{2,0,1:T(8,128)S(1)} %get-tuple-element.17), channel_id=1, source_target_pairs={{1,0},{2,1},{3,2},{4,3},{5,4},{6,5},{7,6},{8,7},{9,8},{10,9},{11,1... | collective-permute-start | bytes 1327112 | tf_op jit(solution)/shard_map/ppermute | solution.py:64
  82.5 26.1 %collective-permute-start.9 = (f32[864,1,128]{2,0,1:T(8,128)S(1)}, f32[864,1,128]{2,0,1:T(8,128)S(1)}, u32[]{:S(2)}, u32[]{:S(2)}) collective-permute-start(f32[864,1,128]{2,0,1:T(8,128)S(1)} %get-tuple-element.16), channel_id=1, source_target_pairs={{0,1},{1,2},{2,3},{3,4},{4,5},{5,6},{6,7},{7,8},{8,9},{9,10},{10,1... | collective-permute-start | bytes 1327112 | tf_op jit(solution)/shard_map/ppermute | solution.py:57
  117.3 4.8 %collective-permute-start.12 = (f32[16,4,128]{2,1,0:T(4,128)S(1)}, f32[16,4,128]{2,1,0:T(4,128)S(1)}, u32[]{:S(2)}, u32[]{:S(2)}) collective-permute-start(f32[16,4,128]{2,1,0:T(4,128)S(1)} %copy.104), channel_id=1, source_target_pairs={{0,64},{16,80},{32,96},{48,112},{64,0},{80,16},{96,32},{112,48},{1... | collective-permute-start | bytes 98312 | tf_op jit(solution)/shard_map/ppermute | solution.py:133
  117.4 5.8 %collective-permute-start.13 = (f32[16,4,128]{2,1,0:T(4,128)S(1)}, f32[16,4,128]{2,1,0:T(4,128)S(1)}, u32[]{:S(2)}, u32[]{:S(2)}) collective-permute-start(f32[16,4,128]{2,1,0:T(4,128)S(1)} %copy.104), channel_id=1, source_target_pairs={{0,128},{16,144},{32,160},{48,176},{64,192},{80,208},{96,224},{112... | collective-permute-start | bytes 98312 | tf_op jit(solution)/shard_map/ppermute | solution.py:133
  120.9 5.1 %collective-permute-start.14 = (f32[16,4,128]{2,1,0:T(4,128)S(1)}, f32[16,4,128]{2,1,0:T(4,128)S(1)}, u32[]{:S(2)}, u32[]{:S(2)}) collective-permute-start(f32[16,4,128]{2,1,0:T(4,128)S(1)} %copy.104), channel_id=1, source_target_pairs={{0,192},{16,208},{32,224},{48,240},{64,128},{80,144},{96,160},{112... | collective-permute-start | bytes 98312 | tf_op jit(solution)/shard_map/ppermute | solution.py:133
  126.1 4.9 %collective-permute-start.16 = (f32[16,4,128]{2,1,0:T(4,128)S(1)}, f32[16,4,128]{2,1,0:T(4,128)S(1)}, u32[]{:S(2)}, u32[]{:S(2)}) collective-permute-start(f32[16,4,128]{2,1,0:T(4,128)S(1)} %add_add_fusion.1), channel_id=1, source_target_pairs={{0,32},{16,48},{32,0},{48,16},{64,96},{80,112},{96,64},{112,80},{1... | collective-permute-start | bytes 98312 | tf_op jit(solution)/shard_map/ppermute | solution.py:133
  126.2 5.8 %collective-permute-start.17 = (f32[16,4,128]{2,1,0:T(4,128)S(1)}, f32[16,4,128]{2,1,0:T(4,128)S(1)}, u32[]{:S(2)}, u32[]{:S(2)}) collective-permute-start(f32[16,4,128]{2,1,0:T(4,128)S(1)} %add_add_fusion.1), channel_id=1, source_target_pairs={{0,48},{16,32},{32,16},{48,0},{64,112},{80,96},{96,80},{112,64},{1... | collective-permute-start | bytes 98312 | tf_op jit(solution)/shard_map/ppermute | solution.py:133
  128.2 4.1 %collective-permute-start.15 = (f32[16,4,128]{2,1,0:T(4,128)S(1)}, f32[16,4,128]{2,1,0:T(4,128)S(1)}, u32[]{:S(2)}, u32[]{:S(2)}) collective-permute-start(f32[16,4,128]{2,1,0:T(4,128)S(1)} %add_add_fusion.1), channel_id=1, source_target_pairs={{0,16},{16,0},{32,48},{48,32},{64,80},{80,64},{96,112},{112,96},{1... | collective-permute-start | bytes 98312 | tf_op jit(solution)/shard_map/ppermute | solution.py:133

commit v8 on v7

--- a/solution.py
+++ b/solution.py
@@ -1,9 +1,12 @@
 import math
+import os
 
 import jax
 import numpy as np
 import jax.numpy as jnp
 from jax import lax
+from jax.experimental import pallas as pl
+from jax.experimental.pallas import tpu as pltpu
 from jax.sharding import PartitionSpec as P
 
 NVX = 24
@@ -104,10 +107,58 @@
     )
 
 
+def face_flux(number, lower, upper, lower_slope, upper_slope):
+    return number * jnp.where(
+        number > 0,
+        lower + 0.5 * (1.0 - number) * lower_slope,
+        upper - 0.5 * (1.0 + number) * upper_slope,
+    )
+
+
+def lane_sweep_kernel(number_ref, swept_ref, out_ref):
+    rows, block, width = swept_ref.shape
+    lane = lax.broadcasted_iota(jnp.int32, (8, width), 1)
+    first = lane == 0
+    last = lane == width - 1
+
+    def slab(i, carry):
+        part = pl.ds(pl.multiple_of(i * 8, 8), 8)
+        number = jnp.broadcast_to(number_ref[part, :], (8, width))
+        for k in range(rows):
+            values = swept_ref[k, part, :]
+            before = jnp.where(first, 0.0, pltpu.roll(values, 1, 1))
+            after = jnp.where(last, 0.0, pltpu.roll(values, width - 1, 1))
+            slope = minmod(values - before, after - values)
+            slope_before = jnp.where(first, 0.0, pltpu.roll(slope, 1, 1))
+            slope_after = jnp.where(last, 0.0, pltpu.roll(slope, width - 1, 1))
+            flux_after = face_flux(number, values, after, slope, slope_after)
+            flux_before = face_flux(number, before, values, slope_before, slope)
+            out_ref[k, part, :] = values - (flux_after - flux_before)
+        return carry
+
+    lax.fori_loop(0, block // 8, slab, 0)
+
+
 def transport(padded, along_x_part, along_y_part):
     swept = sweep(padded, courant * along_x_part[:, None, None], 1)
-    widened = jnp.pad(swept, ((0, 0), (0, 0), (2, 2)))
-    return sweep(widened, courant * along_y_part[:, None, None], 2)
+    amount, rows, width = swept.shape
+    if amount % 8 or width % 128:
+        widened = jnp.pad(swept, ((0, 0), (0, 0), (2, 2)))
+        return sweep(widened, courant * along_y_part[:, None, None], 2)
+    block = 96 if amount % 96 == 0 else 8
+    stacked = jnp.transpose(swept, (1, 0, 2))
+    shifted = pl.pallas_call(
+        lane_sweep_kernel,
+        grid=(amount // block,),
+        in_specs=[
+            pl.BlockSpec((block, 1), lambda i: (i, 0)),
+            pl.BlockSpec((rows, block, width), lambda i: (0, i, 0)),
+        ],
+        out_specs=pl.BlockSpec((rows, block, width), lambda i: (0, i, 0)),
+        out_shape=jax.ShapeDtypeStruct((rows, amount, width), swept.dtype),
+        interpret=os.environ.get("SOLUTION_INTERPRET") == "1",
+    )((courant * along_y_part)[:, None], stacked)
+    return jnp.transpose(shifted, (1, 0, 2))
 
 
 def xor_tree(values):

time: 138 us -> 180 us (1.30)
  Pallas kernels: 0 us -> 38.2 us
  starting transfers between devices: 55.8 us -> 61.5 us
  waiting for transfers between devices: 50.2 us -> 45.3 us
  matrix products: 2.58 us -> 5.13 us
    pallas_call x0 -> x2, Pallas kernels: none -> 38.2 us  [transport(): pl.pallas_call(lane_sweep_kernel, grid=(amount // block,), in_specs=[pl.B...]
    ppermute x2, waiting for transfers between devices: 21.2 us -> 5.86 us  [with_upwind_halo(): lax.ppermute(jnp.where(positive, block[:, rows - 2:rows - 1], block[:, 1:...]
    ppermute x2, waiting for transfers between devices: 9.51 us -> 19.2 us  [with_upwind_halo(): low = lax.ppermute(block[:, rows - 1:], 'space', forward)]
    transpose x0 -> x2, other arithmetic: none -> 5.58 us  [transport(): stacked = jnp.transpose(swept, (1, 0, 2))]
    mul x4 -> x2, other arithmetic: 7.28 us -> 2.15 us  [sweep(): flux = number * jnp.where(number > 0, left_face, right_face)]
    ppermute x12, starting transfers between devices: 31.8 us -> 35.7 us  [vel_sum(): lax.ppermute(local, 'vel', [(i, i ^ mask) for i in range(count)])]
    select_n x2, other arithmetic: 5.35 us -> 8.55 us  [approach_increment(): jnp.where(kind_labels == 1, wall_distribution, jnp.where(kind_labels == 2...]
    sub x4 -> x2, other arithmetic: 4.35 us -> 1.72 us  [sweep(): piece(distribution_table, 1, length)]
  transfers between devices with their start and end apart: 18 -> 18, of which waited for: 15 -> 14; matrix products, arithmetic and copies ran while one was open for 1% -> 1% of each run, Pallas kernels for 0% -> 0%
where the time goes in v8:
time: 180 us; the launch traced here: 179 us
  starting transfers between devices  61.5 us (34%)
  waiting for transfers between devices  45.3 us (25%)
  Pallas kernels  38.2 us (21%)
  other arithmetic  22.2 us (12%)
  local copies, waits for them, and re-layouts  5.29 us (3%)
  matrix products  5.13 us (3%)
    pallas_call x2, Pallas kernels, transport(): pl.pallas_call(lane_sweep_kernel, grid=(amount // block,), in_specs=[pl.B...  38.2 us
    ppermute x12, starting transfers between devices, vel_sum(): lax.ppermute(local, 'vel', [(i, i ^ mask) for i in range(count)])  35.7 us
    ppermute x2, waiting for transfers between devices, with_upwind_halo(): low = lax.ppermute(block[:, rows - 1:], 'space', forward)  19.2 us
    ppermute x12, waiting for transfers between devices, vel_sum(): lax.ppermute(local, 'vel', [(i, i ^ mask) for i in range(count)])  15 us
    ppermute x2, starting transfers between devices, with_upwind_halo(): lax.ppermute(jnp.where(positive, block[:, rows - 2:rows - 1], block[:, 1:...  11 us
    ppermute x2, starting transfers between devices, with_upwind_halo(): high = lax.ppermute(block[:, :1], 'space', backward)  10.9 us
    select_n x2, other arithmetic, approach_increment(): jnp.where(kind_labels == 1, wall_distribution, jnp.where(kind_labels == 2...  8.55 us
    ppermute x2, waiting for transfers between devices, with_upwind_halo(): lax.ppermute(jnp.where(positive, block[:, rows - 2:rows - 1], block[:, 1:...  5.86 us
  transfers between devices with their start and end apart: 18, of which 14 were waited for; matrix products, arithmetic and copies ran while one was open for 1% of the time, Pallas kernels for 0%

profile of v8, /device:TPU:6, one launch (start us, length us, event | category | flops | bytes accessed | tf_op | source)
XLA Modules:
  0.0 179.2 jit_solution(8175666763331124320)
XLA Ops:
  0.6 0.0 copy-start.4
  0.6 1.6 copy.63
  2.3 0.6 dynamic_slice.6
  3.5 1.1 fusion.152
  4.6 1.9 %collective-permute-start = (f32[864,1,128]{2,0,1:T(8,128)}, f32[864,1,128]{2,0,1:T(8,128)S(1)}, u32[]{:S(2)}, u32[]{:S(2)}) collective-permute-start(f32[864,1,128]{2,0,1:T(8,128)} %get-tuple-element.19), channel_id=1, source_target_pairs={{0,1},{1,2},{2,3},{3,4},{4,5},{5,6},{6,7},{7,8},{8,9},{9,10},{10,1... | collective-permute-start | bytes 1327112 | tf_op jit(solution)/shard_map/ppermute | solution.py:60
  6.5 8.8 %collective-permute-start.1 = (f32[864,1,128]{2,0,1:T(8,128)}, f32[864,1,128]{2,0,1:T(8,128)S(1)}, u32[]{:S(2)}, u32[]{:S(2)}) collective-permute-start(f32[864,1,128]{2,0,1:T(8,128)} %get-tuple-element.20), channel_id=1, source_target_pairs={{1,0},{2,1},{3,2},{4,3},{5,4},{6,5},{7,6},{8,7},{9,8},{10,9},{11,1... | collective-permute-start | bytes 1327112 | tf_op jit(solution)/shard_map/ppermute | solution.py:61
  15.3 2.6 %collective-permute-start.2 = (f32[864,1,128]{2,0,1:T(8,128)}, f32[864,1,128]{2,0,1:T(8,128)}, u32[]{:S(2)}, u32[]{:S(2)}) collective-permute-start(f32[864,1,128]{2,0,1:T(8,128)} %get-tuple-element.21), channel_id=1, source_target_pairs={{1,0},{2,1},{3,2},{4,3},{5,4},{6,5},{7,6},{8,7},{9,8},{10,9},{11,1... | collective-permute-start | bytes 1327112 | tf_op jit(solution)/shard_map/ppermute | solution.py:67
  18.0 0.1 fusion.150
  18.0 0.1 fusion.84
  18.1 0.1 fusion.142
  18.2 0.1 fusion.144
  18.3 0.1 fusion.146
  18.4 0.1 fusion.148
  18.4 0.1 add_add_fusion.4
  18.5 0.1 fusion.78
  18.6 0.2 copy.54
  18.9 0.1 stack.2
  19.0 0.8 broadcast_multiply_fusion.number_ref
  19.8 5.2 %collective-permute-done.1 = f32[864,1,128]{2,0,1:T(8,128)S(1)} collective-permute-done((f32[864,1,128]{2,0,1:T(8,128)}, f32[864,1,128]{2,0,1:T(8,128)S(1)}, u32[]{:S(2)}, u32[]{:S(2)}) %collective-permute-start.1) | collective-permute-done | bytes 442400 | tf_op jit(solution)/shard_map/ppermute | solution.py:61
  25.0 5.9 %collective-permute-done.2 = f32[864,1,128]{2,0,1:T(8,128)} collective-permute-done((f32[864,1,128]{2,0,1:T(8,128)}, f32[864,1,128]{2,0,1:T(8,128)}, u32[]{:S(2)}, u32[]{:S(2)}) %collective-permute-start.2) | collective-permute-done | bytes 442400 | tf_op jit(solution)/shard_map/ppermute | solution.py:67
  30.9 1.4 maximum_subtract_fusion
  32.3 0.3 minimum_maximum_fusion.1
  32.7 0.0 copy-start.2
  32.7 1.1 fusion.6
  33.7 0.4 copy-done.2
  34.1 1.4 fusion.51.swept_ref
  35.6 19.1 %shard_map.59 = f32[4,864,128]{2,1,0:T(8,128)} custom-call(f32[864,1]{1,0:T(8,128)} %broadcast_multiply_fusion.number_ref, f32[4,864,128]{2,1,0:T(8,128)} %fusion.51.swept_ref), custom_call_target="tpu_custom_call" | custom-call | tf_op jit(solution)/shard_map/pallas_call | solution.py:150
  54.6 2.6 %fusion.54 = f32[16,4,128]{2,0,1:T(8,128)S(1)} fusion(f32[4,864,128]{2,1,0:T(8,128)} %shard_map.59, f32[16,864]{1,0:T(8,128)S(1)} %stack.2), kind=kOutput, calls=%fused_computation.76 | convolution fusion | flops 84948480 | bytes 1857536 | tf_op jit(solution)/shard_map/kv,vrc->krc/dot_general | solution.py:214
  57.2 18.7 %collective-permute-start.4 = (f32[16,4,128]{2,1,0:T(4,128)S(1)}, f32[16,4,128]{2,1,0:T(4,128)S(1)}, u32[]{:S(2)}, u32[]{:S(2)}) collective-permute-start(f32[16,4,128]{2,1,0:T(4,128)S(1)} %copy.65), channel_id=1, source_target_pairs={{0,128},{16,144},{32,160},{48,176},{64,192},{80,208},{96,224},{112... | collective-permute-start | bytes 98312 | tf_op jit(solution)/shard_map/ppermute | solution.py:184
  75.9 0.7 collective-permute-start.3
  76.6 1.2 collective-permute-done.4
  77.8 2.0 %collective-permute-done.3 = f32[16,4,128]{2,1,0:T(4,128)S(1)} collective-permute-done((f32[16,4,128]{2,1,0:T(4,128)S(1)}, f32[16,4,128]{2,1,0:T(4,128)S(1)}, u32[]{:S(2)}, u32[]{:S(2)}) %collective-permute-start.3) | collective-permute-done | bytes 32800 | tf_op jit(solution)/shard_map/ppermute | solution.py:184
  79.8 1.9 %collective-permute-done.5 = f32[16,4,128]{2,1,0:T(4,128)S(1)} collective-permute-done((f32[16,4,128]{2,1,0:T(4,128)S(1)}, f32[16,4,128]{2,1,0:T(4,128)S(1)}, u32[]{:S(2)}, u32[]{:S(2)}) %collective-permute-start.5) | collective-permute-done | bytes 32800 | tf_op jit(solution)/shard_map/ppermute | solution.py:184
  81.7 0.1 collective-permute-start.8
  81.8 0.8 collective-permute-start.7
  82.6 3.6 %collective-permute-start.6 = (f32[16,4,128]{2,1,0:T(4,128)S(1)}, f32[16,4,128]{2,1,0:T(4,128)S(1)}, u32[]{:S(2)}, u32[]{:S(2)}) collective-permute-start(f32[16,4,128]{2,1,0:T(4,128)S(1)} %add_add_fusion.3), channel_id=1, source_target_pairs={{0,16},{16,0},{32,48},{48,32},{64,80},{80,64},{96,112},{112,96},{1... | collective-permute-start | bytes 98312 | tf_op jit(solution)/shard_map/ppermute | solution.py:184
  86.2 1.3 collective-permute-done.8
  87.5 0.6 collective-permute-done.6
  88.2 4.3 %fusion.27 = f32[864,4,128]{2,0,1:T(8,128)S(1)} fusion(f32[4,864,128]{2,1,0:T(8,128)S(1)} %copy-done, f32[4,128]{1,0:T(4,128)S(1)} %get-tuple-element.29, f32[4,128]{1,0:T(4,128)S(1)} %get-tuple-element.42, f32[4,128]{1,0:T(4,128)S(1)} %fusion.114, f32[4,128]{1,0:T(4,128)S(1)} %get-tuple-element.36, f32[4,128]{1,0:T(4,128)S(1)} %get-tuple-element.37, ...), kind=kLoop, calls=%fused_computation.47 | loop fusion | flops 12828672 | bytes 3581824 | tf_op jit(solution)/shard_map/jit(_where)/select_n | solution.py:310
  92.5 0.1 fusion.151
  92.6 1.9 %collective-permute-start.9 = (f32[864,1,128]{2,0,1:T(8,128)S(1)}, f32[864,1,128]{2,0,1:T(8,128)S(1)}, u32[]{:S(2)}, u32[]{:S(2)}) collective-permute-start(f32[864,1,128]{2,0,1:T(8,128)S(1)} %get-tuple-element.16), channel_id=1, source_target_pairs={{0,1},{1,2},{2,3},{3,4},{4,5},{5,6},{6,7},{7,8},{8,9},{9,10},{10,1... | collective-permute-start | bytes 1327112 | tf_op jit(solution)/shard_map/ppermute | solution.py:60
  94.5 8.4 %collective-permute-start.11 = (f32[864,1,128]{2,0,1:T(8,128)S(1)}, f32[864,1,128]{2,0,1:T(8,128)S(1)}, u32[]{:S(2)}, u32[]{:S(2)}) collective-permute-start(f32[864,1,128]{2,0,1:T(8,128)S(1)} %get-tuple-element.17), channel_id=1, source_target_pairs={{1,0},{2,1},{3,2},{4,3},{5,4},{6,5},{7,6},{8,7},{9,8},{10,9},{11,1... | collective-permute-start | bytes 1327112 | tf_op jit(solution)/shard_map/ppermute | solution.py:67
  103.0 2.1 %collective-permute-start.10 = (f32[864,1,128]{2,0,1:T(8,128)S(1)}, f32[864,1,128]{2,0,1:T(8,128)S(1)}, u32[]{:S(2)}, u32[]{:S(2)}) collective-permute-start(f32[864,1,128]{2,0,1:T(8,128)S(1)} %get-tuple-element.18), channel_id=1, source_target_pairs={{1,0},{2,1},{3,2},{4,3},{5,4},{6,5},{7,6},{8,7},{9,8},{10,9},{11,1... | collective-permute-start | bytes 1327112 | tf_op jit(solution)/shard_map/ppermute | solution.py:61
  105.1 19.2 %collective-permute-done.9 = f32[864,1,128]{2,0,1:T(8,128)S(1)} collective-permute-done((f32[864,1,128]{2,0,1:T(8,128)S(1)}, f32[864,1,128]{2,0,1:T(8,128)S(1)}, u32[]{:S(2)}, u32[]{:S(2)}) %collective-permute-start.9) | collective-permute-done | bytes 442400 | tf_op jit(solution)/shard_map/ppermute | solution.py:60
  124.3 0.3 maximum_subtract_fusion.1
  124.6 0.3 minimum_maximum_fusion
  125.0 1.1 fusion.2
  126.0 4.2 %fusion.49.swept_ref = f32[4,864,128]{2,1,0:T(8,128)} fusion(f32[864,5,128]{2,0,1:T(8,128)S(1)} %fusion.2, f32[4,128]{1,0:T(4,128)S(1)} %get-tuple-element.29, f32[4,128]{1,0:T(4,128)S(1)} %get-tuple-element.42, f32[4,128]{1,0:T(4,128)S(1)} %fusion.114, f32[4,128]{1,0:T(4,128)S(1)} %get-tuple-element.36, f32[4,128]{1,0:T(4,128)S(1)} %get-tuple-element.37, ...), kind=kLoop, calls=%fused_computation.70 | loop fusion | flops 13713408 | bytes 7120768 | tf_op jit(solution)/shard_map/transpose | solution.py:149
  130.2 19.1 %shard_map.60 = f32[4,864,128]{2,1,0:T(8,128)} custom-call(f32[864,1]{1,0:T(8,128)} %broadcast_multiply_fusion.number_ref, f32[4,864,128]{2,1,0:T(8,128)} %fusion.49.swept_ref), custom_call_target="tpu_custom_call" | custom-call | tf_op jit(solution)/shard_map/pallas_call | solution.py:150
  149.3 2.6 %fusion.52 = f32[16,4,128]{2,0,1:T(8,128)S(1)} fusion(f32[4,864,128]{2,1,0:T(8,128)} %shard_map.60, f32[16,864]{1,0:T(8,128)S(1)} %stack.2), kind=kOutput, calls=%fused_computation.74 | convolution fusion | flops 84948480 | bytes 1857536 | tf_op jit(solution)/shard_map/kv,vrc->krc/dot_general | solution.py:214
  151.9 6.8 %collective-permute-start.13 = (f32[16,4,128]{2,1,0:T(4,128)S(1)}, f32[16,4,128]{2,1,0:T(4,128)S(1)}, u32[]{:S(2)}, u32[]{:S(2)}) collective-permute-start(f32[16,4,128]{2,1,0:T(4,128)S(1)} %copy.69), channel_id=1, source_target_pairs={{0,128},{16,144},{32,160},{48,176},{64,192},{80,208},{96,224},{112... | collective-permute-start | bytes 98312 | tf_op jit(solution)/shard_map/ppermute | solution.py:184
  158.7 0.7 collective-permute-start.12
  159.3 1.2 collective-permute-done.13
  160.6 2.0 %collective-permute-done.12 = f32[16,4,128]{2,1,0:T(4,128)S(1)} collective-permute-done((f32[16,4,128]{2,1,0:T(4,128)S(1)}, f32[16,4,128]{2,1,0:T(4,128)S(1)}, u32[]{:S(2)}, u32[]{:S(2)}) %collective-permute-start.12) | collective-permute-done | bytes 32800 | tf_op jit(solution)/shard_map/ppermute | solution.py:184
  162.6 1.9 %collective-permute-done.14 = f32[16,4,128]{2,1,0:T(4,128)S(1)} collective-permute-done((f32[16,4,128]{2,1,0:T(4,128)S(1)}, f32[16,4,128]{2,1,0:T(4,128)S(1)}, u32[]{:S(2)}, u32[]{:S(2)}) %collective-permute-start.14) | collective-permute-done | bytes 32800 | tf_op jit(solution)/shard_map/ppermute | solution.py:184
  164.5 0.1 collective-permute-start.17
  164.6 3.4 %collective-permute-start.16 = (f32[16,4,128]{2,1,0:T(4,128)S(1)}, f32[16,4,128]{2,1,0:T(4,128)S(1)}, u32[]{:S(2)}, u32[]{:S(2)}) collective-permute-start(f32[16,4,128]{2,1,0:T(4,128)S(1)} %add_add_fusion.1), channel_id=1, source_target_pairs={{0,32},{16,48},{32,0},{48,16},{64,96},{80,112},{96,64},{112,80},{1... | collective-permute-start | bytes 98312 | tf_op jit(solution)/shard_map/ppermute | solution.py:184
  167.9 1.0 collective-permute-start.15
  168.9 1.4 collective-permute-done.17
  170.4 0.5 collective-permute-done.16
  170.9 1.0 collective-permute-done.15
  171.9 0.6 fusion.139
  172.5 4.3 %fusion.47 = f32[864,4,128]{2,0,1:T(8,128)S(1)} fusion(f32[4,864,128]{2,1,0:T(8,128)S(1)} %copy-done.1, f32[4,128]{1,0:T(4,128)S(1)} %get-tuple-element.32, f32[4,128]{1,0:T(4,128)S(1)} %get-tuple-element.38, f32[4,128]{1,0:T(4,128)S(1)} %get-tuple-element.31, f32[4,128]{1,0:T(4,128)S(1)} %get-tuple-element.23, f32[4,128]{1,0:T(4,128)S(1)} %get-tuple-element.22, ...), kind=kLoop, calls=%fused_computation.67 | loop fusion | flops 12828672 | bytes 3581824 | tf_op jit(solution)/shard_map/jit(_where)/select_n | solution.py:310
  176.8 2.3 %copy.72 = f32[864,4,128]{2,1,0:T(4,128)} copy(f32[864,4,128]{2,0,1:T(8,128)S(1)} %fusion.47) | data formatting | bytes 3538944
  (34 shorter events, 0.4 us)
Async XLA Ops:
  0.6 1.6 copy-start.4
  3.5 15.5 %copy-start.3 = (s32[4,128]{1,0:T(4,128)S(1)}, s32[4,128]{1,0:T(4,128)}, u32[]{:S(2)}) copy-start(s32[4,128]{1,0:T(4,128)} %param.5) | copy-start | bytes 6148
  4.6 15.2 %collective-permute-start = (f32[864,1,128]{2,0,1:T(8,128)}, f32[864,1,128]{2,0,1:T(8,128)S(1)}, u32[]{:S(2)}, u32[]{:S(2)}) collective-permute-start(f32[864,1,128]{2,0,1:T(8,128)} %get-tuple-element.19), channel_id=1, source_target_pairs={{0,1},{1,2},{2,3},{3,4},{4,5},{5,6},{6,7},{7,8},{8,9},{9,10},{10,1... | collective-permute-start | bytes 1327112 | tf_op jit(solution)/shard_map/ppermute | solution.py:60
  6.5 18.5 %collective-permute-start.1 = (f32[864,1,128]{2,0,1:T(8,128)}, f32[864,1,128]{2,0,1:T(8,128)S(1)}, u32[]{:S(2)}, u32[]{:S(2)}) collective-permute-start(f32[864,1,128]{2,0,1:T(8,128)} %get-tuple-element.20), channel_id=1, source_target_pairs={{1,0},{2,1},{3,2},{4,3},{5,4},{6,5},{7,6},{8,7},{9,8},{10,9},{11,1... | collective-permute-start | bytes 1327112 | tf_op jit(solution)/shard_map/ppermute | solution.py:61
  15.3 15.5 %collective-permute-start.2 = (f32[864,1,128]{2,0,1:T(8,128)}, f32[864,1,128]{2,0,1:T(8,128)}, u32[]{:S(2)}, u32[]{:S(2)}) collective-permute-start(f32[864,1,128]{2,0,1:T(8,128)} %get-tuple-element.21), channel_id=1, source_target_pairs={{1,0},{2,1},{3,2},{4,3},{5,4},{6,5},{7,6},{8,7},{9,8},{10,9},{11,1... | collective-permute-start | bytes 1327112 | tf_op jit(solution)/shard_map/ppermute | solution.py:67
  32.7 1.5 copy-start.2
  54.6 33.5 %copy-start = (f32[4,864,128]{2,1,0:T(8,128)S(1)}, f32[4,864,128]{2,1,0:T(8,128)}, u32[]{:S(2)}) copy-start(f32[4,864,128]{2,1,0:T(8,128)} %shard_map.59) | copy-start | bytes 5308420
  57.2 20.6 %collective-permute-start.4 = (f32[16,4,128]{2,1,0:T(4,128)S(1)}, f32[16,4,128]{2,1,0:T(4,128)S(1)}, u32[]{:S(2)}, u32[]{:S(2)}) collective-permute-start(f32[16,4,128]{2,1,0:T(4,128)S(1)} %copy.65), channel_id=1, source_target_pairs={{0,128},{16,144},{32,160},{48,176},{64,192},{80,208},{96,224},{112... | collective-permute-start | bytes 98312 | tf_op jit(solution)/shard_map/ppermute | solution.py:184
  75.9 3.9 %collective-permute-start.3 = (f32[16,4,128]{2,1,0:T(4,128)S(1)}, f32[16,4,128]{2,1,0:T(4,128)S(1)}, u32[]{:S(2)}, u32[]{:S(2)}) collective-permute-start(f32[16,4,128]{2,1,0:T(4,128)S(1)} %copy.65), channel_id=1, source_target_pairs={{0,64},{16,80},{32,96},{48,112},{64,0},{80,16},{96,32},{112,48},{1... | collective-permute-start | bytes 98312 | tf_op jit(solution)/shard_map/ppermute | solution.py:184
  76.6 5.1 %collective-permute-start.5 = (f32[16,4,128]{2,1,0:T(4,128)S(1)}, f32[16,4,128]{2,1,0:T(4,128)S(1)}, u32[]{:S(2)}, u32[]{:S(2)}) collective-permute-start(f32[16,4,128]{2,1,0:T(4,128)S(1)} %copy.65), channel_id=1, source_target_pairs={{0,192},{16,208},{32,224},{48,240},{64,128},{80,144},{96,160},{112... | collective-permute-start | bytes 98312 | tf_op jit(solution)/shard_map/ppermute | solution.py:184
  81.7 5.8 %collective-permute-start.8 = (f32[16,4,128]{2,1,0:T(4,128)S(1)}, f32[16,4,128]{2,1,0:T(4,128)S(1)}, u32[]{:S(2)}, u32[]{:S(2)}) collective-permute-start(f32[16,4,128]{2,1,0:T(4,128)S(1)} %add_add_fusion.3), channel_id=1, source_target_pairs={{0,48},{16,32},{32,16},{48,0},{64,112},{80,96},{96,80},{112,64},{1... | collective-permute-start | bytes 98312 | tf_op jit(solution)/shard_map/ppermute | solution.py:184
  81.8 5.7 %collective-permute-start.7 = (f32[16,4,128]{2,1,0:T(4,128)S(1)}, f32[16,4,128]{2,1,0:T(4,128)S(1)}, u32[]{:S(2)}, u32[]{:S(2)}) collective-permute-start(f32[16,4,128]{2,1,0:T(4,128)S(1)} %add_add_fusion.3), channel_id=1, source_target_pairs={{0,32},{16,48},{32,0},{48,16},{64,96},{80,112},{96,64},{112,80},{1... | collective-permute-start | bytes 98312 | tf_op jit(solution)/shard_map/ppermute | solution.py:184
  82.6 5.5 %collective-permute-start.6 = (f32[16,4,128]{2,1,0:T(4,128)S(1)}, f32[16,4,128]{2,1,0:T(4,128)S(1)}, u32[]{:S(2)}, u32[]{:S(2)}) collective-permute-start(f32[16,4,128]{2,1,0:T(4,128)S(1)} %add_add_fusion.3), channel_id=1, source_target_pairs={{0,16},{16,0},{32,48},{48,32},{64,80},{80,64},{96,112},{112,96},{1... | collective-permute-start | bytes 98312 | tf_op jit(solution)/shard_map/ppermute | solution.py:184
  92.6 31.7 %collective-permute-start.9 = (f32[864,1,128]{2,0,1:T(8,128)S(1)}, f32[864,1,128]{2,0,1:T(8,128)S(1)}, u32[]{:S(2)}, u32[]{:S(2)}) collective-permute-start(f32[864,1,128]{2,0,1:T(8,128)S(1)} %get-tuple-element.16), channel_id=1, source_target_pairs={{0,1},{1,2},{2,3},{3,4},{4,5},{5,6},{6,7},{7,8},{8,9},{9,10},{10,1... | collective-permute-start | bytes 1327112 | tf_op jit(solution)/shard_map/ppermute | solution.py:60
  94.5 29.8 %collective-permute-start.11 = (f32[864,1,128]{2,0,1:T(8,128)S(1)}, f32[864,1,128]{2,0,1:T(8,128)S(1)}, u32[]{:S(2)}, u32[]{:S(2)}) collective-permute-start(f32[864,1,128]{2,0,1:T(8,128)S(1)} %get-tuple-element.17), channel_id=1, source_target_pairs={{1,0},{2,1},{3,2},{4,3},{5,4},{6,5},{7,6},{8,7},{9,8},{10,9},{11,1... | collective-permute-start | bytes 1327112 | tf_op jit(solution)/shard_map/ppermute | solution.py:67
  103.0 21.4 %collective-permute-start.10 = (f32[864,1,128]{2,0,1:T(8,128)S(1)}, f32[864,1,128]{2,0,1:T(8,128)S(1)}, u32[]{:S(2)}, u32[]{:S(2)}) collective-permute-start(f32[864,1,128]{2,0,1:T(8,128)S(1)} %get-tuple-element.18), channel_id=1, source_target_pairs={{1,0},{2,1},{3,2},{4,3},{5,4},{6,5},{7,6},{8,7},{9,8},{10,9},{11,1... | collective-permute-start | bytes 1327112 | tf_op jit(solution)/shard_map/ppermute | solution.py:61
  149.3 23.2 %copy-start.1 = (f32[4,864,128]{2,1,0:T(8,128)S(1)}, f32[4,864,128]{2,1,0:T(8,128)}, u32[]{:S(2)}) copy-start(f32[4,864,128]{2,1,0:T(8,128)} %shard_map.60) | copy-start | bytes 5308420
  151.9 8.7 %collective-permute-start.13 = (f32[16,4,128]{2,1,0:T(4,128)S(1)}, f32[16,4,128]{2,1,0:T(4,128)S(1)}, u32[]{:S(2)}, u32[]{:S(2)}) collective-permute-start(f32[16,4,128]{2,1,0:T(4,128)S(1)} %copy.69), channel_id=1, source_target_pairs={{0,128},{16,144},{32,160},{48,176},{64,192},{80,208},{96,224},{112... | collective-permute-start | bytes 98312 | tf_op jit(solution)/shard_map/ppermute | solution.py:184
  158.7 3.9 %collective-permute-start.12 = (f32[16,4,128]{2,1,0:T(4,128)S(1)}, f32[16,4,128]{2,1,0:T(4,128)S(1)}, u32[]{:S(2)}, u32[]{:S(2)}) collective-permute-start(f32[16,4,128]{2,1,0:T(4,128)S(1)} %copy.69), channel_id=1, source_target_pairs={{0,64},{16,80},{32,96},{48,112},{64,0},{80,16},{96,32},{112,48},{1... | collective-permute-start | bytes 98312 | tf_op jit(solution)/shard_map/ppermute | solution.py:184
  159.3 5.1 %collective-permute-start.14 = (f32[16,4,128]{2,1,0:T(4,128)S(1)}, f32[16,4,128]{2,1,0:T(4,128)S(1)}, u32[]{:S(2)}, u32[]{:S(2)}) collective-permute-start(f32[16,4,128]{2,1,0:T(4,128)S(1)} %copy.69), channel_id=1, source_target_pairs={{0,192},{16,208},{32,224},{48,240},{64,128},{80,144},{96,160},{112... | collective-permute-start | bytes 98312 | tf_op jit(solution)/shard_map/ppermute | solution.py:184
  164.5 5.9 %collective-permute-start.17 = (f32[16,4,128]{2,1,0:T(4,128)S(1)}, f32[16,4,128]{2,1,0:T(4,128)S(1)}, u32[]{:S(2)}, u32[]{:S(2)}) collective-permute-start(f32[16,4,128]{2,1,0:T(4,128)S(1)} %add_add_fusion.1), channel_id=1, source_target_pairs={{0,48},{16,32},{32,16},{48,0},{64,112},{80,96},{96,80},{112,64},{1... | collective-permute-start | bytes 98312 | tf_op jit(solution)/shard_map/ppermute | solution.py:184
  164.6 6.3 %collective-permute-start.16 = (f32[16,4,128]{2,1,0:T(4,128)S(1)}, f32[16,4,128]{2,1,0:T(4,128)S(1)}, u32[]{:S(2)}, u32[]{:S(2)}) collective-permute-start(f32[16,4,128]{2,1,0:T(4,128)S(1)} %add_add_fusion.1), channel_id=1, source_target_pairs={{0,32},{16,48},{32,0},{48,16},{64,96},{80,112},{96,64},{112,80},{1... | collective-permute-start | bytes 98312 | tf_op jit(solution)/shard_map/ppermute | solution.py:184
  167.9 3.9 %collective-permute-start.15 = (f32[16,4,128]{2,1,0:T(4,128)S(1)}, f32[16,4,128]{2,1,0:T(4,128)S(1)}, u32[]{:S(2)}, u32[]{:S(2)}) collective-permute-start(f32[16,4,128]{2,1,0:T(4,128)S(1)} %add_add_fusion.1), channel_id=1, source_target_pairs={{0,16},{16,0},{32,48},{48,32},{64,80},{80,64},{96,112},{112,96},{1... | collective-permute-start | bytes 98312 | tf_op jit(solution)/shard_map/ppermute | solution.py:184

commit v9 on v7

--- a/solution.py
+++ b/solution.py
@@ -215,10 +215,13 @@
     rel_z = along_z_part[:, None, None] - average_drift_z[None]
     relative_magnitude_square = rel_x * rel_x + rel_y * rel_y + rel_z * rel_z
     stress_scalar_grid = particle_concentration * kelvin_level
+    inverse_level = 1.0 / kelvin_level
+    half_inverse_level = 1.0 / (2.0 * kelvin_level)
+    inverse_scale = 1.0 / (5.0 * stress_scalar_grid * kelvin_level)
     gaussian_local_balance = (
         particle_concentration
         * kelvin_level ** (-1.5)
-        * jnp.exp(-relative_magnitude_square / (2.0 * kelvin_level))
+        * jnp.exp(-relative_magnitude_square * half_inverse_level)
     )
     conductive_vector_slot = (
         rel_x * conductive_transfer[0]
@@ -229,8 +232,8 @@
         1.0
         + (1.0 - diffusivity_ratio)
         * conductive_vector_slot
-        * (relative_magnitude_square / kelvin_level - 5.0)
-        / (5.0 * stress_scalar_grid * kelvin_level)
+        * (relative_magnitude_square * inverse_level - 5.0)
+        * inverse_scale
     )
     approach_rate = (
         encounter_rate * particle_concentration * kelvin_level ** (1.0 - power_law_index)

time: 138 us -> 138 us (level)
  no operation moved by 1% of the time
where the time goes in v9:
time: 138 us
  starting transfers between devices  55.8 us (40%)
  waiting for transfers between devices  50.2 us (36%)
  other arithmetic  22.8 us (17%)
  local copies, waits for them, and re-layouts  5.09 us (4%)
  matrix products  2.58 us (2%)
  between operations  1.66 us (1%)
    ppermute x12, starting transfers between devices, vel_sum(): lax.ppermute(local, 'vel', [(i, i ^ mask) for i in range(count)])  31.8 us
    ppermute x2, waiting for transfers between devices, with_upwind_halo(): lax.ppermute(jnp.where(positive, block[:, rows - 2:rows - 1], block[:, 1:...  21.2 us
    ppermute x12, waiting for transfers between devices, vel_sum(): lax.ppermute(local, 'vel', [(i, i ^ mask) for i in range(count)])  14.2 us
    ppermute x2, starting transfers between devices, with_upwind_halo(): high = lax.ppermute(block[:, :1], 'space', backward)  10.7 us
    ppermute x2, waiting for transfers between devices, with_upwind_halo(): low = lax.ppermute(block[:, rows - 1:], 'space', forward)  9.51 us
    ppermute x2, starting transfers between devices, with_upwind_halo(): lax.ppermute(jnp.where(positive, block[:, rows - 2:rows - 1], block[:, 1:...  9.27 us
    mul x4, other arithmetic, sweep(): flux = number * jnp.where(number > 0, left_face, right_face)  7.28 us
    select_n x2, other arithmetic, approach_increment(): jnp.where(kind_labels == 1, wall_distribution, jnp.where(kind_labels == 2...  5.32 us
  transfers between devices with their start and end apart: 18, of which 15 were waited for; matrix products, arithmetic and copies ran while one was open for 1% of the time, Pallas kernels for 0%

profile of v9, /device:TPU:6, one launch (start us, length us, event | category | flops | bytes accessed | tf_op | source)
XLA Modules:
  0.0 138.0 jit_solution(4545363550964979180)
XLA Ops:
  0.6 1.6 %copy.98 = f32[864,4,128]{2,0,1:T(8,128)S(1)} copy(f32[864,4,128]{2,1,0:T(4,128)} %param.4) | data formatting | bytes 3538944 | tf_op args[0]
  2.3 0.6 dynamic_slice.6
  3.5 1.1 fusion.159
  4.6 1.9 %collective-permute-start = (f32[864,1,128]{2,0,1:T(8,128)}, f32[864,1,128]{2,0,1:T(8,128)S(1)}, u32[]{:S(2)}, u32[]{:S(2)}) collective-permute-start(f32[864,1,128]{2,0,1:T(8,128)} %get-tuple-element.19), channel_id=1, source_target_pairs={{0,1},{1,2},{2,3},{3,4},{4,5},{5,6},{6,7},{7,8},{8,9},{9,10},{10,1... | collective-permute-start | bytes 1327112 | tf_op jit(solution)/shard_map/ppermute | solution.py:57
  6.5 8.8 %collective-permute-start.1 = (f32[864,1,128]{2,0,1:T(8,128)}, f32[864,1,128]{2,0,1:T(8,128)S(1)}, u32[]{:S(2)}, u32[]{:S(2)}) collective-permute-start(f32[864,1,128]{2,0,1:T(8,128)} %get-tuple-element.20), channel_id=1, source_target_pairs={{1,0},{2,1},{3,2},{4,3},{5,4},{6,5},{7,6},{8,7},{9,8},{10,9},{11,1... | collective-permute-start | bytes 1327112 | tf_op jit(solution)/shard_map/ppermute | solution.py:58
  15.3 2.6 %collective-permute-start.2 = (f32[864,1,128]{2,0,1:T(8,128)}, f32[864,1,128]{2,0,1:T(8,128)S(1)}, u32[]{:S(2)}, u32[]{:S(2)}) collective-permute-start(f32[864,1,128]{2,0,1:T(8,128)} %get-tuple-element.21), channel_id=1, source_target_pairs={{1,0},{2,1},{3,2},{4,3},{5,4},{6,5},{7,6},{8,7},{9,8},{10,9},{11,1... | collective-permute-start | bytes 1327112 | tf_op jit(solution)/shard_map/ppermute | solution.py:64
  18.1 0.1 fusion.86
  18.1 0.1 add_add_fusion.4
  18.2 0.1 fusion.147
  18.3 0.1 fusion.149
  18.4 0.1 fusion.151
  18.5 0.1 fusion.153
  18.6 0.1 stack.2
  18.8 0.9 collective-permute-done
  19.7 5.3 %collective-permute-done.1 = f32[864,1,128]{2,0,1:T(8,128)S(1)} collective-permute-done((f32[864,1,128]{2,0,1:T(8,128)}, f32[864,1,128]{2,0,1:T(8,128)S(1)}, u32[]{:S(2)}, u32[]{:S(2)}) %collective-permute-start.1) | collective-permute-done | bytes 442400 | tf_op jit(solution)/shard_map/ppermute | solution.py:58
  25.0 5.9 %collective-permute-done.2 = f32[864,1,128]{2,0,1:T(8,128)S(1)} collective-permute-done((f32[864,1,128]{2,0,1:T(8,128)}, f32[864,1,128]{2,0,1:T(8,128)S(1)}, u32[]{:S(2)}, u32[]{:S(2)}) %collective-permute-start.2) | collective-permute-done | bytes 442400 | tf_op jit(solution)/shard_map/ppermute | solution.py:64
  30.9 0.3 maximum_subtract_fusion
  31.2 0.3 minimum_maximum_fusion.3
  31.5 1.1 fusion.16
  32.6 0.4 copy-done
  33.0 0.2 fusion.61
  33.2 1.9 %fusion.3 = f32[864,4,131]{2,0,1:T(8,128)S(1)} fusion(f32[864,4,128]{2,0,1:T(8,128)S(1)} %fusion.61), kind=kLoop, calls=%fused_computation.11 | loop fusion | flops 452736 | bytes 3580416 | tf_op jit(solution)/shard_map/sub | solution.py:93
  35.1 1.0 minimum_maximum_fusion.1
  36.1 2.6 %fusion.2 = f32[864,4,129]{2,0,1:T(8,128)S(1)} fusion(f32[864,4,128]{2,0,1:T(8,128)S(1)} %fusion.61, f32[864,4,130]{2,0,1:T(8,128)S(1)} %minimum_maximum_fusion.1, f32[864]{0:T(1024)S(1)} %get-tuple-element.48, f32[864]{0:T(1024)S(1)} %get-tuple-element.49, f32[864]{0:T(1024)S(1)} %broadcast_multiply_fusion, pred[864]{0:T(1024)(128)(4,1)S(1)} %broadcast_compare_fusion), kind=kLoop, calls=%fused_computation.10 | loop fusion | flops 2674944 | bytes 7130592 | tf_op jit(solution)/shard_map/mul | solution.py:101
  38.7 1.3 fusion.64
  40.0 1.7 %collective-permute-start.3 = (f32[16,4,128]{2,1,0:T(4,128)S(1)}, f32[16,4,128]{2,1,0:T(4,128)S(1)}, u32[]{:S(2)}, u32[]{:S(2)}) collective-permute-start(f32[16,4,128]{2,1,0:T(4,128)S(1)} %copy.100), channel_id=1, source_target_pairs={{0,64},{16,80},{32,96},{48,112},{64,0},{80,16},{96,32},{112,48},{1... | collective-permute-start | bytes 98312 | tf_op jit(solution)/shard_map/ppermute | solution.py:133
  41.6 18.2 %collective-permute-start.4 = (f32[16,4,128]{2,1,0:T(4,128)S(1)}, f32[16,4,128]{2,1,0:T(4,128)S(1)}, u32[]{:S(2)}, u32[]{:S(2)}) collective-permute-start(f32[16,4,128]{2,1,0:T(4,128)S(1)} %copy.100), channel_id=1, source_target_pairs={{0,128},{16,144},{32,160},{48,176},{64,192},{80,208},{96,224},{112... | collective-permute-start | bytes 98312 | tf_op jit(solution)/shard_map/ppermute | solution.py:133
  59.9 2.2 %collective-permute-done.4 = f32[16,4,128]{2,1,0:T(4,128)S(1)} collective-permute-done((f32[16,4,128]{2,1,0:T(4,128)S(1)}, f32[16,4,128]{2,1,0:T(4,128)S(1)}, u32[]{:S(2)}, u32[]{:S(2)}) %collective-permute-start.4) | collective-permute-done | bytes 32800 | tf_op jit(solution)/shard_map/ppermute | solution.py:133
  62.1 2.9 %collective-permute-done.5 = f32[16,4,128]{2,1,0:T(4,128)S(1)} collective-permute-done((f32[16,4,128]{2,1,0:T(4,128)S(1)}, f32[16,4,128]{2,1,0:T(4,128)S(1)}, u32[]{:S(2)}, u32[]{:S(2)}) %collective-permute-start.5) | collective-permute-done | bytes 32800 | tf_op jit(solution)/shard_map/ppermute | solution.py:133
  65.0 0.1 collective-permute-start.7
  65.1 1.7 %collective-permute-start.8 = (f32[16,4,128]{2,1,0:T(4,128)S(1)}, f32[16,4,128]{2,1,0:T(4,128)S(1)}, u32[]{:S(2)}, u32[]{:S(2)}) collective-permute-start(f32[16,4,128]{2,1,0:T(4,128)S(1)} %add_add_fusion.3), channel_id=1, source_target_pairs={{0,48},{16,32},{32,16},{48,0},{64,112},{80,96},{96,80},{112,64},{1... | collective-permute-start | bytes 98312 | tf_op jit(solution)/shard_map/ppermute | solution.py:133
  66.8 1.8 %collective-permute-start.6 = (f32[16,4,128]{2,1,0:T(4,128)S(1)}, f32[16,4,128]{2,1,0:T(4,128)S(1)}, u32[]{:S(2)}, u32[]{:S(2)}) collective-permute-start(f32[16,4,128]{2,1,0:T(4,128)S(1)} %add_add_fusion.3), channel_id=1, source_target_pairs={{0,16},{16,0},{32,48},{48,32},{64,80},{80,64},{96,112},{112,96},{1... | collective-permute-start | bytes 98312 | tf_op jit(solution)/shard_map/ppermute | solution.py:133
  68.6 1.3 collective-permute-done.7
  69.9 1.1 collective-permute-done.8
  71.0 0.1 collective-permute-done.6
  71.1 2.6 %fusion.31 = f32[864,4,128]{2,0,1:T(8,128)S(1)} fusion(f32[4,128]{1,0:T(4,128)S(1)} %get-tuple-element.29, f32[4,128]{1,0:T(4,128)S(1)} %get-tuple-element.42, f32[4,128]{1,0:T(4,128)S(1)} %fusion.119, f32[4,128]{1,0:T(4,128)S(1)} %get-tuple-element.36, f32[4,128]{1,0:T(4,128)S(1)} %get-tuple-element.37, f32[4,128]{1,0:T(4,128)S(1)} %get-tuple-element.43, ...), kind=kLoop, calls=%fused_computation.65 | loop fusion | flops 13713408 | bytes 7120768 | tf_op jit(solution)/shard_map/jit(_where)/select_n | solution.py:262
  73.8 0.1 fusion.158
  73.9 1.9 %collective-permute-start.10 = (f32[864,1,128]{2,0,1:T(8,128)S(1)}, f32[864,1,128]{2,0,1:T(8,128)S(1)}, u32[]{:S(2)}, u32[]{:S(2)}) collective-permute-start(f32[864,1,128]{2,0,1:T(8,128)S(1)} %get-tuple-element.18), channel_id=1, source_target_pairs={{1,0},{2,1},{3,2},{4,3},{5,4},{6,5},{7,6},{8,7},{9,8},{10,9},{11,1... | collective-permute-start | bytes 1327112 | tf_op jit(solution)/shard_map/ppermute | solution.py:58
  75.8 6.7 %collective-permute-start.11 = (f32[864,1,128]{2,0,1:T(8,128)S(1)}, f32[864,1,128]{2,0,1:T(8,128)S(1)}, u32[]{:S(2)}, u32[]{:S(2)}) collective-permute-start(f32[864,1,128]{2,0,1:T(8,128)S(1)} %get-tuple-element.17), channel_id=1, source_target_pairs={{1,0},{2,1},{3,2},{4,3},{5,4},{6,5},{7,6},{8,7},{9,8},{10,9},{11,1... | collective-permute-start | bytes 1327112 | tf_op jit(solution)/shard_map/ppermute | solution.py:64
  82.5 2.1 %collective-permute-start.9 = (f32[864,1,128]{2,0,1:T(8,128)S(1)}, f32[864,1,128]{2,0,1:T(8,128)S(1)}, u32[]{:S(2)}, u32[]{:S(2)}) collective-permute-start(f32[864,1,128]{2,0,1:T(8,128)S(1)} %get-tuple-element.16), channel_id=1, source_target_pairs={{0,1},{1,2},{2,3},{3,4},{4,5},{5,6},{6,7},{7,8},{8,9},{9,10},{10,1... | collective-permute-start | bytes 1327112 | tf_op jit(solution)/shard_map/ppermute | solution.py:57
  84.6 15.3 %collective-permute-done.11 = f32[864,1,128]{2,0,1:T(8,128)S(1)} collective-permute-done((f32[864,1,128]{2,0,1:T(8,128)S(1)}, f32[864,1,128]{2,0,1:T(8,128)S(1)}, u32[]{:S(2)}, u32[]{:S(2)}) %collective-permute-start.11) | collective-permute-done | bytes 442400 | tf_op jit(solution)/shard_map/ppermute | solution.py:64
  99.9 8.6 %collective-permute-done.9 = f32[864,1,128]{2,0,1:T(8,128)S(1)} collective-permute-done((f32[864,1,128]{2,0,1:T(8,128)S(1)}, f32[864,1,128]{2,0,1:T(8,128)S(1)}, u32[]{:S(2)}, u32[]{:S(2)}) %collective-permute-start.9) | collective-permute-done | bytes 442400 | tf_op jit(solution)/shard_map/ppermute | solution.py:57
  108.6 0.3 maximum_subtract_fusion.1
  108.9 0.3 minimum_maximum_fusion.2
  109.2 1.1 fusion.12
  110.3 0.2 fusion.59
  110.5 1.9 %fusion.8 = f32[864,4,131]{2,0,1:T(8,128)S(1)} fusion(f32[864,4,128]{2,0,1:T(8,128)S(1)} %fusion.59), kind=kLoop, calls=%fused_computation.16 | loop fusion | flops 452736 | bytes 3580416 | tf_op jit(solution)/shard_map/sub | solution.py:93
  112.4 1.0 minimum_maximum_fusion
  113.4 2.6 %fusion.7 = f32[864,4,129]{2,0,1:T(8,128)S(1)} fusion(f32[864,4,128]{2,0,1:T(8,128)S(1)} %fusion.59, f32[864,4,130]{2,0,1:T(8,128)S(1)} %minimum_maximum_fusion, f32[864]{0:T(1024)S(1)} %get-tuple-element.48, f32[864]{0:T(1024)S(1)} %get-tuple-element.49, f32[864]{0:T(1024)S(1)} %broadcast_multiply_fusion, pred[864]{0:T(1024)(128)(4,1)S(1)} %broadcast_compare_fusion), kind=kLoop, calls=%fused_computation.15 | loop fusion | flops 2674944 | bytes 7130592 | tf_op jit(solution)/shard_map/mul | solution.py:101
  116.0 1.3 fusion.62
  117.3 0.1 collective-permute-start.12
  117.4 3.5 %collective-permute-start.13 = (f32[16,4,128]{2,1,0:T(4,128)S(1)}, f32[16,4,128]{2,1,0:T(4,128)S(1)}, u32[]{:S(2)}, u32[]{:S(2)}) collective-permute-start(f32[16,4,128]{2,1,0:T(4,128)S(1)} %copy.104), channel_id=1, source_target_pairs={{0,128},{16,144},{32,160},{48,176},{64,192},{80,208},{96,224},{112... | collective-permute-start | bytes 98312 | tf_op jit(solution)/shard_map/ppermute | solution.py:133
  120.9 1.2 collective-permute-start.14
  122.1 1.1 collective-permute-done.13
  123.2 2.9 %collective-permute-done.14 = f32[16,4,128]{2,1,0:T(4,128)S(1)} collective-permute-done((f32[16,4,128]{2,1,0:T(4,128)S(1)}, f32[16,4,128]{2,1,0:T(4,128)S(1)}, u32[]{:S(2)}, u32[]{:S(2)}) %collective-permute-start.14) | collective-permute-done | bytes 32800 | tf_op jit(solution)/shard_map/ppermute | solution.py:133
  126.1 0.1 collective-permute-start.16
  126.2 2.0 %collective-permute-start.17 = (f32[16,4,128]{2,1,0:T(4,128)S(1)}, f32[16,4,128]{2,1,0:T(4,128)S(1)}, u32[]{:S(2)}, u32[]{:S(2)}) collective-permute-start(f32[16,4,128]{2,1,0:T(4,128)S(1)} %add_add_fusion.1), channel_id=1, source_target_pairs={{0,48},{16,32},{32,16},{48,0},{64,112},{80,96},{96,80},{112,64},{1... | collective-permute-start | bytes 98312 | tf_op jit(solution)/shard_map/ppermute | solution.py:133
  128.2 1.5 %collective-permute-start.15 = (f32[16,4,128]{2,1,0:T(4,128)S(1)}, f32[16,4,128]{2,1,0:T(4,128)S(1)}, u32[]{:S(2)}, u32[]{:S(2)}) collective-permute-start(f32[16,4,128]{2,1,0:T(4,128)S(1)} %add_add_fusion.1), channel_id=1, source_target_pairs={{0,16},{16,0},{32,48},{48,32},{64,80},{80,64},{96,112},{112,96},{1... | collective-permute-start | bytes 98312 | tf_op jit(solution)/shard_map/ppermute | solution.py:133
  129.7 1.3 collective-permute-done.16
  131.0 1.0 collective-permute-done.17
  132.0 0.3 collective-permute-done.15
  132.4 0.6 fusion.144
  133.0 2.7 %fusion.51 = f32[864,4,128]{2,0,1:T(8,128)S(1)} fusion(f32[4,128]{1,0:T(4,128)S(1)} %get-tuple-element.32, f32[4,128]{1,0:T(4,128)S(1)} %get-tuple-element.38, f32[4,128]{1,0:T(4,128)S(1)} %get-tuple-element.31, f32[4,128]{1,0:T(4,128)S(1)} %get-tuple-element.23, f32[4,128]{1,0:T(4,128)S(1)} %get-tuple-element.22, f32[4,128]{1,0:T(4,128)S(1)} %get-tuple-element.39, ...), kind=kLoop, calls=%fused_computation.85 | loop fusion | flops 13713408 | bytes 7120768 | tf_op jit(solution)/shard_map/jit(_where)/select_n | solution.py:262
  135.7 2.3 %copy.107 = f32[864,4,128]{2,1,0:T(4,128)} copy(f32[864,4,128]{2,0,1:T(8,128)S(1)} %fusion.51) | data formatting | bytes 3538944
  (34 shorter events, 0.5 us)
Async XLA Ops:
  0.6 1.6 %copy-start.2 = (s32[16]{0:T(128)S(1)}, s32[16]{0:T(128)}, u32[]{:S(2)}) copy-start(s32[16]{0:T(128)} %constant.98.clone) | copy-start | bytes 196
  2.2 16.6 %copy-start.1 = (s32[4,128]{1,0:T(4,128)S(1)}, s32[4,128]{1,0:T(4,128)}, u32[]{:S(2)}) copy-start(s32[4,128]{1,0:T(4,128)} %param.5) | copy-start | bytes 6148
  4.6 15.1 %collective-permute-start = (f32[864,1,128]{2,0,1:T(8,128)}, f32[864,1,128]{2,0,1:T(8,128)S(1)}, u32[]{:S(2)}, u32[]{:S(2)}) collective-permute-start(f32[864,1,128]{2,0,1:T(8,128)} %get-tuple-element.19), channel_id=1, source_target_pairs={{0,1},{1,2},{2,3},{3,4},{4,5},{5,6},{6,7},{7,8},{8,9},{9,10},{10,1... | collective-permute-start | bytes 1327112 | tf_op jit(solution)/shard_map/ppermute | solution.py:57
  6.5 18.5 %collective-permute-start.1 = (f32[864,1,128]{2,0,1:T(8,128)}, f32[864,1,128]{2,0,1:T(8,128)S(1)}, u32[]{:S(2)}, u32[]{:S(2)}) collective-permute-start(f32[864,1,128]{2,0,1:T(8,128)} %get-tuple-element.20), channel_id=1, source_target_pairs={{1,0},{2,1},{3,2},{4,3},{5,4},{6,5},{7,6},{8,7},{9,8},{10,9},{11,1... | collective-permute-start | bytes 1327112 | tf_op jit(solution)/shard_map/ppermute | solution.py:58
  15.3 15.5 %collective-permute-start.2 = (f32[864,1,128]{2,0,1:T(8,128)}, f32[864,1,128]{2,0,1:T(8,128)S(1)}, u32[]{:S(2)}, u32[]{:S(2)}) collective-permute-start(f32[864,1,128]{2,0,1:T(8,128)} %get-tuple-element.21), channel_id=1, source_target_pairs={{1,0},{2,1},{3,2},{4,3},{5,4},{6,5},{7,6},{8,7},{9,8},{10,9},{11,1... | collective-permute-start | bytes 1327112 | tf_op jit(solution)/shard_map/ppermute | solution.py:64
  31.5 1.5 %copy-start = (f32[864,4,128]{2,1,0:T(4,128)S(1)}, f32[864,4,128]{2,1,0:T(4,128)}, u32[]{:S(2)}) copy-start(f32[864,4,128]{2,1,0:T(4,128)} %param.4) | copy-start | bytes 5308420
  40.0 19.9 %collective-permute-start.3 = (f32[16,4,128]{2,1,0:T(4,128)S(1)}, f32[16,4,128]{2,1,0:T(4,128)S(1)}, u32[]{:S(2)}, u32[]{:S(2)}) collective-permute-start(f32[16,4,128]{2,1,0:T(4,128)S(1)} %copy.100), channel_id=1, source_target_pairs={{0,64},{16,80},{32,96},{48,112},{64,0},{80,16},{96,32},{112,48},{1... | collective-permute-start | bytes 98312 | tf_op jit(solution)/shard_map/ppermute | solution.py:133
  41.6 20.4 %collective-permute-start.4 = (f32[16,4,128]{2,1,0:T(4,128)S(1)}, f32[16,4,128]{2,1,0:T(4,128)S(1)}, u32[]{:S(2)}, u32[]{:S(2)}) collective-permute-start(f32[16,4,128]{2,1,0:T(4,128)S(1)} %copy.100), channel_id=1, source_target_pairs={{0,128},{16,144},{32,160},{48,176},{64,192},{80,208},{96,224},{112... | collective-permute-start | bytes 98312 | tf_op jit(solution)/shard_map/ppermute | solution.py:133
  59.8 5.1 %collective-permute-start.5 = (f32[16,4,128]{2,1,0:T(4,128)S(1)}, f32[16,4,128]{2,1,0:T(4,128)S(1)}, u32[]{:S(2)}, u32[]{:S(2)}) collective-permute-start(f32[16,4,128]{2,1,0:T(4,128)S(1)} %copy.100), channel_id=1, source_target_pairs={{0,192},{16,208},{32,224},{48,240},{64,128},{80,144},{96,160},{112... | collective-permute-start | bytes 98312 | tf_op jit(solution)/shard_map/ppermute | solution.py:133
  65.0 4.9 %collective-permute-start.7 = (f32[16,4,128]{2,1,0:T(4,128)S(1)}, f32[16,4,128]{2,1,0:T(4,128)S(1)}, u32[]{:S(2)}, u32[]{:S(2)}) collective-permute-start(f32[16,4,128]{2,1,0:T(4,128)S(1)} %add_add_fusion.3), channel_id=1, source_target_pairs={{0,32},{16,48},{32,0},{48,16},{64,96},{80,112},{96,64},{112,80},{1... | collective-permute-start | bytes 98312 | tf_op jit(solution)/shard_map/ppermute | solution.py:133
  65.1 5.9 %collective-permute-start.8 = (f32[16,4,128]{2,1,0:T(4,128)S(1)}, f32[16,4,128]{2,1,0:T(4,128)S(1)}, u32[]{:S(2)}, u32[]{:S(2)}) collective-permute-start(f32[16,4,128]{2,1,0:T(4,128)S(1)} %add_add_fusion.3), channel_id=1, source_target_pairs={{0,48},{16,32},{32,16},{48,0},{64,112},{80,96},{96,80},{112,64},{1... | collective-permute-start | bytes 98312 | tf_op jit(solution)/shard_map/ppermute | solution.py:133
  66.8 4.3 %collective-permute-start.6 = (f32[16,4,128]{2,1,0:T(4,128)S(1)}, f32[16,4,128]{2,1,0:T(4,128)S(1)}, u32[]{:S(2)}, u32[]{:S(2)}) collective-permute-start(f32[16,4,128]{2,1,0:T(4,128)S(1)} %add_add_fusion.3), channel_id=1, source_target_pairs={{0,16},{16,0},{32,48},{48,32},{64,80},{80,64},{96,112},{112,96},{1... | collective-permute-start | bytes 98312 | tf_op jit(solution)/shard_map/ppermute | solution.py:133
  73.9 10.7 %collective-permute-start.10 = (f32[864,1,128]{2,0,1:T(8,128)S(1)}, f32[864,1,128]{2,0,1:T(8,128)S(1)}, u32[]{:S(2)}, u32[]{:S(2)}) collective-permute-start(f32[864,1,128]{2,0,1:T(8,128)S(1)} %get-tuple-element.18), channel_id=1, source_target_pairs={{1,0},{2,1},{3,2},{4,3},{5,4},{6,5},{7,6},{8,7},{9,8},{10,9},{11,1... | collective-permute-start | bytes 1327112 | tf_op jit(solution)/shard_map/ppermute | solution.py:58
  75.8 24.1 %collective-permute-start.11 = (f32[864,1,128]{2,0,1:T(8,128)S(1)}, f32[864,1,128]{2,0,1:T(8,128)S(1)}, u32[]{:S(2)}, u32[]{:S(2)}) collective-permute-start(f32[864,1,128]{2,0,1:T(8,128)S(1)} %get-tuple-element.17), channel_id=1, source_target_pairs={{1,0},{2,1},{3,2},{4,3},{5,4},{6,5},{7,6},{8,7},{9,8},{10,9},{11,1... | collective-permute-start | bytes 1327112 | tf_op jit(solution)/shard_map/ppermute | solution.py:64
  82.5 26.1 %collective-permute-start.9 = (f32[864,1,128]{2,0,1:T(8,128)S(1)}, f32[864,1,128]{2,0,1:T(8,128)S(1)}, u32[]{:S(2)}, u32[]{:S(2)}) collective-permute-start(f32[864,1,128]{2,0,1:T(8,128)S(1)} %get-tuple-element.16), channel_id=1, source_target_pairs={{0,1},{1,2},{2,3},{3,4},{4,5},{5,6},{6,7},{7,8},{8,9},{9,10},{10,1... | collective-permute-start | bytes 1327112 | tf_op jit(solution)/shard_map/ppermute | solution.py:57
  117.3 4.8 %collective-permute-start.12 = (f32[16,4,128]{2,1,0:T(4,128)S(1)}, f32[16,4,128]{2,1,0:T(4,128)S(1)}, u32[]{:S(2)}, u32[]{:S(2)}) collective-permute-start(f32[16,4,128]{2,1,0:T(4,128)S(1)} %copy.104), channel_id=1, source_target_pairs={{0,64},{16,80},{32,96},{48,112},{64,0},{80,16},{96,32},{112,48},{1... | collective-permute-start | bytes 98312 | tf_op jit(solution)/shard_map/ppermute | solution.py:133
  117.4 5.8 %collective-permute-start.13 = (f32[16,4,128]{2,1,0:T(4,128)S(1)}, f32[16,4,128]{2,1,0:T(4,128)S(1)}, u32[]{:S(2)}, u32[]{:S(2)}) collective-permute-start(f32[16,4,128]{2,1,0:T(4,128)S(1)} %copy.104), channel_id=1, source_target_pairs={{0,128},{16,144},{32,160},{48,176},{64,192},{80,208},{96,224},{112... | collective-permute-start | bytes 98312 | tf_op jit(solution)/shard_map/ppermute | solution.py:133
  120.9 5.1 %collective-permute-start.14 = (f32[16,4,128]{2,1,0:T(4,128)S(1)}, f32[16,4,128]{2,1,0:T(4,128)S(1)}, u32[]{:S(2)}, u32[]{:S(2)}) collective-permute-start(f32[16,4,128]{2,1,0:T(4,128)S(1)} %copy.104), channel_id=1, source_target_pairs={{0,192},{16,208},{32,224},{48,240},{64,128},{80,144},{96,160},{112... | collective-permute-start | bytes 98312 | tf_op jit(solution)/shard_map/ppermute | solution.py:133
  126.1 4.9 %collective-permute-start.16 = (f32[16,4,128]{2,1,0:T(4,128)S(1)}, f32[16,4,128]{2,1,0:T(4,128)S(1)}, u32[]{:S(2)}, u32[]{:S(2)}) collective-permute-start(f32[16,4,128]{2,1,0:T(4,128)S(1)} %add_add_fusion.1), channel_id=1, source_target_pairs={{0,32},{16,48},{32,0},{48,16},{64,96},{80,112},{96,64},{112,80},{1... | collective-permute-start | bytes 98312 | tf_op jit(solution)/shard_map/ppermute | solution.py:133
  126.2 5.8 %collective-permute-start.17 = (f32[16,4,128]{2,1,0:T(4,128)S(1)}, f32[16,4,128]{2,1,0:T(4,128)S(1)}, u32[]{:S(2)}, u32[]{:S(2)}) collective-permute-start(f32[16,4,128]{2,1,0:T(4,128)S(1)} %add_add_fusion.1), channel_id=1, source_target_pairs={{0,48},{16,32},{32,16},{48,0},{64,112},{80,96},{96,80},{112,64},{1... | collective-permute-start | bytes 98312 | tf_op jit(solution)/shard_map/ppermute | solution.py:133
  128.2 4.1 %collective-permute-start.15 = (f32[16,4,128]{2,1,0:T(4,128)S(1)}, f32[16,4,128]{2,1,0:T(4,128)S(1)}, u32[]{:S(2)}, u32[]{:S(2)}) collective-permute-start(f32[16,4,128]{2,1,0:T(4,128)S(1)} %add_add_fusion.1), channel_id=1, source_target_pairs={{0,16},{16,0},{32,48},{48,32},{64,80},{80,64},{96,112},{112,96},{1... | collective-permute-start | bytes 98312 | tf_op jit(solution)/shard_map/ppermute | solution.py:133

commit v10 on v7

--- a/solution.py
+++ b/solution.py
@@ -54,15 +54,21 @@
     rows = block.shape[1]
     forward = [(i, i + 1) for i in range(count - 1)]
     backward = [(target, source) for source, target in forward]
-    low = lax.ppermute(block[:, rows - 1 :], "space", forward)
-    high = lax.ppermute(block[:, :1], "space", backward)
+    amount, _, width = block.shape
+    flat = block.reshape(amount * rows, width)
+
+    def row(index):
+        return lax.slice(flat, (index, 0), (amount * rows, width), (rows, 1)).reshape(amount, 1, width)
+
+    low = lax.ppermute(row(rows - 1), "space", forward)
+    high = lax.ppermute(row(0), "space", backward)
     pairs = []
     for member, sign in enumerate(signs):
         for source, target in forward if sign > 0 else backward:
             pairs.append((member * count + source, member * count + target))
     positive = jnp.asarray(np.array(signs, np.int32))[lax.axis_index("vel")] > 0
     extra = lax.ppermute(
-        jnp.where(positive, block[:, rows - 2 : rows - 1], block[:, 1:2]), ("vel", "space"), pairs
+        jnp.where(positive, row(rows - 2), row(1)), ("vel", "space"), pairs
     )
     return jnp.concatenate([extra, low, block, high, extra], axis=1)
 

time: 138 us -> 198 us (1.43)
  other arithmetic: 22.8 us -> 74.3 us
  local copies, waits for them, and re-layouts: 5.09 us -> 19.4 us
  waiting for transfers between devices: 50.2 us -> 42.1 us
  starting transfers between devices: 55.8 us -> 57.9 us
    mul x4, other arithmetic: 7.28 us -> 30.3 us  [sweep(): flux = number * jnp.where(number > 0, left_face, right_face)]
    slice x0 -> x8, local copies, waits for them, and re-layouts: none -> 18.4 us  [row(): lax.slice(flat, (index, 0), (amount * rows, width), (rows, 1))]
    ppermute x6, waiting for transfers between devices: 36 us -> 23.6 us  [the longest x2 13.7 us: with_upwind_halo(): lax.ppermute(jnp.where(positive, row(rows - 2), row(1)), ('vel', 'space')...]
    sub x4, other arithmetic: 4.35 us -> 13.2 us  [sweep(): piece(distribution_table, 1, length)]
    select_n x2, other arithmetic: 5.35 us -> 13.8 us  [approach_increment(): jnp.where(kind_labels == 1, wall_distribution, jnp.where(kind_labels == 2...]
    sub x2 -> x4, other arithmetic: 0.41 us -> 8.27 us  [sweep(): piece(distribution_table, 2, length - 2)]
    ppermute x12, waiting for transfers between devices: 14.2 us -> 18.5 us  [vel_sum(): lax.ppermute(local, 'vel', [(i, i ^ mask) for i in range(count)])]
    unnamed x8 -> x102, local copies, waits for them, and re-layouts: 4.35 us -> 0.22 us
  transfers between devices with their start and end apart: 18 -> 18, of which waited for: 15 -> 15; matrix products, arithmetic and copies ran while one was open for 1% -> 5% of each run, Pallas kernels for 0% -> 0%
where the time goes in v10:
time: 198 us
  other arithmetic  74.3 us (38%)
  starting transfers between devices  57.9 us (29%)
  waiting for transfers between devices  42.1 us (21%)
  local copies, waits for them, and re-layouts  19.4 us (10%)
  between operations  2.41 us (1%)
    ppermute x12, starting transfers between devices, vel_sum(): lax.ppermute(local, 'vel', [(i, i ^ mask) for i in range(count)])  32 us
    mul x4, other arithmetic, sweep(): flux = number * jnp.where(number > 0, left_face, right_face)  30.3 us
    ppermute x12, waiting for transfers between devices, vel_sum(): lax.ppermute(local, 'vel', [(i, i ^ mask) for i in range(count)])  18.5 us
    slice x8, local copies, waits for them, and re-layouts, row(): lax.slice(flat, (index, 0), (amount * rows, width), (rows, 1))  18.4 us
    ppermute x2, starting transfers between devices, with_upwind_halo(): high = lax.ppermute(row(0), 'space', backward)  17.4 us
    select_n x2, other arithmetic, approach_increment(): jnp.where(kind_labels == 1, wall_distribution, jnp.where(kind_labels == 2...  13.8 us
    ppermute x2, waiting for transfers between devices, with_upwind_halo(): lax.ppermute(jnp.where(positive, row(rows - 2), row(1)), ('vel', 'space')...  13.7 us
    sub x4, other arithmetic, sweep(): piece(distribution_table, 1, length)  13.2 us
  transfers between devices with their start and end apart: 18, of which 15 were waited for; matrix products, arithmetic and copies ran while one was open for 5% of the time, Pallas kernels for 0%

profile of v10, /device:TPU:6, one launch (start us, length us, event | category | flops | bytes accessed | tf_op | source)
XLA Modules:
  0.0 198.0 jit_solution(11614783220541979181)
XLA Ops:
  0.7 3.5 %slice.222 = f32[864,128]{1,0:T(8,128)} slice(f32[3456,128]{1,0:T(8,128)} %bitcast.119), slice={[3:3456:4], [0:128:1]} | slice | bytes 884736 | tf_op jit(solution)/shard_map/slice | solution.py:61
  4.1 1.9 collective-permute-start
  6.1 3.4 %slice.223 = f32[864,128]{1,0:T(8,128)} slice(f32[3456,128]{1,0:T(8,128)} %bitcast.120), slice={[0:3456:4], [0:128:1]} | slice | bytes 884736 | tf_op jit(solution)/shard_map/slice | solution.py:61
  9.4 8.9 %collective-permute-start.1 = (f32[864,1,128]{2,0,1:T(8,128)}, f32[864,1,128]{2,0,1:T(8,128)S(1)}, u32[]{:S(2)}, u32[]{:S(2)}) collective-permute-start(f32[864,1,128]{2,0,1:T(8,128)} %bitcast.5), channel_id=1, source_target_pairs={{1,0},{2,1},{3,2},{4,3},{5,4},{6,5},{7,6},{8,7},{9,8},{10,9},{11,1... | collective-permute-start | bytes 1327112 | tf_op jit(solution)/shard_map/ppermute | solution.py:64
  18.4 1.4 slice.225
  19.8 1.4 slice.224
  21.2 0.6 dynamic_slice.6
  22.4 0.8 select_bitcast_fusion.1
  23.2 2.6 %collective-permute-start.2 = (f32[864,1,128]{2,0,1:T(8,128)}, f32[864,1,128]{2,0,1:T(8,128)S(1)}, u32[]{:S(2)}, u32[]{:S(2)}) collective-permute-start(f32[864,1,128]{2,0,1:T(8,128)} %select_bitcast_fusion.1), channel_id=1, source_target_pairs={{1,0},{2,1},{3,2},{4,3},{5,4},{6,5},{7,6},{8,7},{9,8},{10,9},{11,1... | collective-permute-start | bytes 1327112 | tf_op jit(solution)/shard_map/ppermute | solution.py:70
  25.9 0.1 fusion.129
  26.5 0.1 stack.2
  26.8 7.9 %collective-permute-done.2 = f32[864,1,128]{2,0,1:T(8,128)S(1)} collective-permute-done((f32[864,1,128]{2,0,1:T(8,128)}, f32[864,1,128]{2,0,1:T(8,128)S(1)}, u32[]{:S(2)}, u32[]{:S(2)}) %collective-permute-start.2) | collective-permute-done | bytes 442400 | tf_op jit(solution)/shard_map/ppermute | solution.py:70
  34.7 2.9 %maximum_subtract_fusion = f32[864,7,128]{2,1,0:T(8,128)S(1)} fusion(f32[864,1,128]{2,1,0:T(1,128)S(1)} %bitcast.135, f32[864,1,128]{2,1,0:T(1,128)S(1)} %bitcast.129, f32[864,4,128]{2,1,0:T(4,128)S(1)} %copy-done, f32[864,1,128]{2,1,0:T(1,128)S(1)} %bitcast.127), kind=kLoop, calls=%fused_computation.34 | loop fusion | flops 5419008 | bytes 6193152 | tf_op jit(solution)/shard_map/sub | solution.py:99
  37.6 0.7 minimum_maximum_fusion.3
  38.3 6.3 %fusion.16 = f32[864,5,128]{2,1,0:T(8,128)S(1)} fusion(f32[864,6,128]{2,1,0:T(8,128)S(1)} %minimum_maximum_fusion.3, f32[864,4,128]{2,1,0:T(4,128)S(1)} %copy-done, f32[864,1,128]{2,1,0:T(1,128)S(1)} %bitcast.128, f32[864,1,128]{2,1,0:T(1,128)S(1)} %bitcast.130, f32[864]{0:T(1024)S(1)} %get-tuple-element.40, f32[864]{0:T(1024)S(1)} %get-tuple-element.41, ...), kind=kLoop, calls=%fused_computation.31 | loop fusion | flops 4423680 | bytes 9300960 | tf_op jit(solution)/shard_map/mul | solution.py:107
  44.6 0.7 fusion.41
  45.3 3.7 %fusion.3 = f32[864,4,131]{2,1,0:T(4,128)S(1)} fusion(f32[864,4,128]{2,1,0:T(4,128)S(1)} %fusion.41), kind=kLoop, calls=%fused_computation.11 | loop fusion | flops 452736 | bytes 3580416 | tf_op jit(solution)/shard_map/sub | solution.py:99
  49.1 2.0 %minimum_maximum_fusion.2 = f32[864,4,130]{2,1,0:T(4,128)S(1)} fusion(f32[864,4,131]{2,1,0:T(4,128)S(1)} %fusion.3), kind=kLoop, calls=%fused_computation.38 | loop fusion | flops 1797120 | bytes 5391360 | tf_op jit(solution)/shard_map/max | solution.py:90
  51.1 8.9 %fusion.2 = f32[864,4,129]{2,1,0:T(4,128)S(1)} fusion(f32[864,4,128]{2,1,0:T(4,128)S(1)} %fusion.41, f32[864,4,130]{2,1,0:T(4,128)S(1)} %minimum_maximum_fusion.2, f32[864]{0:T(1024)S(1)} %get-tuple-element.38, f32[864]{0:T(1024)S(1)} %get-tuple-element.39, f32[864]{0:T(1024)S(1)} %get-tuple-element.48, pred[864]{0:T(1024)(128)(4,1)S(1)} %get-tuple-element.46), kind=kLoop, calls=%fused_computation.10 | loop fusion | flops 2674944 | bytes 7130592 | tf_op jit(solution)/shard_map/mul | solution.py:107
  60.0 1.0 fusion.40
  61.0 1.0 fusion.44
  62.0 11.8 %collective-permute-start.4 = (f32[16,4,128]{2,1,0:T(4,128)S(1)}, f32[16,4,128]{2,1,0:T(4,128)S(1)}, u32[]{:S(2)}, u32[]{:S(2)}) collective-permute-start(f32[16,4,128]{2,1,0:T(4,128)S(1)} %copy.121), channel_id=1, source_target_pairs={{0,128},{16,144},{32,160},{48,176},{64,192},{80,208},{96,224},{112... | collective-permute-start | bytes 98312 | tf_op jit(solution)/shard_map/ppermute | solution.py:139
  73.8 0.7 collective-permute-start.3
  74.5 1.2 collective-permute-done.4
  75.7 2.0 %collective-permute-done.3 = f32[16,4,128]{2,1,0:T(4,128)S(1)} collective-permute-done((f32[16,4,128]{2,1,0:T(4,128)S(1)}, f32[16,4,128]{2,1,0:T(4,128)S(1)}, u32[]{:S(2)}, u32[]{:S(2)}) %collective-permute-start.3) | collective-permute-done | bytes 32800 | tf_op jit(solution)/shard_map/ppermute | solution.py:139
  77.7 2.2 %collective-permute-done.5 = f32[16,4,128]{2,1,0:T(4,128)S(1)} collective-permute-done((f32[16,4,128]{2,1,0:T(4,128)S(1)}, f32[16,4,128]{2,1,0:T(4,128)S(1)}, u32[]{:S(2)}, u32[]{:S(2)}) %collective-permute-start.5) | collective-permute-done | bytes 32800 | tf_op jit(solution)/shard_map/ppermute | solution.py:139
  79.9 6.2 %collective-permute-start.8 = (f32[16,4,128]{2,1,0:T(4,128)S(1)}, f32[16,4,128]{2,1,0:T(4,128)S(1)}, u32[]{:S(2)}, u32[]{:S(2)}) collective-permute-start(f32[16,4,128]{2,1,0:T(4,128)S(1)} %add_add_fusion.3), channel_id=1, source_target_pairs={{0,48},{16,32},{32,16},{48,0},{64,112},{80,96},{96,80},{112,64},{1... | collective-permute-start | bytes 98312 | tf_op jit(solution)/shard_map/ppermute | solution.py:139
  86.1 0.7 collective-permute-start.6
  86.8 1.2 collective-permute-done.8
  88.0 2.9 %collective-permute-done.7 = f32[16,4,128]{2,1,0:T(4,128)S(1)} collective-permute-done((f32[16,4,128]{2,1,0:T(4,128)S(1)}, f32[16,4,128]{2,1,0:T(4,128)S(1)}, u32[]{:S(2)}, u32[]{:S(2)}) %collective-permute-start.7) | collective-permute-done | bytes 32800 | tf_op jit(solution)/shard_map/ppermute | solution.py:139
  91.2 5.5 %select_select_fusion.1 = f32[864,4,128]{2,1,0:T(4,128)S(1)} fusion(f32[864,4,128]{2,1,0:T(4,128)S(1)} %fusion.40, f32[4,128]{1,0:T(4,128)S(1)} %get-tuple-element.19, f32[4,128]{1,0:T(4,128)S(1)} %get-tuple-element.32, f32[4,128]{1,0:T(4,128)S(1)} %fusion.101, f32[4,128]{1,0:T(4,128)S(1)} %get-tuple-element.26, f32[4,128]{1,0:T(4,128)S(1)} %get-tuple-element.27, ...), kind=kLoop, calls=%fused_computation.85 | loop fusion | flops 12828672 | bytes 3581824 | tf_op jit(solution)/shard_map/jit(_where)/select_n | solution.py:265
  96.8 2.2 %slice.259 = f32[864,128]{1,0:T(8,128)} slice(f32[3456,128]{1,0:T(8,128)S(1)} %bitcast.123), slice={[1:3456:4], [0:128:1]} | slice | bytes 884736 | tf_op jit(solution)/shard_map/slice | solution.py:61
  99.0 2.2 %slice.258 = f32[864,128]{1,0:T(8,128)} slice(f32[3456,128]{1,0:T(8,128)S(1)} %bitcast.124), slice={[2:3456:4], [0:128:1]} | slice | bytes 884736 | tf_op jit(solution)/shard_map/slice | solution.py:61
  101.2 2.2 %slice.257 = f32[864,128]{1,0:T(8,128)} slice(f32[3456,128]{1,0:T(8,128)S(1)} %bitcast.125), slice={[0:3456:4], [0:128:1]} | slice | bytes 884736 | tf_op jit(solution)/shard_map/slice | solution.py:61
  103.4 2.2 %slice.256 = f32[864,128]{1,0:T(8,128)} slice(f32[3456,128]{1,0:T(8,128)S(1)} %bitcast.126), slice={[3:3456:4], [0:128:1]} | slice | bytes 884736 | tf_op jit(solution)/shard_map/slice | solution.py:61
  105.6 1.9 collective-permute-start.9
  107.5 8.4 %collective-permute-start.10 = (f32[864,1,128]{2,0,1:T(8,128)}, f32[864,1,128]{2,0,1:T(8,128)S(1)}, u32[]{:S(2)}, u32[]{:S(2)}) collective-permute-start(f32[864,1,128]{2,0,1:T(8,128)} %bitcast.137), channel_id=1, source_target_pairs={{1,0},{2,1},{3,2},{4,3},{5,4},{6,5},{7,6},{8,7},{9,8},{10,9},{11,1... | collective-permute-start | bytes 1327112 | tf_op jit(solution)/shard_map/ppermute | solution.py:64
  115.9 1.1 select_bitcast_fusion
  117.0 2.1 %collective-permute-start.11 = (f32[864,1,128]{2,0,1:T(8,128)S(1)}, f32[864,1,128]{2,0,1:T(8,128)S(1)}, u32[]{:S(2)}, u32[]{:S(2)}) collective-permute-start(f32[864,1,128]{2,0,1:T(8,128)S(1)} %select_bitcast_fusion), channel_id=1, source_target_pairs={{1,0},{2,1},{3,2},{4,3},{5,4},{6,5},{7,6},{8,7},{9,8},{10,9},{11,1... | collective-permute-start | bytes 1327112 | tf_op jit(solution)/shard_map/ppermute | solution.py:70
  119.2 5.4 %collective-permute-done.9 = f32[864,1,128]{2,0,1:T(8,128)S(1)} collective-permute-done((f32[864,1,128]{2,0,1:T(8,128)}, f32[864,1,128]{2,0,1:T(8,128)S(1)}, u32[]{:S(2)}, u32[]{:S(2)}) %collective-permute-start.9) | collective-permute-done | bytes 442400 | tf_op jit(solution)/shard_map/ppermute | solution.py:63
  124.6 4.5 %collective-permute-done.10 = f32[864,1,128]{2,0,1:T(8,128)S(1)} collective-permute-done((f32[864,1,128]{2,0,1:T(8,128)}, f32[864,1,128]{2,0,1:T(8,128)S(1)}, u32[]{:S(2)}, u32[]{:S(2)}) %collective-permute-start.10) | collective-permute-done | bytes 442400 | tf_op jit(solution)/shard_map/ppermute | solution.py:64
  129.1 5.8 %collective-permute-done.11 = f32[864,1,128]{2,0,1:T(8,128)S(1)} collective-permute-done((f32[864,1,128]{2,0,1:T(8,128)S(1)}, f32[864,1,128]{2,0,1:T(8,128)S(1)}, u32[]{:S(2)}, u32[]{:S(2)}) %collective-permute-start.11) | collective-permute-done | bytes 442400 | tf_op jit(solution)/shard_map/ppermute | solution.py:70
  134.9 2.9 %maximum_subtract_fusion.1 = f32[864,7,128]{2,1,0:T(8,128)S(1)} fusion(f32[864,1,128]{2,1,0:T(1,128)S(1)} %bitcast.136, f32[864,1,128]{2,1,0:T(1,128)S(1)} %bitcast.133, f32[864,4,128]{2,1,0:T(4,128)S(1)} %select_select_fusion.1, f32[864,1,128]{2,1,0:T(1,128)S(1)} %bitcast.131), kind=kLoop, calls=%fused_computation.35 | loop fusion | flops 5419008 | bytes 6193152 | tf_op jit(solution)/shard_map/sub | solution.py:99
  137.8 0.7 minimum_maximum_fusion.1
  138.7 6.3 %fusion.12 = f32[864,5,128]{2,1,0:T(8,128)S(1)} fusion(f32[864,6,128]{2,1,0:T(8,128)S(1)} %minimum_maximum_fusion.1, f32[864,4,128]{2,1,0:T(4,128)S(1)} %select_select_fusion.1, f32[864,1,128]{2,1,0:T(1,128)S(1)} %bitcast.132, f32[864,1,128]{2,1,0:T(1,128)S(1)} %bitcast.134, f32[864]{0:T(1024)S(1)} %copy-done.18, f32[864]{0:T(1024)S(1)} %copy-done.20, ...), kind=kLoop, calls=%fused_computation.23 | loop fusion | flops 4423680 | bytes 9300960 | tf_op jit(solution)/shard_map/mul | solution.py:107
  145.1 5.6 %fusion.39 = f32[864,4,128]{2,1,0:T(4,128)S(1)} fusion(f32[864,5,128]{2,1,0:T(8,128)S(1)} %fusion.12, f32[864,4,128]{2,1,0:T(4,128)S(1)} %fusion.40, f32[4,128]{1,0:T(4,128)S(1)} %copy-done.30, f32[4,128]{1,0:T(4,128)S(1)} %copy-done.38, f32[4,128]{1,0:T(4,128)S(1)} %copy-done.26, f32[4,128]{1,0:T(4,128)S(1)} %copy-done.34, f32[4,128]{1,0:T(4,128)S(1)} %copy-done.36, ...), kind=kLoop, calls=%fused_computation.75 | loop fusion | flops 13713408 | bytes 7120768 | tf_op jit(solution)/shard_map/sub | solution.py:108
  150.7 3.7 %fusion.8 = f32[864,4,131]{2,1,0:T(4,128)S(1)} fusion(f32[864,4,128]{2,1,0:T(4,128)S(1)} %fusion.39), kind=kLoop, calls=%fused_computation.16 | loop fusion | flops 452736 | bytes 3580416 | tf_op jit(solution)/shard_map/sub | solution.py:99
  154.4 2.0 %minimum_maximum_fusion = f32[864,4,130]{2,1,0:T(4,128)S(1)} fusion(f32[864,4,131]{2,1,0:T(4,128)S(1)} %fusion.8), kind=kLoop, calls=%fused_computation.36 | loop fusion | flops 1797120 | bytes 5391360 | tf_op jit(solution)/shard_map/max | solution.py:90
  156.5 8.9 %fusion.7 = f32[864,4,129]{2,1,0:T(4,128)S(1)} fusion(f32[864,4,128]{2,1,0:T(4,128)S(1)} %fusion.39, f32[864,4,130]{2,1,0:T(4,128)S(1)} %minimum_maximum_fusion, f32[864]{0:T(1024)S(1)} %copy-done.12, f32[864]{0:T(1024)S(1)} %copy-done.14, f32[864]{0:T(1024)S(1)} %copy-done.16, pred[864]{0:T(1024)(128)(4,1)S(1)} %copy-done.44), kind=kLoop, calls=%fused_computation.15 | loop fusion | flops 2674944 | bytes 7130592 | tf_op jit(solution)/shard_map/mul | solution.py:107
  165.4 1.0 fusion.38
  166.4 1.0 fusion.42
  167.4 3.6 %collective-permute-start.13 = (f32[16,4,128]{2,1,0:T(4,128)S(1)}, f32[16,4,128]{2,1,0:T(4,128)S(1)}, u32[]{:S(2)}, u32[]{:S(2)}) collective-permute-start(f32[16,4,128]{2,1,0:T(4,128)S(1)} %copy.134), channel_id=1, source_target_pairs={{0,128},{16,144},{32,160},{48,176},{64,192},{80,208},{96,224},{112... | collective-permute-start | bytes 98312 | tf_op jit(solution)/shard_map/ppermute | solution.py:139
  171.0 0.7 collective-permute-start.12
  171.7 1.2 collective-permute-done.13
  172.9 2.0 %collective-permute-done.12 = f32[16,4,128]{2,1,0:T(4,128)S(1)} collective-permute-done((f32[16,4,128]{2,1,0:T(4,128)S(1)}, f32[16,4,128]{2,1,0:T(4,128)S(1)}, u32[]{:S(2)}, u32[]{:S(2)}) %collective-permute-start.12) | collective-permute-done | bytes 32800 | tf_op jit(solution)/shard_map/ppermute | solution.py:139
  174.9 1.9 collective-permute-done.14
  176.8 7.1 %collective-permute-start.17 = (f32[16,4,128]{2,1,0:T(4,128)S(1)}, f32[16,4,128]{2,1,0:T(4,128)S(1)}, u32[]{:S(2)}, u32[]{:S(2)}) collective-permute-start(f32[16,4,128]{2,1,0:T(4,128)S(1)} %add_add_fusion.1), channel_id=1, source_target_pairs={{0,48},{16,32},{32,16},{48,0},{64,112},{80,96},{96,80},{112,64},{1... | collective-permute-start | bytes 98312 | tf_op jit(solution)/shard_map/ppermute | solution.py:139
  183.9 0.8 collective-permute-start.16
  184.7 0.5 collective-permute-start.15
  185.2 0.6 collective-permute-done.17
  185.8 3.0 %collective-permute-done.16 = f32[16,4,128]{2,1,0:T(4,128)S(1)} collective-permute-done((f32[16,4,128]{2,1,0:T(4,128)S(1)}, f32[16,4,128]{2,1,0:T(4,128)S(1)}, u32[]{:S(2)}, u32[]{:S(2)}) %collective-permute-start.16) | collective-permute-done | bytes 32800 | tf_op jit(solution)/shard_map/ppermute | solution.py:139
  188.8 0.2 collective-permute-done.15
  189.0 0.6 fusion.126
  189.6 8.4 %select_select_fusion = f32[864,4,128]{2,1,0:T(4,128)} fusion(f32[864,4,128]{2,1,0:T(4,128)S(1)} %fusion.38, f32[4,128]{1,0:T(4,128)S(1)} %get-tuple-element.22, f32[4,128]{1,0:T(4,128)S(1)} %get-tuple-element.28, f32[4,128]{1,0:T(4,128)S(1)} %get-tuple-element.21, f32[4,128]{1,0:T(4,128)S(1)} %get-tuple-element.13, f32[4,128]{1,0:T(4,128)S(1)} %get-tuple-element.12, ...), kind=kLoop, calls=%fused_computation.84 | loop fusion | flops 12828672 | bytes 3581824 | tf_op jit(solution)/shard_map/jit(_where)/select_n | solution.py:265
  (136 shorter events, 1.1 us)
Async XLA Ops:
  0.6 17.7 %copy-start = (f32[864,4,128]{2,1,0:T(4,128)S(1)}, f32[864,4,128]{2,1,0:T(4,128)}, u32[]{:S(2)}) copy-start(f32[864,4,128]{2,1,0:T(4,128)} %param.4) | copy-start | bytes 5308420
  0.6 20.5 %copy-start.50 = (s32[16]{0:T(128)S(1)}, s32[16]{0:T(128)}, u32[]{:S(2)}) copy-start(s32[16]{0:T(128)} %constant.97.clone) | copy-start | bytes 196
  4.1 22.6 %collective-permute-start = (f32[864,1,128]{2,0,1:T(8,128)}, f32[864,1,128]{2,0,1:T(8,128)S(1)}, u32[]{:S(2)}, u32[]{:S(2)}) collective-permute-start(f32[864,1,128]{2,0,1:T(8,128)} %bitcast.2), channel_id=1, source_target_pairs={{0,1},{1,2},{2,3},{3,4},{4,5},{5,6},{6,7},{7,8},{8,9},{9,10},{10,1... | collective-permute-start | bytes 1327112 | tf_op jit(solution)/shard_map/ppermute | solution.py:63
  9.4 17.3 %copy-start.49 = (s32[4,128]{1,0:T(4,128)S(1)}, s32[4,128]{1,0:T(4,128)}, u32[]{:S(2)}) copy-start(s32[4,128]{1,0:T(4,128)} %param.5) | copy-start | bytes 6148
  9.4 17.4 %collective-permute-start.1 = (f32[864,1,128]{2,0,1:T(8,128)}, f32[864,1,128]{2,0,1:T(8,128)S(1)}, u32[]{:S(2)}, u32[]{:S(2)}) collective-permute-start(f32[864,1,128]{2,0,1:T(8,128)} %bitcast.5), channel_id=1, source_target_pairs={{1,0},{2,1},{3,2},{4,3},{5,4},{6,5},{7,6},{8,7},{9,8},{10,9},{11,1... | collective-permute-start | bytes 1327112 | tf_op jit(solution)/shard_map/ppermute | solution.py:64
  23.2 11.5 %collective-permute-start.2 = (f32[864,1,128]{2,0,1:T(8,128)}, f32[864,1,128]{2,0,1:T(8,128)S(1)}, u32[]{:S(2)}, u32[]{:S(2)}) collective-permute-start(f32[864,1,128]{2,0,1:T(8,128)} %select_bitcast_fusion.1), channel_id=1, source_target_pairs={{1,0},{2,1},{3,2},{4,3},{5,4},{6,5},{7,6},{8,7},{9,8},{10,9},{11,1... | collective-permute-start | bytes 1327112 | tf_op jit(solution)/shard_map/ppermute | solution.py:70
  26.4 11.9 %copy-start.17 = (f32[864]{0:T(1024)}, f32[864]{0:T(1024)S(1)}, u32[]{:S(2)}) copy-start(f32[864]{0:T(1024)S(1)} %get-tuple-element.40) | copy-start | bytes 10372
  26.4 11.9 %copy-start.19 = (f32[864]{0:T(1024)}, f32[864]{0:T(1024)S(1)}, u32[]{:S(2)}) copy-start(f32[864]{0:T(1024)S(1)} %get-tuple-element.41) | copy-start | bytes 10372
  26.4 24.6 %copy-start.11 = (f32[864]{0:T(1024)}, f32[864]{0:T(1024)S(1)}, u32[]{:S(2)}) copy-start(f32[864]{0:T(1024)S(1)} %get-tuple-element.38) | copy-start | bytes 10372
  26.4 24.6 %copy-start.13 = (f32[864]{0:T(1024)}, f32[864]{0:T(1024)S(1)}, u32[]{:S(2)}) copy-start(f32[864]{0:T(1024)S(1)} %get-tuple-element.39) | copy-start | bytes 10372
  26.5 11.8 %copy-start.21 = (f32[864]{0:T(1024)}, f32[864]{0:T(1024)S(1)}, u32[]{:S(2)}) copy-start(f32[864]{0:T(1024)S(1)} %get-tuple-element.49) | copy-start | bytes 10372
  26.5 24.6 %copy-start.15 = (f32[864]{0:T(1024)}, f32[864]{0:T(1024)S(1)}, u32[]{:S(2)}) copy-start(f32[864]{0:T(1024)S(1)} %get-tuple-element.48) | copy-start | bytes 10372
  26.6 34.3 %copy-start.1 = (f32[16,864]{1,0:T(8,128)}, f32[16,864]{1,0:T(8,128)S(1)}, u32[]{:S(2)}) copy-start(f32[16,864]{1,0:T(8,128)S(1)} %stack.2) | copy-start | bytes 165892
  26.7 11.6 %copy-start.41 = (pred[864]{0:T(1024)(128)(4,1)}, pred[864]{0:T(1024)(128)(4,1)S(1)}, u32[]{:S(2)}) copy-start(pred[864]{0:T(1024)(128)(4,1)S(1)} %get-tuple-element.47) | copy-start | bytes 2596
  26.7 24.4 %copy-start.43 = (pred[864]{0:T(1024)(128)(4,1)}, pred[864]{0:T(1024)(128)(4,1)S(1)}, u32[]{:S(2)}) copy-start(pred[864]{0:T(1024)(128)(4,1)S(1)} %get-tuple-element.46) | copy-start | bytes 2596
  26.7 64.4 %copy-start.45 = (pred[4,128]{1,0:T(4,128)(4,1)}, pred[4,128]{1,0:T(4,128)(4,1)S(1)}, u32[]{:S(2)}) copy-start(pred[4,128]{1,0:T(4,128)(4,1)S(1)} %get-tuple-element.30) | copy-start | bytes 1540
  26.8 64.4 %copy-start.47 = (pred[4,128]{1,0:T(4,128)(4,1)}, pred[4,128]{1,0:T(4,128)(4,1)S(1)}, u32[]{:S(2)}) copy-start(pred[4,128]{1,0:T(4,128)(4,1)S(1)} %get-tuple-element.31) | copy-start | bytes 1540
  62.0 13.7 %collective-permute-start.4 = (f32[16,4,128]{2,1,0:T(4,128)S(1)}, f32[16,4,128]{2,1,0:T(4,128)S(1)}, u32[]{:S(2)}, u32[]{:S(2)}) collective-permute-start(f32[16,4,128]{2,1,0:T(4,128)S(1)} %copy.121), channel_id=1, source_target_pairs={{0,128},{16,144},{32,160},{48,176},{64,192},{80,208},{96,224},{112... | collective-permute-start | bytes 98312 | tf_op jit(solution)/shard_map/ppermute | solution.py:139
  73.8 3.9 %collective-permute-start.3 = (f32[16,4,128]{2,1,0:T(4,128)S(1)}, f32[16,4,128]{2,1,0:T(4,128)S(1)}, u32[]{:S(2)}, u32[]{:S(2)}) collective-permute-start(f32[16,4,128]{2,1,0:T(4,128)S(1)} %copy.121), channel_id=1, source_target_pairs={{0,64},{16,80},{32,96},{48,112},{64,0},{80,16},{96,32},{112,48},{1... | collective-permute-start | bytes 98312 | tf_op jit(solution)/shard_map/ppermute | solution.py:139
  74.4 5.5 %collective-permute-start.5 = (f32[16,4,128]{2,1,0:T(4,128)S(1)}, f32[16,4,128]{2,1,0:T(4,128)S(1)}, u32[]{:S(2)}, u32[]{:S(2)}) collective-permute-start(f32[16,4,128]{2,1,0:T(4,128)S(1)} %copy.121), channel_id=1, source_target_pairs={{0,192},{16,208},{32,224},{48,240},{64,128},{80,144},{96,160},{112... | collective-permute-start | bytes 98312 | tf_op jit(solution)/shard_map/ppermute | solution.py:139
  79.9 8.1 %collective-permute-start.8 = (f32[16,4,128]{2,1,0:T(4,128)S(1)}, f32[16,4,128]{2,1,0:T(4,128)S(1)}, u32[]{:S(2)}, u32[]{:S(2)}) collective-permute-start(f32[16,4,128]{2,1,0:T(4,128)S(1)} %add_add_fusion.3), channel_id=1, source_target_pairs={{0,48},{16,32},{32,16},{48,0},{64,112},{80,96},{96,80},{112,64},{1... | collective-permute-start | bytes 98312 | tf_op jit(solution)/shard_map/ppermute | solution.py:139
  86.1 4.8 %collective-permute-start.7 = (f32[16,4,128]{2,1,0:T(4,128)S(1)}, f32[16,4,128]{2,1,0:T(4,128)S(1)}, u32[]{:S(2)}, u32[]{:S(2)}) collective-permute-start(f32[16,4,128]{2,1,0:T(4,128)S(1)} %add_add_fusion.3), channel_id=1, source_target_pairs={{0,32},{16,48},{32,0},{48,16},{64,96},{80,112},{96,64},{112,80},{1... | collective-permute-start | bytes 98312 | tf_op jit(solution)/shard_map/ppermute | solution.py:139
  86.1 4.8 %collective-permute-start.6 = (f32[16,4,128]{2,1,0:T(4,128)S(1)}, f32[16,4,128]{2,1,0:T(4,128)S(1)}, u32[]{:S(2)}, u32[]{:S(2)}) collective-permute-start(f32[16,4,128]{2,1,0:T(4,128)S(1)} %add_add_fusion.3), channel_id=1, source_target_pairs={{0,16},{16,0},{32,48},{48,32},{64,80},{80,64},{96,112},{112,96},{1... | collective-permute-start | bytes 98312 | tf_op jit(solution)/shard_map/ppermute | solution.py:139
  86.8 9.8 %copy-start.3 = (f32[864]{0:T(1024)}, f32[864]{0:T(1024)S(1)}, u32[]{:S(2)}) copy-start(f32[864]{0:T(1024)S(1)} %multiply_exponential_fusion.1) | copy-start | bytes 10372
  91.0 5.7 %copy-start.5 = (f32[1,4,128]{2,1,0:T(4,128)}, f32[1,4,128]{2,1,0:T(4,128)S(1)}, u32[]{:S(2)}) copy-start(f32[1,4,128]{2,1,0:T(4,128)S(1)} %get-tuple-element.9) | copy-start | bytes 6148
  91.0 5.7 %copy-start.7 = (f32[1,4,128]{2,1,0:T(4,128)}, f32[1,4,128]{2,1,0:T(4,128)S(1)}, u32[]{:S(2)}) copy-start(f32[1,4,128]{2,1,0:T(4,128)S(1)} %get-tuple-element.10) | copy-start | bytes 6148
  91.0 5.7 %copy-start.9 = (f32[1,4,128]{2,1,0:T(4,128)}, f32[1,4,128]{2,1,0:T(4,128)S(1)}, u32[]{:S(2)}) copy-start(f32[1,4,128]{2,1,0:T(4,128)S(1)} %get-tuple-element.11) | copy-start | bytes 6148
  91.0 5.7 %copy-start.23 = (f32[4,128]{1,0:T(4,128)}, f32[4,128]{1,0:T(4,128)S(1)}, u32[]{:S(2)}) copy-start(f32[4,128]{1,0:T(4,128)S(1)} %get-tuple-element.7) | copy-start | bytes 6148
  91.0 5.7 %copy-start.25 = (f32[4,128]{1,0:T(4,128)}, f32[4,128]{1,0:T(4,128)S(1)}, u32[]{:S(2)}) copy-start(f32[4,128]{1,0:T(4,128)S(1)} %fusion.101) | copy-start | bytes 6148
  91.1 5.6 %copy-start.27 = (f32[4,128]{1,0:T(4,128)}, f32[4,128]{1,0:T(4,128)S(1)}, u32[]{:S(2)}) copy-start(f32[4,128]{1,0:T(4,128)S(1)} %get-tuple-element.18) | copy-start | bytes 6148
  91.1 5.6 %copy-start.29 = (f32[4,128]{1,0:T(4,128)}, f32[4,128]{1,0:T(4,128)S(1)}, u32[]{:S(2)}) copy-start(f32[4,128]{1,0:T(4,128)S(1)} %get-tuple-element.19) | copy-start | bytes 6148
  91.1 5.6 %copy-start.31 = (f32[4,128]{1,0:T(4,128)}, f32[4,128]{1,0:T(4,128)S(1)}, u32[]{:S(2)}) copy-start(f32[4,128]{1,0:T(4,128)S(1)} %get-tuple-element.25) | copy-start | bytes 6148
  91.1 5.6 %copy-start.33 = (f32[4,128]{1,0:T(4,128)}, f32[4,128]{1,0:T(4,128)S(1)}, u32[]{:S(2)}) copy-start(f32[4,128]{1,0:T(4,128)S(1)} %get-tuple-element.26) | copy-start | bytes 6148
  91.1 5.6 %copy-start.35 = (f32[4,128]{1,0:T(4,128)}, f32[4,128]{1,0:T(4,128)S(1)}, u32[]{:S(2)}) copy-start(f32[4,128]{1,0:T(4,128)S(1)} %get-tuple-element.27) | copy-start | bytes 6148
  91.1 5.6 %copy-start.37 = (f32[4,128]{1,0:T(4,128)}, f32[4,128]{1,0:T(4,128)S(1)}, u32[]{:S(2)}) copy-start(f32[4,128]{1,0:T(4,128)S(1)} %get-tuple-element.32) | copy-start | bytes 6148
  91.1 5.6 %copy-start.39 = (f32[4,128]{1,0:T(4,128)}, f32[4,128]{1,0:T(4,128)S(1)}, u32[]{:S(2)}) copy-start(f32[4,128]{1,0:T(4,128)S(1)} %get-tuple-element.33) | copy-start | bytes 6148
  105.6 19.0 %collective-permute-start.9 = (f32[864,1,128]{2,0,1:T(8,128)}, f32[864,1,128]{2,0,1:T(8,128)S(1)}, u32[]{:S(2)}, u32[]{:S(2)}) collective-permute-start(f32[864,1,128]{2,0,1:T(8,128)} %bitcast.138), channel_id=1, source_target_pairs={{0,1},{1,2},{2,3},{3,4},{4,5},{5,6},{6,7},{7,8},{8,9},{9,10},{10,1... | collective-permute-start | bytes 1327112 | tf_op jit(solution)/shard_map/ppermute | solution.py:63
  107.5 21.6 %collective-permute-start.10 = (f32[864,1,128]{2,0,1:T(8,128)}, f32[864,1,128]{2,0,1:T(8,128)S(1)}, u32[]{:S(2)}, u32[]{:S(2)}) collective-permute-start(f32[864,1,128]{2,0,1:T(8,128)} %bitcast.137), channel_id=1, source_target_pairs={{1,0},{2,1},{3,2},{4,3},{5,4},{6,5},{7,6},{8,7},{9,8},{10,9},{11,1... | collective-permute-start | bytes 1327112 | tf_op jit(solution)/shard_map/ppermute | solution.py:64
  117.0 17.8 %collective-permute-start.11 = (f32[864,1,128]{2,0,1:T(8,128)S(1)}, f32[864,1,128]{2,0,1:T(8,128)S(1)}, u32[]{:S(2)}, u32[]{:S(2)}) collective-permute-start(f32[864,1,128]{2,0,1:T(8,128)S(1)} %select_bitcast_fusion), channel_id=1, source_target_pairs={{1,0},{2,1},{3,2},{4,3},{5,4},{6,5},{7,6},{8,7},{9,8},{10,9},{11,1... | collective-permute-start | bytes 1327112 | tf_op jit(solution)/shard_map/ppermute | solution.py:70
  138.5 6.4 %copy-start.4 = (f32[864]{0:T(1024)S(1)}, f32[864]{0:T(1024)}, u32[]{:S(2)}) copy-start(f32[864]{0:T(1024)} %copy-done.3) | copy-start | bytes 10372
  138.5 6.4 %copy-start.6 = (f32[1,4,128]{2,1,0:T(4,128)S(1)}, f32[1,4,128]{2,1,0:T(4,128)}, u32[]{:S(2)}) copy-start(f32[1,4,128]{2,1,0:T(4,128)} %copy-done.5) | copy-start | bytes 6148
  138.5 6.4 %copy-start.8 = (f32[1,4,128]{2,1,0:T(4,128)S(1)}, f32[1,4,128]{2,1,0:T(4,128)}, u32[]{:S(2)}) copy-start(f32[1,4,128]{2,1,0:T(4,128)} %copy-done.7) | copy-start | bytes 6148
  138.6 6.4 %copy-start.10 = (f32[1,4,128]{2,1,0:T(4,128)S(1)}, f32[1,4,128]{2,1,0:T(4,128)}, u32[]{:S(2)}) copy-start(f32[1,4,128]{2,1,0:T(4,128)} %copy-done.9) | copy-start | bytes 6148
  138.6 6.4 %copy-start.24 = (f32[4,128]{1,0:T(4,128)S(1)}, f32[4,128]{1,0:T(4,128)}, u32[]{:S(2)}) copy-start(f32[4,128]{1,0:T(4,128)} %copy-done.23) | copy-start | bytes 6148
  138.6 6.4 %copy-start.26 = (f32[4,128]{1,0:T(4,128)S(1)}, f32[4,128]{1,0:T(4,128)}, u32[]{:S(2)}) copy-start(f32[4,128]{1,0:T(4,128)} %copy-done.25) | copy-start | bytes 6148
  138.6 6.4 %copy-start.28 = (f32[4,128]{1,0:T(4,128)S(1)}, f32[4,128]{1,0:T(4,128)}, u32[]{:S(2)}) copy-start(f32[4,128]{1,0:T(4,128)} %copy-done.27) | copy-start | bytes 6148
  138.6 6.4 %copy-start.30 = (f32[4,128]{1,0:T(4,128)S(1)}, f32[4,128]{1,0:T(4,128)}, u32[]{:S(2)}) copy-start(f32[4,128]{1,0:T(4,128)} %copy-done.29) | copy-start | bytes 6148
  138.6 6.4 %copy-start.32 = (f32[4,128]{1,0:T(4,128)S(1)}, f32[4,128]{1,0:T(4,128)}, u32[]{:S(2)}) copy-start(f32[4,128]{1,0:T(4,128)} %copy-done.31) | copy-start | bytes 6148
  138.6 6.4 %copy-start.34 = (f32[4,128]{1,0:T(4,128)S(1)}, f32[4,128]{1,0:T(4,128)}, u32[]{:S(2)}) copy-start(f32[4,128]{1,0:T(4,128)} %copy-done.33) | copy-start | bytes 6148
  138.6 6.4 %copy-start.36 = (f32[4,128]{1,0:T(4,128)S(1)}, f32[4,128]{1,0:T(4,128)}, u32[]{:S(2)}) copy-start(f32[4,128]{1,0:T(4,128)} %copy-done.35) | copy-start | bytes 6148
  138.6 6.4 %copy-start.38 = (f32[4,128]{1,0:T(4,128)S(1)}, f32[4,128]{1,0:T(4,128)}, u32[]{:S(2)}) copy-start(f32[4,128]{1,0:T(4,128)} %copy-done.37) | copy-start | bytes 6148
  138.6 6.4 %copy-start.40 = (f32[4,128]{1,0:T(4,128)S(1)}, f32[4,128]{1,0:T(4,128)}, u32[]{:S(2)}) copy-start(f32[4,128]{1,0:T(4,128)} %copy-done.39) | copy-start | bytes 6148
  138.7 6.4 %copy-start.46 = (pred[4,128]{1,0:T(4,128)(4,1)S(1)}, pred[4,128]{1,0:T(4,128)(4,1)}, u32[]{:S(2)}) copy-start(pred[4,128]{1,0:T(4,128)(4,1)} %copy-done.45) | copy-start | bytes 1540
  138.7 6.4 %copy-start.48 = (pred[4,128]{1,0:T(4,128)(4,1)S(1)}, pred[4,128]{1,0:T(4,128)(4,1)}, u32[]{:S(2)}) copy-start(pred[4,128]{1,0:T(4,128)(4,1)} %copy-done.47) | copy-start | bytes 1540
  154.4 2.1 %copy-start.12 = (f32[864]{0:T(1024)S(1)}, f32[864]{0:T(1024)}, u32[]{:S(2)}) copy-start(f32[864]{0:T(1024)} %copy-done.11) | copy-start | bytes 10372
  154.4 2.1 %copy-start.14 = (f32[864]{0:T(1024)S(1)}, f32[864]{0:T(1024)}, u32[]{:S(2)}) copy-start(f32[864]{0:T(1024)} %copy-done.13) | copy-start | bytes 10372
  154.4 2.1 %copy-start.16 = (f32[864]{0:T(1024)S(1)}, f32[864]{0:T(1024)}, u32[]{:S(2)}) copy-start(f32[864]{0:T(1024)} %copy-done.15) | copy-start | bytes 10372
  154.4 2.1 %copy-start.44 = (pred[864]{0:T(1024)(128)(4,1)S(1)}, pred[864]{0:T(1024)(128)(4,1)}, u32[]{:S(2)}) copy-start(pred[864]{0:T(1024)(128)(4,1)} %copy-done.43) | copy-start | bytes 2596
  167.4 5.5 %collective-permute-start.13 = (f32[16,4,128]{2,1,0:T(4,128)S(1)}, f32[16,4,128]{2,1,0:T(4,128)S(1)}, u32[]{:S(2)}, u32[]{:S(2)}) collective-permute-start(f32[16,4,128]{2,1,0:T(4,128)S(1)} %copy.134), channel_id=1, source_target_pairs={{0,128},{16,144},{32,160},{48,176},{64,192},{80,208},{96,224},{112... | collective-permute-start | bytes 98312 | tf_op jit(solution)/shard_map/ppermute | solution.py:139
  171.0 3.9 %collective-permute-start.12 = (f32[16,4,128]{2,1,0:T(4,128)S(1)}, f32[16,4,128]{2,1,0:T(4,128)S(1)}, u32[]{:S(2)}, u32[]{:S(2)}) collective-permute-start(f32[16,4,128]{2,1,0:T(4,128)S(1)} %copy.134), channel_id=1, source_target_pairs={{0,64},{16,80},{32,96},{48,112},{64,0},{80,16},{96,32},{112,48},{1... | collective-permute-start | bytes 98312 | tf_op jit(solution)/shard_map/ppermute | solution.py:139
  171.6 5.1 %collective-permute-start.14 = (f32[16,4,128]{2,1,0:T(4,128)S(1)}, f32[16,4,128]{2,1,0:T(4,128)S(1)}, u32[]{:S(2)}, u32[]{:S(2)}) collective-permute-start(f32[16,4,128]{2,1,0:T(4,128)S(1)} %copy.134), channel_id=1, source_target_pairs={{0,192},{16,208},{32,224},{48,240},{64,128},{80,144},{96,160},{112... | collective-permute-start | bytes 98312 | tf_op jit(solution)/shard_map/ppermute | solution.py:139
  176.8 9.0 %collective-permute-start.17 = (f32[16,4,128]{2,1,0:T(4,128)S(1)}, f32[16,4,128]{2,1,0:T(4,128)S(1)}, u32[]{:S(2)}, u32[]{:S(2)}) collective-permute-start(f32[16,4,128]{2,1,0:T(4,128)S(1)} %add_add_fusion.1), channel_id=1, source_target_pairs={{0,48},{16,32},{32,16},{48,0},{64,112},{80,96},{96,80},{112,64},{1... | collective-permute-start | bytes 98312 | tf_op jit(solution)/shard_map/ppermute | solution.py:139
  183.9 4.9 %collective-permute-start.16 = (f32[16,4,128]{2,1,0:T(4,128)S(1)}, f32[16,4,128]{2,1,0:T(4,128)S(1)}, u32[]{:S(2)}, u32[]{:S(2)}) collective-permute-start(f32[16,4,128]{2,1,0:T(4,128)S(1)} %add_add_fusion.1), channel_id=1, source_target_pairs={{0,32},{16,48},{32,0},{48,16},{64,96},{80,112},{96,64},{112,80},{1... | collective-permute-start | bytes 98312 | tf_op jit(solution)/shard_map/ppermute | solution.py:139
  184.7 4.3 %collective-permute-start.15 = (f32[16,4,128]{2,1,0:T(4,128)S(1)}, f32[16,4,128]{2,1,0:T(4,128)S(1)}, u32[]{:S(2)}, u32[]{:S(2)}) collective-permute-start(f32[16,4,128]{2,1,0:T(4,128)S(1)} %add_add_fusion.1), channel_id=1, source_target_pairs={{0,16},{16,0},{32,48},{48,32},{64,80},{80,64},{96,112},{112,96},{1... | collective-permute-start | bytes 98312 | tf_op jit(solution)/shard_map/ppermute | solution.py:139
  (5 other events, 3.9 us)

commit v11 on v7

--- a/solution.py
+++ b/solution.py
@@ -160,7 +160,7 @@
             jnp.zeros_like(along_x_part),
         ]
     )
-    local = jnp.einsum("kv,vrc->krc", table, advected_distribution, precision=lax.Precision.HIGHEST)
+    local = jnp.einsum("kv,vrc->krc", table, advected_distribution, precision=lax.Precision.HIGH)
     totals = vel_sum(local)
     particle_concentration = totals[0]
     average_drift_x = totals[1] / particle_concentration

time: 138 us -> 138 us (level)
  no operation moved by 1% of the time
where the time goes in v11:
time: 138 us; the launch traced here: 137 us
  starting transfers between devices  55.8 us (40%)
  waiting for transfers between devices  50.2 us (36%)
  other arithmetic  22.8 us (17%)
  local copies, waits for them, and re-layouts  5.09 us (4%)
  matrix products  1.78 us (1%)
  between operations  1.66 us (1%)
    ppermute x12, starting transfers between devices, vel_sum(): lax.ppermute(local, 'vel', [(i, i ^ mask) for i in range(count)])  31.8 us
    ppermute x2, waiting for transfers between devices, with_upwind_halo(): lax.ppermute(jnp.where(positive, block[:, rows - 2:rows - 1], block[:, 1:...  21.1 us
    ppermute x12, waiting for transfers between devices, vel_sum(): lax.ppermute(local, 'vel', [(i, i ^ mask) for i in range(count)])  14.2 us
    ppermute x2, starting transfers between devices, with_upwind_halo(): high = lax.ppermute(block[:, :1], 'space', backward)  10.7 us
    ppermute x2, waiting for transfers between devices, with_upwind_halo(): low = lax.ppermute(block[:, rows - 1:], 'space', forward)  9.58 us
    ppermute x2, starting transfers between devices, with_upwind_halo(): lax.ppermute(jnp.where(positive, block[:, rows - 2:rows - 1], block[:, 1:...  9.27 us
    mul x4, other arithmetic, sweep(): flux = number * jnp.where(number > 0, left_face, right_face)  7.28 us
    select_n x2, other arithmetic, approach_increment(): jnp.where(kind_labels == 1, wall_distribution, jnp.where(kind_labels == 2...  5.35 us
  transfers between devices with their start and end apart: 18, of which 15 were waited for; matrix products, arithmetic and copies ran while one was open for 1% of the time, Pallas kernels for 0%

profile of v11, /device:TPU:6, one launch (start us, length us, event | category | flops | bytes accessed | tf_op | source)
XLA Modules:
  0.0 137.3 jit_solution(442169935283762870)
XLA Ops:
  0.6 1.6 %copy.98 = f32[864,4,128]{2,0,1:T(8,128)S(1)} copy(f32[864,4,128]{2,1,0:T(4,128)} %param.4) | data formatting | bytes 3538944 | tf_op args[0]
  2.3 0.6 dynamic_slice.6
  3.5 1.1 fusion.159
  4.6 1.9 %collective-permute-start = (f32[864,1,128]{2,0,1:T(8,128)}, f32[864,1,128]{2,0,1:T(8,128)S(1)}, u32[]{:S(2)}, u32[]{:S(2)}) collective-permute-start(f32[864,1,128]{2,0,1:T(8,128)} %get-tuple-element.19), channel_id=1, source_target_pairs={{0,1},{1,2},{2,3},{3,4},{4,5},{5,6},{6,7},{7,8},{8,9},{9,10},{10,1... | collective-permute-start | bytes 1327112 | tf_op jit(solution)/shard_map/ppermute | solution.py:57
  6.5 8.8 %collective-permute-start.1 = (f32[864,1,128]{2,0,1:T(8,128)}, f32[864,1,128]{2,0,1:T(8,128)S(1)}, u32[]{:S(2)}, u32[]{:S(2)}) collective-permute-start(f32[864,1,128]{2,0,1:T(8,128)} %get-tuple-element.20), channel_id=1, source_target_pairs={{1,0},{2,1},{3,2},{4,3},{5,4},{6,5},{7,6},{8,7},{9,8},{10,9},{11,1... | collective-permute-start | bytes 1327112 | tf_op jit(solution)/shard_map/ppermute | solution.py:58
  15.3 2.6 %collective-permute-start.2 = (f32[864,1,128]{2,0,1:T(8,128)}, f32[864,1,128]{2,0,1:T(8,128)S(1)}, u32[]{:S(2)}, u32[]{:S(2)}) collective-permute-start(f32[864,1,128]{2,0,1:T(8,128)} %get-tuple-element.21), channel_id=1, source_target_pairs={{1,0},{2,1},{3,2},{4,3},{5,4},{6,5},{7,6},{8,7},{9,8},{10,9},{11,1... | collective-permute-start | bytes 1327112 | tf_op jit(solution)/shard_map/ppermute | solution.py:64
  18.1 0.1 fusion.86
  18.1 0.1 add_add_fusion.4
  18.2 0.1 fusion.147
  18.3 0.1 fusion.149
  18.4 0.1 fusion.151
  18.5 0.1 fusion.153
  18.6 0.1 stack.2
  18.8 0.9 collective-permute-done
  19.7 5.3 %collective-permute-done.1 = f32[864,1,128]{2,0,1:T(8,128)S(1)} collective-permute-done((f32[864,1,128]{2,0,1:T(8,128)}, f32[864,1,128]{2,0,1:T(8,128)S(1)}, u32[]{:S(2)}, u32[]{:S(2)}) %collective-permute-start.1) | collective-permute-done | bytes 442400 | tf_op jit(solution)/shard_map/ppermute | solution.py:58
  25.0 5.9 %collective-permute-done.2 = f32[864,1,128]{2,0,1:T(8,128)S(1)} collective-permute-done((f32[864,1,128]{2,0,1:T(8,128)}, f32[864,1,128]{2,0,1:T(8,128)S(1)}, u32[]{:S(2)}, u32[]{:S(2)}) %collective-permute-start.2) | collective-permute-done | bytes 442400 | tf_op jit(solution)/shard_map/ppermute | solution.py:64
  30.9 0.3 maximum_subtract_fusion
  31.2 0.3 minimum_maximum_fusion.3
  31.5 1.1 fusion.16
  32.6 0.4 copy-done
  33.0 0.2 fusion.61
  33.2 1.9 %fusion.3 = f32[864,4,131]{2,0,1:T(8,128)S(1)} fusion(f32[864,4,128]{2,0,1:T(8,128)S(1)} %fusion.61), kind=kLoop, calls=%fused_computation.11 | loop fusion | flops 452736 | bytes 3580416 | tf_op jit(solution)/shard_map/sub | solution.py:93
  35.1 1.0 minimum_maximum_fusion.1
  36.1 2.6 %fusion.2 = f32[864,4,129]{2,0,1:T(8,128)S(1)} fusion(f32[864,4,128]{2,0,1:T(8,128)S(1)} %fusion.61, f32[864,4,130]{2,0,1:T(8,128)S(1)} %minimum_maximum_fusion.1, f32[864]{0:T(1024)S(1)} %get-tuple-element.48, f32[864]{0:T(1024)S(1)} %get-tuple-element.49, f32[864]{0:T(1024)S(1)} %broadcast_multiply_fusion, pred[864]{0:T(1024)(128)(4,1)S(1)} %broadcast_compare_fusion), kind=kLoop, calls=%fused_computation.10 | loop fusion | flops 2674944 | bytes 7130592 | tf_op jit(solution)/shard_map/mul | solution.py:101
  38.7 0.9 fusion.64
  39.6 1.7 %collective-permute-start.3 = (f32[16,4,128]{2,1,0:T(4,128)S(1)}, f32[16,4,128]{2,1,0:T(4,128)S(1)}, u32[]{:S(2)}, u32[]{:S(2)}) collective-permute-start(f32[16,4,128]{2,1,0:T(4,128)S(1)} %copy.100), channel_id=1, source_target_pairs={{0,64},{16,80},{32,96},{48,112},{64,0},{80,16},{96,32},{112,48},{1... | collective-permute-start | bytes 98312 | tf_op jit(solution)/shard_map/ppermute | solution.py:133
  41.2 18.2 %collective-permute-start.4 = (f32[16,4,128]{2,1,0:T(4,128)S(1)}, f32[16,4,128]{2,1,0:T(4,128)S(1)}, u32[]{:S(2)}, u32[]{:S(2)}) collective-permute-start(f32[16,4,128]{2,1,0:T(4,128)S(1)} %copy.100), channel_id=1, source_target_pairs={{0,128},{16,144},{32,160},{48,176},{64,192},{80,208},{96,224},{112... | collective-permute-start | bytes 98312 | tf_op jit(solution)/shard_map/ppermute | solution.py:133
  59.5 2.2 %collective-permute-done.4 = f32[16,4,128]{2,1,0:T(4,128)S(1)} collective-permute-done((f32[16,4,128]{2,1,0:T(4,128)S(1)}, f32[16,4,128]{2,1,0:T(4,128)S(1)}, u32[]{:S(2)}, u32[]{:S(2)}) %collective-permute-start.4) | collective-permute-done | bytes 32800 | tf_op jit(solution)/shard_map/ppermute | solution.py:133
  61.7 2.9 %collective-permute-done.5 = f32[16,4,128]{2,1,0:T(4,128)S(1)} collective-permute-done((f32[16,4,128]{2,1,0:T(4,128)S(1)}, f32[16,4,128]{2,1,0:T(4,128)S(1)}, u32[]{:S(2)}, u32[]{:S(2)}) %collective-permute-start.5) | collective-permute-done | bytes 32800 | tf_op jit(solution)/shard_map/ppermute | solution.py:133
  64.6 0.1 collective-permute-start.7
  64.7 1.7 %collective-permute-start.8 = (f32[16,4,128]{2,1,0:T(4,128)S(1)}, f32[16,4,128]{2,1,0:T(4,128)S(1)}, u32[]{:S(2)}, u32[]{:S(2)}) collective-permute-start(f32[16,4,128]{2,1,0:T(4,128)S(1)} %add_add_fusion.3), channel_id=1, source_target_pairs={{0,48},{16,32},{32,16},{48,0},{64,112},{80,96},{96,80},{112,64},{1... | collective-permute-start | bytes 98312 | tf_op jit(solution)/shard_map/ppermute | solution.py:133
  66.4 1.8 %collective-permute-start.6 = (f32[16,4,128]{2,1,0:T(4,128)S(1)}, f32[16,4,128]{2,1,0:T(4,128)S(1)}, u32[]{:S(2)}, u32[]{:S(2)}) collective-permute-start(f32[16,4,128]{2,1,0:T(4,128)S(1)} %add_add_fusion.3), channel_id=1, source_target_pairs={{0,16},{16,0},{32,48},{48,32},{64,80},{80,64},{96,112},{112,96},{1... | collective-permute-start | bytes 98312 | tf_op jit(solution)/shard_map/ppermute | solution.py:133
  68.2 1.3 collective-permute-done.7
  69.5 1.1 collective-permute-done.8
  70.6 0.1 collective-permute-done.6
  70.7 2.7 %fusion.37 = f32[864,4,128]{2,0,1:T(8,128)S(1)} fusion(f32[4,128]{1,0:T(4,128)S(1)} %get-tuple-element.29, f32[4,128]{1,0:T(4,128)S(1)} %get-tuple-element.42, f32[4,128]{1,0:T(4,128)S(1)} %fusion.119, f32[4,128]{1,0:T(4,128)S(1)} %get-tuple-element.36, f32[4,128]{1,0:T(4,128)S(1)} %get-tuple-element.37, f32[4,128]{1,0:T(4,128)S(1)} %get-tuple-element.43, ...), kind=kLoop, calls=%fused_computation.71 | loop fusion | flops 13713408 | bytes 7120768 | tf_op jit(solution)/shard_map/jit(_where)/select_n | solution.py:259
  73.4 0.1 fusion.158
  73.5 1.9 %collective-permute-start.10 = (f32[864,1,128]{2,0,1:T(8,128)S(1)}, f32[864,1,128]{2,0,1:T(8,128)S(1)}, u32[]{:S(2)}, u32[]{:S(2)}) collective-permute-start(f32[864,1,128]{2,0,1:T(8,128)S(1)} %get-tuple-element.18), channel_id=1, source_target_pairs={{1,0},{2,1},{3,2},{4,3},{5,4},{6,5},{7,6},{8,7},{9,8},{10,9},{11,1... | collective-permute-start | bytes 1327112 | tf_op jit(solution)/shard_map/ppermute | solution.py:58
  75.4 6.7 %collective-permute-start.11 = (f32[864,1,128]{2,0,1:T(8,128)S(1)}, f32[864,1,128]{2,0,1:T(8,128)S(1)}, u32[]{:S(2)}, u32[]{:S(2)}) collective-permute-start(f32[864,1,128]{2,0,1:T(8,128)S(1)} %get-tuple-element.17), channel_id=1, source_target_pairs={{1,0},{2,1},{3,2},{4,3},{5,4},{6,5},{7,6},{8,7},{9,8},{10,9},{11,1... | collective-permute-start | bytes 1327112 | tf_op jit(solution)/shard_map/ppermute | solution.py:64
  82.1 2.1 %collective-permute-start.9 = (f32[864,1,128]{2,0,1:T(8,128)S(1)}, f32[864,1,128]{2,0,1:T(8,128)S(1)}, u32[]{:S(2)}, u32[]{:S(2)}) collective-permute-start(f32[864,1,128]{2,0,1:T(8,128)S(1)} %get-tuple-element.16), channel_id=1, source_target_pairs={{0,1},{1,2},{2,3},{3,4},{4,5},{5,6},{6,7},{7,8},{8,9},{9,10},{10,1... | collective-permute-start | bytes 1327112 | tf_op jit(solution)/shard_map/ppermute | solution.py:57
  84.2 15.3 %collective-permute-done.11 = f32[864,1,128]{2,0,1:T(8,128)S(1)} collective-permute-done((f32[864,1,128]{2,0,1:T(8,128)S(1)}, f32[864,1,128]{2,0,1:T(8,128)S(1)}, u32[]{:S(2)}, u32[]{:S(2)}) %collective-permute-start.11) | collective-permute-done | bytes 442400 | tf_op jit(solution)/shard_map/ppermute | solution.py:64
  99.5 8.7 %collective-permute-done.9 = f32[864,1,128]{2,0,1:T(8,128)S(1)} collective-permute-done((f32[864,1,128]{2,0,1:T(8,128)S(1)}, f32[864,1,128]{2,0,1:T(8,128)S(1)}, u32[]{:S(2)}, u32[]{:S(2)}) %collective-permute-start.9) | collective-permute-done | bytes 442400 | tf_op jit(solution)/shard_map/ppermute | solution.py:57
  108.2 0.3 maximum_subtract_fusion.1
  108.5 0.3 minimum_maximum_fusion.2
  108.9 1.1 fusion.12
  109.9 0.2 fusion.59
  110.1 1.9 %fusion.8 = f32[864,4,131]{2,0,1:T(8,128)S(1)} fusion(f32[864,4,128]{2,0,1:T(8,128)S(1)} %fusion.59), kind=kLoop, calls=%fused_computation.16 | loop fusion | flops 452736 | bytes 3580416 | tf_op jit(solution)/shard_map/sub | solution.py:93
  112.0 1.0 minimum_maximum_fusion
  113.0 2.6 %fusion.7 = f32[864,4,129]{2,0,1:T(8,128)S(1)} fusion(f32[864,4,128]{2,0,1:T(8,128)S(1)} %fusion.59, f32[864,4,130]{2,0,1:T(8,128)S(1)} %minimum_maximum_fusion, f32[864]{0:T(1024)S(1)} %get-tuple-element.48, f32[864]{0:T(1024)S(1)} %get-tuple-element.49, f32[864]{0:T(1024)S(1)} %broadcast_multiply_fusion, pred[864]{0:T(1024)(128)(4,1)S(1)} %broadcast_compare_fusion), kind=kLoop, calls=%fused_computation.15 | loop fusion | flops 2674944 | bytes 7130592 | tf_op jit(solution)/shard_map/mul | solution.py:101
  115.6 0.9 fusion.62
  116.5 0.1 collective-permute-start.12
  116.6 3.5 %collective-permute-start.13 = (f32[16,4,128]{2,1,0:T(4,128)S(1)}, f32[16,4,128]{2,1,0:T(4,128)S(1)}, u32[]{:S(2)}, u32[]{:S(2)}) collective-permute-start(f32[16,4,128]{2,1,0:T(4,128)S(1)} %copy.104), channel_id=1, source_target_pairs={{0,128},{16,144},{32,160},{48,176},{64,192},{80,208},{96,224},{112... | collective-permute-start | bytes 98312 | tf_op jit(solution)/shard_map/ppermute | solution.py:133
  120.2 1.2 collective-permute-start.14
  121.3 1.1 collective-permute-done.13
  122.4 2.9 %collective-permute-done.14 = f32[16,4,128]{2,1,0:T(4,128)S(1)} collective-permute-done((f32[16,4,128]{2,1,0:T(4,128)S(1)}, f32[16,4,128]{2,1,0:T(4,128)S(1)}, u32[]{:S(2)}, u32[]{:S(2)}) %collective-permute-start.14) | collective-permute-done | bytes 32800 | tf_op jit(solution)/shard_map/ppermute | solution.py:133
  125.3 0.1 collective-permute-start.16
  125.4 2.0 %collective-permute-start.17 = (f32[16,4,128]{2,1,0:T(4,128)S(1)}, f32[16,4,128]{2,1,0:T(4,128)S(1)}, u32[]{:S(2)}, u32[]{:S(2)}) collective-permute-start(f32[16,4,128]{2,1,0:T(4,128)S(1)} %add_add_fusion.1), channel_id=1, source_target_pairs={{0,48},{16,32},{32,16},{48,0},{64,112},{80,96},{96,80},{112,64},{1... | collective-permute-start | bytes 98312 | tf_op jit(solution)/shard_map/ppermute | solution.py:133
  127.4 1.5 %collective-permute-start.15 = (f32[16,4,128]{2,1,0:T(4,128)S(1)}, f32[16,4,128]{2,1,0:T(4,128)S(1)}, u32[]{:S(2)}, u32[]{:S(2)}) collective-permute-start(f32[16,4,128]{2,1,0:T(4,128)S(1)} %add_add_fusion.1), channel_id=1, source_target_pairs={{0,16},{16,0},{32,48},{48,32},{64,80},{80,64},{96,112},{112,96},{1... | collective-permute-start | bytes 98312 | tf_op jit(solution)/shard_map/ppermute | solution.py:133
  128.9 1.3 collective-permute-done.16
  130.2 1.0 collective-permute-done.17
  131.2 0.3 collective-permute-done.15
  131.6 0.6 fusion.144
  132.2 2.7 %fusion.57 = f32[864,4,128]{2,0,1:T(8,128)S(1)} fusion(f32[4,128]{1,0:T(4,128)S(1)} %get-tuple-element.32, f32[4,128]{1,0:T(4,128)S(1)} %get-tuple-element.38, f32[4,128]{1,0:T(4,128)S(1)} %get-tuple-element.31, f32[4,128]{1,0:T(4,128)S(1)} %get-tuple-element.23, f32[4,128]{1,0:T(4,128)S(1)} %get-tuple-element.22, f32[4,128]{1,0:T(4,128)S(1)} %get-tuple-element.39, ...), kind=kLoop, calls=%fused_computation.91 | loop fusion | flops 13713408 | bytes 7120768 | tf_op jit(solution)/shard_map/jit(_where)/select_n | solution.py:259
  134.9 2.3 %copy.107 = f32[864,4,128]{2,1,0:T(4,128)} copy(f32[864,4,128]{2,0,1:T(8,128)S(1)} %fusion.57) | data formatting | bytes 3538944
  (34 shorter events, 0.5 us)
Async XLA Ops:
  0.6 1.6 %copy-start.2 = (s32[16]{0:T(128)S(1)}, s32[16]{0:T(128)}, u32[]{:S(2)}) copy-start(s32[16]{0:T(128)} %constant.97.clone) | copy-start | bytes 196
  2.2 16.6 %copy-start.1 = (s32[4,128]{1,0:T(4,128)S(1)}, s32[4,128]{1,0:T(4,128)}, u32[]{:S(2)}) copy-start(s32[4,128]{1,0:T(4,128)} %param.5) | copy-start | bytes 6148
  4.6 15.1 %collective-permute-start = (f32[864,1,128]{2,0,1:T(8,128)}, f32[864,1,128]{2,0,1:T(8,128)S(1)}, u32[]{:S(2)}, u32[]{:S(2)}) collective-permute-start(f32[864,1,128]{2,0,1:T(8,128)} %get-tuple-element.19), channel_id=1, source_target_pairs={{0,1},{1,2},{2,3},{3,4},{4,5},{5,6},{6,7},{7,8},{8,9},{9,10},{10,1... | collective-permute-start | bytes 1327112 | tf_op jit(solution)/shard_map/ppermute | solution.py:57
  6.5 18.5 %collective-permute-start.1 = (f32[864,1,128]{2,0,1:T(8,128)}, f32[864,1,128]{2,0,1:T(8,128)S(1)}, u32[]{:S(2)}, u32[]{:S(2)}) collective-permute-start(f32[864,1,128]{2,0,1:T(8,128)} %get-tuple-element.20), channel_id=1, source_target_pairs={{1,0},{2,1},{3,2},{4,3},{5,4},{6,5},{7,6},{8,7},{9,8},{10,9},{11,1... | collective-permute-start | bytes 1327112 | tf_op jit(solution)/shard_map/ppermute | solution.py:58
  15.3 15.5 %collective-permute-start.2 = (f32[864,1,128]{2,0,1:T(8,128)}, f32[864,1,128]{2,0,1:T(8,128)S(1)}, u32[]{:S(2)}, u32[]{:S(2)}) collective-permute-start(f32[864,1,128]{2,0,1:T(8,128)} %get-tuple-element.21), channel_id=1, source_target_pairs={{1,0},{2,1},{3,2},{4,3},{5,4},{6,5},{7,6},{8,7},{9,8},{10,9},{11,1... | collective-permute-start | bytes 1327112 | tf_op jit(solution)/shard_map/ppermute | solution.py:64
  31.5 1.5 %copy-start = (f32[864,4,128]{2,1,0:T(4,128)S(1)}, f32[864,4,128]{2,1,0:T(4,128)}, u32[]{:S(2)}) copy-start(f32[864,4,128]{2,1,0:T(4,128)} %param.4) | copy-start | bytes 5308420
  39.6 19.9 %collective-permute-start.3 = (f32[16,4,128]{2,1,0:T(4,128)S(1)}, f32[16,4,128]{2,1,0:T(4,128)S(1)}, u32[]{:S(2)}, u32[]{:S(2)}) collective-permute-start(f32[16,4,128]{2,1,0:T(4,128)S(1)} %copy.100), channel_id=1, source_target_pairs={{0,64},{16,80},{32,96},{48,112},{64,0},{80,16},{96,32},{112,48},{1... | collective-permute-start | bytes 98312 | tf_op jit(solution)/shard_map/ppermute | solution.py:133
  41.2 20.4 %collective-permute-start.4 = (f32[16,4,128]{2,1,0:T(4,128)S(1)}, f32[16,4,128]{2,1,0:T(4,128)S(1)}, u32[]{:S(2)}, u32[]{:S(2)}) collective-permute-start(f32[16,4,128]{2,1,0:T(4,128)S(1)} %copy.100), channel_id=1, source_target_pairs={{0,128},{16,144},{32,160},{48,176},{64,192},{80,208},{96,224},{112... | collective-permute-start | bytes 98312 | tf_op jit(solution)/shard_map/ppermute | solution.py:133
  59.4 5.1 %collective-permute-start.5 = (f32[16,4,128]{2,1,0:T(4,128)S(1)}, f32[16,4,128]{2,1,0:T(4,128)S(1)}, u32[]{:S(2)}, u32[]{:S(2)}) collective-permute-start(f32[16,4,128]{2,1,0:T(4,128)S(1)} %copy.100), channel_id=1, source_target_pairs={{0,192},{16,208},{32,224},{48,240},{64,128},{80,144},{96,160},{112... | collective-permute-start | bytes 98312 | tf_op jit(solution)/shard_map/ppermute | solution.py:133
  64.6 4.9 %collective-permute-start.7 = (f32[16,4,128]{2,1,0:T(4,128)S(1)}, f32[16,4,128]{2,1,0:T(4,128)S(1)}, u32[]{:S(2)}, u32[]{:S(2)}) collective-permute-start(f32[16,4,128]{2,1,0:T(4,128)S(1)} %add_add_fusion.3), channel_id=1, source_target_pairs={{0,32},{16,48},{32,0},{48,16},{64,96},{80,112},{96,64},{112,80},{1... | collective-permute-start | bytes 98312 | tf_op jit(solution)/shard_map/ppermute | solution.py:133
  64.7 5.9 %collective-permute-start.8 = (f32[16,4,128]{2,1,0:T(4,128)S(1)}, f32[16,4,128]{2,1,0:T(4,128)S(1)}, u32[]{:S(2)}, u32[]{:S(2)}) collective-permute-start(f32[16,4,128]{2,1,0:T(4,128)S(1)} %add_add_fusion.3), channel_id=1, source_target_pairs={{0,48},{16,32},{32,16},{48,0},{64,112},{80,96},{96,80},{112,64},{1... | collective-permute-start | bytes 98312 | tf_op jit(solution)/shard_map/ppermute | solution.py:133
  66.4 4.3 %collective-permute-start.6 = (f32[16,4,128]{2,1,0:T(4,128)S(1)}, f32[16,4,128]{2,1,0:T(4,128)S(1)}, u32[]{:S(2)}, u32[]{:S(2)}) collective-permute-start(f32[16,4,128]{2,1,0:T(4,128)S(1)} %add_add_fusion.3), channel_id=1, source_target_pairs={{0,16},{16,0},{32,48},{48,32},{64,80},{80,64},{96,112},{112,96},{1... | collective-permute-start | bytes 98312 | tf_op jit(solution)/shard_map/ppermute | solution.py:133
  73.5 10.7 %collective-permute-start.10 = (f32[864,1,128]{2,0,1:T(8,128)S(1)}, f32[864,1,128]{2,0,1:T(8,128)S(1)}, u32[]{:S(2)}, u32[]{:S(2)}) collective-permute-start(f32[864,1,128]{2,0,1:T(8,128)S(1)} %get-tuple-element.18), channel_id=1, source_target_pairs={{1,0},{2,1},{3,2},{4,3},{5,4},{6,5},{7,6},{8,7},{9,8},{10,9},{11,1... | collective-permute-start | bytes 1327112 | tf_op jit(solution)/shard_map/ppermute | solution.py:58
  75.4 24.1 %collective-permute-start.11 = (f32[864,1,128]{2,0,1:T(8,128)S(1)}, f32[864,1,128]{2,0,1:T(8,128)S(1)}, u32[]{:S(2)}, u32[]{:S(2)}) collective-permute-start(f32[864,1,128]{2,0,1:T(8,128)S(1)} %get-tuple-element.17), channel_id=1, source_target_pairs={{1,0},{2,1},{3,2},{4,3},{5,4},{6,5},{7,6},{8,7},{9,8},{10,9},{11,1... | collective-permute-start | bytes 1327112 | tf_op jit(solution)/shard_map/ppermute | solution.py:64
  82.1 26.1 %collective-permute-start.9 = (f32[864,1,128]{2,0,1:T(8,128)S(1)}, f32[864,1,128]{2,0,1:T(8,128)S(1)}, u32[]{:S(2)}, u32[]{:S(2)}) collective-permute-start(f32[864,1,128]{2,0,1:T(8,128)S(1)} %get-tuple-element.16), channel_id=1, source_target_pairs={{0,1},{1,2},{2,3},{3,4},{4,5},{5,6},{6,7},{7,8},{8,9},{9,10},{10,1... | collective-permute-start | bytes 1327112 | tf_op jit(solution)/shard_map/ppermute | solution.py:57
  116.5 4.8 %collective-permute-start.12 = (f32[16,4,128]{2,1,0:T(4,128)S(1)}, f32[16,4,128]{2,1,0:T(4,128)S(1)}, u32[]{:S(2)}, u32[]{:S(2)}) collective-permute-start(f32[16,4,128]{2,1,0:T(4,128)S(1)} %copy.104), channel_id=1, source_target_pairs={{0,64},{16,80},{32,96},{48,112},{64,0},{80,16},{96,32},{112,48},{1... | collective-permute-start | bytes 98312 | tf_op jit(solution)/shard_map/ppermute | solution.py:133
  116.6 5.8 %collective-permute-start.13 = (f32[16,4,128]{2,1,0:T(4,128)S(1)}, f32[16,4,128]{2,1,0:T(4,128)S(1)}, u32[]{:S(2)}, u32[]{:S(2)}) collective-permute-start(f32[16,4,128]{2,1,0:T(4,128)S(1)} %copy.104), channel_id=1, source_target_pairs={{0,128},{16,144},{32,160},{48,176},{64,192},{80,208},{96,224},{112... | collective-permute-start | bytes 98312 | tf_op jit(solution)/shard_map/ppermute | solution.py:133
  120.2 5.1 %collective-permute-start.14 = (f32[16,4,128]{2,1,0:T(4,128)S(1)}, f32[16,4,128]{2,1,0:T(4,128)S(1)}, u32[]{:S(2)}, u32[]{:S(2)}) collective-permute-start(f32[16,4,128]{2,1,0:T(4,128)S(1)} %copy.104), channel_id=1, source_target_pairs={{0,192},{16,208},{32,224},{48,240},{64,128},{80,144},{96,160},{112... | collective-permute-start | bytes 98312 | tf_op jit(solution)/shard_map/ppermute | solution.py:133
  125.3 4.9 %collective-permute-start.16 = (f32[16,4,128]{2,1,0:T(4,128)S(1)}, f32[16,4,128]{2,1,0:T(4,128)S(1)}, u32[]{:S(2)}, u32[]{:S(2)}) collective-permute-start(f32[16,4,128]{2,1,0:T(4,128)S(1)} %add_add_fusion.1), channel_id=1, source_target_pairs={{0,32},{16,48},{32,0},{48,16},{64,96},{80,112},{96,64},{112,80},{1... | collective-permute-start | bytes 98312 | tf_op jit(solution)/shard_map/ppermute | solution.py:133
  125.4 5.8 %collective-permute-start.17 = (f32[16,4,128]{2,1,0:T(4,128)S(1)}, f32[16,4,128]{2,1,0:T(4,128)S(1)}, u32[]{:S(2)}, u32[]{:S(2)}) collective-permute-start(f32[16,4,128]{2,1,0:T(4,128)S(1)} %add_add_fusion.1), channel_id=1, source_target_pairs={{0,48},{16,32},{32,16},{48,0},{64,112},{80,96},{96,80},{112,64},{1... | collective-permute-start | bytes 98312 | tf_op jit(solution)/shard_map/ppermute | solution.py:133
  127.4 4.1 %collective-permute-start.15 = (f32[16,4,128]{2,1,0:T(4,128)S(1)}, f32[16,4,128]{2,1,0:T(4,128)S(1)}, u32[]{:S(2)}, u32[]{:S(2)}) collective-permute-start(f32[16,4,128]{2,1,0:T(4,128)S(1)} %add_add_fusion.1), channel_id=1, source_target_pairs={{0,16},{16,0},{32,48},{48,32},{64,80},{80,64},{96,112},{112,96},{1... | collective-permute-start | bytes 98312 | tf_op jit(solution)/shard_map/ppermute | solution.py:133
